TPU v7x, 32 devices: a whole 2x2x4 slice. The times are simulated.
32 devices in a mesh: groups: 2 (over x), date: 8 (over z, y), row: 2 (over core).
Axes of the slice: x: 2, y: 2, z: 4, core: 2. Of those that a mesh axis runs over, the one named last changes fastest.
Arguments:
- scenes: bfloat16 [16, 4, 512, 1024], P(('groups', 'date'), None, 'row'), parts along dimension 0, may hold values from -6 to 6
- resample_taps: float32 [2, 4, 7], replicated, may hold values from 0 to 0.35
- clear_mask: int32 [16, 128, 8], P('groups', ('row', 'date')), parts along dimension 0, may hold values 0 or 1
Outputs:
- smooth_fine: bfloat16 [16, 4, 512, 1024], P('groups', None, ('row', 'date')), parts along dimension 0
- smooth_half: bfloat16 [16, 4, 256, 512], P('groups', None, ('row', 'date')), parts along dimension 0
- smooth_quarter: bfloat16 [16, 4, 128, 256], P('groups', None, ('row', 'date')), parts along dimension 0
There are 2 independent parts, one for each index of `groups`. A program takes and returns all parts, laid end to end along the dimension named above; an argument that names none is the same for every part. Nothing has to cross between parts.
Inputs may be any that keep to these rules, and one draw needn't show every extreme that they name: `clear_mask`: 1 marks a clear block, 0 a cloudy one.
All inputs are finite; a program needn't handle non-finite values.
Results may differ from a plain program's by a relative error of at most 0.005.
Values may be sent and summed in bfloat16 or wider, within the bound.
No kernel may reach another device: no remote copies, remote signals or barrier semaphores. Data moves between devices by JAX's collectives and lax.ppermute only.
A program may use at most 128 MiB of HBM per device.

v0:
```python
import math

import jax
import jax.numpy as jnp
from jax import lax
from jax.sharding import PartitionSpec as P

gap_weights = [math.exp(-((k - 4) ** 2) / 8.0) for k in range(9)]
savgol_coeffs = [c / 231.0 for c in [-21.0, 14.0, 39.0, 54.0, 59.0, 54.0, 39.0, 14.0, -21.0]]
pyramid_filter = [0.125, 0.375, 0.375, 0.125]


def padded(block, sides, width):
    for axis, dim in sides:
        count = lax.axis_size(axis)
        forward = [(i, i + 1) for i in range(count - 1)]
        backward = [(target, source) for source, target in forward]
        low = lax.ppermute(
            lax.slice_in_dim(block, block.shape[dim] - width, None, axis=dim), axis, forward
        )
        high = lax.ppermute(lax.slice_in_dim(block, 0, width, axis=dim), axis, backward)
        block = jnp.concatenate([low, block, high], axis=dim)
    return block


def valid_taps(values, taps, axis):
    count = values.shape[axis] - 6
    total = jnp.zeros(values.shape[:axis] + (count,) + values.shape[axis + 1 :], jnp.float32)
    for k in range(7):
        shape = [1] * values.ndim
        shape[-3] = taps.shape[0]
        total = total + taps[:, k].reshape(shape) * lax.slice_in_dim(values, k, k + count, 1, axis)
    return total


def column_resample(values, taps):
    width = values.shape[3]
    source = lax.broadcasted_iota(jnp.int32, (width, width), 0)
    target = lax.broadcasted_iota(jnp.int32, (width, width), 1)
    offset = source - target + 3
    table = jnp.zeros((taps.shape[0], width, width), jnp.float32)
    for k in range(7):
        table = table + taps[:, k][:, None, None] * (offset == k).astype(jnp.float32)[None]
    return jnp.einsum(
        "tbrc,bcd->tbrd", values.astype(jnp.float32), table, precision=lax.Precision.HIGHEST
    )


def halve_columns(values):
    width = values.shape[3]
    source = lax.broadcasted_iota(jnp.int32, (width, width // 2), 0)
    target = lax.broadcasted_iota(jnp.int32, (width, width // 2), 1)
    place = source - 2 * target + 1
    table = jnp.zeros((width, width // 2), jnp.float32)
    for p in range(4):
        table = table + pyramid_filter[p] * (place == p).astype(jnp.float32)
    return jnp.dot(values, table, precision=lax.Precision.HIGHEST)


def halve_rows(extended):
    pairs_count = extended.shape[2] // 2
    pairs = extended.reshape(extended.shape[:2] + (pairs_count, 2) + extended.shape[3:])
    even = pairs[:, :, :, 0]
    odd = pairs[:, :, :, 1]
    return (
        pyramid_filter[0] * even[:, :, :-1]
        + pyramid_filter[1] * odd[:, :, :-1]
        + pyramid_filter[2] * even[:, :, 1:]
        + pyramid_filter[3] * odd[:, :, 1:]
    )


def decimate_rim(extended):
    return halve_columns(halve_rows(extended))


def keep_rows(values, first, total):
    places = first + lax.iota(jnp.int32, values.shape[2])
    inside = (places >= 0) & (places < total)
    return jnp.where(inside[None, None, :, None], values, 0.0)


def smooth(level, clear):
    values = level.astype(jnp.float32)
    dates = values.shape[0]
    clear4 = clear[:, None]
    weight = 0.1 + 0.9 * clear4
    weighted = jnp.pad(weight * values, ((4, 4), (0, 0), (0, 0), (0, 0)))
    weight_pad = jnp.pad(weight, ((4, 4), (0, 0), (0, 0), (0, 0)))
    numer = jnp.zeros_like(values)
    denom = jnp.zeros_like(weight)
    for k in range(9):
        numer = numer + gap_weights[k] * weighted[k : k + dates]
        denom = denom + gap_weights[k] * weight_pad[k : k + dates]
    filled = clear4 * values + (1.0 - clear4) * (numer / denom)
    edged = jnp.pad(filled, ((4, 4), (0, 0), (0, 0), (0, 0)), mode="edge")
    result = jnp.zeros_like(values)
    for k in range(9):
        result = result + savgol_coeffs[k] * edged[k : k + dates]
    return result.astype(jnp.bfloat16)


def expand_mask(clear_mask, row_rep, col_rep):
    grown = jnp.repeat(jnp.repeat(clear_mask, row_rep, axis=1), col_rep, axis=2)
    return grown.astype(jnp.float32)


def local(scenes, resample_taps, clear_mask):
    rows = scenes.shape[2]
    extended = padded(scenes, (("row", 2),), 6)
    across = column_resample(extended, resample_taps[0])
    resampled_wide = valid_taps(across, resample_taps[1], 2)
    band_index = lax.axis_index("row")
    total_rows = rows * lax.axis_size("row")
    resampled_wide = keep_rows(resampled_wide, band_index * rows - 3, total_rows)
    half_wide = decimate_rim(resampled_wide)
    half_wide = keep_rows(half_wide, band_index * (rows // 2) - 1, total_rows // 2)
    resampled = resampled_wide[:, :, 3 : 3 + rows]
    half = half_wide[:, :, 1 : 1 + rows // 2]
    quarter = decimate_rim(half_wide)
    level_zero = resampled.astype(jnp.bfloat16)
    level_one = half.astype(jnp.bfloat16)
    level_two = quarter.astype(jnp.bfloat16)
    clear_fine = expand_mask(clear_mask, 4, 128)
    clear_half = expand_mask(clear_mask, 2, 64)
    clear_quarter = expand_mask(clear_mask, 1, 32)
    smooth_fine = smooth(
        lax.all_to_all(level_zero, "date", split_axis=2, concat_axis=0, tiled=True), clear_fine
    )
    smooth_half = smooth(
        lax.all_to_all(level_one, "date", split_axis=2, concat_axis=0, tiled=True), clear_half
    )
    smooth_quarter = smooth(
        lax.all_to_all(level_two, "date", split_axis=2, concat_axis=0, tiled=True), clear_quarter
    )
    return (smooth_fine, smooth_half, smooth_quarter)


def solution(mesh):
    in_specs = (P(("groups", "date"), None, "row", None), P(), P("groups", ("row", "date"), None))
    out_specs = (
        P("groups", None, ("row", "date"), None),
        P("groups", None, ("row", "date"), None),
        P("groups", None, ("row", "date"), None),
    )
    return jax.shard_map(local, mesh=mesh, in_specs=in_specs, out_specs=out_specs, check_vma=False)
```

profile of v0, /device:TPU:0, one launch (start us, length us, event | category | flops | bytes accessed | tf_op | source)
XLA Modules:
  0.0 176.9 jit_solution(12469758215546184341)
XLA Ops:
  0.6 0.9 fusion.313
  1.5 2.4 %collective-permute-start = (bf16[1,4,6,1024]{3,2,1,0:T(8,128)(2,1)S(1)}, bf16[1,4,6,1024]{3,2,1,0:T(8,128)(2,1)S(1)}, u32[]{:S(2)}, u32[]{:S(2)}) collective-permute-start(bf16[1,4,6,1024]{3,2,1,0:T(8,128)(2,1)S(1)} %get-tuple-element.21), channel_id=1, source_target_pairs={{0,1},{2,3},{4,5},{6,7},{8,9},{10,11},{12,13},{14,15},{16,17},{18,... | collective-permute-start | bytes 147464 | tf_op jit(solution)/shard_map/ppermute | solution.py:18
  3.9 1.3 collective-permute-start.1
  5.2 4.3 %fusion.83 = (f32[1024,1024]{1,0:T(8,128)}, f32[1024,1024]{1,0:T(8,128)}) fusion(), kind=kLoop, calls=%fused_computation.132 | loop fusion | flops 6291456 | bytes 8388608 | tf_op jit(solution)/shard_map/convert_element_type | solution.py:43
  9.5 4.3 %fusion.85 = (f32[1024,1024]{1,0:T(8,128)}, f32[1024,1024]{1,0:T(8,128)}) fusion(), kind=kLoop, calls=%fused_computation.134 | loop fusion | flops 6291456 | bytes 8388608 | tf_op jit(solution)/shard_map/convert_element_type | solution.py:43
  13.8 4.3 %fusion.87 = (f32[1024,1024]{1,0:T(8,128)}, f32[1024,1024]{1,0:T(8,128)}) fusion(), kind=kLoop, calls=%fused_computation.136 | loop fusion | flops 6291456 | bytes 8388608 | tf_op jit(solution)/shard_map/convert_element_type | solution.py:43
  18.2 2.5 %fusion.89 = f32[1024,1024]{1,0:T(8,128)} fusion(), kind=kLoop, calls=%fused_computation.138 | loop fusion | flops 4194304 | bytes 4194304 | tf_op jit(solution)/shard_map/convert_element_type | solution.py:43
  21.1 23.7 %fusion.96 = f32[1,4,268,1024]{3,2,1,0:T(8,128)S(1)} fusion(bf16[1,4,6,1024]{3,2,1,0:T(8,128)(2,1)S(1)} %collective-permute-done.1, bf16[1,4,256,1024]{3,2,1,0:T(8,128)(2,1)S(1)} %copy-done.1, bf16[1,4,6,1024]{3,2,1,0:T(8,128)(2,1)S(1)} %collective-permute-done, f32[1024,1024]{1,0:T(8,128)} %fusion.89, f32[4]{0:T(128)S(1)} %get-tuple-element.11, ...), kind=kOutput, calls=%fused_computation.152 | convolution fusion | flops 13549993984 | bytes 35946608 | tf_op jit(solution)/shard_map/tbrc,bcd->tbrd/dot_general | solution.py:44
  44.8 3.8 %fusion.29 = f32[1,4,262,1024]{3,2,1,0:T(8,128)S(1)} fusion(f32[1,4,268,1024]{3,2,1,0:T(8,128)S(1)} %fusion.96, f32[4]{0:T(128)S(1)} %get-tuple-element.42, f32[4]{0:T(128)S(1)} %get-tuple-element.41, f32[4]{0:T(128)S(1)} %get-tuple-element.40, f32[4]{0:T(128)S(1)} %get-tuple-element.39, f32[4]{0:T(128)S(1)} %get-tuple-element.38, ...), kind=kLoop, calls=%fused_computation.66 | loop fusion | flops 15024128 | bytes 34341240 | tf_op jit(solution)/shard_map/jit(_where)/select_n | solution.py:80
  48.6 2.8 %copy.24 = f32[1,4,262,1024]{3,1,2,0:T(4,128)S(1)} copy(f32[1,4,262,1024]{3,2,1,0:T(8,128)S(1)} %fusion.29) | data formatting | bytes 8585216 | tf_op jit(solution)/shard_map/jit(_where)/select_n | solution.py:80
  51.4 1.0 slice_bitcast_fusion.1
  52.4 2.3 %fusion.100 = f32[4,130,1024]{2,0,1:T(4,128)S(1)} fusion(f32[1,4,131,1024]{3,1,2,0:T(4,128)S(1)} %get-tuple-element.18, f32[1,4,131,1024]{3,1,2,0:T(4,128)S(1)} %get-tuple-element.17), kind=kLoop, calls=%fused_computation.157 | loop fusion | flops 3727360 | bytes 10649600 | tf_op jit(solution)/shard_map/reshape.35
  54.7 5.7 %fusion.119 = f32[4,130,512]{2,1,0:T(8,128)S(1)} fusion(f32[4,130,1024]{2,0,1:T(4,128)S(1)} %fusion.100, s32[512]{0:T(512)S(1)} %iota_multiply_fusion, pred[130]{0:T(512)(128)(4,1)S(1)} %compare_and_fusion), kind=kOutput, calls=%fused_computation.182 | convolution fusion | flops 3278639104 | bytes 3197058 | tf_op jit(solution)/shard_map/dot_general | solution.py:57
  61.6 0.9 fusion.124
  63.3 6.7 %all-to-all-start.2 = ((bf16[1,4,64,256]{3,1,0,2:T(4,128)(2,1)}), bf16[1,4,64,256]{3,1,0,2:T(4,128)(2,1)S(1)}, u32[]{:S(2)}, u32[]{:S(2)}) async-start(bf16[1,4,64,256]{3,1,0,2:T(4,128)(2,1)} %copy.32), calls=%async_computation.2 | async-start | bytes 262144 | tf_op jit(solution)/shard_map/all_to_all | solution.py:134
  70.1 1.2 copy.27
  71.3 6.8 %all-to-all-done.2 = bf16[1,4,64,256]{3,1,0,2:T(4,128)(2,1)S(1)} async-done(((bf16[1,4,64,256]{3,1,0,2:T(4,128)(2,1)}), bf16[1,4,64,256]{3,1,0,2:T(4,128)(2,1)S(1)}, u32[]{:S(2)}, u32[]{:S(2)}) %all-to-all-start.2) | async-done | bytes 131104 | tf_op jit(solution)/shard_map/all_to_all | solution.py:134
  78.1 3.5 %all-to-all-start.1 = ((bf16[1,4,128,512]{3,1,0,2:T(4,128)(2,1)}), bf16[1,4,128,512]{3,1,0,2:T(4,128)(2,1)S(1)}, u32[]{:S(2)}, u32[]{:S(2)}) async-start(bf16[1,4,128,512]{3,1,0,2:T(4,128)(2,1)} %copy.27), calls=%async_computation.1 | async-start | bytes 1048576 | tf_op jit(solution)/shard_map/all_to_all | solution.py:131
  81.9 2.8 %slice.1298 = bf16[1,4,256,1024]{3,2,1,0:T(8,128)(2,1)S(1)} slice(f32[1,4,262,1024]{3,2,1,0:T(8,128)} %copy-done), slice={[0:1], [0:4], [3:259], [0:1024]} | slice | bytes 4194304 | tf_op jit(solution)/shard_map/slice | solution.py:118
  84.8 2.9 %copy.22 = bf16[1,4,256,1024]{3,1,0,2:T(4,128)(2,1)} copy(bf16[1,4,256,1024]{3,2,1,0:T(8,128)(2,1)S(1)} %slice.1298) | data formatting | bytes 4194304 | tf_op jit(solution)/shard_map/slice | solution.py:118
  87.7 8.6 %all-to-all-done.1 = bf16[1,4,128,512]{3,1,0,2:T(4,128)(2,1)S(1)} async-done(((bf16[1,4,128,512]{3,1,0,2:T(4,128)(2,1)}), bf16[1,4,128,512]{3,1,0,2:T(4,128)(2,1)S(1)}, u32[]{:S(2)}, u32[]{:S(2)}) %all-to-all-start.1) | async-done | bytes 524320 | tf_op jit(solution)/shard_map/all_to_all | solution.py:131
  96.4 4.6 %all-to-all-start = ((bf16[1,4,256,1024]{3,1,0,2:T(4,128)(2,1)}), bf16[1,4,256,1024]{3,1,0,2:T(4,128)(2,1)}, u32[]{:S(2)}, u32[]{:S(2)}) async-start(bf16[1,4,256,1024]{3,1,0,2:T(4,128)(2,1)} %copy.22), calls=%async_computation | async-start | bytes 4194304 | tf_op jit(solution)/shard_map/all_to_all | solution.py:128
  102.6 1.3 broadcast_in_dim.78
  103.9 1.4 add.471
  105.5 1.4 fusion.155
  106.9 1.2 broadcast_subtract_fusion
  110.5 2.0 %fusion.129 = bf16[8,4,16,512]{3,2,1,0:T(8,128)(2,1)} fusion(f32[8,4,16,512]{3,2,1,0:T(8,128)S(1)} %fusion.182, f32[4,4,16,512]{3,2,1,0:T(8,128)S(1)} %reshape.284, f32[4,4,16,512]{3,2,1,0:T(8,128)S(1)} %reshape.283), kind=kLoop, calls=%fused_computation.205 | loop fusion | flops 6815744 | bytes 2621440 | tf_op jit(solution)/shard_map/convert_element_type | solution.py:100
  112.5 36.2 %all-to-all-done = bf16[1,4,256,1024]{3,1,0,2:T(4,128)(2,1)} async-done(((bf16[1,4,256,1024]{3,1,0,2:T(4,128)(2,1)}), bf16[1,4,256,1024]{3,1,0,2:T(4,128)(2,1)}, u32[]{:S(2)}, u32[]{:S(2)}) %all-to-all-start) | async-done | bytes 2097184 | tf_op jit(solution)/shard_map/all_to_all | solution.py:128
  148.8 2.8 %convert.18 = f32[1,4,8,32,1024]{4,1,3,2,0:T(4,128)S(1)} convert(bf16[1,4,8,32,1024]{4,1,3,2,0:T(4,128)(2,1)} %bitcast.43) | non-fusion elementwise | flops 1048576 | bytes 6291456 | tf_op jit(solution)/shard_map/convert_element_type | solution.py:84
  151.6 4.5 %bitcast_multiply_fusion = f32[8,4,32,1024]{3,2,1,0:T(8,128)} fusion(f32[1,4,8,32,1024]{4,1,3,2,0:T(4,128)S(1)} %convert.18, f32[8,32,1024]{2,1,0:T(8,128)S(1)} %get-tuple-element.28), kind=kLoop, calls=%fused_computation.121 | loop fusion | flops 1048576 | bytes 9437184 | tf_op jit(solution)/shard_map/mul | solution.py:88
  156.1 13.9 %fusion.75 = f32[8,4,32,1024]{3,2,1,0:T(8,128)S(1)} fusion(f32[8,4,32,1024]{3,2,1,0:T(8,128)} %bitcast_multiply_fusion, f32[1,4,8,32,1024]{4,1,3,2,0:T(4,128)S(1)} %convert.18, f32[8,32,1024]{2,1,0:T(8,128)} %fusion.155, f32[8,32,1024]{2,1,0:T(8,128)} %get-tuple-element.27, f32[8,32,1024]{2,1,0:T(8,128)S(1)} %convert_element_type.202), kind=kLoop, calls=%fused_computation.123 | loop fusion | flops 20971520 | bytes 15728640 | tf_op jit(solution)/shard_map/add | solution.py:95
  170.7 5.8 %fusion.39 = bf16[8,4,32,1024]{3,2,1,0:T(8,128)(2,1)} fusion(f32[8,4,32,1024]{3,2,1,0:T(8,128)S(1)} %fusion.75, f32[4,4,32,1024]{3,2,1,0:T(8,128)S(1)} %reshape.280, f32[4,4,32,1024]{3,2,1,0:T(8,128)S(1)} %reshape.279), kind=kLoop, calls=%fused_computation.82 | loop fusion | flops 27262976 | bytes 10485760 | tf_op jit(solution)/shard_map/convert_element_type | solution.py:100
  (62 shorter events, 7.4 us)
Async XLA Ops:
  1.5 19.6 %collective-permute-start = (bf16[1,4,6,1024]{3,2,1,0:T(8,128)(2,1)S(1)}, bf16[1,4,6,1024]{3,2,1,0:T(8,128)(2,1)S(1)}, u32[]{:S(2)}, u32[]{:S(2)}) collective-permute-start(bf16[1,4,6,1024]{3,2,1,0:T(8,128)(2,1)S(1)} %get-tuple-element.21), channel_id=1, source_target_pairs={{0,1},{2,3},{4,5},{6,7},{8,9},{10,11},{12,13},{14,15},{16,17},{18,... | collective-permute-start | bytes 147464 | tf_op jit(solution)/shard_map/ppermute | solution.py:18
  3.9 17.2 %collective-permute-start.1 = (bf16[1,4,6,1024]{3,2,1,0:T(8,128)(2,1)S(1)}, bf16[1,4,6,1024]{3,2,1,0:T(8,128)(2,1)S(1)}, u32[]{:S(2)}, u32[]{:S(2)}) collective-permute-start(bf16[1,4,6,1024]{3,2,1,0:T(8,128)(2,1)S(1)} %get-tuple-element.22), channel_id=1, source_target_pairs={{1,0},{3,2},{5,4},{7,6},{9,8},{11,10},{13,12},{15,14},{17,16},{19,... | collective-permute-start | bytes 147464 | tf_op jit(solution)/shard_map/ppermute | solution.py:21
  18.2 2.5 %copy-start.5 = (f32[2,4,7]{2,1,0:T(4,128)S(1)}, f32[2,4,7]{2,1,0:T(4,128)}, u32[]{:S(2)}) copy-start(f32[2,4,7]{2,1,0:T(4,128)} %param.4) | copy-start | bytes 676
  18.2 2.9 %copy-start.1 = (bf16[1,4,256,1024]{3,2,1,0:T(8,128)(2,1)S(1)}, bf16[1,4,256,1024]{3,2,1,0:T(8,128)(2,1)}, u32[]{:S(2)}) copy-start(bf16[1,4,256,1024]{3,2,1,0:T(8,128)(2,1)} %param.3) | copy-start | bytes 6291460
  48.6 2.8 %copy-start = (f32[1,4,262,1024]{3,2,1,0:T(8,128)}, f32[1,4,262,1024]{3,2,1,0:T(8,128)S(1)}, u32[]{:S(2)}) copy-start(f32[1,4,262,1024]{3,2,1,0:T(8,128)S(1)} %fusion.29) | copy-start | bytes 12877828
  61.6 20.0 %copy-start.4 = (s32[8,8,8]{2,1,0:T(8,128)S(1)}, s32[8,8,8]{2,1,0:T(8,128)}, u32[]{:S(2)}) copy-start(s32[8,8,8]{2,1,0:T(8,128)} %param.5) | copy-start | bytes 6148
  63.3 14.9 %all-to-all-start.2 = ((bf16[1,4,64,256]{3,1,0,2:T(4,128)(2,1)}), bf16[1,4,64,256]{3,1,0,2:T(4,128)(2,1)S(1)}, u32[]{:S(2)}, u32[]{:S(2)}) async-start(bf16[1,4,64,256]{3,1,0,2:T(4,128)(2,1)} %copy.32), calls=%async_computation.2 | async-start | bytes 262144 | tf_op jit(solution)/shard_map/all_to_all | solution.py:134
  78.1 9.6 %copy-start.2 = (bf16[1,4,64,256]{3,1,0,2:T(4,128)(2,1)}, bf16[1,4,64,256]{3,1,0,2:T(4,128)(2,1)S(1)}, u32[]{:S(2)}) copy-start(bf16[1,4,64,256]{3,1,0,2:T(4,128)(2,1)S(1)} %all-to-all-done.2) | copy-start | bytes 393220
  78.1 18.2 %all-to-all-start.1 = ((bf16[1,4,128,512]{3,1,0,2:T(4,128)(2,1)}), bf16[1,4,128,512]{3,1,0,2:T(4,128)(2,1)S(1)}, u32[]{:S(2)}, u32[]{:S(2)}) async-start(bf16[1,4,128,512]{3,1,0,2:T(4,128)(2,1)} %copy.27), calls=%async_computation.1 | async-start | bytes 1048576 | tf_op jit(solution)/shard_map/all_to_all | solution.py:131
  96.4 52.4 %all-to-all-start = ((bf16[1,4,256,1024]{3,1,0,2:T(4,128)(2,1)}), bf16[1,4,256,1024]{3,1,0,2:T(4,128)(2,1)}, u32[]{:S(2)}, u32[]{:S(2)}) async-start(bf16[1,4,256,1024]{3,1,0,2:T(4,128)(2,1)} %copy.22), calls=%async_computation | async-start | bytes 4194304 | tf_op jit(solution)/shard_map/all_to_all | solution.py:128
  103.9 4.2 %copy-start.3 = (bf16[1,4,64,256]{3,1,0,2:T(4,128)(2,1)S(1)}, bf16[1,4,64,256]{3,1,0,2:T(4,128)(2,1)}, u32[]{:S(2)}) copy-start(bf16[1,4,64,256]{3,1,0,2:T(4,128)(2,1)} %copy-done.2) | copy-start | bytes 393220
where the time goes:
time: 180 us; the launch traced here: 177 us
  other arithmetic  56 us (31%)
  waiting for transfers between devices  51.7 us (29%)
  matrix products  30.2 us (17%)
  local copies, waits for them, and re-layouts  19 us (11%)
  starting transfers between devices  18.4 us (10%)
    all_to_all x1, waiting for transfers between devices, local(): lax.all_to_all(level_zero, 'date', split_axis=2, concat_axis=0, tiled=True)  36.2 us
    dot_general x1, matrix products, column_resample(): jnp.einsum('tbrc,bcd->tbrd', values.astype(jnp.float32), table, precision...  23.7 us
    convert_element_type x4, other arithmetic, column_resample(): (offset == k).astype(jnp.float32)[None]  15.4 us
    add x3, other arithmetic, smooth(): filled = clear4 * values + (1.0 - clear4) * (numer / denom)  14.7 us
    convert_element_type x3, other arithmetic, smooth(): return result.astype(jnp.bfloat16)  8.65 us
    all_to_all x1, waiting for transfers between devices, local(): lax.all_to_all(level_one, 'date', split_axis=2, concat_axis=0, tiled=True)  8.64 us
    all_to_all x1, waiting for transfers between devices, local(): lax.all_to_all(level_two, 'date', split_axis=2, concat_axis=0, tiled=True)  6.81 us
    all_to_all x1, starting transfers between devices, local(): lax.all_to_all(level_two, 'date', split_axis=2, concat_axis=0, tiled=True)  6.66 us
  transfers between devices with their start and end apart: 5, of which 3 were waited for; matrix products, arithmetic and copies ran while one was open for 20% of the time, Pallas kernels for 0%

commit v1 on v0

v1 whole, which is shorter than its diff:
```python
import math

import jax
import jax.numpy as jnp
import numpy as np
from jax import lax
from jax.sharding import PartitionSpec as P

gap_weights = [math.exp(-((k - 4) ** 2) / 8.0) for k in range(9)]
savgol_coeffs = [c / 231.0 for c in [-21.0, 14.0, 39.0, 54.0, 59.0, 54.0, 39.0, 14.0, -21.0]]
pyramid_filter = [0.125, 0.375, 0.375, 0.125]


def padded(block, sides, width):
    for axis, dim in sides:
        count = lax.axis_size(axis)
        forward = [(i, i + 1) for i in range(count - 1)]
        backward = [(target, source) for source, target in forward]
        low = lax.ppermute(
            lax.slice_in_dim(block, block.shape[dim] - width, None, axis=dim), axis, forward
        )
        high = lax.ppermute(lax.slice_in_dim(block, 0, width, axis=dim), axis, backward)
        block = jnp.concatenate([low, block, high], axis=dim)
    return block


def column_taps(values, taps):
    width = values.shape[-1]
    wide = jnp.pad(values, ((0, 0), (0, 0), (3, 3)))
    total = taps[0] * wide[..., 0:width]
    for k in range(1, 7):
        total = total + taps[k] * wide[..., k : k + width]
    return total


def row_taps(values, taps):
    count = values.shape[1] - 6
    total = taps[0] * values[:, 0:count]
    for k in range(1, 7):
        total = total + taps[k] * values[:, k : k + count]
    return total


def halve_table(width):
    source = np.arange(width)[:, None]
    target = np.arange(width // 2)[None, :]
    place = source - 2 * target + 1
    table = np.zeros((width, width // 2), np.float32)
    for p in range(4):
        table = table + pyramid_filter[p] * (place == p)
    return jnp.asarray(table, jnp.bfloat16)


def halve_columns(values):
    table = halve_table(values.shape[-1])
    high = values.astype(jnp.bfloat16)
    low = (values - high.astype(jnp.float32)).astype(jnp.bfloat16)
    dims = (((values.ndim - 1,), (0,)), ((), ()))
    return lax.dot_general(high, table, dims, preferred_element_type=jnp.float32) + lax.dot_general(
        low, table, dims, preferred_element_type=jnp.float32
    )


def halve_rows(extended):
    pairs_count = extended.shape[1] // 2
    pairs = extended.reshape(extended.shape[:1] + (pairs_count, 2) + extended.shape[2:])
    even = pairs[:, :, 0]
    odd = pairs[:, :, 1]
    return (
        pyramid_filter[0] * even[:, :-1]
        + pyramid_filter[1] * odd[:, :-1]
        + pyramid_filter[2] * even[:, 1:]
        + pyramid_filter[3] * odd[:, 1:]
    )


def decimate_rim(extended):
    return halve_columns(halve_rows(extended))


def keep_rows(values, first, total):
    places = first + lax.iota(jnp.int32, values.shape[1])
    inside = (places >= 0) & (places < total)
    return jnp.where(inside[None, :, None], values, 0.0)


def smooth_operator(dates):
    clamp = np.zeros((dates, dates), np.float64)
    near = np.zeros((dates, dates), np.float64)
    for t in range(dates):
        for k in range(9):
            clamp[t, min(max(t + k - 4, 0), dates - 1)] += savgol_coeffs[k]
            if 0 <= t + k - 4 < dates:
                near[t, t + k - 4] = gap_weights[k]
    return clamp.astype(np.float32), near.astype(np.float32)


def smooth_coefficients(clear):
    dates = clear.shape[0]
    clamp, near = smooth_operator(dates)
    weight = 0.1 + 0.9 * clear
    denom = jnp.einsum("su,uxy->sxy", near, weight, precision=lax.Precision.HIGHEST)
    gap = (1.0 - clear) / denom
    fill = near[:, :, None, None] * weight[None, :] * gap[:, None]
    fill = fill + jnp.eye(dates, dtype=jnp.float32)[:, :, None, None] * clear[None, :]
    return jnp.einsum("ts,suxy->tuxy", clamp, fill, precision=lax.Precision.HIGHEST)


def expand(coeff, rows, cols):
    lead = coeff.shape[:-2]
    rm, cm = coeff.shape[-2:]
    grown = jnp.broadcast_to(coeff[..., :, None, :, None], lead + (rm, rows, cm, cols))
    return grown.reshape(lead + (rm * rows, cm * cols))


def smooth(level, coeff, rows, cols):
    values = level.astype(jnp.float32)
    grown = expand(coeff, rows, cols)
    return jnp.sum(grown * values[None], axis=1).astype(jnp.bfloat16)


def local(scenes, resample_taps, clear_mask):
    rows = scenes.shape[2]
    bands = scenes.shape[1]
    band_index = lax.axis_index("row")
    total_rows = rows * lax.axis_size("row")
    ndate = lax.axis_size("date")
    extended = padded(scenes, (("row", 2),), 6)
    clear = clear_mask.astype(jnp.float32)
    coeff = smooth_coefficients(clear)
    mask_rows = clear.shape[1]
    mask_cols = clear.shape[2]
    fine_rows = rows // ndate
    width = scenes.shape[3]
    fine = []
    half = []
    quarter = []
    for b in range(bands):
        source = extended[:, b].astype(jnp.float32)
        across = column_taps(source, resample_taps[0, b])
        resampled_wide = row_taps(across, resample_taps[1, b])
        resampled_wide = keep_rows(resampled_wide, band_index * rows - 3, total_rows)
        half_wide = decimate_rim(resampled_wide)
        half_wide = keep_rows(half_wide, band_index * (rows // 2) - 1, total_rows // 2)
        level_zero = resampled_wide[:, 3 : 3 + rows].astype(jnp.bfloat16)
        level_one = half_wide[:, 1 : 1 + rows // 2].astype(jnp.bfloat16)
        level_two = decimate_rim(half_wide).astype(jnp.bfloat16)
        got = [
            lax.all_to_all(level, "date", split_axis=1, concat_axis=0, tiled=True)
            for level in (level_zero, level_one, level_two)
        ]
        fine.append(smooth(got[0], coeff, fine_rows // mask_rows, width // mask_cols))
        half.append(smooth(got[1], coeff, fine_rows // 2 // mask_rows, width // 2 // mask_cols))
        quarter.append(smooth(got[2], coeff, fine_rows // 4 // mask_rows, width // 4 // mask_cols))
    return tuple(jnp.stack(parts, axis=1) for parts in (fine, half, quarter))


def solution(mesh):
    in_specs = (P(("groups", "date"), None, "row", None), P(), P("groups", ("row", "date"), None))
    out_specs = (
        P("groups", None, ("row", "date"), None),
        P("groups", None, ("row", "date"), None),
        P("groups", None, ("row", "date"), None),
    )
    return jax.shard_map(local, mesh=mesh, in_specs=in_specs, out_specs=out_specs, check_vma=False)
```

time: 180 us -> 348 us (1.93)
  other arithmetic: 56 us -> 180 us
  starting transfers between devices: 18.4 us -> 61.1 us
  local copies, waits for them, and re-layouts: 19 us -> 55.6 us
  matrix products: 30.2 us -> 7.96 us
  waiting for transfers between devices: 51.7 us -> 35.1 us
    add x4 -> x3, other arithmetic: 14.7 us -> 77.3 us  [the longest x2 76 us: column_taps(): total = total + taps[k] * wide[..., k:k + width]]
    all_to_all x3 -> x12, starting transfers between devices: 14.7 us -> 57.4 us  [local(): lax.all_to_all(level, 'date', split_axis=1, concat_axis=0, tiled=True)]
    select_n x2 -> x8, other arithmetic: 3.91 us -> 39.8 us  [keep_rows(): return jnp.where(inside[None, :, None], values, 0.0)]
    unnamed x12 -> x99, local copies, waits for them, and re-layouts: 0.03 us -> 31.5 us
    unnamed x0 -> x12, other arithmetic: none -> 23.6 us
    dot_general x3 -> x18, matrix products: 30.2 us -> 7.96 us  [the longest x8 3.39 us: halve_columns(): lax.dot_general(low, table, dims, preferred_element_type=jnp.float32)]
    all_to_all x3 -> x12, waiting for transfers between devices: 51.7 us -> 35.1 us  [local(): lax.all_to_all(level, 'date', split_axis=1, concat_axis=0, tiled=True)]
    reduce_sum x0 -> x3, other arithmetic: none -> 10.4 us  [smooth(): return jnp.sum(grown * values[None], axis=1).astype(jnp.bfloat16)]
  transfers between devices with their start and end apart: 5 -> 14, of which waited for: 3 -> 9; matrix products, arithmetic and copies ran while one was open for 20% -> 48% of each run, Pallas kernels for 0% -> 0%
where the time goes in v1:
time: 348 us; the launch traced here: 342 us
  other arithmetic  180 us (52%)
  starting transfers between devices  61.1 us (18%)
  local copies, waits for them, and re-layouts  55.6 us (16%)
  waiting for transfers between devices  35.1 us (10%)
  matrix products  7.96 us (2%)
    add x2, other arithmetic, column_taps(): total = total + taps[k] * wide[..., k:k + width]  76 us
    all_to_all x12, starting transfers between devices, local(): lax.all_to_all(level, 'date', split_axis=1, concat_axis=0, tiled=True)  57.4 us
    select_n x8, other arithmetic, keep_rows(): return jnp.where(inside[None, :, None], values, 0.0)  39.8 us
    all_to_all x12, waiting for transfers between devices, local(): lax.all_to_all(level, 'date', split_axis=1, concat_axis=0, tiled=True)  35.1 us
    unnamed x99, local copies, waits for them, and re-layouts  31.5 us
    unnamed x12, other arithmetic  23.6 us
    convert_element_type x8, other arithmetic, halve_columns(): low = (values - high.astype(jnp.float32)).astype(jnp.bfloat16)  10.9 us
    reduce_sum x3, other arithmetic, smooth(): return jnp.sum(grown * values[None], axis=1).astype(jnp.bfloat16)  10.4 us
  transfers between devices with their start and end apart: 14, of which 9 were waited for; matrix products, arithmetic and copies ran while one was open for 48% of the time, Pallas kernels for 0%

profile of v1, /device:TPU:0, one launch (start us, length us, event | category | flops | bytes accessed | tf_op | source)
XLA Modules:
  0.0 341.9 jit_solution(5171048793330482264)
XLA Ops:
  14.0 5.1 %constant_dynamic-update-slice_fusion.1 = bf16[1,4,268,1024]{3,0,2,1:T(2,128)(2,1)S(1)} fusion(bf16[1,4,268,1024]{3,0,2,1:T(2,128)(2,1)S(1)} %constant_dynamic-update-slice_fusion.2, bf16[1,4,256,1024]{3,2,1,0:T(8,128)(2,1)} %param.14), kind=kLoop, calls=%fused_computation.245 | loop fusion | bytes 6291456
  19.2 5.8 %fusion.12 = (f32[1,268,1024]{2,0,1:T(1,128)S(1)}, f32[1,268,1024]{2,0,1:T(1,128)S(1)}, f32[1,268,1024]{2,0,1:T(1,128)}, f32[1,268,1024]{2,0,1:T(1,128)}) fusion(bf16[1,4,268,1024]{3,0,2,1:T(2,128)(2,1)S(1)} %constant_dynamic-update-slice_fusion), kind=kLoop, calls=%fused_computation.39 | loop fusion | flops 1097728 | bytes 6586368 | tf_op jit(solution)/shard_map/convert_element_type | solution.py:139
  25.0 37.0 %multiply_add_fusion = (f32[1,268,1024]{2,0,1:T(1,128)S(1)}, f32[1,268,1024]{2,0,1:T(1,128)S(1)}) fusion(f32[1,268,1024]{2,0,1:T(1,128)S(1)} %get-tuple-element.31, f32[]{:T(128)} %bitcast.66, f32[]{:T(128)} %bitcast.65, f32[]{:T(128)} %bitcast.64, f32[]{:T(128)} %bitcast.62, f32[]{:T(128)} %bitcast.61, f32[]{:T(128)} %bitcast.60, f32[]{:T(128)} %bitcast.58, ...), kind=kLoop, calls=%fused_computation.46 | loop fusion | flops 7135232 | bytes 4390968 | tf_op jit(solution)/shard_map/add | solution.py:32
  62.0 9.8 %broadcast_select_fusion = f32[1,262,1024]{2,0,1:T(1,128)S(1)} fusion(pred[262]{0:T(512)(128)(4,1)S(1)} %fusion.89, f32[1,268,1024]{2,0,1:T(1,128)S(1)} %get-tuple-element.109, f32[]{:T(128)} %bitcast.72, f32[]{:T(128)} %bitcast.71, f32[]{:T(128)} %bitcast.70, f32[]{:T(128)} %bitcast.69, f32[]{:T(128)} %bitcast.68, f32[]{:T(128)} %bitcast.67, f32[]{:T(128)} %bitcast.57), kind=kLoop, calls=%fused_computation.8 | loop fusion | flops 3756032 | bytes 8585506 | tf_op jit(solution)/shard_map/jit(_where)/select_n | solution.py:84
  83.2 7.0 %all-to-all-start.11 = ((bf16[8,2,1024]{2,1,0:T(2,128)(2,1)}), bf16[8,2,1024]{2,1,0:T(2,128)(2,1)}, u32[]{:S(2)}, u32[]{:S(2)}) async-start(bf16[8,2,1024]{2,1,0:T(2,128)(2,1)} %reshape.736), calls=%async_computation.11 | async-start | bytes 65536 | tf_op jit(solution)/shard_map/all_to_all | solution.py:149
  90.2 9.8 %broadcast_select_fusion.1 = f32[1,262,1024]{2,0,1:T(1,128)S(1)} fusion(pred[262]{0:T(512)(128)(4,1)S(1)} %fusion.89, f32[1,268,1024]{2,0,1:T(1,128)S(1)} %get-tuple-element.110, f32[]{:T(128)} %bitcast.54, f32[]{:T(128)} %bitcast.53, f32[]{:T(128)} %bitcast.52, f32[]{:T(128)} %bitcast.51, f32[]{:T(128)} %bitcast.50, f32[]{:T(128)} %bitcast.49, f32[]{:T(128)} %bitcast.39), kind=kLoop, calls=%fused_computation.9 | loop fusion | flops 3756032 | bytes 8585506 | tf_op jit(solution)/shard_map/jit(_where)/select_n | solution.py:84
  105.2 38.9 %multiply_add_fusion.2 = (f32[1,268,1024]{2,0,1:T(1,128)S(1)}, f32[1,268,1024]{2,0,1:T(1,128)S(1)}) fusion(f32[1,268,1024]{2,0,1:T(1,128)S(1)} %copy-done.8, f32[]{:T(128)} %bitcast.30, f32[]{:T(128)} %bitcast.29, f32[]{:T(128)} %bitcast.28, f32[]{:T(128)} %bitcast.26, f32[]{:T(128)} %bitcast.25, f32[]{:T(128)} %bitcast.24, f32[]{:T(128)} %bitcast.22, ...), kind=kLoop, calls=%fused_computation.52 | loop fusion | flops 7135232 | bytes 4390968 | tf_op jit(solution)/shard_map/add | solution.py:32
  144.2 9.6 %broadcast_select_fusion.2 = f32[1,262,1024]{2,0,1:T(1,128)S(1)} fusion(pred[262]{0:T(512)(128)(4,1)S(1)} %fusion.89, f32[1,268,1024]{2,0,1:T(1,128)S(1)} %get-tuple-element.111, f32[]{:T(128)} %bitcast.36, f32[]{:T(128)} %bitcast.35, f32[]{:T(128)} %bitcast.34, f32[]{:T(128)} %bitcast.33, f32[]{:T(128)} %bitcast.32, f32[]{:T(128)} %bitcast.31, f32[]{:T(128)} %bitcast.21), kind=kLoop, calls=%fused_computation.10 | loop fusion | flops 3756032 | bytes 8585506 | tf_op jit(solution)/shard_map/jit(_where)/select_n | solution.py:84
  162.9 10.4 %broadcast_select_fusion.3 = f32[1,262,1024]{2,0,1:T(1,128)S(1)} fusion(pred[262]{0:T(512)(128)(4,1)S(1)} %fusion.89, f32[1,268,1024]{2,0,1:T(1,128)S(1)} %get-tuple-element.112, f32[]{:T(128)} %bitcast.18, f32[]{:T(128)} %bitcast.17, f32[]{:T(128)} %bitcast.16, f32[]{:T(128)} %bitcast.15, f32[]{:T(128)} %bitcast.14, f32[]{:T(128)} %bitcast.13, f32[]{:T(128)} %bitcast.3), kind=kLoop, calls=%fused_computation.11 | loop fusion | flops 3756032 | bytes 8585506 | tf_op jit(solution)/shard_map/jit(_where)/select_n | solution.py:84
  179.4 6.0 %all-to-all-start.10 = ((bf16[8,2,1024]{2,1,0:T(2,128)(2,1)}), bf16[8,2,1024]{2,1,0:T(2,128)(2,1)S(1)}, u32[]{:S(2)}, u32[]{:S(2)}) async-start(bf16[8,2,1024]{2,1,0:T(2,128)(2,1)} %reshape.734), calls=%async_computation.10 | async-start | bytes 65536 | tf_op jit(solution)/shard_map/all_to_all | solution.py:149
  187.0 5.1 %all-to-all-done.10 = bf16[8,2,1024]{2,1,0:T(2,128)(2,1)S(1)} async-done(((bf16[8,2,1024]{2,1,0:T(2,128)(2,1)}), bf16[8,2,1024]{2,1,0:T(2,128)(2,1)S(1)}, u32[]{:S(2)}, u32[]{:S(2)}) %all-to-all-start.10) | async-done | bytes 32800 | tf_op jit(solution)/shard_map/all_to_all | solution.py:149
  197.1 5.0 %all-to-all-done.9 = bf16[8,2,1024]{2,1,0:T(2,128)(2,1)S(1)} async-done(((bf16[8,2,1024]{2,1,0:T(2,128)(2,1)}), bf16[8,2,1024]{2,1,0:T(2,128)(2,1)S(1)}, u32[]{:S(2)}, u32[]{:S(2)}) %all-to-all-start.9) | async-done | bytes 32800 | tf_op jit(solution)/shard_map/all_to_all | solution.py:149
  202.0 3.3 all-to-all-start.8
  207.8 4.3 %all-to-all-done.8 = bf16[8,2,1024]{2,1,0:T(2,128)(2,1)S(1)} async-done(((bf16[8,2,1024]{2,1,0:T(2,128)(2,1)}), bf16[8,2,1024]{2,1,0:T(2,128)(2,1)S(1)}, u32[]{:S(2)}, u32[]{:S(2)}) %all-to-all-start.8) | async-done | bytes 32800 | tf_op jit(solution)/shard_map/all_to_all | solution.py:149
  212.0 3.4 all-to-all-start.7
  217.8 4.9 %all-to-all-done.7 = bf16[8,2,4096]{2,1,0:T(2,128)(2,1)S(1)} async-done(((bf16[8,2,4096]{2,1,0:T(2,128)(2,1)}), bf16[8,2,4096]{2,1,0:T(2,128)(2,1)S(1)}, u32[]{:S(2)}, u32[]{:S(2)}) %all-to-all-start.7) | async-done | bytes 131104 | tf_op jit(solution)/shard_map/all_to_all | solution.py:149
  222.7 3.4 all-to-all-start.6
  228.4 4.9 %all-to-all-done.6 = bf16[8,2,4096]{2,1,0:T(2,128)(2,1)S(1)} async-done(((bf16[8,2,4096]{2,1,0:T(2,128)(2,1)}), bf16[8,2,4096]{2,1,0:T(2,128)(2,1)S(1)}, u32[]{:S(2)}, u32[]{:S(2)}) %all-to-all-start.6) | async-done | bytes 131104 | tf_op jit(solution)/shard_map/all_to_all | solution.py:149
  233.3 3.4 all-to-all-start.5
  239.1 4.9 %all-to-all-done.5 = bf16[8,2,4096]{2,1,0:T(2,128)(2,1)S(1)} async-done(((bf16[8,2,4096]{2,1,0:T(2,128)(2,1)}), bf16[8,2,4096]{2,1,0:T(2,128)(2,1)S(1)}, u32[]{:S(2)}, u32[]{:S(2)}) %all-to-all-start.5) | async-done | bytes 131104 | tf_op jit(solution)/shard_map/all_to_all | solution.py:149
  244.0 3.5 %all-to-all-start.4 = ((bf16[8,2,4096]{2,1,0:T(2,128)(2,1)}), bf16[8,2,4096]{2,1,0:T(2,128)(2,1)S(1)}, u32[]{:S(2)}, u32[]{:S(2)}) async-start(bf16[8,2,4096]{2,1,0:T(2,128)(2,1)} %reshape.722), calls=%async_computation.4 | async-start | bytes 262144 | tf_op jit(solution)/shard_map/all_to_all | solution.py:149
  248.3 3.6 %reduce.31 = bf16[256,1024]{1,0:T(8,128)(2,1)S(1)} reduce(bf16[256,1,1024]{2,1,0:T(2,128)(2,1)S(1)} %slice_bitcast_fusion.23, bf16[]{:T(256)} %broadcast.215), dimensions={1}, to_apply=%slice_bitcast_fusion.23.reduce_sub_computation | reduce | bytes 1048578
  254.8 4.4 %all-to-all-start.3 = ((bf16[8,2,16384]{2,1,0:T(2,128)(2,1)}), bf16[8,2,16384]{2,1,0:T(2,128)(2,1)}, u32[]{:S(2)}, u32[]{:S(2)}) async-start(bf16[8,2,16384]{2,1,0:T(2,128)(2,1)} %reshape.720), calls=%async_computation.3 | async-start | bytes 1048576 | tf_op jit(solution)/shard_map/all_to_all | solution.py:149
  260.6 3.7 %reduce.30 = bf16[256,1024]{1,0:T(8,128)(2,1)S(1)} reduce(bf16[256,1,1024]{2,1,0:T(2,128)(2,1)S(1)} %slice_bitcast_fusion.22, bf16[]{:T(256)} %broadcast.215), dimensions={1}, to_apply=%slice_bitcast_fusion.22.reduce_sub_computation | reduce | bytes 1048578
  266.3 3.6 %all-to-all-done.3 = bf16[8,2,16384]{2,1,0:T(2,128)(2,1)} async-done(((bf16[8,2,16384]{2,1,0:T(2,128)(2,1)}), bf16[8,2,16384]{2,1,0:T(2,128)(2,1)}, u32[]{:S(2)}, u32[]{:S(2)}) %all-to-all-start.3) | async-done | bytes 524320 | tf_op jit(solution)/shard_map/all_to_all | solution.py:149
  269.9 5.5 %all-to-all-start.2 = ((bf16[8,2,16384]{2,1,0:T(2,128)(2,1)}), bf16[8,2,16384]{2,1,0:T(2,128)(2,1)}, u32[]{:S(2)}, u32[]{:S(2)}) async-start(bf16[8,2,16384]{2,1,0:T(2,128)(2,1)} %reshape.718), calls=%async_computation.2 | async-start | bytes 1048576 | tf_op jit(solution)/shard_map/all_to_all | solution.py:149
  276.1 3.6 %reduce.29 = bf16[256,1024]{1,0:T(8,128)(2,1)S(1)} reduce(bf16[256,1,1024]{2,1,0:T(2,128)(2,1)S(1)} %slice_bitcast_fusion.21, bf16[]{:T(256)} %broadcast.215), dimensions={1}, to_apply=%slice_bitcast_fusion.21.reduce_sub_computation | reduce | bytes 1048578
  280.9 3.6 %reduce.28 = bf16[256,1024]{1,0:T(8,128)(2,1)S(1)} reduce(bf16[256,1,1024]{2,1,0:T(2,128)(2,1)S(1)} %slice_bitcast_fusion.20, bf16[]{:T(256)} %broadcast.215), dimensions={1}, to_apply=%slice_bitcast_fusion.20.reduce_sub_computation | reduce | bytes 1048578
  290.4 6.4 %all-to-all-start.1 = ((bf16[8,2,16384]{2,1,0:T(2,128)(2,1)}), bf16[8,2,16384]{2,1,0:T(2,128)(2,1)S(1)}, u32[]{:S(2)}, u32[]{:S(2)}) async-start(bf16[8,2,16384]{2,1,0:T(2,128)(2,1)} %reshape.716), calls=%async_computation.1 | async-start | bytes 1048576 | tf_op jit(solution)/shard_map/all_to_all | solution.py:149
  307.4 7.8 %all-to-all-start = ((bf16[8,2,16384]{2,1,0:T(2,128)(2,1)}), bf16[8,2,16384]{2,1,0:T(2,128)(2,1)}, u32[]{:S(2)}, u32[]{:S(2)}) async-start(bf16[8,2,16384]{2,1,0:T(2,128)(2,1)} %reshape.714), calls=%async_computation | async-start | bytes 1048576 | tf_op jit(solution)/shard_map/all_to_all | solution.py:149
  325.7 3.5 %reshape.715 = bf16[256,1,1024]{2,1,0:T(2,128)(2,1)} reshape(bf16[8,2,16384]{2,1,0:T(2,128)(2,1)} %all-to-all-done) | data formatting | bytes 1048576
  331.4 6.1 %multiply_reduce_fusion.3 = (bf16[8,8,4,8,128]{4,3,2,1,0:T(8,128)(2,1)}, bf16[8,8,4,8,128]{4,3,2,1,0:T(8,128)(2,1)}, bf16[8,8,4,8,128]{4,3,2,1,0:T(8,128)(2,1)}, bf16[8,8,4,8,128]{4,3,2,1,0:T(8,128)(2,1)}) fusion(f32[8,8,4,8,128]{4,3,2,1,0:T(8,128)S(1)} %bitcast.303, f32[8,8,8,8]{3,2,1,0:T(8,128)S(1)} %copy.75, f32[8,8,4,8,128]{4,3,2,1,0:T(8,128)S(1)} %bitcast.302, ...), kind=kLoop, calls=%fused_computation.3 | loop fusion | flops 15728640 | bytes 6307840 | tf_op jit(solution)/shard_map/reduce_sum | solution.py:119
  (219 shorter events, 102.4 us)
Async XLA Ops:
  1.6 12.3 %collective-permute-start = (bf16[1,4,6,1024]{3,0,2,1:T(2,128)(2,1)S(1)}, bf16[1,4,6,1024]{3,0,2,1:T(2,128)(2,1)S(1)}, u32[]{:S(2)}, u32[]{:S(2)}) collective-permute-start(bf16[1,4,6,1024]{3,0,2,1:T(2,128)(2,1)S(1)} %copy.168), channel_id=1, source_target_pairs={{0,1},{2,3},{4,5},{6,7},{8,9},{10,11},{12,13},{14,15},{16,17},{18,... | collective-permute-start | bytes 147464 | tf_op jit(solution)/shard_map/ppermute | solution.py:19
  4.1 15.0 %collective-permute-start.1 = (bf16[1,4,6,1024]{3,0,2,1:T(2,128)(2,1)S(1)}, bf16[1,4,6,1024]{3,0,2,1:T(2,128)(2,1)S(1)}, u32[]{:S(2)}, u32[]{:S(2)}) collective-permute-start(bf16[1,4,6,1024]{3,0,2,1:T(2,128)(2,1)S(1)} %copy.169), channel_id=1, source_target_pairs={{1,0},{3,2},{5,4},{7,6},{9,8},{11,10},{13,12},{15,14},{17,16},{19,... | collective-permute-start | bytes 147464 | tf_op jit(solution)/shard_map/ppermute | solution.py:22
  83.2 96.2 %all-to-all-start.11 = ((bf16[8,2,1024]{2,1,0:T(2,128)(2,1)}), bf16[8,2,1024]{2,1,0:T(2,128)(2,1)}, u32[]{:S(2)}, u32[]{:S(2)}) async-start(bf16[8,2,1024]{2,1,0:T(2,128)(2,1)} %reshape.736), calls=%async_computation.11 | async-start | bytes 65536 | tf_op jit(solution)/shard_map/all_to_all | solution.py:149
  177.2 8.2 %copy-start.26 = (bf16[1,64,512]{2,0,1:T(2,128)(2,1)S(1)}, bf16[1,64,512]{2,0,1:T(2,128)(2,1)}, u32[]{:S(2)}) copy-start(bf16[1,64,512]{2,0,1:T(2,128)(2,1)} %get-tuple-element.19) | copy-start | bytes 196612
  177.2 8.2 %copy-start.27 = (f32[64,256]{1,0:T(8,128)S(1)}, f32[64,256]{1,0:T(8,128)}, u32[]{:S(2)}) copy-start(f32[64,256]{1,0:T(8,128)} %fusion.83) | copy-start | bytes 196612
  177.8 27.6 %copy-start.10 = (f32[130,512]{1,0:T(8,128)S(1)}, f32[130,512]{1,0:T(8,128)}, u32[]{:S(2)}) copy-start(f32[130,512]{1,0:T(8,128)} %fusion) | copy-start | bytes 798724
  179.4 12.7 %all-to-all-start.10 = ((bf16[8,2,1024]{2,1,0:T(2,128)(2,1)}), bf16[8,2,1024]{2,1,0:T(2,128)(2,1)S(1)}, u32[]{:S(2)}, u32[]{:S(2)}) async-start(bf16[8,2,1024]{2,1,0:T(2,128)(2,1)} %reshape.734), calls=%async_computation.10 | async-start | bytes 65536 | tf_op jit(solution)/shard_map/all_to_all | solution.py:149
  192.1 10.0 %all-to-all-start.9 = ((bf16[8,2,1024]{2,1,0:T(2,128)(2,1)}), bf16[8,2,1024]{2,1,0:T(2,128)(2,1)S(1)}, u32[]{:S(2)}, u32[]{:S(2)}) async-start(bf16[8,2,1024]{2,1,0:T(2,128)(2,1)} %reshape.732), calls=%async_computation.9 | async-start | bytes 65536 | tf_op jit(solution)/shard_map/all_to_all | solution.py:149
  195.7 19.7 %copy-start.12 = (f32[130,512]{1,0:T(8,128)S(1)}, f32[130,512]{1,0:T(8,128)}, u32[]{:S(2)}) copy-start(f32[130,512]{1,0:T(8,128)} %copy-done.11) | copy-start | bytes 798724
  202.0 10.0 %all-to-all-start.8 = ((bf16[8,2,1024]{2,1,0:T(2,128)(2,1)}), bf16[8,2,1024]{2,1,0:T(2,128)(2,1)S(1)}, u32[]{:S(2)}, u32[]{:S(2)}) async-start(bf16[8,2,1024]{2,1,0:T(2,128)(2,1)} %reshape.730), calls=%async_computation.8 | async-start | bytes 65536 | tf_op jit(solution)/shard_map/all_to_all | solution.py:149
  207.8 18.3 %copy-start.13 = (f32[130,512]{1,0:T(8,128)S(1)}, f32[130,512]{1,0:T(8,128)}, u32[]{:S(2)}) copy-start(f32[130,512]{1,0:T(8,128)} %fusion.2) | copy-start | bytes 798724
  212.0 10.7 %all-to-all-start.7 = ((bf16[8,2,4096]{2,1,0:T(2,128)(2,1)}), bf16[8,2,4096]{2,1,0:T(2,128)(2,1)S(1)}, u32[]{:S(2)}, u32[]{:S(2)}) async-start(bf16[8,2,4096]{2,1,0:T(2,128)(2,1)} %reshape.728), calls=%async_computation.7 | async-start | bytes 262144 | tf_op jit(solution)/shard_map/all_to_all | solution.py:149
  222.7 10.7 %copy-start.17 = (bf16[8,2,4096]{2,1,0:T(2,128)(2,1)}, bf16[8,2,4096]{2,1,0:T(2,128)(2,1)S(1)}, u32[]{:S(2)}) copy-start(bf16[8,2,4096]{2,1,0:T(2,128)(2,1)S(1)} %all-to-all-done.7) | copy-start | bytes 393220
  222.7 10.7 %all-to-all-start.6 = ((bf16[8,2,4096]{2,1,0:T(2,128)(2,1)}), bf16[8,2,4096]{2,1,0:T(2,128)(2,1)S(1)}, u32[]{:S(2)}, u32[]{:S(2)}) async-start(bf16[8,2,4096]{2,1,0:T(2,128)(2,1)} %reshape.726), calls=%async_computation.6 | async-start | bytes 262144 | tf_op jit(solution)/shard_map/all_to_all | solution.py:149
  233.3 10.7 %copy-start.19 = (bf16[8,2,4096]{2,1,0:T(2,128)(2,1)}, bf16[8,2,4096]{2,1,0:T(2,128)(2,1)S(1)}, u32[]{:S(2)}) copy-start(bf16[8,2,4096]{2,1,0:T(2,128)(2,1)S(1)} %all-to-all-done.6) | copy-start | bytes 393220
  233.3 10.7 %all-to-all-start.5 = ((bf16[8,2,4096]{2,1,0:T(2,128)(2,1)}), bf16[8,2,4096]{2,1,0:T(2,128)(2,1)S(1)}, u32[]{:S(2)}, u32[]{:S(2)}) async-start(bf16[8,2,4096]{2,1,0:T(2,128)(2,1)} %reshape.724), calls=%async_computation.5 | async-start | bytes 262144 | tf_op jit(solution)/shard_map/all_to_all | solution.py:149
  244.0 4.3 %copy-start.21 = (bf16[8,2,4096]{2,1,0:T(2,128)(2,1)}, bf16[8,2,4096]{2,1,0:T(2,128)(2,1)S(1)}, u32[]{:S(2)}) copy-start(bf16[8,2,4096]{2,1,0:T(2,128)(2,1)S(1)} %all-to-all-done.5) | copy-start | bytes 393220
  244.0 10.8 %all-to-all-start.4 = ((bf16[8,2,4096]{2,1,0:T(2,128)(2,1)}), bf16[8,2,4096]{2,1,0:T(2,128)(2,1)S(1)}, u32[]{:S(2)}, u32[]{:S(2)}) async-start(bf16[8,2,4096]{2,1,0:T(2,128)(2,1)} %reshape.722), calls=%async_computation.4 | async-start | bytes 262144 | tf_op jit(solution)/shard_map/all_to_all | solution.py:149
  251.9 7.3 %copy-start.28 = (s32[8,8,8]{2,1,0:T(8,128)S(1)}, s32[8,8,8]{2,1,0:T(8,128)}, u32[]{:S(2)}) copy-start(s32[8,8,8]{2,1,0:T(8,128)} %param.16) | copy-start | bytes 6148
  251.9 7.3 %copy-start.29 = (f32[8,8,8]{2,0,1:T(8,128)S(1)}, f32[8,8,8]{2,0,1:T(8,128)}, u32[]{:S(2)}) copy-start(f32[8,8,8]{2,0,1:T(8,128)} %multiply_add_fusion.4) | copy-start | bytes 6148
  252.0 7.4 %copy-start.30 = (f32[8,8,8]{2,0,1:T(8,128)S(1)}, f32[8,8,8]{2,0,1:T(8,128)}, u32[]{:S(2)}) copy-start(f32[8,8,8]{2,0,1:T(8,128)} %convolution_divide_fusion) | copy-start | bytes 6148
  252.0 7.4 %copy-start.31 = (f32[8,8,1,1]{1,0,3,2:T(8,128)S(1)}, f32[8,8,1,1]{1,0,3,2:T(8,128)}, u32[]{:S(2)}) copy-start(f32[8,8,1,1]{1,0,3,2:T(8,128)} %constant.62) | copy-start | bytes 772
  252.0 7.4 %copy-start.32 = (f32[8,8]{0,1:T(8,128)S(1)}, f32[8,8]{0,1:T(8,128)}, u32[]{:S(2)}) copy-start(f32[8,8]{0,1:T(8,128)} %constant.63) | copy-start | bytes 772
  253.2 6.7 %copy-start.3 = (f32[1,262,1024]{2,0,1:T(1,128)S(1)}, f32[1,262,1024]{2,0,1:T(1,128)}, u32[]{:S(2)}) copy-start(f32[1,262,1024]{2,0,1:T(1,128)} %copy-done.2) | copy-start | bytes 3219460
  254.8 5.0 %copy-start.23 = (bf16[8,2,4096]{2,1,0:T(2,128)(2,1)}, bf16[8,2,4096]{2,1,0:T(2,128)(2,1)S(1)}, u32[]{:S(2)}) copy-start(bf16[8,2,4096]{2,1,0:T(2,128)(2,1)S(1)} %all-to-all-done.4) | copy-start | bytes 393220
  254.8 15.0 %all-to-all-start.3 = ((bf16[8,2,16384]{2,1,0:T(2,128)(2,1)}), bf16[8,2,16384]{2,1,0:T(2,128)(2,1)}, u32[]{:S(2)}, u32[]{:S(2)}) async-start(bf16[8,2,16384]{2,1,0:T(2,128)(2,1)} %reshape.720), calls=%async_computation.3 | async-start | bytes 1048576 | tf_op jit(solution)/shard_map/all_to_all | solution.py:149
  260.6 4.9 %copy-start.5 = (f32[1,262,1024]{2,0,1:T(1,128)S(1)}, f32[1,262,1024]{2,0,1:T(1,128)}, u32[]{:S(2)}) copy-start(f32[1,262,1024]{2,0,1:T(1,128)} %copy-done.4) | copy-start | bytes 3219460
  265.5 9.8 %copy-start.7 = (f32[1,262,1024]{2,0,1:T(1,128)S(1)}, f32[1,262,1024]{2,0,1:T(1,128)}, u32[]{:S(2)}) copy-start(f32[1,262,1024]{2,0,1:T(1,128)} %copy-done.6) | copy-start | bytes 3219460
  269.9 20.5 %all-to-all-start.2 = ((bf16[8,2,16384]{2,1,0:T(2,128)(2,1)}), bf16[8,2,16384]{2,1,0:T(2,128)(2,1)}, u32[]{:S(2)}, u32[]{:S(2)}) async-start(bf16[8,2,16384]{2,1,0:T(2,128)(2,1)} %reshape.718), calls=%async_computation.2 | async-start | bytes 1048576 | tf_op jit(solution)/shard_map/all_to_all | solution.py:149
  290.4 7.3 %copy-start.20 = (bf16[8,2,4096]{2,1,0:T(2,128)(2,1)S(1)}, bf16[8,2,4096]{2,1,0:T(2,128)(2,1)}, u32[]{:S(2)}) copy-start(bf16[8,2,4096]{2,1,0:T(2,128)(2,1)} %copy-done.19) | copy-start | bytes 393220
  290.4 17.0 %all-to-all-start.1 = ((bf16[8,2,16384]{2,1,0:T(2,128)(2,1)}), bf16[8,2,16384]{2,1,0:T(2,128)(2,1)S(1)}, u32[]{:S(2)}, u32[]{:S(2)}) async-start(bf16[8,2,16384]{2,1,0:T(2,128)(2,1)} %reshape.716), calls=%async_computation.1 | async-start | bytes 1048576 | tf_op jit(solution)/shard_map/all_to_all | solution.py:149
  307.4 18.3 %all-to-all-start = ((bf16[8,2,16384]{2,1,0:T(2,128)(2,1)}), bf16[8,2,16384]{2,1,0:T(2,128)(2,1)}, u32[]{:S(2)}, u32[]{:S(2)}) async-start(bf16[8,2,16384]{2,1,0:T(2,128)(2,1)} %reshape.714), calls=%async_computation | async-start | bytes 1048576 | tf_op jit(solution)/shard_map/all_to_all | solution.py:149
  (15 other events, 28.1 us)

commit v2 on v0

v2 whole, which is shorter than its diff:
```python
import math

import jax
import jax.numpy as jnp
from jax import lax
from jax.sharding import PartitionSpec as P
from jax.experimental import pallas as pl
from jax.experimental.pallas import tpu as pltpu

gap_weights = [math.exp(-((k - 4) ** 2) / 8.0) for k in range(9)]
savgol_coeffs = [c / 231.0 for c in [-21.0, 14.0, 39.0, 54.0, 59.0, 54.0, 39.0, 14.0, -21.0]]
pyramid_filter = [0.125, 0.375, 0.375, 0.125]


def padded(block, sides, width):
    for axis, dim in sides:
        count = lax.axis_size(axis)
        forward = [(i, i + 1) for i in range(count - 1)]
        backward = [(target, source) for source, target in forward]
        low = lax.ppermute(
            lax.slice_in_dim(block, block.shape[dim] - width, None, axis=dim), axis, forward
        )
        high = lax.ppermute(lax.slice_in_dim(block, 0, width, axis=dim), axis, backward)
        block = jnp.concatenate([low, block, high], axis=dim)
    return block


def filter_matrix(out_count, in_count, step, shift, taps):
    out_at = lax.broadcasted_iota(jnp.int32, (out_count, in_count), 0)
    in_at = lax.broadcasted_iota(jnp.int32, (out_count, in_count), 1)
    place = in_at - step * out_at - shift
    total = jnp.zeros((out_count, in_count), jnp.float32)
    for k in range(len(taps)):
        total = total + jnp.where(place == k, taps[k], 0.0)
    return total


def inside_rows(count, first, total):
    places = first + lax.iota(jnp.int32, count)
    return ((places >= 0) & (places < total)).astype(jnp.float32)


def row_operators(taps, band_index, rows, total_rows, depth):
    hi = lax.Precision.HIGHEST
    wide = rows + 6
    keep_wide = inside_rows(wide, band_index * rows - 3, total_rows)
    keep_half = inside_rows(rows // 2 + 2, band_index * (rows // 2) - 1, total_rows // 2)
    down = filter_matrix(rows // 2 + 2, wide, 2, 0, pyramid_filter)
    down_two = filter_matrix(rows // 4, rows // 2 + 2, 2, 0, pyramid_filter)
    zs, hs, qs = [], [], []
    for b in range(taps.shape[0]):
        resample = filter_matrix(wide, rows + 12, 1, 0, [taps[b, k] for k in range(7)])
        resample = resample * keep_wide[:, None]
        half = jnp.dot(down, resample, precision=hi) * keep_half[:, None]
        quarter = jnp.dot(down_two, half, precision=hi)
        zs.append(resample[3 : 3 + rows])
        hs.append(half[1 : 1 + rows // 2])
        qs.append(quarter)
    pad = ((0, 0), (0, 0), (0, depth - (rows + 12)))
    return tuple(jnp.pad(jnp.stack(m), pad) for m in (zs, hs, qs))


def column_operators(taps, width):
    hi = lax.Precision.HIGHEST
    band = jnp.stack(
        [filter_matrix(128, 3 * 128, 1, 125, [taps[b, k] for k in range(7)]).T for b in range(taps.shape[0])]
    )
    halve = filter_matrix(width // 2, width, 2, -1, pyramid_filter).T
    halve_two = filter_matrix(width // 4, width // 2, 2, -1, pyramid_filter).T
    both = jnp.dot(halve, halve_two, precision=hi)
    return band, halve.astype(jnp.bfloat16), both.astype(jnp.bfloat16)


def split_two(a):
    high = a.astype(jnp.bfloat16)
    low = (a - high.astype(jnp.float32)).astype(jnp.bfloat16)
    return high, low


def mm(a, b):
    return jnp.dot(a, b, preferred_element_type=jnp.float32)


def pyramid_kernel(x_ref, band_ref, z_ref, h_ref, q_ref, halve_ref, both_ref, o0_ref, o1_ref, o2_ref, across_ref):
    x = x_ref[0, 0]
    used = x.shape[0]
    width = x.shape[1]
    tiles = width // 128
    table = band_ref[0]
    t_high = table.astype(jnp.bfloat16)
    rest = table - t_high.astype(jnp.float32)
    t_mid = rest.astype(jnp.bfloat16)
    t_low = (rest - t_mid.astype(jnp.float32)).astype(jnp.bfloat16)
    for j in range(tiles):
        lo = max(j - 1, 0) * 128
        hi_col = min(j + 2, tiles) * 128
        first = lo - (j - 1) * 128
        last = first + (hi_col - lo)
        window = x[:, lo:hi_col]
        acc = mm(window, t_high[first:last]) + mm(window, t_mid[first:last]) + mm(window, t_low[first:last])
        across_ref[0:used, j * 128 : (j + 1) * 128] = acc
    depth = across_ref.shape[0]
    across_ref[used:depth, :] = jnp.zeros((depth - used, width), jnp.float32)
    a_high, a_low = split_two(across_ref[...])

    def rows_of(m_ref):
        m_high, m_low = split_two(m_ref[0])
        return mm(m_high, a_high) + mm(m_high, a_low) + mm(m_low, a_high)

    o0_ref[0, 0] = rows_of(z_ref).astype(o0_ref.dtype)
    h_high, h_low = split_two(rows_of(h_ref))
    o1_ref[0, 0] = (mm(h_high, halve_ref[...]) + mm(h_low, halve_ref[...])).astype(o1_ref.dtype)
    q_high, q_low = split_two(rows_of(q_ref))
    o2_ref[0, 0] = (mm(q_high, both_ref[...]) + mm(q_low, both_ref[...])).astype(o2_ref.dtype)


def pyramid(extended, resample_taps, band_index, total_rows):
    dates, bands, used, width = extended.shape
    rows = used - 16
    depth = ((used + 127) // 128) * 128
    zs, hs, qs = row_operators(resample_taps[1], band_index, rows, total_rows, depth)
    band, halve, both = column_operators(resample_taps[0], width)
    out_shape = (
        jax.ShapeDtypeStruct((dates, bands, rows, width), jnp.bfloat16),
        jax.ShapeDtypeStruct((dates, bands, rows // 2, width // 2), jnp.bfloat16),
        jax.ShapeDtypeStruct((dates, bands, rows // 4, width // 4), jnp.bfloat16),
    )
    return pl.pallas_call(
        pyramid_kernel,
        grid=(dates, bands),
        in_specs=[
            pl.BlockSpec((1, 1, used, width), lambda d, b: (d, b, 0, 0)),
            pl.BlockSpec((1, 3 * 128, 128), lambda d, b: (b, 0, 0)),
            pl.BlockSpec((1, rows, depth), lambda d, b: (b, 0, 0)),
            pl.BlockSpec((1, rows // 2, depth), lambda d, b: (b, 0, 0)),
            pl.BlockSpec((1, rows // 4, depth), lambda d, b: (b, 0, 0)),
            pl.BlockSpec((width, width // 2), lambda d, b: (0, 0)),
            pl.BlockSpec((width, width // 4), lambda d, b: (0, 0)),
        ],
        out_specs=[
            pl.BlockSpec((1, 1, rows, width), lambda d, b: (d, b, 0, 0)),
            pl.BlockSpec((1, 1, rows // 2, width // 2), lambda d, b: (d, b, 0, 0)),
            pl.BlockSpec((1, 1, rows // 4, width // 4), lambda d, b: (d, b, 0, 0)),
        ],
        out_shape=out_shape,
        scratch_shapes=[pltpu.VMEM((depth, width), jnp.float32)],
    )(extended, band, zs, hs, qs, halve, both)


def smooth(level, clear):
    values = level.astype(jnp.float32)
    dates = values.shape[0]
    clear4 = clear[:, None]
    weight = 0.1 + 0.9 * clear4
    weighted = jnp.pad(weight * values, ((4, 4), (0, 0), (0, 0), (0, 0)))
    weight_pad = jnp.pad(weight, ((4, 4), (0, 0), (0, 0), (0, 0)))
    numer = jnp.zeros_like(values)
    denom = jnp.zeros_like(weight)
    for k in range(9):
        numer = numer + gap_weights[k] * weighted[k : k + dates]
        denom = denom + gap_weights[k] * weight_pad[k : k + dates]
    filled = clear4 * values + (1.0 - clear4) * (numer / denom)
    edged = jnp.pad(filled, ((4, 4), (0, 0), (0, 0), (0, 0)), mode="edge")
    result = jnp.zeros_like(values)
    for k in range(9):
        result = result + savgol_coeffs[k] * edged[k : k + dates]
    return result.astype(jnp.bfloat16)


def expand_mask(clear_mask, row_rep, col_rep):
    grown = jnp.repeat(jnp.repeat(clear_mask, row_rep, axis=1), col_rep, axis=2)
    return grown.astype(jnp.float32)


def expand_mask(clear_mask, row_rep, col_rep):
    grown = jnp.repeat(jnp.repeat(clear_mask, row_rep, axis=1), col_rep, axis=2)
    return grown.astype(jnp.float32)


def local(scenes, resample_taps, clear_mask):
    rows = scenes.shape[2]
    band_index = lax.axis_index("row")
    total_rows = rows * lax.axis_size("row")
    extended = padded(scenes, (("row", 2),), 6)
    extended = jnp.pad(extended, ((0, 0), (0, 0), (0, 4), (0, 0)))
    level_zero, level_one, level_two = pyramid(extended, resample_taps, band_index, total_rows)
    clear_fine = expand_mask(clear_mask, 4, 128)
    clear_half = expand_mask(clear_mask, 2, 64)
    clear_quarter = expand_mask(clear_mask, 1, 32)
    smooth_fine = smooth(
        lax.all_to_all(level_zero, "date", split_axis=2, concat_axis=0, tiled=True), clear_fine
    )
    smooth_half = smooth(
        lax.all_to_all(level_one, "date", split_axis=2, concat_axis=0, tiled=True), clear_half
    )
    smooth_quarter = smooth(
        lax.all_to_all(level_two, "date", split_axis=2, concat_axis=0, tiled=True), clear_quarter
    )
    return (smooth_fine, smooth_half, smooth_quarter)


def solution(mesh):
    in_specs = (P(("groups", "date"), None, "row", None), P(), P("groups", ("row", "date"), None))
    out_specs = (
        P("groups", None, ("row", "date"), None),
        P("groups", None, ("row", "date"), None),
        P("groups", None, ("row", "date"), None),
    )
    return jax.shard_map(local, mesh=mesh, in_specs=in_specs, out_specs=out_specs, check_vma=False)
```

time: 180 us -> 215 us (1.19)
  other arithmetic: 56 us -> 80.3 us
  Pallas kernels: 0 us -> 18.8 us
  matrix products: 30.2 us -> 27.5 us
    pallas_call x0 -> x1, Pallas kernels: none -> 18.8 us  [pyramid(): pl.pallas_call(pyramid_kernel, grid=(dates, bands), in_specs=[pl.BlockSpe...]
    mul x2 -> x6, other arithmetic: 0.01 us -> 17.9 us  [the longest x2 17.9 us: row_operators(): resample = resample * keep_wide[:, None]]
    add x0 -> x3, other arithmetic: none -> 17.5 us  [filter_matrix(): total = total + jnp.where(place == k, taps[k], 0.0)]
    convert_element_type x4 -> x3, other arithmetic: 15.4 us -> 1.98 us  [the longest x1 1.97 us: column_operators(): return (band, halve.astype(jnp.bfloat16), both.astype(jnp.bfloat16))]
    pallas_call x0 -> x3, local copies, waits for them, and re-layouts: none -> 7 us  [pyramid(): pl.pallas_call(pyramid_kernel, grid=(dates, bands), in_specs=[pl.BlockSpe...]
    slice x5 -> x3, local copies, waits for them, and re-layouts: 7.49 us -> 2.16 us  [the longest x2 1.45 us: row_operators(): taps[b, k]]
    select_n x2 -> x0, other arithmetic: 3.91 us -> none  [keep_rows(): return jnp.where(inside[None, None, :, None], values, 0.0)]
    select_n x2 -> x0, local copies, waits for them, and re-layouts: 3.45 us -> none  [keep_rows(): return jnp.where(inside[None, None, :, None], values, 0.0)]
  transfers between devices with their start and end apart: 5 -> 5, of which waited for: 3 -> 3; matrix products, arithmetic and copies ran while one was open for 20% -> 43% of each run, Pallas kernels for 0% -> 0%
where the time goes in v2:
time: 215 us; the launch traced here: 213 us
  other arithmetic  80.3 us (37%)
  waiting for transfers between devices  50.5 us (23%)
  matrix products  27.5 us (13%)
  Pallas kernels  18.8 us (9%)
  starting transfers between devices  18.2 us (8%)
  local copies, waits for them, and re-layouts  16.9 us (8%)
    all_to_all x1, waiting for transfers between devices, local(): lax.all_to_all(level_zero, 'date', split_axis=2, concat_axis=0, tiled=True)  33 us
    dot_general x4, matrix products, row_operators(): half = jnp.dot(down, resample, precision=hi) * keep_half[:, None]  20.7 us
    pallas_call x1, Pallas kernels, pyramid(): pl.pallas_call(pyramid_kernel, grid=(dates, bands), in_specs=[pl.BlockSpe...  18.8 us
    mul x2, other arithmetic, row_operators(): resample = resample * keep_wide[:, None]  17.9 us
    add x3, other arithmetic, filter_matrix(): total = total + jnp.where(place == k, taps[k], 0.0)  17.5 us
    add x3, other arithmetic, smooth(): filled = clear4 * values + (1.0 - clear4) * (numer / denom)  14.9 us
    all_to_all x1, waiting for transfers between devices, local(): lax.all_to_all(level_one, 'date', split_axis=2, concat_axis=0, tiled=True)  11.5 us
    convert_element_type x3, other arithmetic, smooth(): return result.astype(jnp.bfloat16)  8.65 us
  transfers between devices with their start and end apart: 5, of which 3 were waited for; matrix products, arithmetic and copies ran while one was open for 43% of the time, Pallas kernels for 0%

profile of v2, /device:TPU:0, one launch (start us, length us, event | category | flops | bytes accessed | tf_op | source)
XLA Modules:
  0.0 213.2 jit_solution(14292266496512269259)
XLA Ops:
  1.5 2.4 %collective-permute-start = (bf16[1,4,6,1024]{3,2,1,0:T(8,128)(2,1)S(1)}, bf16[1,4,6,1024]{3,2,1,0:T(8,128)(2,1)S(1)}, u32[]{:S(2)}, u32[]{:S(2)}) collective-permute-start(bf16[1,4,6,1024]{3,2,1,0:T(8,128)(2,1)S(1)} %get-tuple-element.11), channel_id=1, source_target_pairs={{0,1},{2,3},{4,5},{6,7},{8,9},{10,11},{12,13},{14,15},{16,17},{18,... | collective-permute-start | bytes 147464 | tf_op jit(solution)/shard_map/ppermute | solution.py:20
  8.1 5.1 %convolution_multiply_fusion.3 = f32[130,268]{1,0:T(8,128)S(1)} fusion(f32[262]{0:T(512)S(1)} %fusion.258, f32[]{:T(128)} %bitcast.37, f32[]{:T(128)} %bitcast.36, f32[]{:T(128)} %bitcast.35, f32[]{:T(128)} %bitcast.34, f32[]{:T(128)} %bitcast.33, f32[]{:T(128)} %bitcast.32, f32[]{:T(128)} %bitcast.31, f32[130]{0:T(256)S(1)} %and_convert_fusion, ...), kind=kOutput, calls=%fused_computation.142 | convolution fusion | flops 111525272 | bytes 141476 | tf_op jit(solution)/shard_map/dot_general | solution.py:54
  13.7 5.2 %convolution_multiply_fusion = f32[130,268]{1,0:T(8,128)S(1)} fusion(f32[]{:T(128)} %bitcast.61, f32[]{:T(128)} %bitcast.60, f32[]{:T(128)} %bitcast.59, f32[]{:T(128)} %bitcast.58, f32[]{:T(128)} %bitcast.57, f32[]{:T(128)} %bitcast.56, f32[]{:T(128)} %bitcast.55, f32[262]{0:T(512)S(1)} %fusion.258, f32[130]{0:T(256)S(1)} %and_convert_fusion, ...), kind=kOutput, calls=%fused_computation.139 | convolution fusion | flops 111525272 | bytes 141476 | tf_op jit(solution)/shard_map/dot_general | solution.py:54
  19.2 5.1 %convolution_multiply_fusion.1 = f32[130,268]{1,0:T(8,128)S(1)} fusion(f32[]{:T(128)} %bitcast.53, f32[]{:T(128)} %bitcast.52, f32[]{:T(128)} %bitcast.51, f32[]{:T(128)} %bitcast.50, f32[]{:T(128)} %bitcast.49, f32[]{:T(128)} %bitcast.48, f32[]{:T(128)} %bitcast.47, f32[262]{0:T(512)S(1)} %fusion.258, f32[130]{0:T(256)S(1)} %and_convert_fusion, ...), kind=kOutput, calls=%fused_computation.140 | convolution fusion | flops 111525272 | bytes 141476 | tf_op jit(solution)/shard_map/dot_general | solution.py:54
  24.7 5.2 %convolution_multiply_fusion.2 = f32[130,268]{1,0:T(8,128)S(1)} fusion(f32[]{:T(128)} %bitcast.45, f32[]{:T(128)} %bitcast.44, f32[]{:T(128)} %bitcast.43, f32[]{:T(128)} %bitcast.42, f32[]{:T(128)} %bitcast.41, f32[]{:T(128)} %bitcast.40, f32[]{:T(128)} %bitcast.39, f32[262]{0:T(512)S(1)} %fusion.258, f32[130]{0:T(256)S(1)} %and_convert_fusion, ...), kind=kOutput, calls=%fused_computation.141 | convolution fusion | flops 111525272 | bytes 141476 | tf_op jit(solution)/shard_map/dot_general | solution.py:54
  30.3 9.0 %add_multiply_fusion.3 = (f32[262,268]{1,0:T(8,128)S(1)}, f32[262,268]{1,0:T(8,128)S(1)}) fusion(f32[262]{0:T(512)S(1)} %fusion.258, f32[]{:T(128)} %bitcast.37, f32[]{:T(128)} %bitcast.36, f32[]{:T(128)} %bitcast.35, f32[]{:T(128)} %bitcast.34, f32[]{:T(128)} %bitcast.33, f32[]{:T(128)} %bitcast.32, f32[]{:T(128)} %bitcast.31, f32[]{:T(128)} %bitcast.45, ...), kind=kLoop, calls=%fused_computation.253 | loop fusion | flops 2527776 | bytes 562832 | tf_op jit(solution)/shard_map/mul | solution.py:53
  39.3 8.9 %add_multiply_fusion.1 = (f32[262,268]{1,0:T(8,128)S(1)}, f32[262,268]{1,0:T(8,128)S(1)}) fusion(f32[]{:T(128)} %bitcast.53, f32[]{:T(128)} %bitcast.52, f32[]{:T(128)} %bitcast.51, f32[]{:T(128)} %bitcast.50, f32[]{:T(128)} %bitcast.49, f32[]{:T(128)} %bitcast.48, f32[]{:T(128)} %bitcast.47, f32[262]{0:T(512)S(1)} %fusion.258, f32[]{:T(128)} %bitcast.61, ...), kind=kLoop, calls=%fused_computation.251 | loop fusion | flops 2527776 | bytes 562832 | tf_op jit(solution)/shard_map/mul | solution.py:53
  48.3 2.0 add_convert_fusion.halve_ref
  50.2 5.5 %fusion.66.both_ref = bf16[1024,256]{1,0:T(8,128)(2,1)} fusion(s32[512]{0:T(512)S(1)} %iota_multiply_fusion, s32[256]{0:T(256)S(1)} %iota_multiply_fusion.1), kind=kOutput, calls=%fused_computation.122 | convolution fusion | flops 1619394560 | bytes 527360 | tf_op jit(solution)/shard_map/dot_general | solution.py:70
  56.8 4.3 %select_add_fusion.4 = f32[1,384,128]{2,1,0:T(8,128)S(1)} fusion(f32[]{:T(128)} %bitcast.8, f32[]{:T(128)} %bitcast.7, f32[]{:T(128)} %bitcast.6, f32[]{:T(128)} %bitcast.5, f32[]{:T(128)} %bitcast.4, f32[]{:T(128)} %bitcast.3, f32[]{:T(128)} %bitcast.2), kind=kLoop, calls=%fused_computation.362 | loop fusion | flops 1081344 | bytes 196636 | tf_op jit(solution)/shard_map/add | solution.py:34
  61.2 4.4 %select_add_fusion.3 = f32[1,384,128]{2,1,0:T(8,128)S(1)} fusion(f32[]{:T(128)} %bitcast.15, f32[]{:T(128)} %bitcast.14, f32[]{:T(128)} %bitcast.13, f32[]{:T(128)} %bitcast.12, f32[]{:T(128)} %bitcast.11, f32[]{:T(128)} %bitcast.10, f32[]{:T(128)} %bitcast.9), kind=kLoop, calls=%fused_computation.361 | loop fusion | flops 1081344 | bytes 196636 | tf_op jit(solution)/shard_map/add | solution.py:34
  65.5 8.9 %select_add_fusion.1 = (f32[1,384,128]{2,1,0:T(8,128)S(1)}, f32[1,384,128]{2,1,0:T(8,128)S(1)}) fusion(f32[]{:T(128)} %bitcast.29, f32[]{:T(128)} %bitcast.28, f32[]{:T(128)} %bitcast.27, f32[]{:T(128)} %bitcast.26, f32[]{:T(128)} %bitcast.25, f32[]{:T(128)} %bitcast.24, f32[]{:T(128)} %bitcast.23, f32[]{:T(128)} %bitcast.22, f32[]{:T(128)} %bitcast.21, ...), kind=kLoop, calls=%fused_computation.359 | loop fusion | flops 1720320 | bytes 393272 | tf_op jit(solution)/shard_map/add | solution.py:34
  77.4 2.0 fusion.45.x_ref
  79.5 18.8 %shard_map.58 = (bf16[1,4,256,1024]{3,2,1,0:T(8,128)(2,1)}, bf16[1,4,128,512]{3,2,1,0:T(8,128)(2,1)}, bf16[1,4,64,256]{3,2,1,0:T(8,128)(2,1)}) custom-call(bf16[1,4,272,1024]{3,2,1,0:T(8,128)(2,1)} %fusion.45.x_ref, f32[4,384,128]{2,1,0:T(8,128)} %pad_maximum_fusion.4.band_ref, f32[4,256,384]{2,1,0:T(8,128)} %select_maximum_fusion.z_ref, ...), custom_call_target="tpu_custom_call" | custom-call | tf_op jit(solution)/shard_map/pallas_call | solution.py:128
  98.2 1.8 copy.13
  100.1 6.7 %all-to-all-start.2 = ((bf16[1,4,64,256]{3,1,0,2:T(4,128)(2,1)}), bf16[1,4,64,256]{3,1,0,2:T(4,128)(2,1)S(1)}, u32[]{:S(2)}, u32[]{:S(2)}) async-start(bf16[1,4,64,256]{3,1,0,2:T(4,128)(2,1)} %copy.13), calls=%async_computation.2 | async-start | bytes 262144 | tf_op jit(solution)/shard_map/all_to_all | solution.py:197
  106.7 2.2 %copy.11 = bf16[1,4,128,512]{3,1,0,2:T(4,128)(2,1)} copy(bf16[1,4,128,512]{3,2,1,0:T(8,128)(2,1)} %get-tuple-element.7) | data formatting | bytes 1048576 | tf_op jit(solution)/shard_map/pallas_call | solution.py:128
  109.0 6.0 %all-to-all-done.2 = bf16[1,4,64,256]{3,1,0,2:T(4,128)(2,1)S(1)} async-done(((bf16[1,4,64,256]{3,1,0,2:T(4,128)(2,1)}), bf16[1,4,64,256]{3,1,0,2:T(4,128)(2,1)S(1)}, u32[]{:S(2)}, u32[]{:S(2)}) %all-to-all-start.2) | async-done | bytes 131104 | tf_op jit(solution)/shard_map/all_to_all | solution.py:197
  114.9 3.5 %all-to-all-start.1 = ((bf16[1,4,128,512]{3,1,0,2:T(4,128)(2,1)}), bf16[1,4,128,512]{3,1,0,2:T(4,128)(2,1)S(1)}, u32[]{:S(2)}, u32[]{:S(2)}) async-start(bf16[1,4,128,512]{3,1,0,2:T(4,128)(2,1)} %copy.11), calls=%async_computation.1 | async-start | bytes 1048576 | tf_op jit(solution)/shard_map/all_to_all | solution.py:194
  118.8 2.9 %copy.9 = bf16[1,4,256,1024]{3,1,0,2:T(4,128)(2,1)} copy(bf16[1,4,256,1024]{3,2,1,0:T(8,128)(2,1)S(1)} %copy-done.1) | data formatting | bytes 4194304 | tf_op jit(solution)/shard_map/pallas_call | solution.py:128
  121.7 11.5 %all-to-all-done.1 = bf16[1,4,128,512]{3,1,0,2:T(4,128)(2,1)S(1)} async-done(((bf16[1,4,128,512]{3,1,0,2:T(4,128)(2,1)}), bf16[1,4,128,512]{3,1,0,2:T(4,128)(2,1)S(1)}, u32[]{:S(2)}, u32[]{:S(2)}) %all-to-all-start.1) | async-done | bytes 524320 | tf_op jit(solution)/shard_map/all_to_all | solution.py:194
  133.2 4.4 %all-to-all-start = ((bf16[1,4,256,1024]{3,1,0,2:T(4,128)(2,1)}), bf16[1,4,256,1024]{3,1,0,2:T(4,128)(2,1)}, u32[]{:S(2)}, u32[]{:S(2)}) async-start(bf16[1,4,256,1024]{3,1,0,2:T(4,128)(2,1)} %copy.9), calls=%async_computation | async-start | bytes 4194304 | tf_op jit(solution)/shard_map/all_to_all | solution.py:191
  140.5 1.3 broadcast_in_dim.351
  141.8 1.4 convert_element_type.164
  143.3 2.0 fusion.187
  145.3 1.3 fusion.99
  150.3 2.0 fusion.73
  152.3 33.0 %all-to-all-done = bf16[1,4,256,1024]{3,1,0,2:T(4,128)(2,1)} async-done(((bf16[1,4,256,1024]{3,1,0,2:T(4,128)(2,1)}), bf16[1,4,256,1024]{3,1,0,2:T(4,128)(2,1)}, u32[]{:S(2)}, u32[]{:S(2)}) %all-to-all-start) | async-done | bytes 2097184 | tf_op jit(solution)/shard_map/all_to_all | solution.py:191
  185.3 2.8 %convert.9 = f32[1,4,8,32,1024]{4,1,3,2,0:T(4,128)S(1)} convert(bf16[1,4,8,32,1024]{4,1,3,2,0:T(4,128)(2,1)} %bitcast.95) | non-fusion elementwise | flops 1048576 | bytes 6291456 | tf_op jit(solution)/shard_map/convert_element_type | solution.py:151
  188.1 4.6 %bitcast_multiply_fusion = f32[8,4,32,1024]{3,2,1,0:T(8,128)} fusion(f32[1,4,8,32,1024]{4,1,3,2,0:T(4,128)S(1)} %convert.9, f32[8,32,1024]{2,1,0:T(8,128)S(1)} %get-tuple-element.16), kind=kLoop, calls=%fused_computation.82 | loop fusion | flops 1048576 | bytes 9437184 | tf_op jit(solution)/shard_map/mul | solution.py:155
  192.7 14.1 %fusion.43 = f32[8,4,32,1024]{3,2,1,0:T(8,128)S(1)} fusion(f32[8,4,32,1024]{3,2,1,0:T(8,128)} %bitcast_multiply_fusion, f32[1,4,8,32,1024]{4,1,3,2,0:T(4,128)S(1)} %convert.9, f32[8,32,1024]{2,1,0:T(8,128)} %fusion.99, f32[8,32,1024]{2,1,0:T(8,128)} %get-tuple-element.15, f32[8,32,1024]{2,1,0:T(8,128)S(1)} %convert_element_type.164), kind=kLoop, calls=%fused_computation.84 | loop fusion | flops 20971520 | bytes 15728640 | tf_op jit(solution)/shard_map/add | solution.py:162
  207.4 5.8 %fusion.7 = bf16[8,4,32,1024]{3,2,1,0:T(8,128)(2,1)} fusion(f32[8,4,32,1024]{3,2,1,0:T(8,128)S(1)} %fusion.43, f32[4,4,32,1024]{3,2,1,0:T(8,128)S(1)} %reshape.378, f32[4,4,32,1024]{3,2,1,0:T(8,128)S(1)} %reshape.377), kind=kLoop, calls=%fused_computation.44 | loop fusion | flops 27262976 | bytes 10485760 | tf_op jit(solution)/shard_map/convert_element_type | solution.py:167
  (72 shorter events, 18.1 us)
Async XLA Ops:
  1.5 75.9 %collective-permute-start = (bf16[1,4,6,1024]{3,2,1,0:T(8,128)(2,1)S(1)}, bf16[1,4,6,1024]{3,2,1,0:T(8,128)(2,1)S(1)}, u32[]{:S(2)}, u32[]{:S(2)}) collective-permute-start(bf16[1,4,6,1024]{3,2,1,0:T(8,128)(2,1)S(1)} %get-tuple-element.11), channel_id=1, source_target_pairs={{0,1},{2,3},{4,5},{6,7},{8,9},{10,11},{12,13},{14,15},{16,17},{18,... | collective-permute-start | bytes 147464 | tf_op jit(solution)/shard_map/ppermute | solution.py:20
  3.9 73.5 %collective-permute-start.1 = (bf16[1,4,6,1024]{3,2,1,0:T(8,128)(2,1)S(1)}, bf16[1,4,6,1024]{3,2,1,0:T(8,128)(2,1)S(1)}, u32[]{:S(2)}, u32[]{:S(2)}) collective-permute-start(bf16[1,4,6,1024]{3,2,1,0:T(8,128)(2,1)S(1)} %get-tuple-element.12), channel_id=1, source_target_pairs={{1,0},{3,2},{5,4},{7,6},{9,8},{11,10},{13,12},{15,14},{17,16},{19,... | collective-permute-start | bytes 147464 | tf_op jit(solution)/shard_map/ppermute | solution.py:23
  55.8 21.6 %copy-start = (bf16[1,4,256,1024]{3,2,1,0:T(8,128)(2,1)S(1)}, bf16[1,4,256,1024]{3,2,1,0:T(8,128)(2,1)}, u32[]{:S(2)}) copy-start(bf16[1,4,256,1024]{3,2,1,0:T(8,128)(2,1)} %param.3) | copy-start | bytes 6291460
  79.5 39.0 %copy-start.3 = (s32[8,8,8]{2,1,0:T(8,128)S(1)}, s32[8,8,8]{2,1,0:T(8,128)}, u32[]{:S(2)}) copy-start(s32[8,8,8]{2,1,0:T(8,128)} %param.5) | copy-start | bytes 6148
  98.2 20.5 %copy-start.1 = (bf16[1,4,256,1024]{3,2,1,0:T(8,128)(2,1)S(1)}, bf16[1,4,256,1024]{3,2,1,0:T(8,128)(2,1)}, u32[]{:S(2)}) copy-start(bf16[1,4,256,1024]{3,2,1,0:T(8,128)(2,1)} %get-tuple-element.6) | copy-start | bytes 6291460
  100.1 14.9 %all-to-all-start.2 = ((bf16[1,4,64,256]{3,1,0,2:T(4,128)(2,1)}), bf16[1,4,64,256]{3,1,0,2:T(4,128)(2,1)S(1)}, u32[]{:S(2)}, u32[]{:S(2)}) async-start(bf16[1,4,64,256]{3,1,0,2:T(4,128)(2,1)} %copy.13), calls=%async_computation.2 | async-start | bytes 262144 | tf_op jit(solution)/shard_map/all_to_all | solution.py:197
  114.9 18.2 %all-to-all-start.1 = ((bf16[1,4,128,512]{3,1,0,2:T(4,128)(2,1)}), bf16[1,4,128,512]{3,1,0,2:T(4,128)(2,1)S(1)}, u32[]{:S(2)}, u32[]{:S(2)}) async-start(bf16[1,4,128,512]{3,1,0,2:T(4,128)(2,1)} %copy.11), calls=%async_computation.1 | async-start | bytes 1048576 | tf_op jit(solution)/shard_map/all_to_all | solution.py:194
  133.2 52.2 %all-to-all-start = ((bf16[1,4,256,1024]{3,1,0,2:T(4,128)(2,1)}), bf16[1,4,256,1024]{3,1,0,2:T(4,128)(2,1)}, u32[]{:S(2)}, u32[]{:S(2)}) async-start(bf16[1,4,256,1024]{3,1,0,2:T(4,128)(2,1)} %copy.9), calls=%async_computation | async-start | bytes 4194304 | tf_op jit(solution)/shard_map/all_to_all | solution.py:191
  143.2 4.7 %copy-start.2 = (f32[8,8,256]{2,1,0:T(8,128)S(1)}, f32[8,8,256]{2,1,0:T(8,128)}, u32[]{:S(2)}) copy-start(f32[8,8,256]{2,1,0:T(8,128)} %fusion.243) | copy-start | bytes 196612

commit v3 on v2

--- a/solution.py
+++ b/solution.py
@@ -25,50 +25,11 @@
     return block
 
 
-def filter_matrix(out_count, in_count, step, shift, taps):
-    out_at = lax.broadcasted_iota(jnp.int32, (out_count, in_count), 0)
-    in_at = lax.broadcasted_iota(jnp.int32, (out_count, in_count), 1)
-    place = in_at - step * out_at - shift
-    total = jnp.zeros((out_count, in_count), jnp.float32)
-    for k in range(len(taps)):
-        total = total + jnp.where(place == k, taps[k], 0.0)
-    return total
-
-
-def inside_rows(count, first, total):
-    places = first + lax.iota(jnp.int32, count)
-    return ((places >= 0) & (places < total)).astype(jnp.float32)
-
-
-def row_operators(taps, band_index, rows, total_rows, depth):
-    hi = lax.Precision.HIGHEST
-    wide = rows + 6
-    keep_wide = inside_rows(wide, band_index * rows - 3, total_rows)
-    keep_half = inside_rows(rows // 2 + 2, band_index * (rows // 2) - 1, total_rows // 2)
-    down = filter_matrix(rows // 2 + 2, wide, 2, 0, pyramid_filter)
-    down_two = filter_matrix(rows // 4, rows // 2 + 2, 2, 0, pyramid_filter)
-    zs, hs, qs = [], [], []
-    for b in range(taps.shape[0]):
-        resample = filter_matrix(wide, rows + 12, 1, 0, [taps[b, k] for k in range(7)])
-        resample = resample * keep_wide[:, None]
-        half = jnp.dot(down, resample, precision=hi) * keep_half[:, None]
-        quarter = jnp.dot(down_two, half, precision=hi)
-        zs.append(resample[3 : 3 + rows])
-        hs.append(half[1 : 1 + rows // 2])
-        qs.append(quarter)
-    pad = ((0, 0), (0, 0), (0, depth - (rows + 12)))
-    return tuple(jnp.pad(jnp.stack(m), pad) for m in (zs, hs, qs))
-
-
-def column_operators(taps, width):
-    hi = lax.Precision.HIGHEST
-    band = jnp.stack(
-        [filter_matrix(128, 3 * 128, 1, 125, [taps[b, k] for k in range(7)]).T for b in range(taps.shape[0])]
-    )
-    halve = filter_matrix(width // 2, width, 2, -1, pyramid_filter).T
-    halve_two = filter_matrix(width // 4, width // 2, 2, -1, pyramid_filter).T
-    both = jnp.dot(halve, halve_two, precision=hi)
-    return band, halve.astype(jnp.bfloat16), both.astype(jnp.bfloat16)
+def inside_rows(count, first, valid, total):
+    at = lax.iota(jnp.int32, count)
+    places = first + at
+    keep = (places >= 0) & (places < total) & (at < valid)
+    return keep.astype(jnp.float32)[:, None]
 
 
 def split_two(a):
@@ -81,12 +42,46 @@
     return jnp.dot(a, b, preferred_element_type=jnp.float32)
 
 
-def pyramid_kernel(x_ref, band_ref, z_ref, h_ref, q_ref, halve_ref, both_ref, o0_ref, o1_ref, o2_ref, across_ref):
+def band_table(rows, cols, shift, taps):
+    step, weights = taps
+    s_at = lax.broadcasted_iota(jnp.int32, (rows, cols), 0)
+    c_at = lax.broadcasted_iota(jnp.int32, (rows, cols), 1)
+    place = s_at - step * c_at - shift
+    total = jnp.zeros((rows, cols), jnp.float32)
+    for k, w in enumerate(weights):
+        total = total + jnp.where(place == k, w, 0.0)
+    return total
+
+
+def halve_columns(values, table, out_ref):
+    width = values.shape[1]
+    high, low = split_two(values)
+    for j in range(width // 256):
+        lo = max(256 * j - 128, 0)
+        hi_col = min(256 * j + 384, width)
+        first = lo - (256 * j - 128)
+        last = first + (hi_col - lo)
+        part = table[first:last]
+        out_ref[j] = mm(high[:, lo:hi_col], part) + mm(low[:, lo:hi_col], part)
+
+
+def halve_rows(source_ref, count):
+    total = pyramid_filter[0] * source_ref[:, pl.ds(0, count, stride=2), :]
+    for p in range(1, 4):
+        total = total + pyramid_filter[p] * source_ref[:, pl.ds(p, count, stride=2), :]
+    return jnp.concatenate([total[j] for j in range(total.shape[0])], axis=1)
+
+
+def pyramid_kernel(taps_ref, x_ref, keep_wide_ref, keep_half_ref, o0_ref, o1_ref, o2_ref,
+                   across_ref, wide_ref, half_ref, quarter_ref):
+    b = pl.program_id(1)
     x = x_ref[0, 0]
     used = x.shape[0]
     width = x.shape[1]
     tiles = width // 128
-    table = band_ref[0]
+    column = [taps_ref[0, b, k] for k in range(7)]
+    row = [taps_ref[1, b, k] for k in range(7)]
+    table = band_table(3 * 128, 128, 125, (1, column))
     t_high = table.astype(jnp.bfloat16)
     rest = table - t_high.astype(jnp.float32)
     t_mid = rest.astype(jnp.bfloat16)
@@ -101,25 +96,36 @@
         across_ref[0:used, j * 128 : (j + 1) * 128] = acc
     depth = across_ref.shape[0]
     across_ref[used:depth, :] = jnp.zeros((depth - used, width), jnp.float32)
-    a_high, a_low = split_two(across_ref[...])
-
-    def rows_of(m_ref):
-        m_high, m_low = split_two(m_ref[0])
-        return mm(m_high, a_high) + mm(m_high, a_low) + mm(m_low, a_high)
-
-    o0_ref[0, 0] = rows_of(z_ref).astype(o0_ref.dtype)
-    h_high, h_low = split_two(rows_of(h_ref))
-    o1_ref[0, 0] = (mm(h_high, halve_ref[...]) + mm(h_low, halve_ref[...])).astype(o1_ref.dtype)
-    q_high, q_low = split_two(rows_of(q_ref))
-    o2_ref[0, 0] = (mm(q_high, both_ref[...]) + mm(q_low, both_ref[...])).astype(o2_ref.dtype)
+    n_wide = wide_ref.shape[1]
+    total = row[0] * across_ref[pl.ds(0, n_wide), :]
+    for k in range(1, 7):
+        total = total + row[k] * across_ref[pl.ds(k, n_wide), :]
+    total = total * keep_wide_ref[...]
+    for j in range(tiles):
+        wide_ref[j] = total[:, 128 * j : 128 * (j + 1)]
+    rows = o0_ref.shape[2]
+    for j in range(tiles):
+        o0_ref[0, 0, :, 128 * j : 128 * (j + 1)] = wide_ref[j, pl.ds(3, rows), :].astype(o0_ref.dtype)
+    n_half = keep_half_ref.shape[0]
+    halves = halve_rows(wide_ref, n_half) * keep_half_ref[...]
+    down = band_table(512, 128, 127, (2, pyramid_filter)).astype(jnp.bfloat16)
+    halve_columns(halves, down, half_ref)
+    for j in range(tiles // 2):
+        o1_ref[0, 0, :, 128 * j : 128 * (j + 1)] = half_ref[j, pl.ds(1, rows // 2), :].astype(o1_ref.dtype)
+    quarters = halve_rows(half_ref, rows // 4)
+    halve_columns(quarters, down, quarter_ref)
+    for j in range(tiles // 4):
+        o2_ref[0, 0, :, 128 * j : 128 * (j + 1)] = quarter_ref[j].astype(o2_ref.dtype)
 
 
 def pyramid(extended, resample_taps, band_index, total_rows):
     dates, bands, used, width = extended.shape
     rows = used - 16
-    depth = ((used + 127) // 128) * 128
-    zs, hs, qs = row_operators(resample_taps[1], band_index, rows, total_rows, depth)
-    band, halve, both = column_operators(resample_taps[0], width)
+    n_wide = rows + 24
+    n_half = rows // 2 + 8
+    depth = n_wide + 8
+    keep_wide = inside_rows(n_wide, band_index * rows - 3, rows + 6, total_rows)
+    keep_half = inside_rows(n_half, band_index * (rows // 2) - 1, rows // 2 + 2, total_rows // 2)
     out_shape = (
         jax.ShapeDtypeStruct((dates, bands, rows, width), jnp.bfloat16),
         jax.ShapeDtypeStruct((dates, bands, rows // 2, width // 2), jnp.bfloat16),
@@ -129,13 +135,10 @@
         pyramid_kernel,
         grid=(dates, bands),
         in_specs=[
+            pl.BlockSpec(memory_space=pltpu.SMEM),
             pl.BlockSpec((1, 1, used, width), lambda d, b: (d, b, 0, 0)),
-            pl.BlockSpec((1, 3 * 128, 128), lambda d, b: (b, 0, 0)),
-            pl.BlockSpec((1, rows, depth), lambda d, b: (b, 0, 0)),
-            pl.BlockSpec((1, rows // 2, depth), lambda d, b: (b, 0, 0)),
-            pl.BlockSpec((1, rows // 4, depth), lambda d, b: (b, 0, 0)),
-            pl.BlockSpec((width, width // 2), lambda d, b: (0, 0)),
-            pl.BlockSpec((width, width // 4), lambda d, b: (0, 0)),
+            pl.BlockSpec((n_wide, 1), lambda d, b: (0, 0)),
+            pl.BlockSpec((n_half, 1), lambda d, b: (0, 0)),
         ],
         out_specs=[
             pl.BlockSpec((1, 1, rows, width), lambda d, b: (d, b, 0, 0)),
@@ -143,8 +146,13 @@
             pl.BlockSpec((1, 1, rows // 4, width // 4), lambda d, b: (d, b, 0, 0)),
         ],
         out_shape=out_shape,
-        scratch_shapes=[pltpu.VMEM((depth, width), jnp.float32)],
-    )(extended, band, zs, hs, qs, halve, both)
+        scratch_shapes=[
+            pltpu.VMEM((depth, width), jnp.float32),
+            pltpu.VMEM((width // 128, n_wide, 128), jnp.float32),
+            pltpu.VMEM((width // 256, n_half, 128), jnp.float32),
+            pltpu.VMEM((width // 512, rows // 4, 128), jnp.float32),
+        ],
+    )(resample_taps, extended, keep_wide, keep_half)
 
 
 def smooth(level, clear):

time: 215 us -> 138 us (0.64)
  other arithmetic: 80.3 us -> 41.8 us
  matrix products: 27.5 us -> 0 us
  Pallas kernels: 18.8 us -> 13.5 us
  local copies, waits for them, and re-layouts: 16.9 us -> 13.8 us
    dot_general x9 -> x0, matrix products: 27.5 us -> none  [the longest x4 20.7 us: row_operators(): half = jnp.dot(down, resample, precision=hi) * keep_half[:, None]]
    mul x6 -> x0, other arithmetic: 17.9 us -> none  [the longest x2 17.9 us: row_operators(): resample = resample * keep_wide[:, None]]
    add x3 -> x0, other arithmetic: 17.5 us -> none  [filter_matrix(): total = total + jnp.where(place == k, taps[k], 0.0)]
    pallas_call x1, Pallas kernels: 18.8 us -> 13.5 us  [pyramid(): pl.pallas_call(pyramid_kernel, grid=(dates, bands), in_specs=[pl.BlockSpe...]
    another operation x4 -> x0, other arithmetic: 4.02 us -> none  [the longest x3 3.06 us: row_operators(): return tuple((jnp.pad(jnp.stack(m), pad) for m in (zs, hs, qs)))]
    slice x3 -> x0, local copies, waits for them, and re-layouts: 2.16 us -> none  [the longest x2 1.45 us: row_operators(): taps[b, k]]
  transfers between devices with their start and end apart: 5 -> 5, of which waited for: 3 -> 4; matrix products, arithmetic and copies ran while one was open for 43% -> 15% of each run, Pallas kernels for 0% -> 0%
where the time goes in v3:
time: 138 us
  waiting for transfers between devices  49.3 us (36%)
  other arithmetic  41.8 us (30%)
  starting transfers between devices  18.3 us (13%)
  local copies, waits for them, and re-layouts  13.8 us (10%)
  Pallas kernels  13.5 us (10%)
    all_to_all x1, waiting for transfers between devices, local(): lax.all_to_all(level_zero, 'date', split_axis=2, concat_axis=0, tiled=True)  32.5 us
    add x3, other arithmetic, smooth(): filled = clear4 * values + (1.0 - clear4) * (numer / denom)  15 us
    pallas_call x1, Pallas kernels, pyramid(): pl.pallas_call(pyramid_kernel, grid=(dates, bands), in_specs=[pl.BlockSpe...  13.5 us
    all_to_all x1, waiting for transfers between devices, local(): lax.all_to_all(level_one, 'date', split_axis=2, concat_axis=0, tiled=True)  10.7 us
    convert_element_type x3, other arithmetic, smooth(): return result.astype(jnp.bfloat16)  8.65 us
    pallas_call x3, local copies, waits for them, and re-layouts, pyramid(): pl.pallas_call(pyramid_kernel, grid=(dates, bands), in_specs=[pl.BlockSpe...  7 us
    all_to_all x1, starting transfers between devices, local(): lax.all_to_all(level_two, 'date', split_axis=2, concat_axis=0, tiled=True)  6.66 us
    all_to_all x1, waiting for transfers between devices, local(): lax.all_to_all(level_two, 'date', split_axis=2, concat_axis=0, tiled=True)  5.53 us
  transfers between devices with their start and end apart: 5, of which 4 were waited for; matrix products, arithmetic and copies ran while one was open for 15% of the time, Pallas kernels for 0%

profile of v3, /device:TPU:0, one launch (start us, length us, event | category | flops | bytes accessed | tf_op | source)
XLA Modules:
  0.0 137.7 jit_solution(5404322035275822412)
XLA Ops:
  0.6 0.9 fusion.189
  1.5 2.4 %collective-permute-start = (bf16[1,4,6,1024]{3,2,1,0:T(8,128)(2,1)S(1)}, bf16[1,4,6,1024]{3,2,1,0:T(8,128)(2,1)S(1)}, u32[]{:S(2)}, u32[]{:S(2)}) collective-permute-start(bf16[1,4,6,1024]{3,2,1,0:T(8,128)(2,1)S(1)} %get-tuple-element.11), channel_id=1, source_target_pairs={{0,1},{2,3},{4,5},{6,7},{8,9},{10,11},{12,13},{14,15},{16,17},{18,... | collective-permute-start | bytes 147464 | tf_op jit(solution)/shard_map/ppermute | solution.py:20
  3.9 1.3 collective-permute-start.1
  5.2 0.7 fusion.166.keep_wide_ref
  5.9 0.6 fusion.171.keep_half_ref
  6.5 0.5 collective-permute-done.1
  7.0 3.6 %fusion.45.x_ref = bf16[1,4,272,1024]{3,2,1,0:T(8,128)(2,1)} fusion(bf16[1,4,6,1024]{3,2,1,0:T(8,128)(2,1)S(1)} %collective-permute-done.1, bf16[1,4,256,1024]{3,2,1,0:T(8,128)(2,1)} %param.3, bf16[1,4,6,1024]{3,2,1,0:T(8,128)(2,1)S(1)} %collective-permute-done), kind=kLoop, calls=%fused_computation.92 | loop fusion | flops 11141120 | bytes 4423680 | tf_op jit(solution)/shard_map/concatenate | solution.py:24
  10.7 13.5 %shard_map.58 = (bf16[1,4,256,1024]{3,2,1,0:T(8,128)(2,1)}, bf16[1,4,128,512]{3,2,1,0:T(8,128)(2,1)}, bf16[1,4,64,256]{3,2,1,0:T(8,128)(2,1)}) custom-call(f32[2,4,7]{2,1,0:T(4,128)} %taps_ref.1, bf16[1,4,272,1024]{3,2,1,0:T(8,128)(2,1)} %fusion.45.x_ref, f32[280,1]{1,0:T(8,128)} %fusion.166.keep_wide_ref, f32[136,1]{1,0:T(8,128)} %fusion.171.keep_half_ref), custom_call_target="tpu_custom_call" | custom-call | tf_op jit(solution)/shard_map/pallas_call | solution.py:134
  24.1 1.8 %copy.21 = bf16[1,4,64,256]{3,1,0,2:T(4,128)(2,1)} copy(bf16[1,4,64,256]{3,2,1,0:T(8,128)(2,1)} %get-tuple-element.8) | data formatting | bytes 262144 | tf_op jit(solution)/shard_map/pallas_call | solution.py:134
  25.9 6.7 %all-to-all-start.2 = ((bf16[1,4,64,256]{3,1,0,2:T(4,128)(2,1)}), bf16[1,4,64,256]{3,1,0,2:T(4,128)(2,1)S(1)}, u32[]{:S(2)}, u32[]{:S(2)}) async-start(bf16[1,4,64,256]{3,1,0,2:T(4,128)(2,1)} %copy.21), calls=%async_computation.2 | async-start | bytes 262144 | tf_op jit(solution)/shard_map/all_to_all | solution.py:205
  32.6 2.3 %copy.19 = bf16[1,4,128,512]{3,1,0,2:T(4,128)(2,1)} copy(bf16[1,4,128,512]{3,2,1,0:T(8,128)(2,1)} %get-tuple-element.7) | data formatting | bytes 1048576 | tf_op jit(solution)/shard_map/pallas_call | solution.py:134
  34.9 5.5 %all-to-all-done.2 = bf16[1,4,64,256]{3,1,0,2:T(4,128)(2,1)S(1)} async-done(((bf16[1,4,64,256]{3,1,0,2:T(4,128)(2,1)}), bf16[1,4,64,256]{3,1,0,2:T(4,128)(2,1)S(1)}, u32[]{:S(2)}, u32[]{:S(2)}) %all-to-all-start.2) | async-done | bytes 131104 | tf_op jit(solution)/shard_map/all_to_all | solution.py:205
  40.4 3.5 %all-to-all-start.1 = ((bf16[1,4,128,512]{3,1,0,2:T(4,128)(2,1)}), bf16[1,4,128,512]{3,1,0,2:T(4,128)(2,1)S(1)}, u32[]{:S(2)}, u32[]{:S(2)}) async-start(bf16[1,4,128,512]{3,1,0,2:T(4,128)(2,1)} %copy.19), calls=%async_computation.1 | async-start | bytes 1048576 | tf_op jit(solution)/shard_map/all_to_all | solution.py:202
  44.2 2.9 %copy.17 = bf16[1,4,256,1024]{3,1,0,2:T(4,128)(2,1)} copy(bf16[1,4,256,1024]{3,2,1,0:T(8,128)(2,1)S(1)} %copy-done) | data formatting | bytes 4194304 | tf_op jit(solution)/shard_map/pallas_call | solution.py:134
  47.1 10.7 %all-to-all-done.1 = bf16[1,4,128,512]{3,1,0,2:T(4,128)(2,1)S(1)} async-done(((bf16[1,4,128,512]{3,1,0,2:T(4,128)(2,1)}), bf16[1,4,128,512]{3,1,0,2:T(4,128)(2,1)S(1)}, u32[]{:S(2)}, u32[]{:S(2)}) %all-to-all-start.1) | async-done | bytes 524320 | tf_op jit(solution)/shard_map/all_to_all | solution.py:202
  57.9 4.5 %all-to-all-start = ((bf16[1,4,256,1024]{3,1,0,2:T(4,128)(2,1)}), bf16[1,4,256,1024]{3,1,0,2:T(4,128)(2,1)}, u32[]{:S(2)}, u32[]{:S(2)}) async-start(bf16[1,4,256,1024]{3,1,0,2:T(4,128)(2,1)} %copy.17), calls=%async_computation | async-start | bytes 4194304 | tf_op jit(solution)/shard_map/all_to_all | solution.py:199
  62.4 0.7 fusion.181
  63.6 0.9 add.382
  65.4 1.3 broadcast_in_dim.43
  66.7 1.4 %convert_element_type.158 = f32[8,32,1024]{2,1,0:T(8,128)S(1)} reshape(f32[8,32,8,128]{3,2,1,0:T(8,128)} %broadcast_in_dim.43) | data formatting | bytes 2097152 | tf_op jit(solution)/shard_map/convert_element_type | solution.py:185
  68.1 1.9 %fusion.134 = f32[8,16,512]{2,1,0:T(8,128)S(1)} fusion(f32[8,1,16,512]{3,2,0,1:T(8,128)} %add.382), kind=kLoop, calls=%fused_computation.231 | loop fusion | flops 1048576 | bytes 524288 | tf_op jit(solution)/shard_map/div | solution.py:170
  70.1 1.4 fusion.76
  71.5 1.2 broadcast_subtract_fusion
  73.0 0.8 fusion.108
  73.9 0.3 bitcast_multiply_fusion.2
  74.3 0.7 fusion.103
  75.1 2.0 %fusion.50 = bf16[8,4,16,512]{3,2,1,0:T(8,128)(2,1)} fusion(f32[8,4,16,512]{3,2,1,0:T(8,128)S(1)} %fusion.103, f32[4,4,16,512]{3,2,1,0:T(8,128)S(1)} %reshape.223, f32[4,4,16,512]{3,2,1,0:T(8,128)S(1)} %reshape.222), kind=kLoop, calls=%fused_computation.119 | loop fusion | flops 6815744 | bytes 2621440 | tf_op jit(solution)/shard_map/convert_element_type | solution.py:175
  77.1 32.5 %all-to-all-done = bf16[1,4,256,1024]{3,1,0,2:T(4,128)(2,1)} async-done(((bf16[1,4,256,1024]{3,1,0,2:T(4,128)(2,1)}), bf16[1,4,256,1024]{3,1,0,2:T(4,128)(2,1)}, u32[]{:S(2)}, u32[]{:S(2)}) %all-to-all-start) | async-done | bytes 2097184 | tf_op jit(solution)/shard_map/all_to_all | solution.py:199
  109.7 2.8 %convert.9 = f32[1,4,8,32,1024]{4,1,3,2,0:T(4,128)S(1)} convert(bf16[1,4,8,32,1024]{4,1,3,2,0:T(4,128)(2,1)} %bitcast.25) | non-fusion elementwise | flops 1048576 | bytes 6291456 | tf_op jit(solution)/shard_map/convert_element_type | solution.py:159
  112.5 4.6 %bitcast_multiply_fusion = f32[8,4,32,1024]{3,2,1,0:T(8,128)} fusion(f32[1,4,8,32,1024]{4,1,3,2,0:T(4,128)S(1)} %convert.9, f32[8,32,1024]{2,1,0:T(8,128)S(1)} %get-tuple-element.16), kind=kLoop, calls=%fused_computation.82 | loop fusion | flops 1048576 | bytes 9437184 | tf_op jit(solution)/shard_map/mul | solution.py:163
  117.1 14.2 %fusion.43 = f32[8,4,32,1024]{3,2,1,0:T(8,128)S(1)} fusion(f32[8,4,32,1024]{3,2,1,0:T(8,128)} %bitcast_multiply_fusion, f32[1,4,8,32,1024]{4,1,3,2,0:T(4,128)S(1)} %convert.9, f32[8,32,1024]{2,1,0:T(8,128)} %fusion.76, f32[8,32,1024]{2,1,0:T(8,128)} %get-tuple-element.15, f32[8,32,1024]{2,1,0:T(8,128)S(1)} %convert_element_type.158), kind=kLoop, calls=%fused_computation.84 | loop fusion | flops 20971520 | bytes 15728640 | tf_op jit(solution)/shard_map/add | solution.py:170
  131.9 5.8 %fusion.7 = bf16[8,4,32,1024]{3,2,1,0:T(8,128)(2,1)} fusion(f32[8,4,32,1024]{3,2,1,0:T(8,128)S(1)} %fusion.43, f32[4,4,32,1024]{3,2,1,0:T(8,128)S(1)} %reshape.221, f32[4,4,32,1024]{3,2,1,0:T(8,128)S(1)} %reshape.220), kind=kLoop, calls=%fused_computation.44 | loop fusion | flops 27262976 | bytes 10485760 | tf_op jit(solution)/shard_map/convert_element_type | solution.py:175
  (37 shorter events, 2.8 us)
Async XLA Ops:
  1.5 5.0 %collective-permute-start = (bf16[1,4,6,1024]{3,2,1,0:T(8,128)(2,1)S(1)}, bf16[1,4,6,1024]{3,2,1,0:T(8,128)(2,1)S(1)}, u32[]{:S(2)}, u32[]{:S(2)}) collective-permute-start(bf16[1,4,6,1024]{3,2,1,0:T(8,128)(2,1)S(1)} %get-tuple-element.11), channel_id=1, source_target_pairs={{0,1},{2,3},{4,5},{6,7},{8,9},{10,11},{12,13},{14,15},{16,17},{18,... | collective-permute-start | bytes 147464 | tf_op jit(solution)/shard_map/ppermute | solution.py:20
  3.9 3.1 %collective-permute-start.1 = (bf16[1,4,6,1024]{3,2,1,0:T(8,128)(2,1)S(1)}, bf16[1,4,6,1024]{3,2,1,0:T(8,128)(2,1)S(1)}, u32[]{:S(2)}, u32[]{:S(2)}) collective-permute-start(bf16[1,4,6,1024]{3,2,1,0:T(8,128)(2,1)S(1)} %get-tuple-element.12), channel_id=1, source_target_pairs={{1,0},{3,2},{5,4},{7,6},{9,8},{11,10},{13,12},{15,14},{17,16},{19,... | collective-permute-start | bytes 147464 | tf_op jit(solution)/shard_map/ppermute | solution.py:23
  6.5 37.4 %copy-start.2 = (s32[8,8,8]{2,1,0:T(8,128)S(1)}, s32[8,8,8]{2,1,0:T(8,128)}, u32[]{:S(2)}) copy-start(s32[8,8,8]{2,1,0:T(8,128)} %param.5) | copy-start | bytes 6148
  24.1 20.0 %copy-start = (bf16[1,4,256,1024]{3,2,1,0:T(8,128)(2,1)S(1)}, bf16[1,4,256,1024]{3,2,1,0:T(8,128)(2,1)}, u32[]{:S(2)}) copy-start(bf16[1,4,256,1024]{3,2,1,0:T(8,128)(2,1)} %get-tuple-element.6) | copy-start | bytes 6291460
  25.9 14.4 %all-to-all-start.2 = ((bf16[1,4,64,256]{3,1,0,2:T(4,128)(2,1)}), bf16[1,4,64,256]{3,1,0,2:T(4,128)(2,1)S(1)}, u32[]{:S(2)}, u32[]{:S(2)}) async-start(bf16[1,4,64,256]{3,1,0,2:T(4,128)(2,1)} %copy.21), calls=%async_computation.2 | async-start | bytes 262144 | tf_op jit(solution)/shard_map/all_to_all | solution.py:205
  40.4 17.5 %all-to-all-start.1 = ((bf16[1,4,128,512]{3,1,0,2:T(4,128)(2,1)}), bf16[1,4,128,512]{3,1,0,2:T(4,128)(2,1)S(1)}, u32[]{:S(2)}, u32[]{:S(2)}) async-start(bf16[1,4,128,512]{3,1,0,2:T(4,128)(2,1)} %copy.19), calls=%async_computation.1 | async-start | bytes 1048576 | tf_op jit(solution)/shard_map/all_to_all | solution.py:202
  57.9 51.8 %all-to-all-start = ((bf16[1,4,256,1024]{3,1,0,2:T(4,128)(2,1)}), bf16[1,4,256,1024]{3,1,0,2:T(4,128)(2,1)}, u32[]{:S(2)}, u32[]{:S(2)}) async-start(bf16[1,4,256,1024]{3,1,0,2:T(4,128)(2,1)} %copy.17), calls=%async_computation | async-start | bytes 4194304 | tf_op jit(solution)/shard_map/all_to_all | solution.py:199
  68.1 4.7 %copy-start.1 = (f32[8,8,256]{2,1,0:T(8,128)S(1)}, f32[8,8,256]{2,1,0:T(8,128)}, u32[]{:S(2)}) copy-start(f32[8,8,256]{2,1,0:T(8,128)} %fusion.181) | copy-start | bytes 196612

commit v4 on v3

--- a/solution.py
+++ b/solution.py
@@ -192,19 +192,29 @@
     extended = padded(scenes, (("row", 2),), 6)
     extended = jnp.pad(extended, ((0, 0), (0, 0), (0, 4), (0, 0)))
     level_zero, level_one, level_two = pyramid(extended, resample_taps, band_index, total_rows)
-    clear_fine = expand_mask(clear_mask, 4, 128)
-    clear_half = expand_mask(clear_mask, 2, 64)
-    clear_quarter = expand_mask(clear_mask, 1, 32)
-    smooth_fine = smooth(
-        lax.all_to_all(level_zero, "date", split_axis=2, concat_axis=0, tiled=True), clear_fine
+    ndate = lax.axis_size("date")
+    levels = (level_zero, level_one, level_two)
+    pieces = []
+    for level in levels:
+        dates, bands, count, width = level.shape
+        block = level.reshape(dates, bands, ndate, count // ndate, width)
+        pieces.append(jnp.moveaxis(block, 2, 0).reshape(ndate, dates, bands, -1))
+    packed = jnp.concatenate(pieces, axis=3)
+    got = lax.all_to_all(packed, "date", split_axis=0, concat_axis=0, tiled=True)
+    masks = (
+        expand_mask(clear_mask, 4, 128),
+        expand_mask(clear_mask, 2, 64),
+        expand_mask(clear_mask, 1, 32),
     )
-    smooth_half = smooth(
-        lax.all_to_all(level_one, "date", split_axis=2, concat_axis=0, tiled=True), clear_half
-    )
-    smooth_quarter = smooth(
-        lax.all_to_all(level_two, "date", split_axis=2, concat_axis=0, tiled=True), clear_quarter
-    )
-    return (smooth_fine, smooth_half, smooth_quarter)
+    outs = []
+    start = 0
+    for level, piece, clear in zip(levels, pieces, masks):
+        dates, bands, count, width = level.shape
+        size = piece.shape[3]
+        part = got[:, :, :, start : start + size].reshape(ndate * dates, bands, count // ndate, width)
+        start += size
+        outs.append(smooth(part, clear))
+    return tuple(outs)
 
 
 def solution(mesh):

time: 138 us -> 156 us (1.13)
  local copies, waits for them, and re-layouts: 13.8 us -> 34.4 us
  other arithmetic: 41.8 us -> 57.4 us
  waiting for transfers between devices: 49.3 us -> 38.8 us
  starting transfers between devices: 18.3 us -> 10.3 us
    all_to_all x3 -> x1, waiting for transfers between devices: 48.8 us -> 38.3 us  [local(): lax.all_to_all(packed, 'date', split_axis=0, concat_axis=0, tiled=True)]
    convert_element_type x0 -> x3, local copies, waits for them, and re-layouts: none -> 9.21 us  [smooth(): values = level.astype(jnp.float32)]
    reshape x0 -> x6, local copies, waits for them, and re-layouts: none -> 8.33 us  [local(): pieces.append(jnp.moveaxis(block, 2, 0).reshape(ndate, dates, bands, -1))]
    all_to_all x3 -> x1, starting transfers between devices: 14.7 us -> 6.67 us  [local(): lax.all_to_all(packed, 'date', split_axis=0, concat_axis=0, tiled=True)]
    pallas_call x3 -> x0, local copies, waits for them, and re-layouts: 7 us -> none  [pyramid(): pl.pallas_call(pyramid_kernel, grid=(dates, bands), in_specs=[pl.BlockSpe...]
    concatenate x0 -> x1, other arithmetic: none -> 5.19 us  [local(): packed = jnp.concatenate(pieces, axis=3)]
    div x3, other arithmetic: 3.94 us -> 8.02 us  [smooth(): filled = clear4 * values + (1.0 - clear4) * (numer / denom)]
    broadcast_in_dim x10, local copies, waits for them, and re-layouts: 2.37 us -> 5.72 us  [expand_mask(): grown = jnp.repeat(jnp.repeat(clear_mask, row_rep, axis=1), col_rep, axis=2)]
  transfers between devices with their start and end apart: 5 -> 3, of which waited for: 4 -> 2; matrix products, arithmetic and copies ran while one was open for 15% -> 17% of each run, Pallas kernels for 0% -> 0%
where the time goes in v4:
time: 156 us; the launch traced here: 155 us
  other arithmetic  57.4 us (37%)
  waiting for transfers between devices  38.8 us (25%)
  local copies, waits for them, and re-layouts  34.4 us (22%)
  Pallas kernels  13.5 us (9%)
  starting transfers between devices  10.3 us (7%)
    all_to_all x1, waiting for transfers between devices, local(): lax.all_to_all(packed, 'date', split_axis=0, concat_axis=0, tiled=True)  38.3 us
    add x3, other arithmetic, smooth(): filled = clear4 * values + (1.0 - clear4) * (numer / denom)  16.5 us
    pallas_call x1, Pallas kernels, pyramid(): pl.pallas_call(pyramid_kernel, grid=(dates, bands), in_specs=[pl.BlockSpe...  13.5 us
    convert_element_type x3, local copies, waits for them, and re-layouts, smooth(): values = level.astype(jnp.float32)  9.21 us
    convert_element_type x3, other arithmetic, smooth(): return result.astype(jnp.bfloat16)  8.62 us
    reshape x6, local copies, waits for them, and re-layouts, local(): pieces.append(jnp.moveaxis(block, 2, 0).reshape(ndate, dates, bands, -1))  8.33 us
    div x3, other arithmetic, smooth(): filled = clear4 * values + (1.0 - clear4) * (numer / denom)  8.02 us
    mul x3, other arithmetic, smooth(): weighted = jnp.pad(weight * values, ((4, 4), (0, 0), (0, 0), (0, 0)))  7.5 us
  transfers between devices with their start and end apart: 3, of which 2 were waited for; matrix products, arithmetic and copies ran while one was open for 17% of the time, Pallas kernels for 0%

profile of v4, /device:TPU:0, one launch (start us, length us, event | category | flops | bytes accessed | tf_op | source)
XLA Modules:
  0.0 155.4 jit_solution(767566030793684506)
XLA Ops:
  0.6 0.9 fusion.186
  1.5 2.4 %collective-permute-start = (bf16[1,4,6,1024]{3,2,1,0:T(8,128)(2,1)S(1)}, bf16[1,4,6,1024]{3,2,1,0:T(8,128)(2,1)S(1)}, u32[]{:S(2)}, u32[]{:S(2)}) collective-permute-start(bf16[1,4,6,1024]{3,2,1,0:T(8,128)(2,1)S(1)} %get-tuple-element.11), channel_id=1, source_target_pairs={{0,1},{2,3},{4,5},{6,7},{8,9},{10,11},{12,13},{14,15},{16,17},{18,... | collective-permute-start | bytes 147464 | tf_op jit(solution)/shard_map/ppermute | solution.py:20
  3.9 1.3 collective-permute-start.1
  7.0 3.6 %fusion.44.x_ref = bf16[1,4,272,1024]{3,2,1,0:T(8,128)(2,1)} fusion(bf16[1,4,6,1024]{3,2,1,0:T(8,128)(2,1)S(1)} %collective-permute-done.1, bf16[1,4,256,1024]{3,2,1,0:T(8,128)(2,1)} %param.3, bf16[1,4,6,1024]{3,2,1,0:T(8,128)(2,1)S(1)} %collective-permute-done), kind=kLoop, calls=%fused_computation.91 | loop fusion | flops 11141120 | bytes 4423680 | tf_op jit(solution)/shard_map/concatenate | solution.py:24
  10.7 13.5 %shard_map.58 = (bf16[1,4,256,1024]{3,2,1,0:T(8,128)(2,1)}, bf16[1,4,128,512]{3,2,1,0:T(8,128)(2,1)}, bf16[1,4,64,256]{3,2,1,0:T(8,128)(2,1)}) custom-call(f32[2,4,7]{2,1,0:T(4,128)} %taps_ref.1, bf16[1,4,272,1024]{3,2,1,0:T(8,128)(2,1)} %fusion.44.x_ref, f32[280,1]{1,0:T(8,128)} %fusion.163.keep_wide_ref, f32[136,1]{1,0:T(8,128)} %fusion.168.keep_half_ref), custom_call_target="tpu_custom_call" | custom-call | tf_op jit(solution)/shard_map/pallas_call | solution.py:134
  24.2 4.3 %reshape.250 = bf16[8,1,4,32768]{3,0,2,1:T(8,128)(2,1)} reshape(bf16[8,1,4,32,1024]{4,3,0,2,1:T(8,128)(2,1)} %bitcast.55) | data formatting | bytes 4194304 | tf_op jit(solution)/shard_map/reshape | solution.py:201
  28.4 3.2 %copy.17 = bf16[8,1,4,32768]{3,2,1,0:T(4,128)(2,1)S(1)} copy(bf16[8,1,4,32768]{3,0,2,1:T(8,128)(2,1)} %reshape.250) | data formatting | bytes 4194304 | tf_op jit(solution)/shard_map/reshape | solution.py:201
  32.6 5.2 %pad_maximum_fusion.2 = bf16[8,1,4,43008]{3,2,1,0:T(4,128)(2,1)} fusion(bf16[8,1,4,2048]{3,2,1,0:T(4,128)(2,1)S(1)} %copy.19, bf16[8,1,4,8192]{3,2,1,0:T(4,128)(2,1)S(1)} %copy.18, bf16[8,1,4,32768]{3,2,1,0:T(4,128)(2,1)S(1)} %copy.17), kind=kLoop, calls=%fused_computation.89 | loop fusion | flops 8257536 | bytes 5505024 | tf_op jit(solution)/shard_map/concatenate | solution.py:202
  37.7 6.7 %all-to-all-start = ((bf16[8,1,4,43008]{3,2,1,0:T(4,128)(2,1)}), bf16[8,1,4,43008]{3,2,1,0:T(4,128)(2,1)S(1)}, u32[]{:S(2)}, u32[]{:S(2)}) async-start(bf16[8,1,4,43008]{3,2,1,0:T(4,128)(2,1)} %pad_maximum_fusion.2), calls=%async_computation | async-start | bytes 5505024 | tf_op jit(solution)/shard_map/all_to_all | solution.py:203
  47.5 1.0 broadcast_in_dim.47
  48.5 1.2 convert_element_type.147
  50.5 1.3 broadcast_in_dim.45
  51.8 2.4 %add.353 = f32[8,1,32,1024]{3,2,0,1:T(8,128)} reshape(f32[8,32,8,128]{3,2,1,0:T(8,128)} %broadcast_in_dim.45) | data formatting | bytes 2097152 | tf_op jit(solution)/shard_map/add | solution.py:162
  54.2 1.3 broadcast_in_dim.43
  55.5 2.5 %convert_element_type.140 = f32[8,32,1024]{2,1,0:T(8,128)} reshape(f32[8,32,8,128]{3,2,1,0:T(8,128)} %broadcast_in_dim.43) | data formatting | bytes 2097152 | tf_op jit(solution)/shard_map/convert_element_type | solution.py:185
  58.0 1.9 %fusion.178 = f32[8,8,256]{2,1,0:T(8,128)} fusion(f32[8,1,8,256]{3,2,0,1:T(8,128)} %add.410), kind=kLoop, calls=%fused_computation.291 | loop fusion | flops 262144 | bytes 131072 | tf_op jit(solution)/shard_map/div | solution.py:170
  61.3 0.9 broadcast_subtract_fusion.1
  62.2 5.4 %fusion.75 = f32[8,32,1024]{2,1,0:T(8,128)} fusion(f32[8,1,32,1024]{3,2,0,1:T(8,128)} %add.353), kind=kLoop, calls=%fused_computation.146 | loop fusion | flops 4194304 | bytes 2097152 | tf_op jit(solution)/shard_map/div | solution.py:170
  67.5 1.7 %broadcast_subtract_fusion = (f32[8,32,1024]{2,1,0:T(8,128)}, f32[8,32,1024]{2,1,0:T(8,128)}) fusion(f32[8,32,1024]{2,1,0:T(8,128)S(1)} %copy-done.1), kind=kLoop, calls=%fused_computation.187 | loop fusion | flops 786432 | bytes 3145728 | tf_op jit(solution)/shard_map/sub | solution.py:170
  69.2 38.3 %all-to-all-done = bf16[8,1,4,43008]{3,2,1,0:T(4,128)(2,1)S(1)} async-done(((bf16[8,1,4,43008]{3,2,1,0:T(4,128)(2,1)}), bf16[8,1,4,43008]{3,2,1,0:T(4,128)(2,1)S(1)}, u32[]{:S(2)}, u32[]{:S(2)}) %all-to-all-start) | async-done | bytes 2752544 | tf_op jit(solution)/shard_map/all_to_all | solution.py:203
  108.5 1.0 multiply_add_fusion.3
  110.2 1.0 slice_convert_fusion.1
  111.2 3.0 %reshape.248 = f32[8,4,16,512]{3,2,1,0:T(8,128)} reshape(f32[8,1,4,8192]{3,2,1,0:T(4,128)} %slice_convert_fusion.1) | data formatting | bytes 2097152 | tf_op jit(solution)/shard_map/convert_element_type | solution.py:159
  114.2 1.4 broadcast_multiply_fusion.1
  115.6 1.7 %multiply_add_fusion.1 = f32[8,4,16,512]{3,2,1,0:T(8,128)S(1)} fusion(f32[8,4,16,512]{3,2,1,0:T(8,128)} %reshape.248, f32[8,4,16,512]{3,2,1,0:T(8,128)S(1)} %broadcast_multiply_fusion.1, f32[8,16,512]{2,1,0:T(8,128)} %fusion.132, f32[8,16,512]{2,1,0:T(8,128)S(1)} %copy-done.6, f32[8,16,512]{2,1,0:T(8,128)S(1)} %convert_element_type.147), kind=kLoop, calls=%fused_computation.175 | loop fusion | flops 5242880 | bytes 3932160 | tf_op jit(solution)/shard_map/add | solution.py:170
  117.3 1.0 copy-done.3
  118.3 2.3 %slice_convert_fusion = f32[8,1,4,32768]{3,2,1,0:T(4,128)} fusion(bf16[8,1,4,43008]{3,2,1,0:T(4,128)(2,1)S(1)} %all-to-all-done), kind=kLoop, calls=%fused_computation.92 | loop fusion | flops 1048576 | bytes 6291456 | tf_op jit(solution)/shard_map/convert_element_type | solution.py:159
  120.6 6.1 %reshape.247 = f32[8,4,32,1024]{3,2,1,0:T(8,128)} reshape(f32[8,1,4,32768]{3,2,1,0:T(4,128)} %slice_convert_fusion) | data formatting | bytes 8388608 | tf_op jit(solution)/shard_map/convert_element_type | solution.py:159
  126.8 5.2 %broadcast_multiply_fusion = f32[8,4,32,1024]{3,2,1,0:T(8,128)} fusion(f32[8,4,32,1024]{3,2,1,0:T(8,128)} %reshape.247, f32[8,32,1024]{2,1,0:T(8,128)S(1)} %copy-done.5), kind=kLoop, calls=%fused_computation.93 | loop fusion | flops 1048576 | bytes 9437184 | tf_op jit(solution)/shard_map/mul | solution.py:163
  132.0 13.8 %multiply_add_fusion = f32[8,4,32,1024]{3,2,1,0:T(8,128)S(1)} fusion(f32[8,4,32,1024]{3,2,1,0:T(8,128)S(1)} %copy-done, f32[8,4,32,1024]{3,2,1,0:T(8,128)} %broadcast_multiply_fusion, f32[8,32,1024]{2,1,0:T(8,128)} %fusion.75, f32[8,32,1024]{2,1,0:T(8,128)} %get-tuple-element.15, f32[8,32,1024]{2,1,0:T(8,128)S(1)} %copy-done.2), kind=kLoop, calls=%fused_computation.82 | loop fusion | flops 20971520 | bytes 15728640 | tf_op jit(solution)/shard_map/add | solution.py:170
  147.0 2.0 %fusion.49 = bf16[8,4,16,512]{3,2,1,0:T(8,128)(2,1)} fusion(f32[8,4,16,512]{3,2,1,0:T(8,128)S(1)} %copy-done.4, f32[4,4,16,512]{3,2,1,0:T(8,128)S(1)} %reshape.244, f32[4,4,16,512]{3,2,1,0:T(8,128)S(1)} %reshape.243), kind=kLoop, calls=%fused_computation.120 | loop fusion | flops 6815744 | bytes 2621440 | tf_op jit(solution)/shard_map/convert_element_type | solution.py:175
  149.5 5.8 %fusion.7 = bf16[8,4,32,1024]{3,2,1,0:T(8,128)(2,1)} fusion(f32[8,4,32,1024]{3,2,1,0:T(8,128)S(1)} %multiply_add_fusion, f32[4,4,32,1024]{3,2,1,0:T(8,128)S(1)} %reshape.242, f32[4,4,32,1024]{3,2,1,0:T(8,128)S(1)} %reshape.241), kind=kLoop, calls=%fused_computation.44 | loop fusion | flops 27262976 | bytes 10485760 | tf_op jit(solution)/shard_map/convert_element_type | solution.py:175
  (66 shorter events, 11.3 us)
Async XLA Ops:
  1.5 5.0 %collective-permute-start = (bf16[1,4,6,1024]{3,2,1,0:T(8,128)(2,1)S(1)}, bf16[1,4,6,1024]{3,2,1,0:T(8,128)(2,1)S(1)}, u32[]{:S(2)}, u32[]{:S(2)}) collective-permute-start(bf16[1,4,6,1024]{3,2,1,0:T(8,128)(2,1)S(1)} %get-tuple-element.11), channel_id=1, source_target_pairs={{0,1},{2,3},{4,5},{6,7},{8,9},{10,11},{12,13},{14,15},{16,17},{18,... | collective-permute-start | bytes 147464 | tf_op jit(solution)/shard_map/ppermute | solution.py:20
  3.9 3.1 %collective-permute-start.1 = (bf16[1,4,6,1024]{3,2,1,0:T(8,128)(2,1)S(1)}, bf16[1,4,6,1024]{3,2,1,0:T(8,128)(2,1)S(1)}, u32[]{:S(2)}, u32[]{:S(2)}) collective-permute-start(bf16[1,4,6,1024]{3,2,1,0:T(8,128)(2,1)S(1)} %get-tuple-element.12), channel_id=1, source_target_pairs={{1,0},{3,2},{5,4},{7,6},{9,8},{11,10},{13,12},{15,14},{17,16},{19,... | collective-permute-start | bytes 147464 | tf_op jit(solution)/shard_map/ppermute | solution.py:23
  24.1 7.5 %copy-start.11 = (bf16[1,4,128,512]{3,2,1,0:T(8,128)(2,1)S(1)}, bf16[1,4,128,512]{3,2,1,0:T(8,128)(2,1)}, u32[]{:S(2)}) copy-start(bf16[1,4,128,512]{3,2,1,0:T(8,128)(2,1)} %get-tuple-element.7) | copy-start | bytes 1572868
  28.4 3.9 %copy-start.12 = (bf16[1,4,64,256]{3,2,1,0:T(8,128)(2,1)S(1)}, bf16[1,4,64,256]{3,2,1,0:T(8,128)(2,1)}, u32[]{:S(2)}) copy-start(bf16[1,4,64,256]{3,2,1,0:T(8,128)(2,1)} %get-tuple-element.8) | copy-start | bytes 393220
  32.5 11.9 %copy-start.13 = (s32[8,8,8]{2,1,0:T(8,128)S(1)}, s32[8,8,8]{2,1,0:T(8,128)}, u32[]{:S(2)}) copy-start(s32[8,8,8]{2,1,0:T(8,128)} %param.5) | copy-start | bytes 6148
  37.7 69.8 %all-to-all-start = ((bf16[8,1,4,43008]{3,2,1,0:T(4,128)(2,1)}), bf16[8,1,4,43008]{3,2,1,0:T(4,128)(2,1)S(1)}, u32[]{:S(2)}, u32[]{:S(2)}) async-start(bf16[8,1,4,43008]{3,2,1,0:T(4,128)(2,1)} %pad_maximum_fusion.2), calls=%async_computation | async-start | bytes 5505024 | tf_op jit(solution)/shard_map/all_to_all | solution.py:203
  44.4 1.8 %copy-start.8 = (f32[8,8,8]{2,1,0:T(8,128)}, f32[8,8,8]{2,1,0:T(8,128)S(1)}, u32[]{:S(2)}) copy-start(f32[8,8,8]{2,1,0:T(8,128)S(1)} %convert_element_type.138) | copy-start | bytes 6148
  44.5 1.8 %copy-start.10 = (f32[8,8,8]{2,1,0:T(8,128)}, f32[8,8,8]{2,1,0:T(8,128)S(1)}, u32[]{:S(2)}) copy-start(f32[8,8,8]{2,1,0:T(8,128)S(1)} %multiply_add_fusion.6) | copy-start | bytes 6148
  46.6 7.5 %copy-start.9 = (f32[8,8,8]{2,1,0:T(8,128)S(1)}, f32[8,8,8]{2,1,0:T(8,128)}, u32[]{:S(2)}) copy-start(f32[8,8,8]{2,1,0:T(8,128)} %copy-done.8) | copy-start | bytes 6148
  47.5 12.3 %copy-start.7 = (f32[8,8,256]{2,1,0:T(8,128)S(1)}, f32[8,8,256]{2,1,0:T(8,128)}, u32[]{:S(2)}) copy-start(f32[8,8,256]{2,1,0:T(8,128)} %convert_element_type.151) | copy-start | bytes 196612
  58.0 9.6 %copy-start.1 = (f32[8,32,1024]{2,1,0:T(8,128)S(1)}, f32[8,32,1024]{2,1,0:T(8,128)}, u32[]{:S(2)}) copy-start(f32[8,32,1024]{2,1,0:T(8,128)} %convert_element_type.140) | copy-start | bytes 3145732
  109.6 6.0 %copy-start.6 = (f32[8,16,512]{2,1,0:T(8,128)S(1)}, f32[8,16,512]{2,1,0:T(8,128)}, u32[]{:S(2)}) copy-start(f32[8,16,512]{2,1,0:T(8,128)} %get-tuple-element.19) | copy-start | bytes 786436
  117.3 1.0 copy-start.3
  120.6 6.1 %copy-start.5 = (f32[8,32,1024]{2,1,0:T(8,128)S(1)}, f32[8,32,1024]{2,1,0:T(8,128)}, u32[]{:S(2)}) copy-start(f32[8,32,1024]{2,1,0:T(8,128)} %get-tuple-element.16) | copy-start | bytes 3145732
  126.8 5.3 %copy-start = (f32[8,4,32,1024]{3,2,1,0:T(8,128)S(1)}, f32[8,4,32,1024]{3,2,1,0:T(8,128)}, u32[]{:S(2)}) copy-start(f32[8,4,32,1024]{3,2,1,0:T(8,128)} %reshape.247) | copy-start | bytes 12582916
  126.8 5.3 %copy-start.2 = (f32[8,32,1024]{2,1,0:T(8,128)S(1)}, f32[8,32,1024]{2,1,0:T(8,128)}, u32[]{:S(2)}) copy-start(f32[8,32,1024]{2,1,0:T(8,128)} %convert_element_type.140) | copy-start | bytes 3145732
  132.0 13.9 %copy-start.15 = (f32[4,8,256]{2,1,0:T(8,128)S(1)}, f32[4,8,256]{2,1,0:T(8,128)}, u32[]{:S(2)}) copy-start(f32[4,8,256]{2,1,0:T(8,128)} %get-tuple-element.17) | copy-start | bytes 98308
  132.0 13.9 %copy-start.14 = (f32[4,8,256]{2,1,0:T(8,128)S(1)}, f32[4,8,256]{2,1,0:T(8,128)}, u32[]{:S(2)}) copy-start(f32[4,8,256]{2,1,0:T(8,128)} %get-tuple-element.18) | copy-start | bytes 98308
  145.8 1.2 copy-start.4

commit v5 on v3

--- a/solution.py
+++ b/solution.py
@@ -1,6 +1,7 @@
 import math
 
 import jax
+import numpy as np
 import jax.numpy as jnp
 from jax import lax
 from jax.sharding import PartitionSpec as P
@@ -155,34 +156,68 @@
     )(resample_taps, extended, keep_wide, keep_half)
 
 
-def smooth(level, clear):
-    values = level.astype(jnp.float32)
-    dates = values.shape[0]
-    clear4 = clear[:, None]
-    weight = 0.1 + 0.9 * clear4
-    weighted = jnp.pad(weight * values, ((4, 4), (0, 0), (0, 0), (0, 0)))
-    weight_pad = jnp.pad(weight, ((4, 4), (0, 0), (0, 0), (0, 0)))
-    numer = jnp.zeros_like(values)
-    denom = jnp.zeros_like(weight)
-    for k in range(9):
-        numer = numer + gap_weights[k] * weighted[k : k + dates]
-        denom = denom + gap_weights[k] * weight_pad[k : k + dates]
-    filled = clear4 * values + (1.0 - clear4) * (numer / denom)
-    edged = jnp.pad(filled, ((4, 4), (0, 0), (0, 0), (0, 0)), mode="edge")
-    result = jnp.zeros_like(values)
-    for k in range(9):
-        result = result + savgol_coeffs[k] * edged[k : k + dates]
-    return result.astype(jnp.bfloat16)
-
-
-def expand_mask(clear_mask, row_rep, col_rep):
-    grown = jnp.repeat(jnp.repeat(clear_mask, row_rep, axis=1), col_rep, axis=2)
-    return grown.astype(jnp.float32)
-
-
-def expand_mask(clear_mask, row_rep, col_rep):
-    grown = jnp.repeat(jnp.repeat(clear_mask, row_rep, axis=1), col_rep, axis=2)
-    return grown.astype(jnp.float32)
+def smooth_operator(dates):
+    clamp = np.zeros((dates, dates), np.float64)
+    near = np.zeros((dates, dates), np.float64)
+    for t in range(dates):
+        for k in range(9):
+            clamp[t, min(max(t + k - 4, 0), dates - 1)] += savgol_coeffs[k]
+            if 0 <= t + k - 4 < dates:
+                near[t, t + k - 4] = gap_weights[k]
+    return clamp.astype(np.float32), near.astype(np.float32)
+
+
+def smooth_coefficients(clear):
+    dates = clear.shape[0]
+    clamp, near = smooth_operator(dates)
+    hi = lax.Precision.HIGHEST
+    weight = 0.1 + 0.9 * clear
+    denom = jnp.einsum("su,uxy->sxy", near, weight, precision=hi)
+    gap = (1.0 - clear) / denom
+    fill = near[:, :, None, None] * weight[None, :] * gap[:, None]
+    fill = fill + np.eye(dates, dtype=np.float32)[:, :, None, None] * clear[None, :]
+    return jnp.einsum("ts,suxy->tuxy", clamp, fill, precision=hi)
+
+
+def smooth_kernel(level_ref, coeff_ref, out_ref):
+    dates = level_ref.shape[0]
+    rows = level_ref.shape[2]
+    width = level_ref.shape[3]
+    mask_cols = coeff_ref.shape[3]
+    span = width // mask_cols
+    per_tile = 128 // span
+    lane_group = lax.broadcasted_iota(jnp.int32, (rows, 128), 1) // span
+    for j in range(width // 128):
+        values = [level_ref[u, 0, :, 128 * j : 128 * (j + 1)].astype(jnp.float32) for u in range(dates)]
+
+        def one_date(t, carry):
+            acc = jnp.zeros((rows, 128), jnp.float32)
+            for u in range(dates):
+                c = coeff_ref[t, u]
+                tile = jnp.broadcast_to(c[:, per_tile * j : per_tile * j + 1], (rows, 128))
+                for g in range(1, per_tile):
+                    m = per_tile * j + g
+                    tile = jnp.where(lane_group == g, jnp.broadcast_to(c[:, m : m + 1], (rows, 128)), tile)
+                acc = acc + tile * values[u]
+            out_ref[t, 0, :, 128 * j : 128 * (j + 1)] = acc.astype(out_ref.dtype)
+            return carry
+
+        lax.fori_loop(0, dates, one_date, 0)
+
+
+def smooth(level, coeff):
+    dates, bands, rows, width = level.shape
+    grown = jnp.repeat(coeff, rows // coeff.shape[2], axis=2)
+    return pl.pallas_call(
+        smooth_kernel,
+        grid=(bands,),
+        in_specs=[
+            pl.BlockSpec((dates, 1, rows, width), lambda b: (0, b, 0, 0)),
+            pl.BlockSpec(grown.shape, lambda b: (0, 0, 0, 0)),
+        ],
+        out_specs=pl.BlockSpec((dates, 1, rows, width), lambda b: (0, b, 0, 0)),
+        out_shape=jax.ShapeDtypeStruct(level.shape, jnp.bfloat16),
+    )(level, grown)
 
 
 def local(scenes, resample_taps, clear_mask):
@@ -191,20 +226,12 @@
     total_rows = rows * lax.axis_size("row")
     extended = padded(scenes, (("row", 2),), 6)
     extended = jnp.pad(extended, ((0, 0), (0, 0), (0, 4), (0, 0)))
-    level_zero, level_one, level_two = pyramid(extended, resample_taps, band_index, total_rows)
-    clear_fine = expand_mask(clear_mask, 4, 128)
-    clear_half = expand_mask(clear_mask, 2, 64)
-    clear_quarter = expand_mask(clear_mask, 1, 32)
-    smooth_fine = smooth(
-        lax.all_to_all(level_zero, "date", split_axis=2, concat_axis=0, tiled=True), clear_fine
+    levels = pyramid(extended, resample_taps, band_index, total_rows)
+    coeff = smooth_coefficients(clear_mask.astype(jnp.float32))
+    return tuple(
+        smooth(lax.all_to_all(level, "date", split_axis=2, concat_axis=0, tiled=True), coeff)
+        for level in levels
     )
-    smooth_half = smooth(
-        lax.all_to_all(level_one, "date", split_axis=2, concat_axis=0, tiled=True), clear_half
-    )
-    smooth_quarter = smooth(
-        lax.all_to_all(level_two, "date", split_axis=2, concat_axis=0, tiled=True), clear_quarter
-    )
-    return (smooth_fine, smooth_half, smooth_quarter)
 
 
 def solution(mesh):

time: 138 us -> 142 us (1.029)
  Pallas kernels: 13.5 us -> 69.1 us
  other arithmetic: 41.8 us -> 5 us
  waiting for transfers between devices: 49.3 us -> 33.5 us
  local copies, waits for them, and re-layouts: 13.8 us -> 15.5 us
    pallas_call x0 -> x3, Pallas kernels: none -> 55.6 us  [smooth(): pl.pallas_call(smooth_kernel, grid=(bands,), in_specs=[pl.BlockSpec((date...]
    all_to_all x3, waiting for transfers between devices: 48.8 us -> 33 us  [local(): lax.all_to_all(level, 'date', split_axis=2, concat_axis=0, tiled=True)]
    add x4 -> x1, other arithmetic: 15.1 us -> 0.01 us  [smooth_coefficients(): weight = 0.1 + 0.9 * clear]
    convert_element_type x7 -> x1, other arithmetic: 11.6 us -> 0.01 us  [local(): coeff = smooth_coefficients(clear_mask.astype(jnp.float32))]
    mul x3 -> x0, other arithmetic: 4.98 us -> none  [smooth(): weighted = jnp.pad(weight * values, ((4, 4), (0, 0), (0, 0), (0, 0)))]
    div x3 -> x0, other arithmetic: 3.94 us -> none  [smooth(): filled = clear4 * values + (1.0 - clear4) * (numer / denom)]
    all_to_all x0 -> x3, local copies, waits for them, and re-layouts: none -> 3.61 us  [local(): lax.all_to_all(level, 'date', split_axis=2, concat_axis=0, tiled=True)]
    convert_element_type x3 -> x1, local copies, waits for them, and re-layouts: 1.66 us -> 0.01 us  [local(): coeff = smooth_coefficients(clear_mask.astype(jnp.float32))]
  transfers between devices with their start and end apart: 5 -> 5, of which waited for: 4 -> 4; matrix products, arithmetic and copies ran while one was open for 15% -> 8% of each run, Pallas kernels for 0% -> 19%
where the time goes in v5:
time: 142 us
  Pallas kernels  69.1 us (49%)
  waiting for transfers between devices  33.5 us (24%)
  starting transfers between devices  17.4 us (12%)
  local copies, waits for them, and re-layouts  15.5 us (11%)
  other arithmetic  5 us (4%)
    pallas_call x3, Pallas kernels, smooth(): pl.pallas_call(smooth_kernel, grid=(bands,), in_specs=[pl.BlockSpec((date...  55.6 us
    all_to_all x3, waiting for transfers between devices, local(): lax.all_to_all(level, 'date', split_axis=2, concat_axis=0, tiled=True)  33 us
    all_to_all x3, starting transfers between devices, local(): lax.all_to_all(level, 'date', split_axis=2, concat_axis=0, tiled=True)  13.8 us
    pallas_call x1, Pallas kernels, pyramid(): pl.pallas_call(pyramid_kernel, grid=(dates, bands), in_specs=[pl.BlockSpe...  13.5 us
    pallas_call x3, local copies, waits for them, and re-layouts, pyramid(): pl.pallas_call(pyramid_kernel, grid=(dates, bands), in_specs=[pl.BlockSpe...  7 us
    concatenate x1, other arithmetic, padded(): block = jnp.concatenate([low, block, high], axis=dim)  3.63 us
    all_to_all x3, local copies, waits for them, and re-layouts, local(): lax.all_to_all(level, 'date', split_axis=2, concat_axis=0, tiled=True)  3.61 us
    broadcast_in_dim x2, local copies, waits for them, and re-layouts, smooth(): grown = jnp.repeat(coeff, rows // coeff.shape[2], axis=2)  3.19 us
  transfers between devices with their start and end apart: 5, of which 4 were waited for; matrix products, arithmetic and copies ran while one was open for 8% of the time, Pallas kernels for 19%

profile of v5, /device:TPU:0, one launch (start us, length us, event | category | flops | bytes accessed | tf_op | source)
XLA Modules:
  0.0 141.8 jit_solution(10285840572084833216)
XLA Ops:
  0.6 0.9 fusion.27
  1.5 2.4 %collective-permute-start = (bf16[1,4,6,1024]{3,2,1,0:T(8,128)(2,1)S(1)}, bf16[1,4,6,1024]{3,2,1,0:T(8,128)(2,1)S(1)}, u32[]{:S(2)}, u32[]{:S(2)}) collective-permute-start(bf16[1,4,6,1024]{3,2,1,0:T(8,128)(2,1)S(1)} %get-tuple-element.9), channel_id=1, source_target_pairs={{0,1},{2,3},{4,5},{6,7},{8,9},{10,11},{12,13},{14,15},{16,17},{18,... | collective-permute-start | bytes 147464 | tf_op jit(solution)/shard_map/ppermute | solution.py:21
  3.9 1.3 collective-permute-start.1
  5.2 0.7 fusion.14.keep_wide_ref
  5.9 0.6 fusion.24.keep_half_ref
  6.5 0.0 collective-permute-done
  6.6 0.5 collective-permute-done.1
  7.0 3.6 %fusion.4.x_ref = bf16[1,4,272,1024]{3,2,1,0:T(8,128)(2,1)} fusion(bf16[1,4,6,1024]{3,2,1,0:T(8,128)(2,1)S(1)} %collective-permute-done.1, bf16[1,4,256,1024]{3,2,1,0:T(8,128)(2,1)} %param.7, bf16[1,4,6,1024]{3,2,1,0:T(8,128)(2,1)S(1)} %collective-permute-done), kind=kLoop, calls=%fused_computation.5 | loop fusion | flops 11141120 | bytes 4423680 | tf_op jit(solution)/shard_map/concatenate | solution.py:25
  10.7 13.5 %shard_map.94 = (bf16[1,4,256,1024]{3,2,1,0:T(8,128)(2,1)}, bf16[1,4,128,512]{3,2,1,0:T(8,128)(2,1)}, bf16[1,4,64,256]{3,2,1,0:T(8,128)(2,1)}) custom-call(f32[2,4,7]{2,1,0:T(4,128)} %taps_ref.1, bf16[1,4,272,1024]{3,2,1,0:T(8,128)(2,1)} %fusion.4.x_ref, f32[280,1]{1,0:T(8,128)} %fusion.14.keep_wide_ref, f32[136,1]{1,0:T(8,128)} %fusion.24.keep_half_ref), custom_call_target="tpu_custom_call" | custom-call | tf_op jit(solution)/shard_map/pallas_call | solution.py:135
  24.1 1.8 %copy.51 = bf16[1,4,64,256]{3,1,0,2:T(4,128)(2,1)} copy(bf16[1,4,64,256]{3,2,1,0:T(8,128)(2,1)} %get-tuple-element.8) | data formatting | bytes 262144 | tf_op jit(solution)/shard_map/pallas_call | solution.py:135
  26.0 6.7 %all-to-all-start.2 = ((bf16[1,4,64,256]{3,1,0,2:T(4,128)(2,1)}), bf16[1,4,64,256]{3,1,0,2:T(4,128)(2,1)S(1)}, u32[]{:S(2)}, u32[]{:S(2)}) async-start(bf16[1,4,64,256]{3,1,0,2:T(4,128)(2,1)} %copy.51), calls=%async_computation.2 | async-start | bytes 262144 | tf_op jit(solution)/shard_map/all_to_all | solution.py:232
  32.6 2.2 %copy.47 = bf16[1,4,128,512]{3,1,0,2:T(4,128)(2,1)} copy(bf16[1,4,128,512]{3,2,1,0:T(8,128)(2,1)} %get-tuple-element.7) | data formatting | bytes 1048576 | tf_op jit(solution)/shard_map/pallas_call | solution.py:135
  34.9 5.5 %all-to-all-done.2 = bf16[1,4,64,256]{3,1,0,2:T(4,128)(2,1)S(1)} async-done(((bf16[1,4,64,256]{3,1,0,2:T(4,128)(2,1)}), bf16[1,4,64,256]{3,1,0,2:T(4,128)(2,1)S(1)}, u32[]{:S(2)}, u32[]{:S(2)}) %all-to-all-start.2) | async-done | bytes 131104 | tf_op jit(solution)/shard_map/all_to_all | solution.py:232
  40.4 3.5 %all-to-all-start.1 = ((bf16[1,4,128,512]{3,1,0,2:T(4,128)(2,1)}), bf16[1,4,128,512]{3,1,0,2:T(4,128)(2,1)S(1)}, u32[]{:S(2)}, u32[]{:S(2)}) async-start(bf16[1,4,128,512]{3,1,0,2:T(4,128)(2,1)} %copy.47), calls=%async_computation.1 | async-start | bytes 1048576 | tf_op jit(solution)/shard_map/all_to_all | solution.py:232
  43.9 0.0 copy-done.1
  43.9 2.9 %copy.39 = bf16[1,4,256,1024]{3,1,0,2:T(4,128)(2,1)} copy(bf16[1,4,256,1024]{3,2,1,0:T(8,128)(2,1)S(1)} %copy-done.1) | data formatting | bytes 4194304 | tf_op jit(solution)/shard_map/pallas_call | solution.py:135
  46.9 0.0 copy-start.5
  46.9 11.0 %all-to-all-done.1 = bf16[1,4,128,512]{3,1,0,2:T(4,128)(2,1)S(1)} async-done(((bf16[1,4,128,512]{3,1,0,2:T(4,128)(2,1)}), bf16[1,4,128,512]{3,1,0,2:T(4,128)(2,1)S(1)}, u32[]{:S(2)}, u32[]{:S(2)}) %all-to-all-start.1) | async-done | bytes 524320 | tf_op jit(solution)/shard_map/all_to_all | solution.py:232
  57.9 3.6 %all-to-all-start = ((bf16[1,4,256,1024]{3,1,0,2:T(4,128)(2,1)}), bf16[1,4,256,1024]{3,1,0,2:T(4,128)(2,1)S(1)}, u32[]{:S(2)}, u32[]{:S(2)}) async-start(bf16[1,4,256,1024]{3,1,0,2:T(4,128)(2,1)} %copy.39), calls=%async_computation | async-start | bytes 4194304 | tf_op jit(solution)/shard_map/all_to_all | solution.py:232
  61.5 0.0 copy-done.2
  61.6 0.2 convolution_divide_fusion
  61.8 0.4 fusion.5
  62.2 0.8 copy.46.coeff_ref
  63.0 0.7 copy.76
  63.7 9.6 %shard_map.97 = bf16[8,4,8,256]{3,2,1,0:T(8,128)(2,1)} custom-call(bf16[8,4,8,256]{3,2,1,0:T(8,128)(2,1)} %bitcast.33, f32[8,8,8,8]{3,2,1,0:T(8,128)} %copy.46.coeff_ref), custom_call_target="tpu_custom_call" | custom-call | tf_op jit(solution)/shard_map/pallas_call | solution.py:211
  73.2 0.9 copy.75
  74.1 1.9 %broadcast_in_dim.5 = f32[8,8,8,2,8]{4,3,2,1,0:T(2,128)} broadcast(f32[8,8,8,8]{3,2,1,0:T(8,128)} %copy.46.coeff_ref), dimensions={0,1,2,4} | broadcast | bytes 49152 | tf_op jit(solution)/shard_map/broadcast_in_dim | solution.py:210
  76.1 17.0 %shard_map.96 = bf16[8,4,16,512]{3,2,1,0:T(8,128)(2,1)} custom-call(bf16[8,4,16,512]{3,2,1,0:T(8,128)(2,1)} %bitcast.29, f32[8,8,16,8]{3,2,1,0:T(8,128)} %bitcast.30), custom_call_target="tpu_custom_call" | custom-call | tf_op jit(solution)/shard_map/pallas_call | solution.py:211
  93.1 16.4 %all-to-all-done = bf16[1,4,256,1024]{3,1,0,2:T(4,128)(2,1)S(1)} async-done(((bf16[1,4,256,1024]{3,1,0,2:T(4,128)(2,1)}), bf16[1,4,256,1024]{3,1,0,2:T(4,128)(2,1)S(1)}, u32[]{:S(2)}, u32[]{:S(2)}) %all-to-all-start) | async-done | bytes 2097184 | tf_op jit(solution)/shard_map/all_to_all | solution.py:232
  109.5 2.0 %copy.74 = bf16[1,4,8,32,1024]{4,3,1,2,0:T(8,128)(2,1)} copy(bf16[1,4,8,32,1024]{4,1,3,2,0:T(4,128)(2,1)S(1)} %bitcast.26) | data formatting | bytes 4194304 | tf_op jit(solution)/shard_map/all_to_all | solution.py:232
  111.5 1.3 broadcast_in_dim.4
  112.8 29.0 %shard_map.95 = bf16[8,4,32,1024]{3,2,1,0:T(8,128)(2,1)} custom-call(bf16[8,4,32,1024]{3,2,1,0:T(8,128)(2,1)} %bitcast.27, f32[8,8,32,8]{3,2,1,0:T(8,128)} %bitcast.28), custom_call_target="tpu_custom_call" | custom-call | tf_op jit(solution)/shard_map/pallas_call | solution.py:211
  (15 shorter events, 0.1 us)
Async XLA Ops:
  1.5 5.0 %collective-permute-start = (bf16[1,4,6,1024]{3,2,1,0:T(8,128)(2,1)S(1)}, bf16[1,4,6,1024]{3,2,1,0:T(8,128)(2,1)S(1)}, u32[]{:S(2)}, u32[]{:S(2)}) collective-permute-start(bf16[1,4,6,1024]{3,2,1,0:T(8,128)(2,1)S(1)} %get-tuple-element.9), channel_id=1, source_target_pairs={{0,1},{2,3},{4,5},{6,7},{8,9},{10,11},{12,13},{14,15},{16,17},{18,... | collective-permute-start | bytes 147464 | tf_op jit(solution)/shard_map/ppermute | solution.py:21
  3.9 3.1 %collective-permute-start.1 = (bf16[1,4,6,1024]{3,2,1,0:T(8,128)(2,1)S(1)}, bf16[1,4,6,1024]{3,2,1,0:T(8,128)(2,1)S(1)}, u32[]{:S(2)}, u32[]{:S(2)}) collective-permute-start(bf16[1,4,6,1024]{3,2,1,0:T(8,128)(2,1)S(1)} %get-tuple-element.10), channel_id=1, source_target_pairs={{1,0},{3,2},{5,4},{7,6},{9,8},{11,10},{13,12},{15,14},{17,16},{19,... | collective-permute-start | bytes 147464 | tf_op jit(solution)/shard_map/ppermute | solution.py:24
  24.1 19.8 %copy-start.1 = (bf16[1,4,256,1024]{3,2,1,0:T(8,128)(2,1)S(1)}, bf16[1,4,256,1024]{3,2,1,0:T(8,128)(2,1)}, u32[]{:S(2)}) copy-start(bf16[1,4,256,1024]{3,2,1,0:T(8,128)(2,1)} %get-tuple-element.6) | copy-start | bytes 6291460
  26.0 14.4 %all-to-all-start.2 = ((bf16[1,4,64,256]{3,1,0,2:T(4,128)(2,1)}), bf16[1,4,64,256]{3,1,0,2:T(4,128)(2,1)S(1)}, u32[]{:S(2)}, u32[]{:S(2)}) async-start(bf16[1,4,64,256]{3,1,0,2:T(4,128)(2,1)} %copy.51), calls=%async_computation.2 | async-start | bytes 262144 | tf_op jit(solution)/shard_map/all_to_all | solution.py:232
  40.4 17.5 %all-to-all-start.1 = ((bf16[1,4,128,512]{3,1,0,2:T(4,128)(2,1)}), bf16[1,4,128,512]{3,1,0,2:T(4,128)(2,1)S(1)}, u32[]{:S(2)}, u32[]{:S(2)}) async-start(bf16[1,4,128,512]{3,1,0,2:T(4,128)(2,1)} %copy.47), calls=%async_computation.1 | async-start | bytes 1048576 | tf_op jit(solution)/shard_map/all_to_all | solution.py:232
  46.9 14.6 %copy-start.2 = (s32[8,8,8]{2,1,0:T(8,128)S(1)}, s32[8,8,8]{2,1,0:T(8,128)}, u32[]{:S(2)}) copy-start(s32[8,8,8]{2,1,0:T(8,128)} %param.9) | copy-start | bytes 6148
  46.9 14.7 %copy-start.6 = (f32[8,8,1]{1,0,2:T(8,128)S(1)}, f32[8,8,1]{1,0,2:T(8,128)}, u32[]{:S(2)}) copy-start(f32[8,8,1]{1,0,2:T(8,128)} %constant.53) | copy-start | bytes 772
  46.9 14.9 %copy-start.3 = (f32[8,8]{0,1:T(8,128)S(1)}, f32[8,8]{0,1:T(8,128)}, u32[]{:S(2)}) copy-start(f32[8,8]{0,1:T(8,128)} %constant.50) | copy-start | bytes 772
  46.9 14.9 %copy-start.4 = (f32[8,8,1,1]{1,0,3,2:T(8,128)S(1)}, f32[8,8,1,1]{1,0,3,2:T(8,128)}, u32[]{:S(2)}) copy-start(f32[8,8,1,1]{1,0,3,2:T(8,128)} %constant.51) | copy-start | bytes 772
  46.9 14.9 %copy-start.5 = (f32[8,8]{0,1:T(8,128)S(1)}, f32[8,8]{0,1:T(8,128)}, u32[]{:S(2)}) copy-start(f32[8,8]{0,1:T(8,128)} %constant.52) | copy-start | bytes 772
  57.9 51.6 %all-to-all-start = ((bf16[1,4,256,1024]{3,1,0,2:T(4,128)(2,1)}), bf16[1,4,256,1024]{3,1,0,2:T(4,128)(2,1)S(1)}, u32[]{:S(2)}, u32[]{:S(2)}) async-start(bf16[1,4,256,1024]{3,1,0,2:T(4,128)(2,1)} %copy.39), calls=%async_computation | async-start | bytes 4194304 | tf_op jit(solution)/shard_map/all_to_all | solution.py:232
  93.1 18.5 %copy-start = (f32[8,8,8,8]{3,2,1,0:T(8,128)S(1)}, f32[8,8,8,8]{3,2,1,0:T(8,128)}, u32[]{:S(2)}) copy-start(f32[8,8,8,8]{3,2,1,0:T(8,128)} %copy.46.coeff_ref) | copy-start | bytes 49156

commit v6 on v5

--- a/solution.py
+++ b/solution.py
@@ -179,27 +179,29 @@
     return jnp.einsum("ts,suxy->tuxy", clamp, fill, precision=hi)
 
 
-def smooth_kernel(level_ref, coeff_ref, out_ref):
-    dates = level_ref.shape[0]
-    rows = level_ref.shape[2]
-    width = level_ref.shape[3]
+def smooth_kernel(level_ref, coeff_ref, out_ref, values_ref):
+    dates, bands, rows, width = level_ref.shape
     mask_cols = coeff_ref.shape[3]
     span = width // mask_cols
     per_tile = 128 // span
     lane_group = lax.broadcasted_iota(jnp.int32, (rows, 128), 1) // span
     for j in range(width // 128):
-        values = [level_ref[u, 0, :, 128 * j : 128 * (j + 1)].astype(jnp.float32) for u in range(dates)]
+        values_ref[...] = level_ref[:, :, :, 128 * j : 128 * (j + 1)].astype(jnp.float32)
 
         def one_date(t, carry):
-            acc = jnp.zeros((rows, 128), jnp.float32)
+            tiles = []
             for u in range(dates):
                 c = coeff_ref[t, u]
                 tile = jnp.broadcast_to(c[:, per_tile * j : per_tile * j + 1], (rows, 128))
                 for g in range(1, per_tile):
                     m = per_tile * j + g
                     tile = jnp.where(lane_group == g, jnp.broadcast_to(c[:, m : m + 1], (rows, 128)), tile)
-                acc = acc + tile * values[u]
-            out_ref[t, 0, :, 128 * j : 128 * (j + 1)] = acc.astype(out_ref.dtype)
+                tiles.append(tile)
+            for band in range(bands):
+                acc = tiles[0] * values_ref[0, band]
+                for u in range(1, dates):
+                    acc = acc + tiles[u] * values_ref[u, band]
+                out_ref[t, band, :, 128 * j : 128 * (j + 1)] = acc.astype(out_ref.dtype)
             return carry
 
         lax.fori_loop(0, dates, one_date, 0)
@@ -210,13 +212,13 @@
     grown = jnp.repeat(coeff, rows // coeff.shape[2], axis=2)
     return pl.pallas_call(
         smooth_kernel,
-        grid=(bands,),
         in_specs=[
-            pl.BlockSpec((dates, 1, rows, width), lambda b: (0, b, 0, 0)),
-            pl.BlockSpec(grown.shape, lambda b: (0, 0, 0, 0)),
-        ],
-        out_specs=pl.BlockSpec((dates, 1, rows, width), lambda b: (0, b, 0, 0)),
+            pl.BlockSpec(level.shape, lambda: (0, 0, 0, 0)),
+            pl.BlockSpec(grown.shape, lambda: (0, 0, 0, 0)),
+        ],
+        out_specs=pl.BlockSpec(level.shape, lambda: (0, 0, 0, 0)),
         out_shape=jax.ShapeDtypeStruct(level.shape, jnp.bfloat16),
+        scratch_shapes=[pltpu.VMEM((dates, bands, rows, 128), jnp.float32)],
     )(level, grown)
 
 

time: 142 us -> 124 us (0.87)
  Pallas kernels: 69.1 us -> 33.6 us
  waiting for transfers between devices: 33.5 us -> 50.5 us
    pallas_call x3, Pallas kernels: 55.6 us -> 20.2 us  [smooth(): pl.pallas_call(smooth_kernel, in_specs=[pl.BlockSpec(level.shape, lambda:...]
    all_to_all x3, waiting for transfers between devices: 33 us -> 50 us  [local(): lax.all_to_all(level, 'date', split_axis=2, concat_axis=0, tiled=True)]
  transfers between devices with their start and end apart: 5 -> 5, of which waited for: 4 -> 4; matrix products, arithmetic and copies ran while one was open for 8% -> 9% of each run, Pallas kernels for 19% -> 8%
where the time goes in v6:
time: 124 us; the launch traced here: 123 us
  waiting for transfers between devices  50.5 us (41%)
  Pallas kernels  33.6 us (27%)
  starting transfers between devices  17.4 us (14%)
  local copies, waits for them, and re-layouts  15.5 us (12%)
  other arithmetic  5 us (4%)
    all_to_all x3, waiting for transfers between devices, local(): lax.all_to_all(level, 'date', split_axis=2, concat_axis=0, tiled=True)  50 us
    pallas_call x3, Pallas kernels, smooth(): pl.pallas_call(smooth_kernel, in_specs=[pl.BlockSpec(level.shape, lambda:...  20.2 us
    all_to_all x3, starting transfers between devices, local(): lax.all_to_all(level, 'date', split_axis=2, concat_axis=0, tiled=True)  13.8 us
    pallas_call x1, Pallas kernels, pyramid(): pl.pallas_call(pyramid_kernel, grid=(dates, bands), in_specs=[pl.BlockSpe...  13.5 us
    pallas_call x3, local copies, waits for them, and re-layouts, pyramid(): pl.pallas_call(pyramid_kernel, grid=(dates, bands), in_specs=[pl.BlockSpe...  7 us
    concatenate x1, other arithmetic, padded(): block = jnp.concatenate([low, block, high], axis=dim)  3.63 us
    all_to_all x3, local copies, waits for them, and re-layouts, local(): lax.all_to_all(level, 'date', split_axis=2, concat_axis=0, tiled=True)  3.61 us
    broadcast_in_dim x2, local copies, waits for them, and re-layouts, smooth(): grown = jnp.repeat(coeff, rows // coeff.shape[2], axis=2)  3.19 us
  transfers between devices with their start and end apart: 5, of which 4 were waited for; matrix products, arithmetic and copies ran while one was open for 9% of the time, Pallas kernels for 8%

profile of v6, /device:TPU:0, one launch (start us, length us, event | category | flops | bytes accessed | tf_op | source)
XLA Modules:
  0.0 123.4 jit_solution(2424746823896194070)
XLA Ops:
  0.6 0.9 fusion.27
  1.5 2.4 %collective-permute-start = (bf16[1,4,6,1024]{3,2,1,0:T(8,128)(2,1)S(1)}, bf16[1,4,6,1024]{3,2,1,0:T(8,128)(2,1)S(1)}, u32[]{:S(2)}, u32[]{:S(2)}) collective-permute-start(bf16[1,4,6,1024]{3,2,1,0:T(8,128)(2,1)S(1)} %get-tuple-element.9), channel_id=1, source_target_pairs={{0,1},{2,3},{4,5},{6,7},{8,9},{10,11},{12,13},{14,15},{16,17},{18,... | collective-permute-start | bytes 147464 | tf_op jit(solution)/shard_map/ppermute | solution.py:21
  3.9 1.3 %collective-permute-start.1 = (bf16[1,4,6,1024]{3,2,1,0:T(8,128)(2,1)S(1)}, bf16[1,4,6,1024]{3,2,1,0:T(8,128)(2,1)S(1)}, u32[]{:S(2)}, u32[]{:S(2)}) collective-permute-start(bf16[1,4,6,1024]{3,2,1,0:T(8,128)(2,1)S(1)} %get-tuple-element.10), channel_id=1, source_target_pairs={{1,0},{3,2},{5,4},{7,6},{9,8},{11,10},{13,12},{15,14},{17,16},{19,... | collective-permute-start | bytes 147464 | tf_op jit(solution)/shard_map/ppermute | solution.py:24
  5.2 0.7 fusion.14.keep_wide_ref
  5.9 0.6 fusion.24.keep_half_ref
  6.5 0.0 collective-permute-done
  6.6 0.5 collective-permute-done.1
  7.0 3.6 %fusion.4.x_ref = bf16[1,4,272,1024]{3,2,1,0:T(8,128)(2,1)} fusion(bf16[1,4,6,1024]{3,2,1,0:T(8,128)(2,1)S(1)} %collective-permute-done.1, bf16[1,4,256,1024]{3,2,1,0:T(8,128)(2,1)} %param.7, bf16[1,4,6,1024]{3,2,1,0:T(8,128)(2,1)S(1)} %collective-permute-done), kind=kLoop, calls=%fused_computation.5 | loop fusion | flops 11141120 | bytes 4423680 | tf_op jit(solution)/shard_map/concatenate | solution.py:25
  10.7 13.5 %shard_map.94 = (bf16[1,4,256,1024]{3,2,1,0:T(8,128)(2,1)}, bf16[1,4,128,512]{3,2,1,0:T(8,128)(2,1)}, bf16[1,4,64,256]{3,2,1,0:T(8,128)(2,1)}) custom-call(f32[2,4,7]{2,1,0:T(4,128)} %taps_ref.1, bf16[1,4,272,1024]{3,2,1,0:T(8,128)(2,1)} %fusion.4.x_ref, f32[280,1]{1,0:T(8,128)} %fusion.14.keep_wide_ref, f32[136,1]{1,0:T(8,128)} %fusion.24.keep_half_ref), custom_call_target="tpu_custom_call" | custom-call | tf_op jit(solution)/shard_map/pallas_call | solution.py:135
  24.1 1.8 %copy.51 = bf16[1,4,64,256]{3,1,0,2:T(4,128)(2,1)} copy(bf16[1,4,64,256]{3,2,1,0:T(8,128)(2,1)} %get-tuple-element.8) | data formatting | bytes 262144 | tf_op jit(solution)/shard_map/pallas_call | solution.py:135
  26.0 6.7 %all-to-all-start.2 = ((bf16[1,4,64,256]{3,1,0,2:T(4,128)(2,1)}), bf16[1,4,64,256]{3,1,0,2:T(4,128)(2,1)S(1)}, u32[]{:S(2)}, u32[]{:S(2)}) async-start(bf16[1,4,64,256]{3,1,0,2:T(4,128)(2,1)} %copy.51), calls=%async_computation.2 | async-start | bytes 262144 | tf_op jit(solution)/shard_map/all_to_all | solution.py:234
  32.6 2.2 %copy.47 = bf16[1,4,128,512]{3,1,0,2:T(4,128)(2,1)} copy(bf16[1,4,128,512]{3,2,1,0:T(8,128)(2,1)} %get-tuple-element.7) | data formatting | bytes 1048576 | tf_op jit(solution)/shard_map/pallas_call | solution.py:135
  34.9 5.5 %all-to-all-done.2 = bf16[1,4,64,256]{3,1,0,2:T(4,128)(2,1)S(1)} async-done(((bf16[1,4,64,256]{3,1,0,2:T(4,128)(2,1)}), bf16[1,4,64,256]{3,1,0,2:T(4,128)(2,1)S(1)}, u32[]{:S(2)}, u32[]{:S(2)}) %all-to-all-start.2) | async-done | bytes 131104 | tf_op jit(solution)/shard_map/all_to_all | solution.py:234
  40.4 3.5 %all-to-all-start.1 = ((bf16[1,4,128,512]{3,1,0,2:T(4,128)(2,1)}), bf16[1,4,128,512]{3,1,0,2:T(4,128)(2,1)S(1)}, u32[]{:S(2)}, u32[]{:S(2)}) async-start(bf16[1,4,128,512]{3,1,0,2:T(4,128)(2,1)} %copy.47), calls=%async_computation.1 | async-start | bytes 1048576 | tf_op jit(solution)/shard_map/all_to_all | solution.py:234
  43.9 0.0 copy-done.1
  43.9 2.9 %copy.39 = bf16[1,4,256,1024]{3,1,0,2:T(4,128)(2,1)} copy(bf16[1,4,256,1024]{3,2,1,0:T(8,128)(2,1)S(1)} %copy-done.1) | data formatting | bytes 4194304 | tf_op jit(solution)/shard_map/pallas_call | solution.py:135
  46.9 0.0 copy-start.5
  46.9 11.0 %all-to-all-done.1 = bf16[1,4,128,512]{3,1,0,2:T(4,128)(2,1)S(1)} async-done(((bf16[1,4,128,512]{3,1,0,2:T(4,128)(2,1)}), bf16[1,4,128,512]{3,1,0,2:T(4,128)(2,1)S(1)}, u32[]{:S(2)}, u32[]{:S(2)}) %all-to-all-start.1) | async-done | bytes 524320 | tf_op jit(solution)/shard_map/all_to_all | solution.py:234
  57.9 3.6 %all-to-all-start = ((bf16[1,4,256,1024]{3,1,0,2:T(4,128)(2,1)}), bf16[1,4,256,1024]{3,1,0,2:T(4,128)(2,1)S(1)}, u32[]{:S(2)}, u32[]{:S(2)}) async-start(bf16[1,4,256,1024]{3,1,0,2:T(4,128)(2,1)} %copy.39), calls=%async_computation | async-start | bytes 4194304 | tf_op jit(solution)/shard_map/all_to_all | solution.py:234
  61.5 0.0 copy-done.2
  61.6 0.2 convolution_divide_fusion
  61.8 0.4 fusion.5
  62.2 0.8 copy.46.coeff_ref
  63.0 0.7 copy.76
  63.7 3.7 %shard_map.97 = bf16[8,4,8,256]{3,2,1,0:T(8,128)(2,1)} custom-call(bf16[8,4,8,256]{3,2,1,0:T(8,128)(2,1)} %bitcast.33, f32[8,8,8,8]{3,2,1,0:T(8,128)} %copy.46.coeff_ref), custom_call_target="tpu_custom_call" | custom-call | tf_op jit(solution)/shard_map/pallas_call | solution.py:213
  67.3 0.9 copy.75
  68.3 1.9 %broadcast_in_dim.5 = f32[8,8,8,2,8]{4,3,2,1,0:T(2,128)} broadcast(f32[8,8,8,8]{3,2,1,0:T(8,128)} %copy.46.coeff_ref), dimensions={0,1,2,4} | broadcast | bytes 49152 | tf_op jit(solution)/shard_map/broadcast_in_dim | solution.py:212
  70.2 5.9 %shard_map.96 = bf16[8,4,16,512]{3,2,1,0:T(8,128)(2,1)} custom-call(bf16[8,4,16,512]{3,2,1,0:T(8,128)(2,1)} %bitcast.29, f32[8,8,16,8]{3,2,1,0:T(8,128)} %bitcast.30), custom_call_target="tpu_custom_call" | custom-call | tf_op jit(solution)/shard_map/pallas_call | solution.py:213
  76.0 33.5 %all-to-all-done = bf16[1,4,256,1024]{3,1,0,2:T(4,128)(2,1)S(1)} async-done(((bf16[1,4,256,1024]{3,1,0,2:T(4,128)(2,1)}), bf16[1,4,256,1024]{3,1,0,2:T(4,128)(2,1)S(1)}, u32[]{:S(2)}, u32[]{:S(2)}) %all-to-all-start) | async-done | bytes 2097184 | tf_op jit(solution)/shard_map/all_to_all | solution.py:234
  109.5 2.0 %copy.74 = bf16[1,4,8,32,1024]{4,3,1,2,0:T(8,128)(2,1)} copy(bf16[1,4,8,32,1024]{4,1,3,2,0:T(4,128)(2,1)S(1)} %bitcast.26) | data formatting | bytes 4194304 | tf_op jit(solution)/shard_map/all_to_all | solution.py:234
  111.5 1.3 %broadcast_in_dim.4 = f32[8,8,8,4,8]{4,3,2,1,0:T(4,128)} broadcast(f32[8,8,8,8]{3,2,1,0:T(8,128)S(1)} %copy-done), dimensions={0,1,2,4} | broadcast | bytes 81920 | tf_op jit(solution)/shard_map/broadcast_in_dim | solution.py:212
  112.8 10.6 %shard_map.95 = bf16[8,4,32,1024]{3,2,1,0:T(8,128)(2,1)} custom-call(bf16[8,4,32,1024]{3,2,1,0:T(8,128)(2,1)} %bitcast.27, f32[8,8,32,8]{3,2,1,0:T(8,128)} %bitcast.28), custom_call_target="tpu_custom_call" | custom-call | tf_op jit(solution)/shard_map/pallas_call | solution.py:213
  (15 shorter events, 0.1 us)
Async XLA Ops:
  1.5 5.0 %collective-permute-start = (bf16[1,4,6,1024]{3,2,1,0:T(8,128)(2,1)S(1)}, bf16[1,4,6,1024]{3,2,1,0:T(8,128)(2,1)S(1)}, u32[]{:S(2)}, u32[]{:S(2)}) collective-permute-start(bf16[1,4,6,1024]{3,2,1,0:T(8,128)(2,1)S(1)} %get-tuple-element.9), channel_id=1, source_target_pairs={{0,1},{2,3},{4,5},{6,7},{8,9},{10,11},{12,13},{14,15},{16,17},{18,... | collective-permute-start | bytes 147464 | tf_op jit(solution)/shard_map/ppermute | solution.py:21
  3.9 3.1 %collective-permute-start.1 = (bf16[1,4,6,1024]{3,2,1,0:T(8,128)(2,1)S(1)}, bf16[1,4,6,1024]{3,2,1,0:T(8,128)(2,1)S(1)}, u32[]{:S(2)}, u32[]{:S(2)}) collective-permute-start(bf16[1,4,6,1024]{3,2,1,0:T(8,128)(2,1)S(1)} %get-tuple-element.10), channel_id=1, source_target_pairs={{1,0},{3,2},{5,4},{7,6},{9,8},{11,10},{13,12},{15,14},{17,16},{19,... | collective-permute-start | bytes 147464 | tf_op jit(solution)/shard_map/ppermute | solution.py:24
  24.1 19.8 %copy-start.1 = (bf16[1,4,256,1024]{3,2,1,0:T(8,128)(2,1)S(1)}, bf16[1,4,256,1024]{3,2,1,0:T(8,128)(2,1)}, u32[]{:S(2)}) copy-start(bf16[1,4,256,1024]{3,2,1,0:T(8,128)(2,1)} %get-tuple-element.6) | copy-start | bytes 6291460
  26.0 14.4 %all-to-all-start.2 = ((bf16[1,4,64,256]{3,1,0,2:T(4,128)(2,1)}), bf16[1,4,64,256]{3,1,0,2:T(4,128)(2,1)S(1)}, u32[]{:S(2)}, u32[]{:S(2)}) async-start(bf16[1,4,64,256]{3,1,0,2:T(4,128)(2,1)} %copy.51), calls=%async_computation.2 | async-start | bytes 262144 | tf_op jit(solution)/shard_map/all_to_all | solution.py:234
  40.4 17.5 %all-to-all-start.1 = ((bf16[1,4,128,512]{3,1,0,2:T(4,128)(2,1)}), bf16[1,4,128,512]{3,1,0,2:T(4,128)(2,1)S(1)}, u32[]{:S(2)}, u32[]{:S(2)}) async-start(bf16[1,4,128,512]{3,1,0,2:T(4,128)(2,1)} %copy.47), calls=%async_computation.1 | async-start | bytes 1048576 | tf_op jit(solution)/shard_map/all_to_all | solution.py:234
  46.9 14.6 %copy-start.2 = (s32[8,8,8]{2,1,0:T(8,128)S(1)}, s32[8,8,8]{2,1,0:T(8,128)}, u32[]{:S(2)}) copy-start(s32[8,8,8]{2,1,0:T(8,128)} %param.9) | copy-start | bytes 6148
  46.9 14.7 %copy-start.6 = (f32[8,8,1]{1,0,2:T(8,128)S(1)}, f32[8,8,1]{1,0,2:T(8,128)}, u32[]{:S(2)}) copy-start(f32[8,8,1]{1,0,2:T(8,128)} %constant.53) | copy-start | bytes 772
  46.9 14.9 %copy-start.3 = (f32[8,8]{0,1:T(8,128)S(1)}, f32[8,8]{0,1:T(8,128)}, u32[]{:S(2)}) copy-start(f32[8,8]{0,1:T(8,128)} %constant.50) | copy-start | bytes 772
  46.9 14.9 %copy-start.4 = (f32[8,8,1,1]{1,0,3,2:T(8,128)S(1)}, f32[8,8,1,1]{1,0,3,2:T(8,128)}, u32[]{:S(2)}) copy-start(f32[8,8,1,1]{1,0,3,2:T(8,128)} %constant.51) | copy-start | bytes 772
  46.9 14.9 %copy-start.5 = (f32[8,8]{0,1:T(8,128)S(1)}, f32[8,8]{0,1:T(8,128)}, u32[]{:S(2)}) copy-start(f32[8,8]{0,1:T(8,128)} %constant.52) | copy-start | bytes 772
  57.9 51.6 %all-to-all-start = ((bf16[1,4,256,1024]{3,1,0,2:T(4,128)(2,1)}), bf16[1,4,256,1024]{3,1,0,2:T(4,128)(2,1)S(1)}, u32[]{:S(2)}, u32[]{:S(2)}) async-start(bf16[1,4,256,1024]{3,1,0,2:T(4,128)(2,1)} %copy.39), calls=%async_computation | async-start | bytes 4194304 | tf_op jit(solution)/shard_map/all_to_all | solution.py:234
  76.0 35.5 %copy-start = (f32[8,8,8,8]{3,2,1,0:T(8,128)S(1)}, f32[8,8,8,8]{3,2,1,0:T(8,128)}, u32[]{:S(2)}) copy-start(f32[8,8,8,8]{3,2,1,0:T(8,128)} %copy.46.coeff_ref) | copy-start | bytes 49156

commit v7 on v6

--- a/solution.py
+++ b/solution.py
@@ -1,3 +1,4 @@
+import functools
 import math
 
 import jax
@@ -63,7 +64,7 @@
         first = lo - (256 * j - 128)
         last = first + (hi_col - lo)
         part = table[first:last]
-        out_ref[j] = mm(high[:, lo:hi_col], part) + mm(low[:, lo:hi_col], part)
+        out_ref[j, 0 : values.shape[0]] = mm(high[:, lo:hi_col], part) + mm(low[:, lo:hi_col], part)
 
 
 def halve_rows(source_ref, count):
@@ -73,13 +74,19 @@
     return jnp.concatenate([total[j] for j in range(total.shape[0])], axis=1)
 
 
-def pyramid_kernel(taps_ref, x_ref, keep_wide_ref, keep_half_ref, o0_ref, o1_ref, o2_ref,
+def piece_rows(rows, ndate):
+    fine = rows // ndate
+    return (fine, max(fine // 2, 8), max(fine // 4, 8))
+
+
+def pyramid_kernel(ndate, taps_ref, x_ref, keep_wide_ref, keep_half_ref, packed_ref,
                    across_ref, wide_ref, half_ref, quarter_ref):
     b = pl.program_id(1)
     x = x_ref[0, 0]
     used = x.shape[0]
     width = x.shape[1]
     tiles = width // 128
+    rows = used - 16
     column = [taps_ref[0, b, k] for k in range(7)]
     row = [taps_ref[1, b, k] for k in range(7)]
     table = band_table(3 * 128, 128, 125, (1, column))
@@ -104,36 +111,34 @@
     total = total * keep_wide_ref[...]
     for j in range(tiles):
         wide_ref[j] = total[:, 128 * j : 128 * (j + 1)]
-    rows = o0_ref.shape[2]
-    for j in range(tiles):
-        o0_ref[0, 0, :, 128 * j : 128 * (j + 1)] = wide_ref[j, pl.ds(3, rows), :].astype(o0_ref.dtype)
     n_half = keep_half_ref.shape[0]
     halves = halve_rows(wide_ref, n_half) * keep_half_ref[...]
     down = band_table(512, 128, 127, (2, pyramid_filter)).astype(jnp.bfloat16)
     halve_columns(halves, down, half_ref)
-    for j in range(tiles // 2):
-        o1_ref[0, 0, :, 128 * j : 128 * (j + 1)] = half_ref[j, pl.ds(1, rows // 2), :].astype(o1_ref.dtype)
     quarters = halve_rows(half_ref, rows // 4)
+    n_quarter = quarter_ref.shape[1]
+    quarter_ref[:, rows // 4 : n_quarter, :] = jnp.zeros((tiles // 4, n_quarter - rows // 4, 128), jnp.float32)
     halve_columns(quarters, down, quarter_ref)
-    for j in range(tiles // 4):
-        o2_ref[0, 0, :, 128 * j : 128 * (j + 1)] = quarter_ref[j].astype(o2_ref.dtype)
-
-
-def pyramid(extended, resample_taps, band_index, total_rows):
+    fine, p_half, p_quarter = piece_rows(rows, ndate)
+    for q in range(ndate):
+        parts = [wide_ref[j, pl.ds(3 + fine * q, fine), :] for j in range(tiles)]
+        parts += [half_ref[j, pl.ds(1 + (fine // 2) * q, p_half), :] for j in range(tiles // 2)]
+        parts += [quarter_ref[j, pl.ds((fine // 4) * q, p_quarter), :] for j in range(tiles // 4)]
+        packed_ref[q, 0, 0] = jnp.concatenate(parts, axis=0).astype(packed_ref.dtype)
+
+
+def pyramid(extended, resample_taps, band_index, total_rows, ndate):
     dates, bands, used, width = extended.shape
     rows = used - 16
     n_wide = rows + 24
     n_half = rows // 2 + 8
     depth = n_wide + 8
+    fine, p_half, p_quarter = piece_rows(rows, ndate)
+    count = (width // 128) * fine + (width // 256) * p_half + (width // 512) * p_quarter
     keep_wide = inside_rows(n_wide, band_index * rows - 3, rows + 6, total_rows)
     keep_half = inside_rows(n_half, band_index * (rows // 2) - 1, rows // 2 + 2, total_rows // 2)
-    out_shape = (
-        jax.ShapeDtypeStruct((dates, bands, rows, width), jnp.bfloat16),
-        jax.ShapeDtypeStruct((dates, bands, rows // 2, width // 2), jnp.bfloat16),
-        jax.ShapeDtypeStruct((dates, bands, rows // 4, width // 4), jnp.bfloat16),
-    )
     return pl.pallas_call(
-        pyramid_kernel,
+        functools.partial(pyramid_kernel, ndate),
         grid=(dates, bands),
         in_specs=[
             pl.BlockSpec(memory_space=pltpu.SMEM),
@@ -141,17 +146,13 @@
             pl.BlockSpec((n_wide, 1), lambda d, b: (0, 0)),
             pl.BlockSpec((n_half, 1), lambda d, b: (0, 0)),
         ],
-        out_specs=[
-            pl.BlockSpec((1, 1, rows, width), lambda d, b: (d, b, 0, 0)),
-            pl.BlockSpec((1, 1, rows // 2, width // 2), lambda d, b: (d, b, 0, 0)),
-            pl.BlockSpec((1, 1, rows // 4, width // 4), lambda d, b: (d, b, 0, 0)),
-        ],
-        out_shape=out_shape,
+        out_specs=pl.BlockSpec((ndate, 1, 1, count, 128), lambda d, b: (0, d, b, 0, 0)),
+        out_shape=jax.ShapeDtypeStruct((ndate, dates, bands, count, 128), jnp.bfloat16),
         scratch_shapes=[
             pltpu.VMEM((depth, width), jnp.float32),
             pltpu.VMEM((width // 128, n_wide, 128), jnp.float32),
             pltpu.VMEM((width // 256, n_half, 128), jnp.float32),
-            pltpu.VMEM((width // 512, rows // 4, 128), jnp.float32),
+            pltpu.VMEM((width // 512, rows // 4 + 8, 128), jnp.float32),
         ],
     )(resample_taps, extended, keep_wide, keep_half)
 
@@ -179,61 +180,78 @@
     return jnp.einsum("ts,suxy->tuxy", clamp, fill, precision=hi)
 
 
-def smooth_kernel(level_ref, coeff_ref, out_ref, values_ref):
-    dates, bands, rows, width = level_ref.shape
+def smooth_level(got_ref, start, piece, coeff_ref, out_ref, section_ref):
+    dates, bands, rows, width = out_ref.shape
+    tiles = width // 128
     mask_cols = coeff_ref.shape[3]
     span = width // mask_cols
     per_tile = 128 // span
     lane_group = lax.broadcasted_iota(jnp.int32, (rows, 128), 1) // span
-    for j in range(width // 128):
-        values_ref[...] = level_ref[:, :, :, 128 * j : 128 * (j + 1)].astype(jnp.float32)
+    section_ref[...] = got_ref[:, :, start : start + tiles * piece, :].astype(jnp.float32)
+    for j in range(tiles):
 
         def one_date(t, carry):
-            tiles = []
+            coeffs = []
             for u in range(dates):
                 c = coeff_ref[t, u]
                 tile = jnp.broadcast_to(c[:, per_tile * j : per_tile * j + 1], (rows, 128))
                 for g in range(1, per_tile):
                     m = per_tile * j + g
                     tile = jnp.where(lane_group == g, jnp.broadcast_to(c[:, m : m + 1], (rows, 128)), tile)
-                tiles.append(tile)
+                coeffs.append(tile)
             for band in range(bands):
-                acc = tiles[0] * values_ref[0, band]
+                acc = coeffs[0] * section_ref[0, band, j * piece : j * piece + rows, :]
                 for u in range(1, dates):
-                    acc = acc + tiles[u] * values_ref[u, band]
+                    acc = acc + coeffs[u] * section_ref[u, band, j * piece : j * piece + rows, :]
                 out_ref[t, band, :, 128 * j : 128 * (j + 1)] = acc.astype(out_ref.dtype)
             return carry
 
         lax.fori_loop(0, dates, one_date, 0)
 
 
-def smooth(level, coeff):
-    dates, bands, rows, width = level.shape
-    grown = jnp.repeat(coeff, rows // coeff.shape[2], axis=2)
+def smooth_kernel(pieces, got_ref, c0_ref, c1_ref, c2_ref, o0_ref, o1_ref, o2_ref, s0_ref, s1_ref, s2_ref):
+    start = 0
+    for piece, c_ref, o_ref, s_ref in zip(pieces, (c0_ref, c1_ref, c2_ref), (o0_ref, o1_ref, o2_ref), (s0_ref, s1_ref, s2_ref)):
+        smooth_level(got_ref, start, piece, c_ref, o_ref, s_ref)
+        start += (o_ref.shape[3] // 128) * piece
+
+
+def smooth_all(got, coeff, shapes, pieces):
+    dates, bands = got.shape[:2]
+    grown = [jnp.repeat(coeff, shape[2] // coeff.shape[2], axis=2) for shape in shapes]
+    full = lambda a: pl.BlockSpec(a.shape, lambda: (0,) * len(a.shape))
+    outs = [jax.ShapeDtypeStruct(shape, jnp.bfloat16) for shape in shapes]
     return pl.pallas_call(
-        smooth_kernel,
-        in_specs=[
-            pl.BlockSpec(level.shape, lambda: (0, 0, 0, 0)),
-            pl.BlockSpec(grown.shape, lambda: (0, 0, 0, 0)),
+        functools.partial(smooth_kernel, pieces),
+        in_specs=[full(got)] + [full(g) for g in grown],
+        out_specs=[full(o) for o in outs],
+        out_shape=outs,
+        scratch_shapes=[
+            pltpu.VMEM((dates, bands, (shape[3] // 128) * piece, 128), jnp.float32)
+            for shape, piece in zip(shapes, pieces)
         ],
-        out_specs=pl.BlockSpec(level.shape, lambda: (0, 0, 0, 0)),
-        out_shape=jax.ShapeDtypeStruct(level.shape, jnp.bfloat16),
-        scratch_shapes=[pltpu.VMEM((dates, bands, rows, 128), jnp.float32)],
-    )(level, grown)
+    )(got, *grown)
 
 
 def local(scenes, resample_taps, clear_mask):
-    rows = scenes.shape[2]
+    dates, bands, rows, width = scenes.shape
     band_index = lax.axis_index("row")
     total_rows = rows * lax.axis_size("row")
+    ndate = lax.axis_size("date")
     extended = padded(scenes, (("row", 2),), 6)
     extended = jnp.pad(extended, ((0, 0), (0, 0), (0, 4), (0, 0)))
-    levels = pyramid(extended, resample_taps, band_index, total_rows)
+    packed = pyramid(extended, resample_taps, band_index, total_rows, ndate)
     coeff = smooth_coefficients(clear_mask.astype(jnp.float32))
-    return tuple(
-        smooth(lax.all_to_all(level, "date", split_axis=2, concat_axis=0, tiled=True), coeff)
-        for level in levels
+    got = lax.all_to_all(packed, "date", split_axis=0, concat_axis=0, tiled=True)
+    got = got.reshape((ndate * dates,) + got.shape[2:])
+    fine = rows // ndate
+    total = ndate * dates
+    shapes = (
+        (total, bands, fine, width),
+        (total, bands, fine // 2, width // 2),
+        (total, bands, fine // 4, width // 4),
     )
+    return tuple(smooth_all(got, coeff, shapes, piece_rows(rows, ndate)))
 
 
 def solution(mesh):

time: 124 us -> 113 us (0.911)
  waiting for transfers between devices: 50.5 us -> 62.8 us
  local copies, waits for them, and re-layouts: 15.5 us -> 3.41 us
  starting transfers between devices: 17.4 us -> 10.5 us
  Pallas kernels: 33.6 us -> 30 us
    all_to_all x3 -> x1, waiting for transfers between devices: 50 us -> 62.3 us  [local(): lax.all_to_all(packed, 'date', split_axis=0, concat_axis=0, tiled=True)]
    pallas_call x3 -> x0, local copies, waits for them, and re-layouts: 7 us -> none  [pyramid(): pl.pallas_call(pyramid_kernel, grid=(dates, bands), in_specs=[pl.BlockSpe...]
    all_to_all x3 -> x1, starting transfers between devices: 13.8 us -> 6.8 us  [local(): lax.all_to_all(packed, 'date', split_axis=0, concat_axis=0, tiled=True)]
    pallas_call x4 -> x2, Pallas kernels: 33.6 us -> 30 us  [the longest x1 16.8 us: smooth_all(): pl.pallas_call(functools.partial(smooth_kernel, pieces), in_specs=[full(g...]
    all_to_all x3 -> x0, local copies, waits for them, and re-layouts: 3.61 us -> none  [local(): lax.all_to_all(level, 'date', split_axis=2, concat_axis=0, tiled=True)]
  transfers between devices with their start and end apart: 5 -> 3, of which waited for: 4 -> 2; matrix products, arithmetic and copies ran while one was open for 9% -> 2% of each run, Pallas kernels for 8% -> 0%
where the time goes in v7:
time: 113 us
  waiting for transfers between devices  62.8 us (56%)
  Pallas kernels  30 us (27%)
  starting transfers between devices  10.5 us (9%)
  other arithmetic  5.02 us (4%)
  local copies, waits for them, and re-layouts  3.41 us (3%)
    all_to_all x1, waiting for transfers between devices, local(): lax.all_to_all(packed, 'date', split_axis=0, concat_axis=0, tiled=True)  62.3 us
    pallas_call x1, Pallas kernels, smooth_all(): pl.pallas_call(functools.partial(smooth_kernel, pieces), in_specs=[full(g...  16.8 us
    pallas_call x1, Pallas kernels, pyramid(): pl.pallas_call(functools.partial(pyramid_kernel, ndate), grid=(dates, ban...  13.2 us
    all_to_all x1, starting transfers between devices, local(): lax.all_to_all(packed, 'date', split_axis=0, concat_axis=0, tiled=True)  6.8 us
    concatenate x1, other arithmetic, padded(): block = jnp.concatenate([low, block, high], axis=dim)  3.65 us
    broadcast_in_dim x2, local copies, waits for them, and re-layouts, smooth_all(): jnp.repeat(coeff, shape[2] // coeff.shape[2], axis=2)  2.41 us
    ppermute x1, starting transfers between devices, padded(): lax.ppermute(lax.slice_in_dim(block, block.shape[dim] - width, None, axis...  2.36 us
  transfers between devices with their start and end apart: 3, of which 2 were waited for; matrix products, arithmetic and copies ran while one was open for 2% of the time, Pallas kernels for 0%

profile of v7, /device:TPU:0, one launch (start us, length us, event | category | flops | bytes accessed | tf_op | source)
XLA Modules:
  0.0 113.0 jit_solution(18127927899979132732)
XLA Ops:
  0.6 0.9 fusion.27
  1.5 2.4 %collective-permute-start = (bf16[1,4,6,1024]{3,2,1,0:T(8,128)(2,1)S(1)}, bf16[1,4,6,1024]{3,2,1,0:T(8,128)(2,1)S(1)}, u32[]{:S(2)}, u32[]{:S(2)}) collective-permute-start(bf16[1,4,6,1024]{3,2,1,0:T(8,128)(2,1)S(1)} %get-tuple-element.3), channel_id=1, source_target_pairs={{0,1},{2,3},{4,5},{6,7},{8,9},{10,11},{12,13},{14,15},{16,17},{18,... | collective-permute-start | bytes 147464 | tf_op jit(solution)/shard_map/ppermute | solution.py:22
  3.9 1.3 %collective-permute-start.1 = (bf16[1,4,6,1024]{3,2,1,0:T(8,128)(2,1)S(1)}, bf16[1,4,6,1024]{3,2,1,0:T(8,128)(2,1)S(1)}, u32[]{:S(2)}, u32[]{:S(2)}) collective-permute-start(bf16[1,4,6,1024]{3,2,1,0:T(8,128)(2,1)S(1)} %get-tuple-element.4), channel_id=1, source_target_pairs={{1,0},{3,2},{5,4},{7,6},{9,8},{11,10},{13,12},{15,14},{17,16},{19,... | collective-permute-start | bytes 147464 | tf_op jit(solution)/shard_map/ppermute | solution.py:25
  5.2 0.7 fusion.14.keep_wide_ref
  5.9 0.7 fusion.24.keep_half_ref
  6.6 0.0 collective-permute-done
  6.6 0.5 collective-permute-done.1
  7.0 3.7 %fusion.4.x_ref = bf16[1,4,272,1024]{3,2,1,0:T(8,128)(2,1)} fusion(bf16[1,4,6,1024]{3,2,1,0:T(8,128)(2,1)S(1)} %collective-permute-done.1, bf16[1,4,256,1024]{3,2,1,0:T(8,128)(2,1)} %param.7, bf16[1,4,6,1024]{3,2,1,0:T(8,128)(2,1)S(1)} %collective-permute-done), kind=kLoop, calls=%fused_computation.5 | loop fusion | flops 11141120 | bytes 4423680 | tf_op jit(solution)/shard_map/concatenate | solution.py:26
  10.7 13.2 %shard_map.94 = bf16[8,1,4,336,128]{4,3,2,1,0:T(8,128)(2,1)} custom-call(f32[2,4,7]{2,1,0:T(4,128)} %taps_ref.1, bf16[1,4,272,1024]{3,2,1,0:T(8,128)(2,1)} %fusion.4.x_ref, f32[280,1]{1,0:T(8,128)} %fusion.14.keep_wide_ref, f32[136,1]{1,0:T(8,128)} %fusion.24.keep_half_ref), custom_call_target="tpu_custom_call" | custom-call | tf_op jit(solution)/shard_map/pallas_call | solution.py:140
  23.9 0.0 copy-start.2
  23.9 0.0 copy-start.6
  23.9 0.0 copy-start.3
  23.9 0.0 copy-start.4
  23.9 0.0 copy-start.5
  23.9 6.8 %all-to-all-start = ((bf16[8,1,4,336,128]{4,3,2,1,0:T(8,128)(2,1)}), bf16[8,1,4,336,128]{4,3,2,1,0:T(8,128)(2,1)S(1)}, u32[]{:S(2)}, u32[]{:S(2)}) async-start(bf16[8,1,4,336,128]{4,3,2,1,0:T(8,128)(2,1)} %shard_map.94), calls=%async_computation | async-start | bytes 5505024 | tf_op jit(solution)/shard_map/all_to_all | solution.py:245
  30.8 0.0 copy-done.2
  30.8 0.0 copy-done.6
  30.8 0.2 convolution_divide_fusion
  31.0 0.0 copy-done.3
  31.0 0.0 copy-done.4
  31.0 0.0 copy-done.5
  31.0 0.4 fusion.5
  31.5 0.1 copy.25.c2_ref
  31.5 0.0 copy-start.1
  31.5 62.3 %all-to-all-done = bf16[8,1,4,336,128]{4,3,2,1,0:T(8,128)(2,1)S(1)} async-done(((bf16[8,1,4,336,128]{4,3,2,1,0:T(8,128)(2,1)}), bf16[8,1,4,336,128]{4,3,2,1,0:T(8,128)(2,1)S(1)}, u32[]{:S(2)}, u32[]{:S(2)}) %all-to-all-start) | async-done | bytes 2752544 | tf_op jit(solution)/shard_map/all_to_all | solution.py:245
  93.8 0.0 copy-start
  93.8 1.4 %broadcast_in_dim.4 = f32[8,8,8,4,8]{4,3,2,1,0:T(4,128)} broadcast(f32[8,8,8,8]{3,2,1,0:T(8,128)S(1)} %copy.25.c2_ref), dimensions={0,1,2,4} | broadcast | bytes 81920 | tf_op jit(solution)/shard_map/broadcast_in_dim | solution.py:221
  95.3 1.0 broadcast_in_dim.5
  96.3 0.0 copy-done.1
  96.3 0.0 copy-done
  96.3 16.8 %shard_map.95 = (bf16[8,4,32,1024]{3,2,1,0:T(8,128)(2,1)}, bf16[8,4,16,512]{3,2,1,0:T(8,128)(2,1)}, bf16[8,4,8,256]{3,2,1,0:T(8,128)(2,1)}) custom-call(bf16[8,4,336,128]{3,2,1,0:T(8,128)(2,1)} %bitcast.9, f32[8,8,32,8]{3,2,1,0:T(8,128)} %bitcast.10, f32[8,8,16,8]{3,2,1,0:T(8,128)} %bitcast.11, f32[8,8,8,8]{3,2,1,0:T(8,128)} %copy-done.1), custom_call_target="tpu_custom_call" | custom-call | tf_op jit(solution)/shard_map/pallas_call | solution.py:224
  (4 shorter events, 0.0 us)
Async XLA Ops:
  1.5 5.0 %collective-permute-start = (bf16[1,4,6,1024]{3,2,1,0:T(8,128)(2,1)S(1)}, bf16[1,4,6,1024]{3,2,1,0:T(8,128)(2,1)S(1)}, u32[]{:S(2)}, u32[]{:S(2)}) collective-permute-start(bf16[1,4,6,1024]{3,2,1,0:T(8,128)(2,1)S(1)} %get-tuple-element.3), channel_id=1, source_target_pairs={{0,1},{2,3},{4,5},{6,7},{8,9},{10,11},{12,13},{14,15},{16,17},{18,... | collective-permute-start | bytes 147464 | tf_op jit(solution)/shard_map/ppermute | solution.py:22
  3.9 3.1 %collective-permute-start.1 = (bf16[1,4,6,1024]{3,2,1,0:T(8,128)(2,1)S(1)}, bf16[1,4,6,1024]{3,2,1,0:T(8,128)(2,1)S(1)}, u32[]{:S(2)}, u32[]{:S(2)}) collective-permute-start(bf16[1,4,6,1024]{3,2,1,0:T(8,128)(2,1)S(1)} %get-tuple-element.4), channel_id=1, source_target_pairs={{1,0},{3,2},{5,4},{7,6},{9,8},{11,10},{13,12},{15,14},{17,16},{19,... | collective-permute-start | bytes 147464 | tf_op jit(solution)/shard_map/ppermute | solution.py:25
  23.9 6.8 %copy-start.2 = (s32[8,8,8]{2,1,0:T(8,128)S(1)}, s32[8,8,8]{2,1,0:T(8,128)}, u32[]{:S(2)}) copy-start(s32[8,8,8]{2,1,0:T(8,128)} %param.9) | copy-start | bytes 6148
  23.9 6.9 %copy-start.6 = (f32[8,8,1]{1,0,2:T(8,128)S(1)}, f32[8,8,1]{1,0,2:T(8,128)}, u32[]{:S(2)}) copy-start(f32[8,8,1]{1,0,2:T(8,128)} %constant.53) | copy-start | bytes 772
  23.9 7.1 %copy-start.3 = (f32[8,8]{0,1:T(8,128)S(1)}, f32[8,8]{0,1:T(8,128)}, u32[]{:S(2)}) copy-start(f32[8,8]{0,1:T(8,128)} %constant.50) | copy-start | bytes 772
  23.9 7.1 %copy-start.4 = (f32[8,8,1,1]{1,0,3,2:T(8,128)S(1)}, f32[8,8,1,1]{1,0,3,2:T(8,128)}, u32[]{:S(2)}) copy-start(f32[8,8,1,1]{1,0,3,2:T(8,128)} %constant.51) | copy-start | bytes 772
  23.9 7.1 %copy-start.5 = (f32[8,8]{0,1:T(8,128)S(1)}, f32[8,8]{0,1:T(8,128)}, u32[]{:S(2)}) copy-start(f32[8,8]{0,1:T(8,128)} %constant.52) | copy-start | bytes 772
  23.9 69.9 %all-to-all-start = ((bf16[8,1,4,336,128]{4,3,2,1,0:T(8,128)(2,1)}), bf16[8,1,4,336,128]{4,3,2,1,0:T(8,128)(2,1)S(1)}, u32[]{:S(2)}, u32[]{:S(2)}) async-start(bf16[8,1,4,336,128]{4,3,2,1,0:T(8,128)(2,1)} %shard_map.94), calls=%async_computation | async-start | bytes 5505024 | tf_op jit(solution)/shard_map/all_to_all | solution.py:245
  31.5 64.7 %copy-start.1 = (f32[8,8,8,8]{3,2,1,0:T(8,128)}, f32[8,8,8,8]{3,2,1,0:T(8,128)S(1)}, u32[]{:S(2)}) copy-start(f32[8,8,8,8]{3,2,1,0:T(8,128)S(1)} %copy.25.c2_ref) | copy-start | bytes 49156
  93.8 2.4 %copy-start = (bf16[8,1,4,336,128]{4,3,2,1,0:T(8,128)(2,1)}, bf16[8,1,4,336,128]{4,3,2,1,0:T(8,128)(2,1)S(1)}, u32[]{:S(2)}) copy-start(bf16[8,1,4,336,128]{4,3,2,1,0:T(8,128)(2,1)S(1)} %all-to-all-done) | copy-start | bytes 8257540

commit v8 on v7

--- a/solution.py
+++ b/solution.py
@@ -209,28 +209,39 @@
         lax.fori_loop(0, dates, one_date, 0)
 
 
-def smooth_kernel(pieces, got_ref, c0_ref, c1_ref, c2_ref, o0_ref, o1_ref, o2_ref, s0_ref, s1_ref, s2_ref):
+def smooth_kernel(pieces, got_ref, c0_ref, c1_ref, c2_ref, *rest):
+    o0_ref, o1_ref, o2_ref, s0_ref, s1_ref, s2_ref = rest[-6:]
     start = 0
     for piece, c_ref, o_ref, s_ref in zip(pieces, (c0_ref, c1_ref, c2_ref), (o0_ref, o1_ref, o2_ref), (s0_ref, s1_ref, s2_ref)):
         smooth_level(got_ref, start, piece, c_ref, o_ref, s_ref)
         start += (o_ref.shape[3] // 128) * piece
 
 
-def smooth_all(got, coeff, shapes, pieces):
+def smooth_all(got, grown, shapes, pieces, chunk, previous):
     dates, bands = got.shape[:2]
-    grown = [jnp.repeat(coeff, shape[2] // coeff.shape[2], axis=2) for shape in shapes]
-    full = lambda a: pl.BlockSpec(a.shape, lambda: (0,) * len(a.shape))
+    full = lambda a: pl.BlockSpec(a.shape, lambda i: (0,) * len(a.shape))
     outs = [jax.ShapeDtypeStruct(shape, jnp.bfloat16) for shape in shapes]
+    out_specs = [pl.BlockSpec((dates, bands) + shape[2:], lambda i: (0, chunk, 0, 0)) for shape in shapes]
+    in_specs = [full(got)] + [full(g) for g in grown]
+    args = [got] + list(grown)
+    aliases = {}
+    if previous is not None:
+        for i, prev in enumerate(previous):
+            aliases[len(args)] = i
+            in_specs.append(pl.BlockSpec(memory_space=pl.ANY))
+            args.append(prev)
     return pl.pallas_call(
         functools.partial(smooth_kernel, pieces),
-        in_specs=[full(got)] + [full(g) for g in grown],
-        out_specs=[full(o) for o in outs],
+        grid=(1,),
+        in_specs=in_specs,
+        out_specs=out_specs,
         out_shape=outs,
+        input_output_aliases=aliases,
         scratch_shapes=[
             pltpu.VMEM((dates, bands, (shape[3] // 128) * piece, 128), jnp.float32)
             for shape, piece in zip(shapes, pieces)
         ],
-    )(got, *grown)
+    )(*args)
 
 
 def local(scenes, resample_taps, clear_mask):
@@ -240,10 +251,7 @@
     ndate = lax.axis_size("date")
     extended = padded(scenes, (("row", 2),), 6)
     extended = jnp.pad(extended, ((0, 0), (0, 0), (0, 4), (0, 0)))
-    packed = pyramid(extended, resample_taps, band_index, total_rows, ndate)
     coeff = smooth_coefficients(clear_mask.astype(jnp.float32))
-    got = lax.all_to_all(packed, "date", split_axis=0, concat_axis=0, tiled=True)
-    got = got.reshape((ndate * dates,) + got.shape[2:])
     fine = rows // ndate
     total = ndate * dates
     shapes = (
@@ -251,7 +259,17 @@
         (total, bands, fine // 2, width // 2),
         (total, bands, fine // 4, width // 4),
     )
-    return tuple(smooth_all(got, coeff, shapes, piece_rows(rows, ndate)))
+    grown = [jnp.repeat(coeff, shape[2] // coeff.shape[2], axis=2) for shape in shapes]
+    chunks = 2 if bands % 2 == 0 else 1
+    step = bands // chunks
+    outs = None
+    for chunk in range(chunks):
+        part = slice(chunk * step, (chunk + 1) * step)
+        packed = pyramid(extended[:, part], resample_taps[:, part], band_index, total_rows, ndate)
+        got = lax.all_to_all(packed, "date", split_axis=0, concat_axis=0, tiled=True)
+        got = got.reshape((total,) + got.shape[2:])
+        outs = smooth_all(got, grown, shapes, piece_rows(rows, ndate), chunk, outs)
+    return tuple(outs)
 
 
 def solution(mesh):

time: 113 us -> 114 us (level)
  waiting for transfers between devices: 62.8 us -> 41.3 us
  Pallas kernels: 30 us -> 46.3 us
  local copies, waits for them, and re-layouts: 3.41 us -> 7.25 us
  starting transfers between devices: 10.5 us -> 13.9 us
  other arithmetic: 5.02 us -> 3.62 us
    all_to_all x1 -> x2, waiting for transfers between devices: 62.3 us -> 41.3 us  [local(): lax.all_to_all(packed, 'date', split_axis=0, concat_axis=0, tiled=True)]
    pallas_call x1 -> x2, Pallas kernels: 16.8 us -> 31.1 us  [smooth_all(): pl.pallas_call(functools.partial(smooth_kernel, pieces), grid=(1,), in_sp...]
    all_to_all x1 -> x2, starting transfers between devices: 6.8 us -> 10.2 us  [local(): lax.all_to_all(packed, 'date', split_axis=0, concat_axis=0, tiled=True)]
    slice x0 -> x2, local copies, waits for them, and re-layouts: none -> 2.93 us  [the longest x1 1.55 us: local(): extended[:, part]]
    pallas_call x1 -> x2, Pallas kernels: 13.2 us -> 15.1 us  [pyramid(): pl.pallas_call(functools.partial(pyramid_kernel, ndate), grid=(dates, ban...]
    concatenate x1, other arithmetic: 3.65 us -> 2.25 us  [padded(): block = jnp.concatenate([low, block, high], axis=dim)]
  transfers between devices with their start and end apart: 3 -> 4, of which waited for: 2 -> 2; matrix products, arithmetic and copies ran while one was open for 2% -> 5% of each run, Pallas kernels for 0% -> 20%
where the time goes in v8:
time: 114 us
  Pallas kernels  46.3 us (41%)
  waiting for transfers between devices  41.3 us (36%)
  starting transfers between devices  13.9 us (12%)
  local copies, waits for them, and re-layouts  7.25 us (6%)
  other arithmetic  3.62 us (3%)
    all_to_all x2, waiting for transfers between devices, local(): lax.all_to_all(packed, 'date', split_axis=0, concat_axis=0, tiled=True)  41.3 us
    pallas_call x2, Pallas kernels, smooth_all(): pl.pallas_call(functools.partial(smooth_kernel, pieces), grid=(1,), in_sp...  31.1 us
    pallas_call x2, Pallas kernels, pyramid(): pl.pallas_call(functools.partial(pyramid_kernel, ndate), grid=(dates, ban...  15.1 us
    all_to_all x2, starting transfers between devices, local(): lax.all_to_all(packed, 'date', split_axis=0, concat_axis=0, tiled=True)  10.2 us
    ppermute x1, starting transfers between devices, padded(): lax.ppermute(lax.slice_in_dim(block, block.shape[dim] - width, None, axis...  2.36 us
  transfers between devices with their start and end apart: 4, of which 2 were waited for; matrix products, arithmetic and copies ran while one was open for 5% of the time, Pallas kernels for 20%

profile of v8, /device:TPU:0, one launch (start us, length us, event | category | flops | bytes accessed | tf_op | source)
XLA Modules:
  0.0 113.7 jit_solution(15652102697929923345)
XLA Ops:
  0.6 0.9 fusion.28
  1.5 2.4 %collective-permute-start = (bf16[1,4,6,1024]{3,2,1,0:T(8,128)(2,1)S(1)}, bf16[1,4,6,1024]{3,2,1,0:T(8,128)(2,1)S(1)}, u32[]{:S(2)}, u32[]{:S(2)}) collective-permute-start(bf16[1,4,6,1024]{3,2,1,0:T(8,128)(2,1)S(1)} %get-tuple-element.11), channel_id=1, source_target_pairs={{0,1},{2,3},{4,5},{6,7},{8,9},{10,11},{12,13},{14,15},{16,17},{18,... | collective-permute-start | bytes 147464 | tf_op jit(solution)/shard_map/ppermute | solution.py:22
  3.9 1.3 %collective-permute-start.1 = (bf16[1,4,6,1024]{3,2,1,0:T(8,128)(2,1)S(1)}, bf16[1,4,6,1024]{3,2,1,0:T(8,128)(2,1)S(1)}, u32[]{:S(2)}, u32[]{:S(2)}) collective-permute-start(bf16[1,4,6,1024]{3,2,1,0:T(8,128)(2,1)S(1)} %get-tuple-element.12), channel_id=1, source_target_pairs={{1,0},{3,2},{5,4},{7,6},{9,8},{11,10},{13,12},{15,14},{17,16},{19,... | collective-permute-start | bytes 147464 | tf_op jit(solution)/shard_map/ppermute | solution.py:25
  5.2 1.4 %fusion.29 = (f32[2,2,7]{2,1,0:T(2,128)}, f32[2,2,7]{2,1,0:T(2,128)}) fusion(f32[2,4,7]{2,1,0:T(4,128)} %param.8), kind=kLoop, calls=%fused_computation.37 | loop fusion | bytes 448 | tf_op jit(solution)/shard_map/slice | solution.py:268
  6.6 0.7 fusion.14.keep_wide_ref
  7.3 0.7 fusion.24.keep_half_ref
  7.9 0.0 collective-permute-done
  7.9 0.0 collective-permute-done.1
  7.9 2.3 %fusion.4 = bf16[1,4,272,1024]{3,2,1,0:T(8,128)(2,1)S(1)} fusion(bf16[1,4,6,1024]{3,2,1,0:T(8,128)(2,1)S(1)} %collective-permute-done.1, bf16[1,4,256,1024]{3,2,1,0:T(8,128)(2,1)} %param.7, bf16[1,4,6,1024]{3,2,1,0:T(8,128)(2,1)S(1)} %collective-permute-done), kind=kLoop, calls=%fused_computation.5 | loop fusion | flops 11141120 | bytes 4423680 | tf_op jit(solution)/shard_map/concatenate | solution.py:26
  10.2 1.6 %fusion.27 = (bf16[1,2,272,1024]{3,2,1,0:T(8,128)(2,1)}, bf16[1,2,272,1024]{3,2,1,0:T(8,128)(2,1)}) fusion(bf16[1,4,272,1024]{3,2,1,0:T(8,128)(2,1)S(1)} %fusion.4), kind=kLoop, calls=%fused_computation.35 | loop fusion | bytes 4456448 | tf_op jit(solution)/shard_map/slice | solution.py:268
  11.7 7.6 %shard_map.95 = bf16[8,1,2,336,128]{4,3,2,1,0:T(8,128)(2,1)} custom-call(f32[2,2,7]{2,1,0:T(2,128)} %get-tuple-element.13.taps_ref, bf16[1,2,272,1024]{3,2,1,0:T(8,128)(2,1)} %get-tuple-element.9.x_ref, f32[280,1]{1,0:T(8,128)} %fusion.14.keep_wide_ref, f32[136,1]{1,0:T(8,128)} %fusion.24.keep_half_ref), custom_call_target="tpu_custom_call" | custom-call | tf_op jit(solution)/shard_map/pallas_call | solution.py:140
  19.3 6.7 %all-to-all-start.1 = ((bf16[8,1,2,336,128]{4,3,2,1,0:T(8,128)(2,1)}), bf16[8,1,2,336,128]{4,3,2,1,0:T(8,128)(2,1)S(1)}, u32[]{:S(2)}, u32[]{:S(2)}) async-start(bf16[8,1,2,336,128]{4,3,2,1,0:T(8,128)(2,1)} %shard_map.95), calls=%async_computation.1 | async-start | bytes 2752512 | tf_op jit(solution)/shard_map/all_to_all | solution.py:269
  26.0 0.0 copy-start.7
  26.0 7.6 %shard_map.94 = bf16[8,1,2,336,128]{4,3,2,1,0:T(8,128)(2,1)} custom-call(f32[2,2,7]{2,1,0:T(2,128)} %get-tuple-element.14.taps_ref, bf16[1,2,272,1024]{3,2,1,0:T(8,128)(2,1)} %get-tuple-element.10.x_ref, f32[280,1]{1,0:T(8,128)} %fusion.14.keep_wide_ref, f32[136,1]{1,0:T(8,128)} %fusion.24.keep_half_ref), custom_call_target="tpu_custom_call" | custom-call | tf_op jit(solution)/shard_map/pallas_call | solution.py:140
  33.6 26.7 %all-to-all-done.1 = bf16[8,1,2,336,128]{4,3,2,1,0:T(8,128)(2,1)S(1)} async-done(((bf16[8,1,2,336,128]{4,3,2,1,0:T(8,128)(2,1)}), bf16[8,1,2,336,128]{4,3,2,1,0:T(8,128)(2,1)S(1)}, u32[]{:S(2)}, u32[]{:S(2)}) %all-to-all-start.1) | async-done | bytes 1376288 | tf_op jit(solution)/shard_map/all_to_all | solution.py:269
  60.3 3.6 %all-to-all-start = ((bf16[8,1,2,336,128]{4,3,2,1,0:T(8,128)(2,1)}), bf16[8,1,2,336,128]{4,3,2,1,0:T(8,128)(2,1)S(1)}, u32[]{:S(2)}, u32[]{:S(2)}) async-start(bf16[8,1,2,336,128]{4,3,2,1,0:T(8,128)(2,1)} %shard_map.94), calls=%async_computation | async-start | bytes 2752512 | tf_op jit(solution)/shard_map/all_to_all | solution.py:269
  63.9 0.0 copy-done.3
  64.0 0.0 copy-done.7
  64.0 0.2 convolution_divide_fusion
  64.1 0.0 copy-done.4
  64.2 0.0 copy-done.5
  64.2 0.0 copy-done.6
  64.2 0.4 fusion.5
  64.6 0.1 copy.31.c2_ref
  64.7 0.0 copy-start
  64.7 1.0 broadcast_in_dim.5
  65.6 0.0 copy-done.1
  65.6 1.3 %broadcast_in_dim.4 = f32[8,8,8,4,8]{4,3,2,1,0:T(4,128)} broadcast(f32[8,8,8,8]{3,2,1,0:T(8,128)S(1)} %copy.31.c2_ref), dimensions={0,1,2,4} | broadcast | bytes 81920 | tf_op jit(solution)/shard_map/broadcast_in_dim | solution.py:262
  66.9 15.6 %shard_map.96 = (bf16[8,4,32,1024]{3,2,1,0:T(8,128)(2,1)}, bf16[8,4,16,512]{3,2,1,0:T(8,128)(2,1)}, bf16[8,4,8,256]{3,2,1,0:T(8,128)(2,1)}) custom-call(bf16[8,2,336,128]{3,2,1,0:T(8,128)(2,1)} %bitcast.12, f32[8,8,32,8]{3,2,1,0:T(8,128)} %bitcast.10, f32[8,8,16,8]{3,2,1,0:T(8,128)} %bitcast.14, f32[8,8,8,8]{3,2,1,0:T(8,128)} %copy-done), custom_call_target="tpu_custom_call" | custom-call | tf_op jit(solution)/shard_map/pallas_call | solution.py:233
  82.5 14.5 %all-to-all-done = bf16[8,1,2,336,128]{4,3,2,1,0:T(8,128)(2,1)S(1)} async-done(((bf16[8,1,2,336,128]{4,3,2,1,0:T(8,128)(2,1)}), bf16[8,1,2,336,128]{4,3,2,1,0:T(8,128)(2,1)S(1)}, u32[]{:S(2)}, u32[]{:S(2)}) %all-to-all-start) | async-done | bytes 1376288 | tf_op jit(solution)/shard_map/all_to_all | solution.py:269
  97.0 1.1 copy-done.2
  98.1 15.6 %shard_map.97 = (bf16[8,4,32,1024]{3,2,1,0:T(8,128)(2,1)}, bf16[8,4,16,512]{3,2,1,0:T(8,128)(2,1)}, bf16[8,4,8,256]{3,2,1,0:T(8,128)(2,1)}) custom-call(bf16[8,2,336,128]{3,2,1,0:T(8,128)(2,1)} %bitcast.13, f32[8,8,32,8]{3,2,1,0:T(8,128)} %bitcast.11, f32[8,8,16,8]{3,2,1,0:T(8,128)} %bitcast.15, ...), custom_call_target="tpu_custom_call", output_to_operand_aliasing={{0}: (4, {}), {1}: (5, {}), {2}: (6, {})} | custom-call | tf_op jit(solution)/shard_map/pallas_call | solution.py:233
  (11 shorter events, 0.1 us)
Async XLA Ops:
  1.5 6.4 %collective-permute-start = (bf16[1,4,6,1024]{3,2,1,0:T(8,128)(2,1)S(1)}, bf16[1,4,6,1024]{3,2,1,0:T(8,128)(2,1)S(1)}, u32[]{:S(2)}, u32[]{:S(2)}) collective-permute-start(bf16[1,4,6,1024]{3,2,1,0:T(8,128)(2,1)S(1)} %get-tuple-element.11), channel_id=1, source_target_pairs={{0,1},{2,3},{4,5},{6,7},{8,9},{10,11},{12,13},{14,15},{16,17},{18,... | collective-permute-start | bytes 147464 | tf_op jit(solution)/shard_map/ppermute | solution.py:22
  3.9 4.0 %collective-permute-start.1 = (bf16[1,4,6,1024]{3,2,1,0:T(8,128)(2,1)S(1)}, bf16[1,4,6,1024]{3,2,1,0:T(8,128)(2,1)S(1)}, u32[]{:S(2)}, u32[]{:S(2)}) collective-permute-start(bf16[1,4,6,1024]{3,2,1,0:T(8,128)(2,1)S(1)} %get-tuple-element.12), channel_id=1, source_target_pairs={{1,0},{3,2},{5,4},{7,6},{9,8},{11,10},{13,12},{15,14},{17,16},{19,... | collective-permute-start | bytes 147464 | tf_op jit(solution)/shard_map/ppermute | solution.py:25
  19.3 41.0 %all-to-all-start.1 = ((bf16[8,1,2,336,128]{4,3,2,1,0:T(8,128)(2,1)}), bf16[8,1,2,336,128]{4,3,2,1,0:T(8,128)(2,1)S(1)}, u32[]{:S(2)}, u32[]{:S(2)}) async-start(bf16[8,1,2,336,128]{4,3,2,1,0:T(8,128)(2,1)} %shard_map.95), calls=%async_computation.1 | async-start | bytes 2752512 | tf_op jit(solution)/shard_map/all_to_all | solution.py:269
  26.0 37.9 %copy-start.3 = (s32[8,8,8]{2,1,0:T(8,128)S(1)}, s32[8,8,8]{2,1,0:T(8,128)}, u32[]{:S(2)}) copy-start(s32[8,8,8]{2,1,0:T(8,128)} %param.9) | copy-start | bytes 6148
  26.0 38.0 %copy-start.7 = (f32[8,8,1]{1,0,2:T(8,128)S(1)}, f32[8,8,1]{1,0,2:T(8,128)}, u32[]{:S(2)}) copy-start(f32[8,8,1]{1,0,2:T(8,128)} %constant.53) | copy-start | bytes 772
  33.6 30.6 %copy-start.4 = (f32[8,8]{0,1:T(8,128)S(1)}, f32[8,8]{0,1:T(8,128)}, u32[]{:S(2)}) copy-start(f32[8,8]{0,1:T(8,128)} %constant.52) | copy-start | bytes 772
  33.6 30.6 %copy-start.5 = (f32[8,8,1,1]{1,0,3,2:T(8,128)S(1)}, f32[8,8,1,1]{1,0,3,2:T(8,128)}, u32[]{:S(2)}) copy-start(f32[8,8,1,1]{1,0,3,2:T(8,128)} %constant.51) | copy-start | bytes 772
  33.6 30.6 %copy-start.6 = (f32[8,8]{0,1:T(8,128)S(1)}, f32[8,8]{0,1:T(8,128)}, u32[]{:S(2)}) copy-start(f32[8,8]{0,1:T(8,128)} %constant.50) | copy-start | bytes 772
  60.3 5.3 %copy-start.1 = (bf16[8,1,2,336,128]{4,3,2,1,0:T(8,128)(2,1)}, bf16[8,1,2,336,128]{4,3,2,1,0:T(8,128)(2,1)S(1)}, u32[]{:S(2)}) copy-start(bf16[8,1,2,336,128]{4,3,2,1,0:T(8,128)(2,1)S(1)} %all-to-all-done.1) | copy-start | bytes 4128772
  60.3 36.7 %all-to-all-start = ((bf16[8,1,2,336,128]{4,3,2,1,0:T(8,128)(2,1)}), bf16[8,1,2,336,128]{4,3,2,1,0:T(8,128)(2,1)S(1)}, u32[]{:S(2)}, u32[]{:S(2)}) async-start(bf16[8,1,2,336,128]{4,3,2,1,0:T(8,128)(2,1)} %shard_map.94), calls=%async_computation | async-start | bytes 2752512 | tf_op jit(solution)/shard_map/all_to_all | solution.py:269
  64.7 2.3 %copy-start = (f32[8,8,8,8]{3,2,1,0:T(8,128)}, f32[8,8,8,8]{3,2,1,0:T(8,128)S(1)}, u32[]{:S(2)}) copy-start(f32[8,8,8,8]{3,2,1,0:T(8,128)S(1)} %copy.31.c2_ref) | copy-start | bytes 49156
  97.0 1.1 copy-start.2

commit v9 on v7

--- a/solution.py
+++ b/solution.py
@@ -180,57 +180,55 @@
     return jnp.einsum("ts,suxy->tuxy", clamp, fill, precision=hi)
 
 
-def smooth_level(got_ref, start, piece, coeff_ref, out_ref, section_ref):
-    dates, bands, rows, width = out_ref.shape
-    tiles = width // 128
-    mask_cols = coeff_ref.shape[3]
-    span = width // mask_cols
-    per_tile = 128 // span
-    lane_group = lax.broadcasted_iota(jnp.int32, (rows, 128), 1) // span
-    section_ref[...] = got_ref[:, :, start : start + tiles * piece, :].astype(jnp.float32)
-    for j in range(tiles):
-
-        def one_date(t, carry):
-            coeffs = []
-            for u in range(dates):
-                c = coeff_ref[t, u]
-                tile = jnp.broadcast_to(c[:, per_tile * j : per_tile * j + 1], (rows, 128))
-                for g in range(1, per_tile):
-                    m = per_tile * j + g
-                    tile = jnp.where(lane_group == g, jnp.broadcast_to(c[:, m : m + 1], (rows, 128)), tile)
-                coeffs.append(tile)
+def smooth_kernel(got_ref, coeff_ref, *rest):
+    out_ref = rest[-1]
+    dates, bands, rows = out_ref.shape[:3]
+
+    def one_date(t, carry):
+        accs = [None] * bands
+        for u in range(dates):
+            c = coeff_ref[t, u]
             for band in range(bands):
-                acc = coeffs[0] * section_ref[0, band, j * piece : j * piece + rows, :]
-                for u in range(1, dates):
-                    acc = acc + coeffs[u] * section_ref[u, band, j * piece : j * piece + rows, :]
-                out_ref[t, band, :, 128 * j : 128 * (j + 1)] = acc.astype(out_ref.dtype)
-            return carry
-
-        lax.fori_loop(0, dates, one_date, 0)
-
-
-def smooth_kernel(pieces, got_ref, c0_ref, c1_ref, c2_ref, o0_ref, o1_ref, o2_ref, s0_ref, s1_ref, s2_ref):
-    start = 0
-    for piece, c_ref, o_ref, s_ref in zip(pieces, (c0_ref, c1_ref, c2_ref), (o0_ref, o1_ref, o2_ref), (s0_ref, s1_ref, s2_ref)):
-        smooth_level(got_ref, start, piece, c_ref, o_ref, s_ref)
-        start += (o_ref.shape[3] // 128) * piece
-
-
-def smooth_all(got, coeff, shapes, pieces):
+                term = c * got_ref[u, band, 0:rows, :].astype(jnp.float32)
+                accs[band] = term if accs[band] is None else accs[band] + term
+        for band in range(bands):
+            out_ref[t, band] = accs[band].astype(out_ref.dtype)
+        return carry
+
+    lax.fori_loop(0, dates, one_date, 0)
+
+
+def smooth_level(got, grown, shape, piece, first, chunk, previous):
     dates, bands = got.shape[:2]
-    grown = [jnp.repeat(coeff, shape[2] // coeff.shape[2], axis=2) for shape in shapes]
-    full = lambda a: pl.BlockSpec(a.shape, lambda: (0,) * len(a.shape))
-    outs = [jax.ShapeDtypeStruct(shape, jnp.bfloat16) for shape in shapes]
+    rows = shape[2]
+    tiles = shape[3] // 128
+    in_specs = [
+        pl.BlockSpec((dates, bands, piece, 128), lambda j: (0, 0, first + j, 0)),
+        pl.BlockSpec((dates, dates, rows, 128), lambda j: (0, 0, 0, j)),
+    ]
+    args = [got, grown]
+    aliases = {}
+    if previous is not None:
+        aliases[2] = 0
+        in_specs.append(pl.BlockSpec(memory_space=pl.ANY))
+        args.append(previous)
     return pl.pallas_call(
-        functools.partial(smooth_kernel, pieces),
-        in_specs=[full(got)] + [full(g) for g in grown],
-        out_specs=[full(o) for o in outs],
-        out_shape=outs,
-        scratch_shapes=[
-            pltpu.VMEM((dates, bands, (shape[3] // 128) * piece, 128), jnp.float32)
-            for shape, piece in zip(shapes, pieces)
-        ],
-    )(got, *grown)
+        smooth_kernel,
+        grid=(tiles,),
+        in_specs=in_specs,
+        out_specs=pl.BlockSpec((dates, bands, rows, 128), lambda j: (0, chunk, 0, j)),
+        out_shape=jax.ShapeDtypeStruct(shape, jnp.bfloat16),
+        input_output_aliases=aliases,
+    )(*args)
+
+
+def expand(coeff, rows, width):
+    dates, _, mask_rows, mask_cols = coeff.shape
+    grown = jnp.broadcast_to(
+        coeff[:, :, :, None, :, None],
+        (dates, dates, mask_rows, rows // mask_rows, mask_cols, width // mask_cols),
+    )
+    return grown.reshape(dates, dates, rows, width)
 
 
 def local(scenes, resample_taps, clear_mask):
@@ -240,10 +238,7 @@
     ndate = lax.axis_size("date")
     extended = padded(scenes, (("row", 2),), 6)
     extended = jnp.pad(extended, ((0, 0), (0, 0), (0, 4), (0, 0)))
-    packed = pyramid(extended, resample_taps, band_index, total_rows, ndate)
     coeff = smooth_coefficients(clear_mask.astype(jnp.float32))
-    got = lax.all_to_all(packed, "date", split_axis=0, concat_axis=0, tiled=True)
-    got = got.reshape((ndate * dates,) + got.shape[2:])
     fine = rows // ndate
     total = ndate * dates
     shapes = (
@@ -251,7 +246,26 @@
         (total, bands, fine // 2, width // 2),
         (total, bands, fine // 4, width // 4),
     )
-    return tuple(smooth_all(got, coeff, shapes, piece_rows(rows, ndate)))
+    grown = [expand(coeff, shape[2], shape[3]) for shape in shapes]
+    pieces = piece_rows(rows, ndate)
+    firsts = []
+    start = 0
+    for shape, piece in zip(shapes, pieces):
+        firsts.append(start // piece)
+        start += (shape[3] // 128) * piece
+    chunks = 2 if bands % 2 == 0 else 1
+    step = bands // chunks
+    outs = [None, None, None]
+    for chunk in range(chunks):
+        part = slice(chunk * step, (chunk + 1) * step)
+        packed = pyramid(extended[:, part], resample_taps[:, part], band_index, total_rows, ndate)
+        got = lax.all_to_all(packed, "date", split_axis=0, concat_axis=0, tiled=True)
+        got = got.reshape((total,) + got.shape[2:])
+        outs = [
+            smooth_level(got, g, shape, piece, first, chunk, prev)
+            for g, shape, piece, first, prev in zip(grown, shapes, pieces, firsts, outs)
+        ]
+    return tuple(outs)
 
 
 def solution(mesh):

time: 113 us -> 117 us (1.035); the launches traced: 113 us -> 116 us
  waiting for transfers between devices: 62.8 us -> 26.7 us
  local copies, waits for them, and re-layouts: 3.41 us -> 28.3 us
  Pallas kernels: 30 us -> 41.8 us
  starting transfers between devices: 10.5 us -> 13.9 us
  other arithmetic: 5.02 us -> 3.6 us
    all_to_all x1 -> x2, waiting for transfers between devices: 62.3 us -> 26.7 us  [local(): lax.all_to_all(packed, 'date', split_axis=0, concat_axis=0, tiled=True)]
    reshape x0 -> x2, local copies, waits for them, and re-layouts: none -> 14.1 us  [expand(): return grown.reshape(dates, dates, rows, width)]
    pallas_call x1 -> x6, Pallas kernels: 16.8 us -> 26.7 us  [smooth_level(): pl.pallas_call(smooth_kernel, grid=(tiles,), in_specs=in_specs, out_specs...]
    broadcast_in_dim x2 -> x4, local copies, waits for them, and re-layouts: 2.41 us -> 9.2 us  [expand(): jnp.broadcast_to(coeff[:, :, :, None, :, None], (dates, dates, mask_rows,...]
    all_to_all x1 -> x2, starting transfers between devices: 6.8 us -> 10.2 us  [local(): lax.all_to_all(packed, 'date', split_axis=0, concat_axis=0, tiled=True)]
    slice x0 -> x2, local copies, waits for them, and re-layouts: none -> 2.96 us  [the longest x1 1.6 us: local(): extended[:, part]]
    pallas_call x1 -> x2, Pallas kernels: 13.2 us -> 15.1 us  [pyramid(): pl.pallas_call(functools.partial(pyramid_kernel, ndate), grid=(dates, ban...]
    concatenate x1, other arithmetic: 3.65 us -> 2.23 us  [padded(): block = jnp.concatenate([low, block, high], axis=dim)]
  transfers between devices with their start and end apart: 3 -> 4, of which waited for: 2 -> 1; matrix products, arithmetic and copies ran while one was open for 2% -> 23% of each run, Pallas kernels for 0% -> 17%
where the time goes in v9:
time: 117 us; the launch traced here: 116 us
  Pallas kernels  41.8 us (36%)
  local copies, waits for them, and re-layouts  28.3 us (24%)
  waiting for transfers between devices  26.7 us (23%)
  starting transfers between devices  13.9 us (12%)
  other arithmetic  3.6 us (3%)
    all_to_all x2, waiting for transfers between devices, local(): lax.all_to_all(packed, 'date', split_axis=0, concat_axis=0, tiled=True)  26.7 us
    pallas_call x6, Pallas kernels, smooth_level(): pl.pallas_call(smooth_kernel, grid=(tiles,), in_specs=in_specs, out_specs...  26.7 us
    pallas_call x2, Pallas kernels, pyramid(): pl.pallas_call(functools.partial(pyramid_kernel, ndate), grid=(dates, ban...  15.1 us
    reshape x2, local copies, waits for them, and re-layouts, expand(): return grown.reshape(dates, dates, rows, width)  14.1 us
    all_to_all x2, starting transfers between devices, local(): lax.all_to_all(packed, 'date', split_axis=0, concat_axis=0, tiled=True)  10.2 us
    broadcast_in_dim x4, local copies, waits for them, and re-layouts, expand(): jnp.broadcast_to(coeff[:, :, :, None, :, None], (dates, dates, mask_rows,...  9.2 us
    ppermute x1, starting transfers between devices, padded(): lax.ppermute(lax.slice_in_dim(block, block.shape[dim] - width, None, axis...  2.36 us
  transfers between devices with their start and end apart: 4, of which 1 were waited for; matrix products, arithmetic and copies ran while one was open for 23% of the time, Pallas kernels for 17%

profile of v9, /device:TPU:0, one launch (start us, length us, event | category | flops | bytes accessed | tf_op | source)
XLA Modules:
  0.0 115.8 jit_solution(4021910534337613061)
XLA Ops:
  0.6 0.9 fusion.28
  1.5 2.4 %collective-permute-start = (bf16[1,4,6,1024]{3,2,1,0:T(8,128)(2,1)S(1)}, bf16[1,4,6,1024]{3,2,1,0:T(8,128)(2,1)S(1)}, u32[]{:S(2)}, u32[]{:S(2)}) collective-permute-start(bf16[1,4,6,1024]{3,2,1,0:T(8,128)(2,1)S(1)} %get-tuple-element.5), channel_id=1, source_target_pairs={{0,1},{2,3},{4,5},{6,7},{8,9},{10,11},{12,13},{14,15},{16,17},{18,... | collective-permute-start | bytes 147464 | tf_op jit(solution)/shard_map/ppermute | solution.py:22
  3.9 1.3 %collective-permute-start.1 = (bf16[1,4,6,1024]{3,2,1,0:T(8,128)(2,1)S(1)}, bf16[1,4,6,1024]{3,2,1,0:T(8,128)(2,1)S(1)}, u32[]{:S(2)}, u32[]{:S(2)}) collective-permute-start(bf16[1,4,6,1024]{3,2,1,0:T(8,128)(2,1)S(1)} %get-tuple-element.6), channel_id=1, source_target_pairs={{1,0},{3,2},{5,4},{7,6},{9,8},{11,10},{13,12},{15,14},{17,16},{19,... | collective-permute-start | bytes 147464 | tf_op jit(solution)/shard_map/ppermute | solution.py:25
  5.2 0.7 fusion.14.keep_wide_ref
  5.9 1.4 %fusion.29 = (f32[2,2,7]{2,1,0:T(2,128)}, f32[2,2,7]{2,1,0:T(2,128)}) fusion(f32[2,4,7]{2,1,0:T(4,128)} %param.8), kind=kLoop, calls=%fused_computation.37 | loop fusion | bytes 448 | tf_op jit(solution)/shard_map/slice | solution.py:261
  7.3 0.7 fusion.24.keep_half_ref
  7.9 0.0 collective-permute-done
  7.9 2.2 %fusion.4 = bf16[1,4,272,1024]{3,2,1,0:T(8,128)(2,1)S(1)} fusion(bf16[1,4,6,1024]{3,2,1,0:T(8,128)(2,1)S(1)} %collective-permute-done.1, bf16[1,4,256,1024]{3,2,1,0:T(8,128)(2,1)} %param.7, bf16[1,4,6,1024]{3,2,1,0:T(8,128)(2,1)S(1)} %collective-permute-done), kind=kLoop, calls=%fused_computation.5 | loop fusion | flops 11141120 | bytes 4423680 | tf_op jit(solution)/shard_map/concatenate | solution.py:26
  10.2 1.6 %fusion.27 = (bf16[1,2,272,1024]{3,2,1,0:T(8,128)(2,1)}, bf16[1,2,272,1024]{3,2,1,0:T(8,128)(2,1)}) fusion(bf16[1,4,272,1024]{3,2,1,0:T(8,128)(2,1)S(1)} %fusion.4), kind=kLoop, calls=%fused_computation.35 | loop fusion | bytes 4456448 | tf_op jit(solution)/shard_map/slice | solution.py:261
  11.8 7.5 %shard_map.95 = bf16[8,1,2,336,128]{4,3,2,1,0:T(8,128)(2,1)} custom-call(f32[2,2,7]{2,1,0:T(2,128)} %get-tuple-element.7.taps_ref, bf16[1,2,272,1024]{3,2,1,0:T(8,128)(2,1)} %get-tuple-element.3.x_ref, f32[280,1]{1,0:T(8,128)} %fusion.14.keep_wide_ref, f32[136,1]{1,0:T(8,128)} %fusion.24.keep_half_ref), custom_call_target="tpu_custom_call" | custom-call | tf_op jit(solution)/shard_map/pallas_call | solution.py:140
  19.3 6.7 %all-to-all-start.1 = ((bf16[8,1,2,336,128]{4,3,2,1,0:T(8,128)(2,1)}), bf16[8,1,2,336,128]{4,3,2,1,0:T(8,128)(2,1)S(1)}, u32[]{:S(2)}, u32[]{:S(2)}) async-start(bf16[8,1,2,336,128]{4,3,2,1,0:T(8,128)(2,1)} %shard_map.95), calls=%async_computation.1 | async-start | bytes 2752512 | tf_op jit(solution)/shard_map/all_to_all | solution.py:262
  26.0 0.0 copy-start.7
  26.0 7.6 %shard_map.94 = bf16[8,1,2,336,128]{4,3,2,1,0:T(8,128)(2,1)} custom-call(f32[2,2,7]{2,1,0:T(2,128)} %get-tuple-element.8.taps_ref, bf16[1,2,272,1024]{3,2,1,0:T(8,128)(2,1)} %get-tuple-element.4.x_ref, f32[280,1]{1,0:T(8,128)} %fusion.14.keep_wide_ref, f32[136,1]{1,0:T(8,128)} %fusion.24.keep_half_ref), custom_call_target="tpu_custom_call" | custom-call | tf_op jit(solution)/shard_map/pallas_call | solution.py:140
  33.6 26.7 %all-to-all-done.1 = bf16[8,1,2,336,128]{4,3,2,1,0:T(8,128)(2,1)S(1)} async-done(((bf16[8,1,2,336,128]{4,3,2,1,0:T(8,128)(2,1)}), bf16[8,1,2,336,128]{4,3,2,1,0:T(8,128)(2,1)S(1)}, u32[]{:S(2)}, u32[]{:S(2)}) %all-to-all-start.1) | async-done | bytes 1376288 | tf_op jit(solution)/shard_map/all_to_all | solution.py:262
  60.3 3.6 %all-to-all-start = ((bf16[8,1,2,336,128]{4,3,2,1,0:T(8,128)(2,1)}), bf16[8,1,2,336,128]{4,3,2,1,0:T(8,128)(2,1)S(1)}, u32[]{:S(2)}, u32[]{:S(2)}) async-start(bf16[8,1,2,336,128]{4,3,2,1,0:T(8,128)(2,1)} %shard_map.94), calls=%async_computation | async-start | bytes 2752512 | tf_op jit(solution)/shard_map/all_to_all | solution.py:262
  64.0 0.2 convolution_divide_fusion
  64.2 0.4 fusion.5
  64.6 0.1 copy.29
  64.7 0.0 copy-start.2
  64.7 3.7 %broadcast_in_dim.8 = f32[8,8,8,4,8,128]{5,4,3,2,1,0:T(8,128)} broadcast(f32[8,8,8,8]{3,2,1,0:T(8,128)S(1)} %copy.29), dimensions={0,1,2,4} | broadcast | bytes 8404992 | tf_op jit(solution)/shard_map/broadcast_in_dim | solution.py:227
  68.4 9.3 %reshape.82.coeff_ref = f32[8,8,32,1024]{3,2,1,0:T(8,128)} reshape(f32[8,8,8,4,8,128]{5,4,3,2,1,0:T(8,128)} %broadcast_in_dim.8) | data formatting | bytes 16777216 | tf_op jit(solution)/shard_map/reshape | solution.py:231
  77.7 2.6 %broadcast_in_dim.9 = f32[8,8,8,2,8,64]{5,4,3,2,1,0:T(8,128)} broadcast(f32[8,8,8,8]{3,2,1,0:T(8,128)S(1)} %copy.29), dimensions={0,1,2,4} | broadcast | bytes 2113536 | tf_op jit(solution)/shard_map/broadcast_in_dim | solution.py:227
  80.2 4.8 %reshape.84.coeff_ref = f32[8,8,16,512]{3,2,1,0:T(8,128)} reshape(f32[8,8,8,2,8,64]{5,4,3,2,1,0:T(8,128)} %broadcast_in_dim.9) | data formatting | bytes 4194304 | tf_op jit(solution)/shard_map/reshape | solution.py:231
  85.0 1.5 %broadcast_in_dim.10 = f32[8,8,8,8,32]{4,3,2,1,0:T(8,128)S(1)} broadcast(f32[8,8,8,8]{3,2,1,0:T(8,128)} %copy-done.2), dimensions={0,1,2,3} | broadcast | bytes 540672 | tf_op jit(solution)/shard_map/broadcast_in_dim | solution.py:227
  86.6 1.4 %broadcast_in_dim.11.coeff_ref = f32[8,8,8,256]{3,2,1,0:T(8,128)} reshape(f32[8,8,8,8,32]{4,3,2,1,0:T(8,128)S(1)} %broadcast_in_dim.10) | data formatting | bytes 1048576 | tf_op jit(solution)/shard_map/broadcast_in_dim | solution.py:227
  88.0 7.8 %shard_map.96.rest_0_ = bf16[8,4,32,1024]{3,2,1,0:T(8,128)(2,1)} custom-call(bf16[8,2,336,128]{3,2,1,0:T(8,128)(2,1)} %bitcast.17, f32[8,8,32,1024]{3,2,1,0:T(8,128)} %reshape.82.coeff_ref), custom_call_target="tpu_custom_call" | custom-call | tf_op jit(solution)/shard_map/pallas_call | solution.py:215
  95.8 3.7 %shard_map.98.rest_0_ = bf16[8,4,16,512]{3,2,1,0:T(8,128)(2,1)} custom-call(bf16[8,2,336,128]{3,2,1,0:T(8,128)(2,1)} %bitcast.18, f32[8,8,16,512]{3,2,1,0:T(8,128)} %reshape.84.coeff_ref), custom_call_target="tpu_custom_call" | custom-call | tf_op jit(solution)/shard_map/pallas_call | solution.py:215
  99.5 1.1 copy-done
  100.6 7.8 %shard_map.97 = bf16[8,4,32,1024]{3,2,1,0:T(8,128)(2,1)} custom-call(bf16[8,2,336,128]{3,2,1,0:T(8,128)(2,1)} %bitcast.14, f32[8,8,32,1024]{3,2,1,0:T(8,128)} %reshape.82.coeff_ref, bf16[8,4,32,1024]{3,2,1,0:T(8,128)(2,1)} %shard_map.96.rest_0_), custom_call_target="tpu_custom_call", output_to_operand_aliasing={{}: (2, {})} | custom-call | tf_op jit(solution)/shard_map/pallas_call | solution.py:215
  108.4 3.7 %shard_map.99 = bf16[8,4,16,512]{3,2,1,0:T(8,128)(2,1)} custom-call(bf16[8,2,336,128]{3,2,1,0:T(8,128)(2,1)} %bitcast.15, f32[8,8,16,512]{3,2,1,0:T(8,128)} %reshape.84.coeff_ref, bf16[8,4,16,512]{3,2,1,0:T(8,128)(2,1)} %shard_map.98.rest_0_), custom_call_target="tpu_custom_call", output_to_operand_aliasing={{}: (2, {})} | custom-call | tf_op jit(solution)/shard_map/pallas_call | solution.py:215
  112.1 1.8 %shard_map.100.rest_0_ = bf16[8,4,8,256]{3,2,1,0:T(8,128)(2,1)} custom-call(bf16[8,2,336,128]{3,2,1,0:T(8,128)(2,1)} %bitcast.19, f32[8,8,8,256]{3,2,1,0:T(8,128)} %broadcast_in_dim.11.coeff_ref), custom_call_target="tpu_custom_call" | custom-call | tf_op jit(solution)/shard_map/pallas_call | solution.py:215
  113.9 1.8 %shard_map.101 = bf16[8,4,8,256]{3,2,1,0:T(8,128)(2,1)} custom-call(bf16[8,2,336,128]{3,2,1,0:T(8,128)(2,1)} %bitcast.16, f32[8,8,8,256]{3,2,1,0:T(8,128)} %broadcast_in_dim.11.coeff_ref, bf16[8,4,8,256]{3,2,1,0:T(8,128)(2,1)} %shard_map.100.rest_0_), custom_call_target="tpu_custom_call", output_to_operand_aliasing={{}: (2, {})} | custom-call | tf_op jit(solution)/shard_map/pallas_call | solution.py:215
  (19 shorter events, 0.1 us)
Async XLA Ops:
  1.5 6.4 %collective-permute-start = (bf16[1,4,6,1024]{3,2,1,0:T(8,128)(2,1)S(1)}, bf16[1,4,6,1024]{3,2,1,0:T(8,128)(2,1)S(1)}, u32[]{:S(2)}, u32[]{:S(2)}) collective-permute-start(bf16[1,4,6,1024]{3,2,1,0:T(8,128)(2,1)S(1)} %get-tuple-element.5), channel_id=1, source_target_pairs={{0,1},{2,3},{4,5},{6,7},{8,9},{10,11},{12,13},{14,15},{16,17},{18,... | collective-permute-start | bytes 147464 | tf_op jit(solution)/shard_map/ppermute | solution.py:22
  3.9 4.0 %collective-permute-start.1 = (bf16[1,4,6,1024]{3,2,1,0:T(8,128)(2,1)S(1)}, bf16[1,4,6,1024]{3,2,1,0:T(8,128)(2,1)S(1)}, u32[]{:S(2)}, u32[]{:S(2)}) collective-permute-start(bf16[1,4,6,1024]{3,2,1,0:T(8,128)(2,1)S(1)} %get-tuple-element.6), channel_id=1, source_target_pairs={{1,0},{3,2},{5,4},{7,6},{9,8},{11,10},{13,12},{15,14},{17,16},{19,... | collective-permute-start | bytes 147464 | tf_op jit(solution)/shard_map/ppermute | solution.py:25
  19.3 41.0 %all-to-all-start.1 = ((bf16[8,1,2,336,128]{4,3,2,1,0:T(8,128)(2,1)}), bf16[8,1,2,336,128]{4,3,2,1,0:T(8,128)(2,1)S(1)}, u32[]{:S(2)}, u32[]{:S(2)}) async-start(bf16[8,1,2,336,128]{4,3,2,1,0:T(8,128)(2,1)} %shard_map.95), calls=%async_computation.1 | async-start | bytes 2752512 | tf_op jit(solution)/shard_map/all_to_all | solution.py:262
  26.0 37.9 %copy-start.3 = (s32[8,8,8]{2,1,0:T(8,128)S(1)}, s32[8,8,8]{2,1,0:T(8,128)}, u32[]{:S(2)}) copy-start(s32[8,8,8]{2,1,0:T(8,128)} %param.9) | copy-start | bytes 6148
  26.0 38.0 %copy-start.7 = (f32[8,8,1]{1,0,2:T(8,128)S(1)}, f32[8,8,1]{1,0,2:T(8,128)}, u32[]{:S(2)}) copy-start(f32[8,8,1]{1,0,2:T(8,128)} %constant.53) | copy-start | bytes 772
  33.6 30.6 %copy-start.4 = (f32[8,8]{0,1:T(8,128)S(1)}, f32[8,8]{0,1:T(8,128)}, u32[]{:S(2)}) copy-start(f32[8,8]{0,1:T(8,128)} %constant.50) | copy-start | bytes 772
  33.6 30.6 %copy-start.5 = (f32[8,8,1,1]{1,0,3,2:T(8,128)S(1)}, f32[8,8,1,1]{1,0,3,2:T(8,128)}, u32[]{:S(2)}) copy-start(f32[8,8,1,1]{1,0,3,2:T(8,128)} %constant.51) | copy-start | bytes 772
  33.6 30.6 %copy-start.6 = (f32[8,8]{0,1:T(8,128)S(1)}, f32[8,8]{0,1:T(8,128)}, u32[]{:S(2)}) copy-start(f32[8,8]{0,1:T(8,128)} %constant.52) | copy-start | bytes 772
  60.3 8.1 %copy-start.1 = (bf16[8,1,2,336,128]{4,3,2,1,0:T(8,128)(2,1)}, bf16[8,1,2,336,128]{4,3,2,1,0:T(8,128)(2,1)S(1)}, u32[]{:S(2)}) copy-start(bf16[8,1,2,336,128]{4,3,2,1,0:T(8,128)(2,1)S(1)} %all-to-all-done.1) | copy-start | bytes 4128772
  60.3 39.2 %all-to-all-start = ((bf16[8,1,2,336,128]{4,3,2,1,0:T(8,128)(2,1)}), bf16[8,1,2,336,128]{4,3,2,1,0:T(8,128)(2,1)S(1)}, u32[]{:S(2)}, u32[]{:S(2)}) async-start(bf16[8,1,2,336,128]{4,3,2,1,0:T(8,128)(2,1)} %shard_map.94), calls=%async_computation | async-start | bytes 2752512 | tf_op jit(solution)/shard_map/all_to_all | solution.py:262
  64.7 13.0 %copy-start.2 = (f32[8,8,8,8]{3,2,1,0:T(8,128)}, f32[8,8,8,8]{3,2,1,0:T(8,128)S(1)}, u32[]{:S(2)}) copy-start(f32[8,8,8,8]{3,2,1,0:T(8,128)S(1)} %copy.29) | copy-start | bytes 49156
  99.5 1.1 copy-start

commit v10 on v7

--- a/solution.py
+++ b/solution.py
@@ -180,57 +180,68 @@
     return jnp.einsum("ts,suxy->tuxy", clamp, fill, precision=hi)
 
 
-def smooth_level(got_ref, start, piece, coeff_ref, out_ref, section_ref):
+def split_three(a):
+    high = a.astype(jnp.bfloat16)
+    rest = a - high.astype(jnp.float32)
+    mid = rest.astype(jnp.bfloat16)
+    low = (rest - mid.astype(jnp.float32)).astype(jnp.bfloat16)
+    return high, mid, low
+
+
+def smooth_level(mask_cols, got_ref, start, piece, coeff_ref, out_ref, section_ref, tiles_ref):
     dates, bands, rows, width = out_ref.shape
     tiles = width // 128
-    mask_cols = coeff_ref.shape[3]
     span = width // mask_cols
-    per_tile = 128 // span
-    lane_group = lax.broadcasted_iota(jnp.int32, (rows, 128), 1) // span
     section_ref[...] = got_ref[:, :, start : start + tiles * piece, :].astype(jnp.float32)
+    parts = split_three(coeff_ref[...])
+    m_at = lax.broadcasted_iota(jnp.int32, (128, 128), 0)
+    lane = lax.broadcasted_iota(jnp.int32, (128, 128), 1)
     for j in range(tiles):
+        pick = (m_at == (128 * j + lane) // span).astype(jnp.bfloat16)
+        grown = mm(parts[0], pick) + mm(parts[1], pick) + mm(parts[2], pick)
+        tiles_ref[...] = grown.reshape(tiles_ref.shape)
 
         def one_date(t, carry):
-            coeffs = []
-            for u in range(dates):
-                c = coeff_ref[t, u]
-                tile = jnp.broadcast_to(c[:, per_tile * j : per_tile * j + 1], (rows, 128))
-                for g in range(1, per_tile):
-                    m = per_tile * j + g
-                    tile = jnp.where(lane_group == g, jnp.broadcast_to(c[:, m : m + 1], (rows, 128)), tile)
-                coeffs.append(tile)
             for band in range(bands):
-                acc = coeffs[0] * section_ref[0, band, j * piece : j * piece + rows, :]
+                acc = tiles_ref[t, 0] * section_ref[0, band, j * piece : j * piece + rows, :]
                 for u in range(1, dates):
-                    acc = acc + coeffs[u] * section_ref[u, band, j * piece : j * piece + rows, :]
+                    acc = acc + tiles_ref[t, u] * section_ref[u, band, j * piece : j * piece + rows, :]
                 out_ref[t, band, :, 128 * j : 128 * (j + 1)] = acc.astype(out_ref.dtype)
             return carry
 
         lax.fori_loop(0, dates, one_date, 0)
 
 
-def smooth_kernel(pieces, got_ref, c0_ref, c1_ref, c2_ref, o0_ref, o1_ref, o2_ref, s0_ref, s1_ref, s2_ref):
+def smooth_kernel(mask_cols, pieces, got_ref, c0_ref, c1_ref, c2_ref, o0_ref, o1_ref, o2_ref,
+                  s0_ref, s1_ref, s2_ref, t0_ref, t1_ref, t2_ref):
     start = 0
-    for piece, c_ref, o_ref, s_ref in zip(pieces, (c0_ref, c1_ref, c2_ref), (o0_ref, o1_ref, o2_ref), (s0_ref, s1_ref, s2_ref)):
-        smooth_level(got_ref, start, piece, c_ref, o_ref, s_ref)
+    levels = zip(pieces, (c0_ref, c1_ref, c2_ref), (o0_ref, o1_ref, o2_ref), (s0_ref, s1_ref, s2_ref), (t0_ref, t1_ref, t2_ref))
+    for piece, c_ref, o_ref, s_ref, t_ref in levels:
+        smooth_level(mask_cols, got_ref, start, piece, c_ref, o_ref, s_ref, t_ref)
         start += (o_ref.shape[3] // 128) * piece
 
 
 def smooth_all(got, coeff, shapes, pieces):
     dates, bands = got.shape[:2]
-    grown = [jnp.repeat(coeff, shape[2] // coeff.shape[2], axis=2) for shape in shapes]
+    mask_cols = coeff.shape[3]
+    flat = []
+    for shape in shapes:
+        grown = jnp.repeat(coeff, shape[2] // coeff.shape[2], axis=2)
+        grown = grown.reshape(-1, mask_cols)
+        flat.append(jnp.pad(grown, ((0, 0), (0, 128 - mask_cols))))
     full = lambda a: pl.BlockSpec(a.shape, lambda: (0,) * len(a.shape))
     outs = [jax.ShapeDtypeStruct(shape, jnp.bfloat16) for shape in shapes]
     return pl.pallas_call(
-        functools.partial(smooth_kernel, pieces),
-        in_specs=[full(got)] + [full(g) for g in grown],
+        functools.partial(smooth_kernel, mask_cols, pieces),
+        in_specs=[full(got)] + [full(g) for g in flat],
         out_specs=[full(o) for o in outs],
         out_shape=outs,
         scratch_shapes=[
             pltpu.VMEM((dates, bands, (shape[3] // 128) * piece, 128), jnp.float32)
             for shape, piece in zip(shapes, pieces)
-        ],
-    )(got, *grown)
+        ]
+        + [pltpu.VMEM((dates, dates, shape[2], 128), jnp.float32) for shape in shapes],
+    )(got, *flat)
 
 
 def local(scenes, resample_taps, clear_mask):

time: 113 us -> 114 us (level)
  waiting for transfers between devices: 62.8 us -> 59.7 us
  local copies, waits for them, and re-layouts: 3.41 us -> 5.59 us
  Pallas kernels: 30 us -> 31.5 us
    all_to_all x1, waiting for transfers between devices: 62.3 us -> 59.2 us  [local(): lax.all_to_all(packed, 'date', split_axis=0, concat_axis=0, tiled=True)]
    pad x0 -> x3, local copies, waits for them, and re-layouts: none -> 2.6 us  [smooth_all(): flat.append(jnp.pad(grown, ((0, 0), (0, 128 - mask_cols))))]
    broadcast_in_dim x2, local copies, waits for them, and re-layouts: 2.41 us -> 0.46 us  [smooth_all(): grown = jnp.repeat(coeff, shape[2] // coeff.shape[2], axis=2)]
    unnamed x14 -> x12, local copies, waits for them, and re-layouts: 0.03 us -> 1.57 us
    pallas_call x1, Pallas kernels: 16.8 us -> 18.3 us  [smooth_all(): pl.pallas_call(functools.partial(smooth_kernel, mask_cols, pieces), in_sp...]
  transfers between devices with their start and end apart: 3 -> 3, of which waited for: 2 -> 2; matrix products, arithmetic and copies ran while one was open for 2% -> 4% of each run, Pallas kernels for 0% -> 0%
where the time goes in v10:
time: 114 us
  waiting for transfers between devices  59.7 us (52%)
  Pallas kernels  31.5 us (28%)
  starting transfers between devices  10.5 us (9%)
  local copies, waits for them, and re-layouts  5.59 us (5%)
  other arithmetic  5.03 us (4%)
    all_to_all x1, waiting for transfers between devices, local(): lax.all_to_all(packed, 'date', split_axis=0, concat_axis=0, tiled=True)  59.2 us
    pallas_call x1, Pallas kernels, smooth_all(): pl.pallas_call(functools.partial(smooth_kernel, mask_cols, pieces), in_sp...  18.3 us
    pallas_call x1, Pallas kernels, pyramid(): pl.pallas_call(functools.partial(pyramid_kernel, ndate), grid=(dates, ban...  13.2 us
    all_to_all x1, starting transfers between devices, local(): lax.all_to_all(packed, 'date', split_axis=0, concat_axis=0, tiled=True)  6.8 us
    concatenate x1, other arithmetic, padded(): block = jnp.concatenate([low, block, high], axis=dim)  3.66 us
    pad x3, local copies, waits for them, and re-layouts, smooth_all(): flat.append(jnp.pad(grown, ((0, 0), (0, 128 - mask_cols))))  2.6 us
    ppermute x1, starting transfers between devices, padded(): lax.ppermute(lax.slice_in_dim(block, block.shape[dim] - width, None, axis...  2.36 us
  transfers between devices with their start and end apart: 3, of which 2 were waited for; matrix products, arithmetic and copies ran while one was open for 4% of the time, Pallas kernels for 0%

profile of v10, /device:TPU:0, one launch (start us, length us, event | category | flops | bytes accessed | tf_op | source)
XLA Modules:
  0.0 113.7 jit_solution(4542059290788416478)
XLA Ops:
  0.6 0.9 fusion.27
  1.5 2.4 %collective-permute-start = (bf16[1,4,6,1024]{3,2,1,0:T(8,128)(2,1)S(1)}, bf16[1,4,6,1024]{3,2,1,0:T(8,128)(2,1)S(1)}, u32[]{:S(2)}, u32[]{:S(2)}) collective-permute-start(bf16[1,4,6,1024]{3,2,1,0:T(8,128)(2,1)S(1)} %get-tuple-element.3), channel_id=1, source_target_pairs={{0,1},{2,3},{4,5},{6,7},{8,9},{10,11},{12,13},{14,15},{16,17},{18,... | collective-permute-start | bytes 147464 | tf_op jit(solution)/shard_map/ppermute | solution.py:22
  3.9 1.3 %collective-permute-start.1 = (bf16[1,4,6,1024]{3,2,1,0:T(8,128)(2,1)S(1)}, bf16[1,4,6,1024]{3,2,1,0:T(8,128)(2,1)S(1)}, u32[]{:S(2)}, u32[]{:S(2)}) collective-permute-start(bf16[1,4,6,1024]{3,2,1,0:T(8,128)(2,1)S(1)} %get-tuple-element.4), channel_id=1, source_target_pairs={{1,0},{3,2},{5,4},{7,6},{9,8},{11,10},{13,12},{15,14},{17,16},{19,... | collective-permute-start | bytes 147464 | tf_op jit(solution)/shard_map/ppermute | solution.py:25
  5.2 0.7 fusion.14.keep_wide_ref
  5.9 0.7 fusion.24.keep_half_ref
  6.6 0.0 collective-permute-done
  6.6 0.5 collective-permute-done.1
  7.0 3.7 %fusion.4.x_ref = bf16[1,4,272,1024]{3,2,1,0:T(8,128)(2,1)} fusion(bf16[1,4,6,1024]{3,2,1,0:T(8,128)(2,1)S(1)} %collective-permute-done.1, bf16[1,4,256,1024]{3,2,1,0:T(8,128)(2,1)} %param.7, bf16[1,4,6,1024]{3,2,1,0:T(8,128)(2,1)S(1)} %collective-permute-done), kind=kLoop, calls=%fused_computation.5 | loop fusion | flops 11141120 | bytes 4423680 | tf_op jit(solution)/shard_map/concatenate | solution.py:26
  10.7 13.2 %shard_map.94 = bf16[8,1,4,336,128]{4,3,2,1,0:T(8,128)(2,1)} custom-call(f32[2,4,7]{2,1,0:T(4,128)} %taps_ref.1, bf16[1,4,272,1024]{3,2,1,0:T(8,128)(2,1)} %fusion.4.x_ref, f32[280,1]{1,0:T(8,128)} %fusion.14.keep_wide_ref, f32[136,1]{1,0:T(8,128)} %fusion.24.keep_half_ref), custom_call_target="tpu_custom_call" | custom-call | tf_op jit(solution)/shard_map/pallas_call | solution.py:140
  23.9 0.0 copy-start.1
  23.9 0.0 copy-start.5
  23.9 0.0 copy-start.2
  23.9 0.0 copy-start.3
  23.9 0.0 copy-start.4
  24.0 6.8 %all-to-all-start = ((bf16[8,1,4,336,128]{4,3,2,1,0:T(8,128)(2,1)}), bf16[8,1,4,336,128]{4,3,2,1,0:T(8,128)(2,1)S(1)}, u32[]{:S(2)}, u32[]{:S(2)}) async-start(bf16[8,1,4,336,128]{4,3,2,1,0:T(8,128)(2,1)} %shard_map.94), calls=%async_computation | async-start | bytes 5505024 | tf_op jit(solution)/shard_map/all_to_all | solution.py:256
  30.8 0.0 copy-done.1
  30.8 0.0 copy-done.5
  30.8 0.2 convolution_divide_fusion
  31.0 0.0 copy-done.2
  31.0 0.0 copy-done.3
  31.0 0.0 copy-done.4
  31.1 0.4 fusion.5
  31.5 0.1 copy.25
  31.5 0.3 broadcast_in_dim.4
  31.8 1.0 pad.17.c0_ref
  32.9 0.2 broadcast_in_dim.5
  33.1 0.8 pad.18.c1_ref
  33.9 0.7 pad.19.c2_ref
  34.6 59.2 %all-to-all-done = bf16[8,1,4,336,128]{4,3,2,1,0:T(8,128)(2,1)S(1)} async-done(((bf16[8,1,4,336,128]{4,3,2,1,0:T(8,128)(2,1)}), bf16[8,1,4,336,128]{4,3,2,1,0:T(8,128)(2,1)S(1)}, u32[]{:S(2)}, u32[]{:S(2)}) %all-to-all-start) | async-done | bytes 2752544 | tf_op jit(solution)/shard_map/all_to_all | solution.py:256
  93.8 0.0 copy-start
  93.9 1.5 %copy-done = bf16[8,1,4,336,128]{4,3,2,1,0:T(8,128)(2,1)} copy-done((bf16[8,1,4,336,128]{4,3,2,1,0:T(8,128)(2,1)}, bf16[8,1,4,336,128]{4,3,2,1,0:T(8,128)(2,1)S(1)}, u32[]{:S(2)}) %copy-start) | copy-done | bytes 2752536
  95.4 18.3 %shard_map.95 = (bf16[8,4,32,1024]{3,2,1,0:T(8,128)(2,1)}, bf16[8,4,16,512]{3,2,1,0:T(8,128)(2,1)}, bf16[8,4,8,256]{3,2,1,0:T(8,128)(2,1)}) custom-call(bf16[8,4,336,128]{3,2,1,0:T(8,128)(2,1)} %bitcast.10, f32[2048,128]{1,0:T(8,128)} %pad.17.c0_ref, f32[1024,128]{1,0:T(8,128)} %pad.18.c1_ref, f32[512,128]{1,0:T(8,128)} %pad.19.c2_ref), custom_call_target="tpu_custom_call" | custom-call | tf_op jit(solution)/shard_map/pallas_call | solution.py:234
  (4 shorter events, 0.0 us)
Async XLA Ops:
  1.5 5.0 %collective-permute-start = (bf16[1,4,6,1024]{3,2,1,0:T(8,128)(2,1)S(1)}, bf16[1,4,6,1024]{3,2,1,0:T(8,128)(2,1)S(1)}, u32[]{:S(2)}, u32[]{:S(2)}) collective-permute-start(bf16[1,4,6,1024]{3,2,1,0:T(8,128)(2,1)S(1)} %get-tuple-element.3), channel_id=1, source_target_pairs={{0,1},{2,3},{4,5},{6,7},{8,9},{10,11},{12,13},{14,15},{16,17},{18,... | collective-permute-start | bytes 147464 | tf_op jit(solution)/shard_map/ppermute | solution.py:22
  3.9 3.1 %collective-permute-start.1 = (bf16[1,4,6,1024]{3,2,1,0:T(8,128)(2,1)S(1)}, bf16[1,4,6,1024]{3,2,1,0:T(8,128)(2,1)S(1)}, u32[]{:S(2)}, u32[]{:S(2)}) collective-permute-start(bf16[1,4,6,1024]{3,2,1,0:T(8,128)(2,1)S(1)} %get-tuple-element.4), channel_id=1, source_target_pairs={{1,0},{3,2},{5,4},{7,6},{9,8},{11,10},{13,12},{15,14},{17,16},{19,... | collective-permute-start | bytes 147464 | tf_op jit(solution)/shard_map/ppermute | solution.py:25
  23.9 6.8 %copy-start.1 = (s32[8,8,8]{2,1,0:T(8,128)S(1)}, s32[8,8,8]{2,1,0:T(8,128)}, u32[]{:S(2)}) copy-start(s32[8,8,8]{2,1,0:T(8,128)} %param.9) | copy-start | bytes 6148
  23.9 6.9 %copy-start.5 = (f32[8,8,1]{1,0,2:T(8,128)S(1)}, f32[8,8,1]{1,0,2:T(8,128)}, u32[]{:S(2)}) copy-start(f32[8,8,1]{1,0,2:T(8,128)} %constant.61) | copy-start | bytes 772
  23.9 7.1 %copy-start.2 = (f32[8,8]{0,1:T(8,128)S(1)}, f32[8,8]{0,1:T(8,128)}, u32[]{:S(2)}) copy-start(f32[8,8]{0,1:T(8,128)} %constant.58) | copy-start | bytes 772
  23.9 7.1 %copy-start.3 = (f32[8,8,1,1]{1,0,3,2:T(8,128)S(1)}, f32[8,8,1,1]{1,0,3,2:T(8,128)}, u32[]{:S(2)}) copy-start(f32[8,8,1,1]{1,0,3,2:T(8,128)} %constant.59) | copy-start | bytes 772
  23.9 7.1 %copy-start.4 = (f32[8,8]{0,1:T(8,128)S(1)}, f32[8,8]{0,1:T(8,128)}, u32[]{:S(2)}) copy-start(f32[8,8]{0,1:T(8,128)} %constant.60) | copy-start | bytes 772
  24.0 69.9 %all-to-all-start = ((bf16[8,1,4,336,128]{4,3,2,1,0:T(8,128)(2,1)}), bf16[8,1,4,336,128]{4,3,2,1,0:T(8,128)(2,1)S(1)}, u32[]{:S(2)}, u32[]{:S(2)}) async-start(bf16[8,1,4,336,128]{4,3,2,1,0:T(8,128)(2,1)} %shard_map.94), calls=%async_computation | async-start | bytes 5505024 | tf_op jit(solution)/shard_map/all_to_all | solution.py:256
  93.8 1.5 %copy-start = (bf16[8,1,4,336,128]{4,3,2,1,0:T(8,128)(2,1)}, bf16[8,1,4,336,128]{4,3,2,1,0:T(8,128)(2,1)S(1)}, u32[]{:S(2)}) copy-start(bf16[8,1,4,336,128]{4,3,2,1,0:T(8,128)(2,1)S(1)} %all-to-all-done) | copy-start | bytes 8257540

commit v11 on v10

--- a/solution.py
+++ b/solution.py
@@ -201,15 +201,24 @@
         grown = mm(parts[0], pick) + mm(parts[1], pick) + mm(parts[2], pick)
         tiles_ref[...] = grown.reshape(tiles_ref.shape)
 
-        def one_date(t, carry):
-            for band in range(bands):
-                acc = tiles_ref[t, 0] * section_ref[0, band, j * piece : j * piece + rows, :]
-                for u in range(1, dates):
-                    acc = acc + tiles_ref[t, u] * section_ref[u, band, j * piece : j * piece + rows, :]
-                out_ref[t, band, :, 128 * j : 128 * (j + 1)] = acc.astype(out_ref.dtype)
+        step = min(rows, 8)
+
+        def one_block(r, carry):
+            r0 = pl.multiple_of(r * step, step)
+            values = [
+                [section_ref[u, band, pl.ds(j * piece + r0, step), :] for band in range(bands)]
+                for u in range(dates)
+            ]
+            for t in range(dates):
+                weights = [tiles_ref[t, u, pl.ds(r0, step), :] for u in range(dates)]
+                for band in range(bands):
+                    acc = weights[0] * values[0][band]
+                    for u in range(1, dates):
+                        acc = acc + weights[u] * values[u][band]
+                    out_ref[t, band, pl.ds(r0, step), 128 * j : 128 * (j + 1)] = acc.astype(out_ref.dtype)
             return carry
 
-        lax.fori_loop(0, dates, one_date, 0)
+        lax.fori_loop(0, rows // step, one_block, 0)
 
 
 def smooth_kernel(mask_cols, pieces, got_ref, c0_ref, c1_ref, c2_ref, o0_ref, o1_ref, o2_ref,

time: 114 us -> 113 us (level)
  transfers between devices with their start and end apart: 3 -> 3, of which waited for: 2 -> 2; matrix products, arithmetic and copies ran while one was open for 4% -> 5% of each run, Pallas kernels for 0% -> 0%
where the time goes in v11:
time: 113 us
  waiting for transfers between devices  59.7 us (53%)
  Pallas kernels  30.5 us (27%)
  starting transfers between devices  10.5 us (9%)
  local copies, waits for them, and re-layouts  5.59 us (5%)
  other arithmetic  5.03 us (4%)
    all_to_all x1, waiting for transfers between devices, local(): lax.all_to_all(packed, 'date', split_axis=0, concat_axis=0, tiled=True)  59.2 us
    pallas_call x1, Pallas kernels, smooth_all(): pl.pallas_call(functools.partial(smooth_kernel, mask_cols, pieces), in_sp...  17.3 us
    pallas_call x1, Pallas kernels, pyramid(): pl.pallas_call(functools.partial(pyramid_kernel, ndate), grid=(dates, ban...  13.2 us
    all_to_all x1, starting transfers between devices, local(): lax.all_to_all(packed, 'date', split_axis=0, concat_axis=0, tiled=True)  6.8 us
    concatenate x1, other arithmetic, padded(): block = jnp.concatenate([low, block, high], axis=dim)  3.66 us
    pad x3, local copies, waits for them, and re-layouts, smooth_all(): flat.append(jnp.pad(grown, ((0, 0), (0, 128 - mask_cols))))  2.6 us
    ppermute x1, starting transfers between devices, padded(): lax.ppermute(lax.slice_in_dim(block, block.shape[dim] - width, None, axis...  2.36 us
  transfers between devices with their start and end apart: 3, of which 2 were waited for; matrix products, arithmetic and copies ran while one was open for 5% of the time, Pallas kernels for 0%

profile of v11, /device:TPU:0, one launch (start us, length us, event | category | flops | bytes accessed | tf_op | source)
XLA Modules:
  0.0 112.7 jit_solution(2888973710183788937)
XLA Ops:
  0.6 0.9 fusion.27
  1.5 2.4 %collective-permute-start = (bf16[1,4,6,1024]{3,2,1,0:T(8,128)(2,1)S(1)}, bf16[1,4,6,1024]{3,2,1,0:T(8,128)(2,1)S(1)}, u32[]{:S(2)}, u32[]{:S(2)}) collective-permute-start(bf16[1,4,6,1024]{3,2,1,0:T(8,128)(2,1)S(1)} %get-tuple-element.3), channel_id=1, source_target_pairs={{0,1},{2,3},{4,5},{6,7},{8,9},{10,11},{12,13},{14,15},{16,17},{18,... | collective-permute-start | bytes 147464 | tf_op jit(solution)/shard_map/ppermute | solution.py:22
  3.9 1.3 %collective-permute-start.1 = (bf16[1,4,6,1024]{3,2,1,0:T(8,128)(2,1)S(1)}, bf16[1,4,6,1024]{3,2,1,0:T(8,128)(2,1)S(1)}, u32[]{:S(2)}, u32[]{:S(2)}) collective-permute-start(bf16[1,4,6,1024]{3,2,1,0:T(8,128)(2,1)S(1)} %get-tuple-element.4), channel_id=1, source_target_pairs={{1,0},{3,2},{5,4},{7,6},{9,8},{11,10},{13,12},{15,14},{17,16},{19,... | collective-permute-start | bytes 147464 | tf_op jit(solution)/shard_map/ppermute | solution.py:25
  5.2 0.7 fusion.14.keep_wide_ref
  5.9 0.7 fusion.24.keep_half_ref
  6.6 0.0 collective-permute-done
  6.6 0.5 collective-permute-done.1
  7.0 3.7 %fusion.4.x_ref = bf16[1,4,272,1024]{3,2,1,0:T(8,128)(2,1)} fusion(bf16[1,4,6,1024]{3,2,1,0:T(8,128)(2,1)S(1)} %collective-permute-done.1, bf16[1,4,256,1024]{3,2,1,0:T(8,128)(2,1)} %param.7, bf16[1,4,6,1024]{3,2,1,0:T(8,128)(2,1)S(1)} %collective-permute-done), kind=kLoop, calls=%fused_computation.5 | loop fusion | flops 11141120 | bytes 4423680 | tf_op jit(solution)/shard_map/concatenate | solution.py:26
  10.7 13.2 %shard_map.94 = bf16[8,1,4,336,128]{4,3,2,1,0:T(8,128)(2,1)} custom-call(f32[2,4,7]{2,1,0:T(4,128)} %taps_ref.1, bf16[1,4,272,1024]{3,2,1,0:T(8,128)(2,1)} %fusion.4.x_ref, f32[280,1]{1,0:T(8,128)} %fusion.14.keep_wide_ref, f32[136,1]{1,0:T(8,128)} %fusion.24.keep_half_ref), custom_call_target="tpu_custom_call" | custom-call | tf_op jit(solution)/shard_map/pallas_call | solution.py:140
  23.9 0.0 copy-start.1
  23.9 0.0 copy-start.5
  23.9 0.0 copy-start.2
  23.9 0.0 copy-start.3
  23.9 0.0 copy-start.4
  24.0 6.8 %all-to-all-start = ((bf16[8,1,4,336,128]{4,3,2,1,0:T(8,128)(2,1)}), bf16[8,1,4,336,128]{4,3,2,1,0:T(8,128)(2,1)S(1)}, u32[]{:S(2)}, u32[]{:S(2)}) async-start(bf16[8,1,4,336,128]{4,3,2,1,0:T(8,128)(2,1)} %shard_map.94), calls=%async_computation | async-start | bytes 5505024 | tf_op jit(solution)/shard_map/all_to_all | solution.py:265
  30.8 0.0 copy-done.1
  30.8 0.0 copy-done.5
  30.8 0.2 convolution_divide_fusion
  31.0 0.0 copy-done.2
  31.0 0.0 copy-done.3
  31.0 0.0 copy-done.4
  31.1 0.4 fusion.5
  31.5 0.1 copy.25
  31.5 0.3 broadcast_in_dim.4
  31.8 1.0 pad.17.c0_ref
  32.9 0.2 broadcast_in_dim.5
  33.1 0.8 pad.18.c1_ref
  33.9 0.7 pad.19.c2_ref
  34.6 59.2 %all-to-all-done = bf16[8,1,4,336,128]{4,3,2,1,0:T(8,128)(2,1)S(1)} async-done(((bf16[8,1,4,336,128]{4,3,2,1,0:T(8,128)(2,1)}), bf16[8,1,4,336,128]{4,3,2,1,0:T(8,128)(2,1)S(1)}, u32[]{:S(2)}, u32[]{:S(2)}) %all-to-all-start) | async-done | bytes 2752544 | tf_op jit(solution)/shard_map/all_to_all | solution.py:265
  93.8 0.0 copy-start
  93.9 1.5 %copy-done = bf16[8,1,4,336,128]{4,3,2,1,0:T(8,128)(2,1)} copy-done((bf16[8,1,4,336,128]{4,3,2,1,0:T(8,128)(2,1)}, bf16[8,1,4,336,128]{4,3,2,1,0:T(8,128)(2,1)S(1)}, u32[]{:S(2)}) %copy-start) | copy-done | bytes 2752536
  95.4 17.3 %shard_map.95 = (bf16[8,4,32,1024]{3,2,1,0:T(8,128)(2,1)}, bf16[8,4,16,512]{3,2,1,0:T(8,128)(2,1)}, bf16[8,4,8,256]{3,2,1,0:T(8,128)(2,1)}) custom-call(bf16[8,4,336,128]{3,2,1,0:T(8,128)(2,1)} %bitcast.10, f32[2048,128]{1,0:T(8,128)} %pad.17.c0_ref, f32[1024,128]{1,0:T(8,128)} %pad.18.c1_ref, f32[512,128]{1,0:T(8,128)} %pad.19.c2_ref), custom_call_target="tpu_custom_call" | custom-call | tf_op jit(solution)/shard_map/pallas_call | solution.py:243
  (4 shorter events, 0.0 us)
Async XLA Ops:
  1.5 5.0 %collective-permute-start = (bf16[1,4,6,1024]{3,2,1,0:T(8,128)(2,1)S(1)}, bf16[1,4,6,1024]{3,2,1,0:T(8,128)(2,1)S(1)}, u32[]{:S(2)}, u32[]{:S(2)}) collective-permute-start(bf16[1,4,6,1024]{3,2,1,0:T(8,128)(2,1)S(1)} %get-tuple-element.3), channel_id=1, source_target_pairs={{0,1},{2,3},{4,5},{6,7},{8,9},{10,11},{12,13},{14,15},{16,17},{18,... | collective-permute-start | bytes 147464 | tf_op jit(solution)/shard_map/ppermute | solution.py:22
  3.9 3.1 %collective-permute-start.1 = (bf16[1,4,6,1024]{3,2,1,0:T(8,128)(2,1)S(1)}, bf16[1,4,6,1024]{3,2,1,0:T(8,128)(2,1)S(1)}, u32[]{:S(2)}, u32[]{:S(2)}) collective-permute-start(bf16[1,4,6,1024]{3,2,1,0:T(8,128)(2,1)S(1)} %get-tuple-element.4), channel_id=1, source_target_pairs={{1,0},{3,2},{5,4},{7,6},{9,8},{11,10},{13,12},{15,14},{17,16},{19,... | collective-permute-start | bytes 147464 | tf_op jit(solution)/shard_map/ppermute | solution.py:25
  23.9 6.8 %copy-start.1 = (s32[8,8,8]{2,1,0:T(8,128)S(1)}, s32[8,8,8]{2,1,0:T(8,128)}, u32[]{:S(2)}) copy-start(s32[8,8,8]{2,1,0:T(8,128)} %param.9) | copy-start | bytes 6148
  23.9 6.9 %copy-start.5 = (f32[8,8,1]{1,0,2:T(8,128)S(1)}, f32[8,8,1]{1,0,2:T(8,128)}, u32[]{:S(2)}) copy-start(f32[8,8,1]{1,0,2:T(8,128)} %constant.61) | copy-start | bytes 772
  23.9 7.1 %copy-start.2 = (f32[8,8]{0,1:T(8,128)S(1)}, f32[8,8]{0,1:T(8,128)}, u32[]{:S(2)}) copy-start(f32[8,8]{0,1:T(8,128)} %constant.58) | copy-start | bytes 772
  23.9 7.1 %copy-start.3 = (f32[8,8,1,1]{1,0,3,2:T(8,128)S(1)}, f32[8,8,1,1]{1,0,3,2:T(8,128)}, u32[]{:S(2)}) copy-start(f32[8,8,1,1]{1,0,3,2:T(8,128)} %constant.59) | copy-start | bytes 772
  23.9 7.1 %copy-start.4 = (f32[8,8]{0,1:T(8,128)S(1)}, f32[8,8]{0,1:T(8,128)}, u32[]{:S(2)}) copy-start(f32[8,8]{0,1:T(8,128)} %constant.60) | copy-start | bytes 772
  24.0 69.9 %all-to-all-start = ((bf16[8,1,4,336,128]{4,3,2,1,0:T(8,128)(2,1)}), bf16[8,1,4,336,128]{4,3,2,1,0:T(8,128)(2,1)S(1)}, u32[]{:S(2)}, u32[]{:S(2)}) async-start(bf16[8,1,4,336,128]{4,3,2,1,0:T(8,128)(2,1)} %shard_map.94), calls=%async_computation | async-start | bytes 5505024 | tf_op jit(solution)/shard_map/all_to_all | solution.py:265
  93.8 1.5 %copy-start = (bf16[8,1,4,336,128]{4,3,2,1,0:T(8,128)(2,1)}, bf16[8,1,4,336,128]{4,3,2,1,0:T(8,128)(2,1)S(1)}, u32[]{:S(2)}) copy-start(bf16[8,1,4,336,128]{4,3,2,1,0:T(8,128)(2,1)S(1)} %all-to-all-done) | copy-start | bytes 8257540

commit v12 on v11

--- a/solution.py
+++ b/solution.py
@@ -12,26 +12,6 @@
 gap_weights = [math.exp(-((k - 4) ** 2) / 8.0) for k in range(9)]
 savgol_coeffs = [c / 231.0 for c in [-21.0, 14.0, 39.0, 54.0, 59.0, 54.0, 39.0, 14.0, -21.0]]
 pyramid_filter = [0.125, 0.375, 0.375, 0.125]
-
-
-def padded(block, sides, width):
-    for axis, dim in sides:
-        count = lax.axis_size(axis)
-        forward = [(i, i + 1) for i in range(count - 1)]
-        backward = [(target, source) for source, target in forward]
-        low = lax.ppermute(
-            lax.slice_in_dim(block, block.shape[dim] - width, None, axis=dim), axis, forward
-        )
-        high = lax.ppermute(lax.slice_in_dim(block, 0, width, axis=dim), axis, backward)
-        block = jnp.concatenate([low, block, high], axis=dim)
-    return block
-
-
-def inside_rows(count, first, valid, total):
-    at = lax.iota(jnp.int32, count)
-    places = first + at
-    keep = (places >= 0) & (places < total) & (at < valid)
-    return keep.astype(jnp.float32)[:, None]
 
 
 def split_two(a):
@@ -79,14 +59,13 @@
     return (fine, max(fine // 2, 8), max(fine // 4, 8))
 
 
-def pyramid_kernel(ndate, taps_ref, x_ref, keep_wide_ref, keep_half_ref, packed_ref,
+def pyramid_kernel(ndate, total_rows, taps_ref, where_ref, low_ref, x_ref, high_ref, packed_ref,
                    across_ref, wide_ref, half_ref, quarter_ref):
     b = pl.program_id(1)
-    x = x_ref[0, 0]
-    used = x.shape[0]
-    width = x.shape[1]
+    rows = x_ref.shape[2]
+    width = x_ref.shape[3]
+    edge = low_ref.shape[2]
     tiles = width // 128
-    rows = used - 16
     column = [taps_ref[0, b, k] for k in range(7)]
     row = [taps_ref[1, b, k] for k in range(7)]
     table = band_table(3 * 128, 128, 125, (1, column))
@@ -94,25 +73,38 @@
     rest = table - t_high.astype(jnp.float32)
     t_mid = rest.astype(jnp.bfloat16)
     t_low = (rest - t_mid.astype(jnp.float32)).astype(jnp.bfloat16)
-    for j in range(tiles):
-        lo = max(j - 1, 0) * 128
-        hi_col = min(j + 2, tiles) * 128
-        first = lo - (j - 1) * 128
-        last = first + (hi_col - lo)
-        window = x[:, lo:hi_col]
-        acc = mm(window, t_high[first:last]) + mm(window, t_mid[first:last]) + mm(window, t_low[first:last])
-        across_ref[0:used, j * 128 : (j + 1) * 128] = acc
+    sources = ((low_ref, 0), (x_ref, edge), (high_ref, edge + rows))
+    for source_ref, at in sources:
+        x = source_ref[0, 0]
+        count = x.shape[0]
+        for j in range(tiles):
+            lo = max(j - 1, 0) * 128
+            hi_col = min(j + 2, tiles) * 128
+            first = lo - (j - 1) * 128
+            last = first + (hi_col - lo)
+            window = x[:, lo:hi_col]
+            acc = mm(window, t_high[first:last]) + mm(window, t_mid[first:last]) + mm(window, t_low[first:last])
+            across_ref[at : at + count, j * 128 : (j + 1) * 128] = acc
+    used = 2 * edge + rows
     depth = across_ref.shape[0]
     across_ref[used:depth, :] = jnp.zeros((depth - used, width), jnp.float32)
+    band_index = where_ref[0]
     n_wide = wide_ref.shape[1]
-    total = row[0] * across_ref[pl.ds(0, n_wide), :]
-    for k in range(1, 7):
-        total = total + row[k] * across_ref[pl.ds(k, n_wide), :]
-    total = total * keep_wide_ref[...]
+    wide_at = lax.broadcasted_iota(jnp.int32, (n_wide, 128), 0)
+    wide_row = band_index * rows - 3 + wide_at
+    keep_wide = ((wide_row >= 0) & (wide_row < total_rows) & (wide_at < rows + 6)).astype(jnp.float32)
+    shift = edge - 6
     for j in range(tiles):
-        wide_ref[j] = total[:, 128 * j : 128 * (j + 1)]
-    n_half = keep_half_ref.shape[0]
-    halves = halve_rows(wide_ref, n_half) * keep_half_ref[...]
+        cols = slice(128 * j, 128 * (j + 1))
+        total = row[0] * across_ref[pl.ds(shift, n_wide), cols]
+        for k in range(1, 7):
+            total = total + row[k] * across_ref[pl.ds(shift + k, n_wide), cols]
+        wide_ref[j] = total * keep_wide
+    n_half = half_ref.shape[1]
+    half_at = lax.broadcasted_iota(jnp.int32, (n_half, 1), 0)
+    half_row = band_index * (rows // 2) - 1 + half_at
+    keep_half = ((half_row >= 0) & (half_row < total_rows // 2) & (half_at < rows // 2 + 2)).astype(jnp.float32)
+    halves = halve_rows(wide_ref, n_half) * keep_half
     down = band_table(512, 128, 127, (2, pyramid_filter)).astype(jnp.bfloat16)
     halve_columns(halves, down, half_ref)
     quarters = halve_rows(half_ref, rows // 4)
@@ -127,24 +119,24 @@
         packed_ref[q, 0, 0] = jnp.concatenate(parts, axis=0).astype(packed_ref.dtype)
 
 
-def pyramid(extended, resample_taps, band_index, total_rows, ndate):
-    dates, bands, used, width = extended.shape
-    rows = used - 16
+def pyramid(low, scenes, high, resample_taps, band_index, total_rows, ndate):
+    dates, bands, rows, width = scenes.shape
+    edge = low.shape[2]
     n_wide = rows + 24
     n_half = rows // 2 + 8
-    depth = n_wide + 8
+    depth = max(n_wide + 8, 2 * edge + rows)
     fine, p_half, p_quarter = piece_rows(rows, ndate)
     count = (width // 128) * fine + (width // 256) * p_half + (width // 512) * p_quarter
-    keep_wide = inside_rows(n_wide, band_index * rows - 3, rows + 6, total_rows)
-    keep_half = inside_rows(n_half, band_index * (rows // 2) - 1, rows // 2 + 2, total_rows // 2)
+    where = jnp.reshape(band_index, (1,)).astype(jnp.int32)
     return pl.pallas_call(
-        functools.partial(pyramid_kernel, ndate),
+        functools.partial(pyramid_kernel, ndate, total_rows),
         grid=(dates, bands),
         in_specs=[
             pl.BlockSpec(memory_space=pltpu.SMEM),
-            pl.BlockSpec((1, 1, used, width), lambda d, b: (d, b, 0, 0)),
-            pl.BlockSpec((n_wide, 1), lambda d, b: (0, 0)),
-            pl.BlockSpec((n_half, 1), lambda d, b: (0, 0)),
+            pl.BlockSpec(memory_space=pltpu.SMEM),
+            pl.BlockSpec((1, 1, edge, width), lambda d, b: (d, b, 0, 0)),
+            pl.BlockSpec((1, 1, rows, width), lambda d, b: (d, b, 0, 0)),
+            pl.BlockSpec((1, 1, edge, width), lambda d, b: (d, b, 0, 0)),
         ],
         out_specs=pl.BlockSpec((ndate, 1, 1, count, 128), lambda d, b: (0, d, b, 0, 0)),
         out_shape=jax.ShapeDtypeStruct((ndate, dates, bands, count, 128), jnp.bfloat16),
@@ -154,7 +146,7 @@
             pltpu.VMEM((width // 256, n_half, 128), jnp.float32),
             pltpu.VMEM((width // 512, rows // 4 + 8, 128), jnp.float32),
         ],
-    )(resample_taps, extended, keep_wide, keep_half)
+    )(resample_taps, where, low, scenes, high)
 
 
 def smooth_operator(dates):
@@ -258,9 +250,12 @@
     band_index = lax.axis_index("row")
     total_rows = rows * lax.axis_size("row")
     ndate = lax.axis_size("date")
-    extended = padded(scenes, (("row", 2),), 6)
-    extended = jnp.pad(extended, ((0, 0), (0, 0), (0, 4), (0, 0)))
-    packed = pyramid(extended, resample_taps, band_index, total_rows, ndate)
+    count = lax.axis_size("row")
+    forward = [(i, i + 1) for i in range(count - 1)]
+    backward = [(target, source) for source, target in forward]
+    low = lax.ppermute(scenes[:, :, rows - 8 :], "row", forward)
+    high = lax.ppermute(scenes[:, :, :8], "row", backward)
+    packed = pyramid(low, scenes, high, resample_taps, band_index, total_rows, ndate)
     coeff = smooth_coefficients(clear_mask.astype(jnp.float32))
     got = lax.all_to_all(packed, "date", split_axis=0, concat_axis=0, tiled=True)
     got = got.reshape((ndate * dates,) + got.shape[2:])

time: 113 us -> 111 us (0.982)
  other arithmetic: 5.03 us -> 0.04 us
  Pallas kernels: 30.5 us -> 32 us
    concatenate x1 -> x0, other arithmetic: 3.66 us -> none  [padded(): block = jnp.concatenate([low, block, high], axis=dim)]
    pallas_call x1, Pallas kernels: 13.2 us -> 14.7 us  [pyramid(): pl.pallas_call(functools.partial(pyramid_kernel, ndate, total_rows), grid...]
    convert_element_type x2 -> x0, other arithmetic: 1.35 us -> none  [inside_rows(): return keep.astype(jnp.float32)[:, None]]
    ppermute x2, waiting for transfers between devices: 0.49 us -> 1.82 us  [the longest x1 1.82 us: local(): high = lax.ppermute(scenes[:, :, :8], 'row', backward)]
  transfers between devices with their start and end apart: 3 -> 3, of which waited for: 2 -> 2; matrix products, arithmetic and copies ran while one was open for 5% -> 3% of each run, Pallas kernels for 0% -> 0%
where the time goes in v12:
time: 111 us
  waiting for transfers between devices  60.5 us (55%)
  Pallas kernels  32 us (29%)
  starting transfers between devices  10.5 us (9%)
  local copies, waits for them, and re-layouts  6.22 us (6%)
    all_to_all x1, waiting for transfers between devices, local(): lax.all_to_all(packed, 'date', split_axis=0, concat_axis=0, tiled=True)  58.7 us
    pallas_call x1, Pallas kernels, smooth_all(): pl.pallas_call(functools.partial(smooth_kernel, mask_cols, pieces), in_sp...  17.3 us
    pallas_call x1, Pallas kernels, pyramid(): pl.pallas_call(functools.partial(pyramid_kernel, ndate, total_rows), grid...  14.7 us
    all_to_all x1, starting transfers between devices, local(): lax.all_to_all(packed, 'date', split_axis=0, concat_axis=0, tiled=True)  6.8 us
    pad x3, local copies, waits for them, and re-layouts, smooth_all(): flat.append(jnp.pad(grown, ((0, 0), (0, 128 - mask_cols))))  2.62 us
    ppermute x1, starting transfers between devices, local(): low = lax.ppermute(scenes[:, :, rows - 8:], 'row', forward)  2.36 us
  transfers between devices with their start and end apart: 3, of which 2 were waited for; matrix products, arithmetic and copies ran while one was open for 3% of the time, Pallas kernels for 0%

profile of v12, /device:TPU:0, one launch (start us, length us, event | category | flops | bytes accessed | tf_op | source)
XLA Modules:
  0.0 110.7 jit_solution(755158818610075468)
XLA Ops:
  0.6 0.9 fusion.12
  1.5 2.4 %collective-permute-start = (bf16[1,4,8,1024]{3,2,1,0:T(8,128)(2,1)S(1)}, bf16[1,4,8,1024]{3,2,1,0:T(8,128)(2,1)S(1)}, u32[]{:S(2)}, u32[]{:S(2)}) collective-permute-start(bf16[1,4,8,1024]{3,2,1,0:T(8,128)(2,1)S(1)} %get-tuple-element.4), channel_id=1, source_target_pairs={{0,1},{2,3},{4,5},{6,7},{8,9},{10,11},{12,13},{14,15},{16,17},{18,... | collective-permute-start | bytes 196616 | tf_op jit(solution)/shard_map/ppermute | solution.py:256
  3.9 1.3 %collective-permute-start.1 = (bf16[1,4,8,1024]{3,2,1,0:T(8,128)(2,1)S(1)}, bf16[1,4,8,1024]{3,2,1,0:T(8,128)(2,1)S(1)}, u32[]{:S(2)}, u32[]{:S(2)}) collective-permute-start(bf16[1,4,8,1024]{3,2,1,0:T(8,128)(2,1)S(1)} %get-tuple-element.3), channel_id=1, source_target_pairs={{1,0},{3,2},{5,4},{7,6},{9,8},{11,10},{13,12},{15,14},{17,16},{19,... | collective-permute-start | bytes 196616 | tf_op jit(solution)/shard_map/ppermute | solution.py:257
  5.2 0.0 collective-permute-done.low_ref
  5.2 0.0 copy-start.2
  5.2 1.8 %collective-permute-done.1.high_ref = bf16[1,4,8,1024]{3,2,1,0:T(8,128)(2,1)S(1)} collective-permute-done((bf16[1,4,8,1024]{3,2,1,0:T(8,128)(2,1)S(1)}, bf16[1,4,8,1024]{3,2,1,0:T(8,128)(2,1)S(1)}, u32[]{:S(2)}, u32[]{:S(2)}) %collective-permute-start.1) | collective-permute-done | bytes 65568 | tf_op jit(solution)/shard_map/ppermute | solution.py:257
  7.0 0.0 copy-start.3
  7.0 0.0 copy-done.2
  7.0 0.6 copy-done.3
  7.7 14.7 %shard_map.94 = bf16[8,1,4,336,128]{4,3,2,1,0:T(8,128)(2,1)} custom-call(f32[2,4,7]{2,1,0:T(4,128)} %taps_ref.1, s32[1]{0:T(128)} %bitcast.where_ref, bf16[1,4,8,1024]{3,2,1,0:T(8,128)(2,1)} %copy-done.2, bf16[1,4,256,1024]{3,2,1,0:T(8,128)(2,1)} %x_ref.1, bf16[1,4,8,1024]{3,2,1,0:T(8,128)(2,1)} %copy-done.3), custom_call_target="tpu_custom_call" | custom-call | tf_op jit(solution)/shard_map/pallas_call | solution.py:131
  22.4 0.0 copy-start.1
  22.4 0.0 copy-start.7
  22.4 0.0 copy-start.4
  22.4 0.0 copy-start.5
  22.4 0.0 copy-start.6
  22.4 6.8 %all-to-all-start = ((bf16[8,1,4,336,128]{4,3,2,1,0:T(8,128)(2,1)}), bf16[8,1,4,336,128]{4,3,2,1,0:T(8,128)(2,1)S(1)}, u32[]{:S(2)}, u32[]{:S(2)}) async-start(bf16[8,1,4,336,128]{4,3,2,1,0:T(8,128)(2,1)} %shard_map.94), calls=%async_computation | async-start | bytes 5505024 | tf_op jit(solution)/shard_map/all_to_all | solution.py:260
  29.2 0.0 copy-done.1
  29.2 0.0 copy-done.7
  29.3 0.2 fusion.10
  29.5 0.0 copy-done.4
  29.5 0.0 copy-done.5
  29.5 0.0 copy-done.6
  29.6 0.4 fusion
  30.0 0.1 copy.16
  30.0 0.3 broadcast_in_dim.4
  30.3 1.0 pad.12.c0_ref
  31.4 0.2 broadcast_in_dim.10
  31.6 0.8 pad.13.c1_ref
  32.4 0.7 pad.14.c2_ref
  33.1 58.7 %all-to-all-done = bf16[8,1,4,336,128]{4,3,2,1,0:T(8,128)(2,1)S(1)} async-done(((bf16[8,1,4,336,128]{4,3,2,1,0:T(8,128)(2,1)}), bf16[8,1,4,336,128]{4,3,2,1,0:T(8,128)(2,1)S(1)}, u32[]{:S(2)}, u32[]{:S(2)}) %all-to-all-start) | async-done | bytes 2752544 | tf_op jit(solution)/shard_map/all_to_all | solution.py:260
  91.8 1.5 %copy-done = bf16[8,1,4,336,128]{4,3,2,1,0:T(8,128)(2,1)} copy-done((bf16[8,1,4,336,128]{4,3,2,1,0:T(8,128)(2,1)}, bf16[8,1,4,336,128]{4,3,2,1,0:T(8,128)(2,1)S(1)}, u32[]{:S(2)}) %copy-start) | copy-done | bytes 2752536
  93.4 17.3 %shard_map.95 = (bf16[8,4,32,1024]{3,2,1,0:T(8,128)(2,1)}, bf16[8,4,16,512]{3,2,1,0:T(8,128)(2,1)}, bf16[8,4,8,256]{3,2,1,0:T(8,128)(2,1)}) custom-call(bf16[8,4,336,128]{3,2,1,0:T(8,128)(2,1)} %bitcast.11, f32[2048,128]{1,0:T(8,128)} %pad.12.c0_ref, f32[1024,128]{1,0:T(8,128)} %pad.13.c1_ref, f32[512,128]{1,0:T(8,128)} %pad.14.c2_ref), custom_call_target="tpu_custom_call" | custom-call | tf_op jit(solution)/shard_map/pallas_call | solution.py:235
  (5 shorter events, 0.0 us)
Async XLA Ops:
  1.5 3.7 %collective-permute-start = (bf16[1,4,8,1024]{3,2,1,0:T(8,128)(2,1)S(1)}, bf16[1,4,8,1024]{3,2,1,0:T(8,128)(2,1)S(1)}, u32[]{:S(2)}, u32[]{:S(2)}) collective-permute-start(bf16[1,4,8,1024]{3,2,1,0:T(8,128)(2,1)S(1)} %get-tuple-element.4), channel_id=1, source_target_pairs={{0,1},{2,3},{4,5},{6,7},{8,9},{10,11},{12,13},{14,15},{16,17},{18,... | collective-permute-start | bytes 196616 | tf_op jit(solution)/shard_map/ppermute | solution.py:256
  3.9 3.1 %collective-permute-start.1 = (bf16[1,4,8,1024]{3,2,1,0:T(8,128)(2,1)S(1)}, bf16[1,4,8,1024]{3,2,1,0:T(8,128)(2,1)S(1)}, u32[]{:S(2)}, u32[]{:S(2)}) collective-permute-start(bf16[1,4,8,1024]{3,2,1,0:T(8,128)(2,1)S(1)} %get-tuple-element.3), channel_id=1, source_target_pairs={{1,0},{3,2},{5,4},{7,6},{9,8},{11,10},{13,12},{15,14},{17,16},{19,... | collective-permute-start | bytes 196616 | tf_op jit(solution)/shard_map/ppermute | solution.py:257
  5.2 1.8 %copy-start.2 = (bf16[1,4,8,1024]{3,2,1,0:T(8,128)(2,1)}, bf16[1,4,8,1024]{3,2,1,0:T(8,128)(2,1)S(1)}, u32[]{:S(2)}) copy-start(bf16[1,4,8,1024]{3,2,1,0:T(8,128)(2,1)S(1)} %collective-permute-done.low_ref) | copy-start | bytes 196612
  7.0 0.6 copy-start.3
  22.4 6.8 %copy-start.1 = (s32[8,8,8]{2,1,0:T(8,128)S(1)}, s32[8,8,8]{2,1,0:T(8,128)}, u32[]{:S(2)}) copy-start(s32[8,8,8]{2,1,0:T(8,128)} %param.9) | copy-start | bytes 6148
  22.4 6.9 %copy-start.7 = (f32[8,8,1]{0,1,2:T(8,128)S(1)}, f32[8,8,1]{0,1,2:T(8,128)}, u32[]{:S(2)}) copy-start(f32[8,8,1]{0,1,2:T(8,128)} %constant.36) | copy-start | bytes 772
  22.4 7.2 %copy-start.4 = (f32[8,8,1,1]{1,0,3,2:T(8,128)S(1)}, f32[8,8,1,1]{1,0,3,2:T(8,128)}, u32[]{:S(2)}) copy-start(f32[8,8,1,1]{1,0,3,2:T(8,128)} %constant.35) | copy-start | bytes 772
  22.4 7.2 %copy-start.5 = (f32[8,8]{0,1:T(8,128)S(1)}, f32[8,8]{0,1:T(8,128)}, u32[]{:S(2)}) copy-start(f32[8,8]{0,1:T(8,128)} %constant.34) | copy-start | bytes 772
  22.4 7.2 %copy-start.6 = (f32[8,8]{0,1:T(8,128)S(1)}, f32[8,8]{0,1:T(8,128)}, u32[]{:S(2)}) copy-start(f32[8,8]{0,1:T(8,128)} %constant.21.clone) | copy-start | bytes 772
  22.4 69.4 %all-to-all-start = ((bf16[8,1,4,336,128]{4,3,2,1,0:T(8,128)(2,1)}), bf16[8,1,4,336,128]{4,3,2,1,0:T(8,128)(2,1)S(1)}, u32[]{:S(2)}, u32[]{:S(2)}) async-start(bf16[8,1,4,336,128]{4,3,2,1,0:T(8,128)(2,1)} %shard_map.94), calls=%async_computation | async-start | bytes 5505024 | tf_op jit(solution)/shard_map/all_to_all | solution.py:260
  91.8 1.5 %copy-start = (bf16[8,1,4,336,128]{4,3,2,1,0:T(8,128)(2,1)}, bf16[8,1,4,336,128]{4,3,2,1,0:T(8,128)(2,1)S(1)}, u32[]{:S(2)}) copy-start(bf16[8,1,4,336,128]{4,3,2,1,0:T(8,128)(2,1)S(1)} %all-to-all-done) | copy-start | bytes 8257540

commit v13 on v12

--- a/solution.py
+++ b/solution.py
@@ -213,8 +213,8 @@
         lax.fori_loop(0, rows // step, one_block, 0)
 
 
-def smooth_kernel(mask_cols, pieces, got_ref, c0_ref, c1_ref, c2_ref, o0_ref, o1_ref, o2_ref,
-                  s0_ref, s1_ref, s2_ref, t0_ref, t1_ref, t2_ref):
+def smooth_kernel(mask_cols, pieces, got_ref, c0_ref, c1_ref, c2_ref, *rest):
+    o0_ref, o1_ref, o2_ref, s0_ref, s1_ref, s2_ref, t0_ref, t1_ref, t2_ref = rest[-9:]
     start = 0
     levels = zip(pieces, (c0_ref, c1_ref, c2_ref), (o0_ref, o1_ref, o2_ref), (s0_ref, s1_ref, s2_ref), (t0_ref, t1_ref, t2_ref))
     for piece, c_ref, o_ref, s_ref, t_ref in levels:
@@ -222,27 +222,32 @@
         start += (o_ref.shape[3] // 128) * piece
 
 
-def smooth_all(got, coeff, shapes, pieces):
+def smooth_all(got, flat, shapes, pieces, mask_cols, chunk, previous):
     dates, bands = got.shape[:2]
-    mask_cols = coeff.shape[3]
-    flat = []
-    for shape in shapes:
-        grown = jnp.repeat(coeff, shape[2] // coeff.shape[2], axis=2)
-        grown = grown.reshape(-1, mask_cols)
-        flat.append(jnp.pad(grown, ((0, 0), (0, 128 - mask_cols))))
-    full = lambda a: pl.BlockSpec(a.shape, lambda: (0,) * len(a.shape))
+    full = lambda a: pl.BlockSpec(a.shape, lambda i: (0,) * len(a.shape))
     outs = [jax.ShapeDtypeStruct(shape, jnp.bfloat16) for shape in shapes]
+    out_specs = [pl.BlockSpec((dates, bands) + shape[2:], lambda i: (0, chunk, 0, 0)) for shape in shapes]
+    in_specs = [full(got)] + [full(g) for g in flat]
+    args = [got] + list(flat)
+    aliases = {}
+    if previous is not None:
+        for i, prev in enumerate(previous):
+            aliases[len(args)] = i
+            in_specs.append(pl.BlockSpec(memory_space=pl.ANY))
+            args.append(prev)
     return pl.pallas_call(
         functools.partial(smooth_kernel, mask_cols, pieces),
-        in_specs=[full(got)] + [full(g) for g in flat],
-        out_specs=[full(o) for o in outs],
+        grid=(1,),
+        in_specs=in_specs,
+        out_specs=out_specs,
         out_shape=outs,
+        input_output_aliases=aliases,
         scratch_shapes=[
             pltpu.VMEM((dates, bands, (shape[3] // 128) * piece, 128), jnp.float32)
             for shape, piece in zip(shapes, pieces)
         ]
         + [pltpu.VMEM((dates, dates, shape[2], 128), jnp.float32) for shape in shapes],
-    )(got, *flat)
+    )(*args)
 
 
 def local(scenes, resample_taps, clear_mask):
@@ -255,10 +260,7 @@
     backward = [(target, source) for source, target in forward]
     low = lax.ppermute(scenes[:, :, rows - 8 :], "row", forward)
     high = lax.ppermute(scenes[:, :, :8], "row", backward)
-    packed = pyramid(low, scenes, high, resample_taps, band_index, total_rows, ndate)
     coeff = smooth_coefficients(clear_mask.astype(jnp.float32))
-    got = lax.all_to_all(packed, "date", split_axis=0, concat_axis=0, tiled=True)
-    got = got.reshape((ndate * dates,) + got.shape[2:])
     fine = rows // ndate
     total = ndate * dates
     shapes = (
@@ -266,7 +268,23 @@
         (total, bands, fine // 2, width // 2),
         (total, bands, fine // 4, width // 4),
     )
-    return tuple(smooth_all(got, coeff, shapes, piece_rows(rows, ndate)))
+    mask_cols = coeff.shape[3]
+    flat = []
+    for shape in shapes:
+        grown = jnp.repeat(coeff, shape[2] // coeff.shape[2], axis=2).reshape(-1, mask_cols)
+        flat.append(jnp.pad(grown, ((0, 0), (0, 128 - mask_cols))))
+    pieces = piece_rows(rows, ndate)
+    chunks = 2 if bands % 2 == 0 else 1
+    step = bands // chunks
+    outs = None
+    for chunk in range(chunks):
+        part = slice(chunk * step, (chunk + 1) * step)
+        packed = pyramid(low[:, part], scenes[:, part], high[:, part], resample_taps[:, part],
+                         band_index, total_rows, ndate)
+        got = lax.all_to_all(packed, "date", split_axis=0, concat_axis=0, tiled=True)
+        got = got.reshape((total,) + got.shape[2:])
+        outs = smooth_all(got, flat, shapes, pieces, mask_cols, chunk, outs)
+    return tuple(outs)
 
 
 def solution(mesh):

time: 111 us -> 112 us (level)
  waiting for transfers between devices: 60.5 us -> 38.1 us
  Pallas kernels: 32 us -> 46.4 us
  starting transfers between devices: 10.5 us -> 15.4 us
  local copies, waits for them, and re-layouts: 6.22 us -> 10 us
    all_to_all x1 -> x2, waiting for transfers between devices: 58.7 us -> 38 us  [local(): lax.all_to_all(packed, 'date', split_axis=0, concat_axis=0, tiled=True)]
    pallas_call x1 -> x2, Pallas kernels: 17.3 us -> 29.8 us  [smooth_all(): pl.pallas_call(functools.partial(smooth_kernel, mask_cols, pieces), grid=...]
    slice x0 -> x4, local copies, waits for them, and re-layouts: none -> 4.89 us  [the longest x1 3.03 us: local(): scenes[:, part]]
    all_to_all x1 -> x2, starting transfers between devices: 6.8 us -> 11 us  [local(): lax.all_to_all(packed, 'date', split_axis=0, concat_axis=0, tiled=True)]
    pallas_call x1 -> x2, Pallas kernels: 14.7 us -> 16.6 us  [pyramid(): pl.pallas_call(functools.partial(pyramid_kernel, ndate, total_rows), grid...]
    ppermute x1, waiting for transfers between devices: 1.82 us -> 0.01 us  [local(): high = lax.ppermute(scenes[:, :, :8], 'row', backward)]
  transfers between devices with their start and end apart: 3 -> 4, of which waited for: 2 -> 2; matrix products, arithmetic and copies ran while one was open for 3% -> 7% of each run, Pallas kernels for 0% -> 21%
where the time goes in v13:
time: 112 us; the launch traced here: 111 us
  Pallas kernels  46.4 us (41%)
  waiting for transfers between devices  38.1 us (34%)
  starting transfers between devices  15.4 us (14%)
  local copies, waits for them, and re-layouts  10 us (9%)
    all_to_all x2, waiting for transfers between devices, local(): lax.all_to_all(packed, 'date', split_axis=0, concat_axis=0, tiled=True)  38 us
    pallas_call x2, Pallas kernels, smooth_all(): pl.pallas_call(functools.partial(smooth_kernel, mask_cols, pieces), grid=...  29.8 us
    pallas_call x2, Pallas kernels, pyramid(): pl.pallas_call(functools.partial(pyramid_kernel, ndate, total_rows), grid...  16.6 us
    all_to_all x2, starting transfers between devices, local(): lax.all_to_all(packed, 'date', split_axis=0, concat_axis=0, tiled=True)  11 us
    ppermute x1, starting transfers between devices, local(): low = lax.ppermute(scenes[:, :, rows - 8:], 'row', forward)  3.03 us
    slice x1, local copies, waits for them, and re-layouts, local(): scenes[:, part]  3.03 us
    pad x3, local copies, waits for them, and re-layouts, local(): flat.append(jnp.pad(grown, ((0, 0), (0, 128 - mask_cols))))  2.6 us
  transfers between devices with their start and end apart: 4, of which 2 were waited for; matrix products, arithmetic and copies ran while one was open for 7% of the time, Pallas kernels for 21%

profile of v13, /device:TPU:0, one launch (start us, length us, event | category | flops | bytes accessed | tf_op | source)
XLA Modules:
  0.0 111.3 jit_solution(9298465462692586017)
XLA Ops:
  0.6 0.9 fusion.13
  1.5 1.3 %collective-permute-start.1 = (bf16[1,4,8,1024]{3,2,1,0:T(8,128)(2,1)S(1)}, bf16[1,4,8,1024]{3,2,1,0:T(8,128)(2,1)S(1)}, u32[]{:S(2)}, u32[]{:S(2)}) collective-permute-start(bf16[1,4,8,1024]{3,2,1,0:T(8,128)(2,1)S(1)} %get-tuple-element.11), channel_id=1, source_target_pairs={{1,0},{3,2},{5,4},{7,6},{9,8},{11,10},{13,12},{15,14},{17,16},{19,... | collective-permute-start | bytes 196616 | tf_op jit(solution)/shard_map/ppermute | solution.py:262
  2.8 0.0 copy-start.7
  2.8 3.0 %collective-permute-start = (bf16[1,4,8,1024]{3,2,1,0:T(8,128)(2,1)S(1)}, bf16[1,4,8,1024]{3,2,1,0:T(8,128)(2,1)S(1)}, u32[]{:S(2)}, u32[]{:S(2)}) collective-permute-start(bf16[1,4,8,1024]{3,2,1,0:T(8,128)(2,1)S(1)} %get-tuple-element.12), channel_id=1, source_target_pairs={{0,1},{2,3},{4,5},{6,7},{8,9},{10,11},{12,13},{14,15},{16,17},{18,... | collective-permute-start | bytes 196616 | tf_op jit(solution)/shard_map/ppermute | solution.py:261
  5.9 3.0 %fusion.12 = (bf16[1,2,256,1024]{3,2,1,0:T(8,128)(2,1)}, bf16[1,2,256,1024]{3,2,1,0:T(8,128)(2,1)}) fusion(bf16[1,4,256,1024]{3,2,1,0:T(8,128)(2,1)} %param.7), kind=kLoop, calls=%fused_computation.14 | loop fusion | bytes 4194304 | tf_op jit(solution)/shard_map/slice | solution.py:282
  8.9 0.0 copy-done.7
  8.9 0.6 fusion.16
  9.5 0.0 collective-permute-done.1
  9.5 0.6 fusion.14
  10.1 0.0 collective-permute-done
  10.1 0.6 fusion.15
  10.8 8.3 %shard_map.95 = bf16[8,1,2,336,128]{4,3,2,1,0:T(8,128)(2,1)} custom-call(f32[2,2,7]{2,1,0:T(2,128)} %get-tuple-element.17.taps_ref, s32[1]{0:T(128)} %bitcast.where_ref, bf16[1,2,8,1024]{3,2,1,0:T(8,128)(2,1)} %get-tuple-element.15.low_ref, bf16[1,2,256,1024]{3,2,1,0:T(8,128)(2,1)} %get-tuple-element.9.x_ref, bf16[1,2,8,1024]{3,2,1,0:T(8,128)(2,1)} %get-tuple-element.13.high_ref), custom_call_target="tpu_custom_call" | custom-call | tf_op jit(solution)/shard_map/pallas_call | solution.py:131
  19.0 7.3 %all-to-all-start.1 = ((bf16[8,1,2,336,128]{4,3,2,1,0:T(8,128)(2,1)}), bf16[8,1,2,336,128]{4,3,2,1,0:T(8,128)(2,1)S(1)}, u32[]{:S(2)}, u32[]{:S(2)}) async-start(bf16[8,1,2,336,128]{4,3,2,1,0:T(8,128)(2,1)} %shard_map.95), calls=%async_computation.1 | async-start | bytes 2752512 | tf_op jit(solution)/shard_map/all_to_all | solution.py:284
  26.3 0.0 copy-start.6
  26.3 8.3 %shard_map.94 = bf16[8,1,2,336,128]{4,3,2,1,0:T(8,128)(2,1)} custom-call(f32[2,2,7]{2,1,0:T(2,128)} %get-tuple-element.18.taps_ref, s32[1]{0:T(128)} %bitcast.where_ref, bf16[1,2,8,1024]{3,2,1,0:T(8,128)(2,1)} %get-tuple-element.16.low_ref, bf16[1,2,256,1024]{3,2,1,0:T(8,128)(2,1)} %get-tuple-element.10.x_ref, bf16[1,2,8,1024]{3,2,1,0:T(8,128)(2,1)} %get-tuple-element.14.high_ref), custom_call_target="tpu_custom_call" | custom-call | tf_op jit(solution)/shard_map/pallas_call | solution.py:131
  34.6 24.0 %all-to-all-done.1 = bf16[8,1,2,336,128]{4,3,2,1,0:T(8,128)(2,1)S(1)} async-done(((bf16[8,1,2,336,128]{4,3,2,1,0:T(8,128)(2,1)}), bf16[8,1,2,336,128]{4,3,2,1,0:T(8,128)(2,1)S(1)}, u32[]{:S(2)}, u32[]{:S(2)}) %all-to-all-start.1) | async-done | bytes 1376288 | tf_op jit(solution)/shard_map/all_to_all | solution.py:284
  58.7 3.8 %all-to-all-start = ((bf16[8,1,2,336,128]{4,3,2,1,0:T(8,128)(2,1)}), bf16[8,1,2,336,128]{4,3,2,1,0:T(8,128)(2,1)S(1)}, u32[]{:S(2)}, u32[]{:S(2)}) async-start(bf16[8,1,2,336,128]{4,3,2,1,0:T(8,128)(2,1)} %shard_map.94), calls=%async_computation | async-start | bytes 2752512 | tf_op jit(solution)/shard_map/all_to_all | solution.py:284
  62.4 0.0 copy-done.2
  62.5 0.0 copy-done.6
  62.5 0.2 fusion.10
  62.7 0.0 copy-done.3
  62.8 0.4 fusion
  63.2 0.1 copy.20
  63.3 0.7 pad.14.c2_ref
  64.0 0.2 broadcast_in_dim.10
  64.2 0.8 pad.13.c1_ref
  65.0 0.3 broadcast_in_dim.4
  65.3 1.0 pad.12.c0_ref
  66.3 14.9 %shard_map.96 = (bf16[8,4,32,1024]{3,2,1,0:T(8,128)(2,1)}, bf16[8,4,16,512]{3,2,1,0:T(8,128)(2,1)}, bf16[8,4,8,256]{3,2,1,0:T(8,128)(2,1)}) custom-call(bf16[8,2,336,128]{3,2,1,0:T(8,128)(2,1)} %bitcast.12, f32[2048,128]{1,0:T(8,128)} %pad.12.c0_ref, f32[1024,128]{1,0:T(8,128)} %pad.13.c1_ref, f32[512,128]{1,0:T(8,128)} %pad.14.c2_ref), custom_call_target="tpu_custom_call" | custom-call | tf_op jit(solution)/shard_map/pallas_call | solution.py:238
  81.2 14.0 %all-to-all-done = bf16[8,1,2,336,128]{4,3,2,1,0:T(8,128)(2,1)S(1)} async-done(((bf16[8,1,2,336,128]{4,3,2,1,0:T(8,128)(2,1)}), bf16[8,1,2,336,128]{4,3,2,1,0:T(8,128)(2,1)S(1)}, u32[]{:S(2)}, u32[]{:S(2)}) %all-to-all-start) | async-done | bytes 1376288 | tf_op jit(solution)/shard_map/all_to_all | solution.py:284
  95.3 1.1 copy-done.1
  96.4 14.9 %shard_map.97 = (bf16[8,4,32,1024]{3,2,1,0:T(8,128)(2,1)}, bf16[8,4,16,512]{3,2,1,0:T(8,128)(2,1)}, bf16[8,4,8,256]{3,2,1,0:T(8,128)(2,1)}) custom-call(bf16[8,2,336,128]{3,2,1,0:T(8,128)(2,1)} %bitcast.13, f32[2048,128]{1,0:T(8,128)} %pad.12.c0_ref, f32[1024,128]{1,0:T(8,128)} %pad.13.c1_ref, ...), custom_call_target="tpu_custom_call", output_to_operand_aliasing={{0}: (4, {}), {1}: (5, {}), {2}: (6, {})} | custom-call | tf_op jit(solution)/shard_map/pallas_call | solution.py:238
  (13 shorter events, 0.1 us)
Async XLA Ops:
  1.5 8.0 %collective-permute-start.1 = (bf16[1,4,8,1024]{3,2,1,0:T(8,128)(2,1)S(1)}, bf16[1,4,8,1024]{3,2,1,0:T(8,128)(2,1)S(1)}, u32[]{:S(2)}, u32[]{:S(2)}) collective-permute-start(bf16[1,4,8,1024]{3,2,1,0:T(8,128)(2,1)S(1)} %get-tuple-element.11), channel_id=1, source_target_pairs={{1,0},{3,2},{5,4},{7,6},{9,8},{11,10},{13,12},{15,14},{17,16},{19,... | collective-permute-start | bytes 196616 | tf_op jit(solution)/shard_map/ppermute | solution.py:262
  2.8 6.1 %copy-start.7 = (f32[2,4,7]{2,1,0:T(4,128)S(1)}, f32[2,4,7]{2,1,0:T(4,128)}, u32[]{:S(2)}) copy-start(f32[2,4,7]{2,1,0:T(4,128)} %param.8) | copy-start | bytes 676
  2.8 7.3 %collective-permute-start = (bf16[1,4,8,1024]{3,2,1,0:T(8,128)(2,1)S(1)}, bf16[1,4,8,1024]{3,2,1,0:T(8,128)(2,1)S(1)}, u32[]{:S(2)}, u32[]{:S(2)}) collective-permute-start(bf16[1,4,8,1024]{3,2,1,0:T(8,128)(2,1)S(1)} %get-tuple-element.12), channel_id=1, source_target_pairs={{0,1},{2,3},{4,5},{6,7},{8,9},{10,11},{12,13},{14,15},{16,17},{18,... | collective-permute-start | bytes 196616 | tf_op jit(solution)/shard_map/ppermute | solution.py:261
  19.0 39.6 %all-to-all-start.1 = ((bf16[8,1,2,336,128]{4,3,2,1,0:T(8,128)(2,1)}), bf16[8,1,2,336,128]{4,3,2,1,0:T(8,128)(2,1)S(1)}, u32[]{:S(2)}, u32[]{:S(2)}) async-start(bf16[8,1,2,336,128]{4,3,2,1,0:T(8,128)(2,1)} %shard_map.95), calls=%async_computation.1 | async-start | bytes 2752512 | tf_op jit(solution)/shard_map/all_to_all | solution.py:284
  26.3 36.1 %copy-start.2 = (s32[8,8,8]{2,1,0:T(8,128)S(1)}, s32[8,8,8]{2,1,0:T(8,128)}, u32[]{:S(2)}) copy-start(s32[8,8,8]{2,1,0:T(8,128)} %param.9) | copy-start | bytes 6148
  26.3 36.1 %copy-start.6 = (f32[8,8,1]{0,1,2:T(8,128)S(1)}, f32[8,8,1]{0,1,2:T(8,128)}, u32[]{:S(2)}) copy-start(f32[8,8,1]{0,1,2:T(8,128)} %constant.36) | copy-start | bytes 772
  34.6 28.1 %copy-start.3 = (f32[8,8,1,1]{1,0,3,2:T(8,128)S(1)}, f32[8,8,1,1]{1,0,3,2:T(8,128)}, u32[]{:S(2)}) copy-start(f32[8,8,1,1]{1,0,3,2:T(8,128)} %constant.35) | copy-start | bytes 772
  34.6 28.1 %copy-start.4 = (f32[8,8]{0,1:T(8,128)S(1)}, f32[8,8]{0,1:T(8,128)}, u32[]{:S(2)}) copy-start(f32[8,8]{0,1:T(8,128)} %constant.34) | copy-start | bytes 772
  34.6 28.1 %copy-start.5 = (f32[8,8]{0,1:T(8,128)S(1)}, f32[8,8]{0,1:T(8,128)}, u32[]{:S(2)}) copy-start(f32[8,8]{0,1:T(8,128)} %constant.21.clone) | copy-start | bytes 772
  58.7 5.3 %copy-start = (bf16[8,1,2,336,128]{4,3,2,1,0:T(8,128)(2,1)}, bf16[8,1,2,336,128]{4,3,2,1,0:T(8,128)(2,1)S(1)}, u32[]{:S(2)}) copy-start(bf16[8,1,2,336,128]{4,3,2,1,0:T(8,128)(2,1)S(1)} %all-to-all-done.1) | copy-start | bytes 4128772
  58.7 36.6 %all-to-all-start = ((bf16[8,1,2,336,128]{4,3,2,1,0:T(8,128)(2,1)}), bf16[8,1,2,336,128]{4,3,2,1,0:T(8,128)(2,1)S(1)}, u32[]{:S(2)}, u32[]{:S(2)}) async-start(bf16[8,1,2,336,128]{4,3,2,1,0:T(8,128)(2,1)} %shard_map.94), calls=%async_computation | async-start | bytes 2752512 | tf_op jit(solution)/shard_map/all_to_all | solution.py:284
  95.3 1.1 copy-start.1

commit v14 on v12

--- a/solution.py
+++ b/solution.py
@@ -172,25 +172,17 @@
     return jnp.einsum("ts,suxy->tuxy", clamp, fill, precision=hi)
 
 
-def split_three(a):
-    high = a.astype(jnp.bfloat16)
-    rest = a - high.astype(jnp.float32)
-    mid = rest.astype(jnp.bfloat16)
-    low = (rest - mid.astype(jnp.float32)).astype(jnp.bfloat16)
-    return high, mid, low
-
-
 def smooth_level(mask_cols, got_ref, start, piece, coeff_ref, out_ref, section_ref, tiles_ref):
     dates, bands, rows, width = out_ref.shape
     tiles = width // 128
     span = width // mask_cols
     section_ref[...] = got_ref[:, :, start : start + tiles * piece, :].astype(jnp.float32)
-    parts = split_three(coeff_ref[...])
+    parts = split_two(coeff_ref[...])
     m_at = lax.broadcasted_iota(jnp.int32, (128, 128), 0)
     lane = lax.broadcasted_iota(jnp.int32, (128, 128), 1)
     for j in range(tiles):
         pick = (m_at == (128 * j + lane) // span).astype(jnp.bfloat16)
-        grown = mm(parts[0], pick) + mm(parts[1], pick) + mm(parts[2], pick)
+        grown = mm(parts[0], pick) + mm(parts[1], pick)
         tiles_ref[...] = grown.reshape(tiles_ref.shape)
 
         step = min(rows, 8)

time: 111 us -> 108 us (0.973)
  Pallas kernels: 32 us -> 29.3 us
    pallas_call x1, Pallas kernels: 17.3 us -> 14.6 us  [smooth_all(): pl.pallas_call(functools.partial(smooth_kernel, mask_cols, pieces), in_sp...]
  transfers between devices with their start and end apart: 3 -> 3, of which waited for: 2 -> 2; matrix products, arithmetic and copies ran while one was open for 3% -> 4% of each run, Pallas kernels for 0% -> 0%
where the time goes in v14:
time: 108 us
  waiting for transfers between devices  60.5 us (56%)
  Pallas kernels  29.3 us (27%)
  starting transfers between devices  10.5 us (10%)
  local copies, waits for them, and re-layouts  6.22 us (6%)
    all_to_all x1, waiting for transfers between devices, local(): lax.all_to_all(packed, 'date', split_axis=0, concat_axis=0, tiled=True)  58.7 us
    pallas_call x1, Pallas kernels, pyramid(): pl.pallas_call(functools.partial(pyramid_kernel, ndate, total_rows), grid...  14.7 us
    pallas_call x1, Pallas kernels, smooth_all(): pl.pallas_call(functools.partial(smooth_kernel, mask_cols, pieces), in_sp...  14.6 us
    all_to_all x1, starting transfers between devices, local(): lax.all_to_all(packed, 'date', split_axis=0, concat_axis=0, tiled=True)  6.8 us
    pad x3, local copies, waits for them, and re-layouts, smooth_all(): flat.append(jnp.pad(grown, ((0, 0), (0, 128 - mask_cols))))  2.62 us
    ppermute x1, starting transfers between devices, local(): low = lax.ppermute(scenes[:, :, rows - 8:], 'row', forward)  2.36 us
    unnamed x16, local copies, waits for them, and re-layouts  2.19 us
  transfers between devices with their start and end apart: 3, of which 2 were waited for; matrix products, arithmetic and copies ran while one was open for 4% of the time, Pallas kernels for 0%

profile of v14, /device:TPU:0, one launch (start us, length us, event | category | flops | bytes accessed | tf_op | source)
XLA Modules:
  0.0 107.9 jit_solution(12936449012338499075)
XLA Ops:
  0.6 0.9 fusion.12
  1.5 2.4 %collective-permute-start = (bf16[1,4,8,1024]{3,2,1,0:T(8,128)(2,1)S(1)}, bf16[1,4,8,1024]{3,2,1,0:T(8,128)(2,1)S(1)}, u32[]{:S(2)}, u32[]{:S(2)}) collective-permute-start(bf16[1,4,8,1024]{3,2,1,0:T(8,128)(2,1)S(1)} %get-tuple-element.4), channel_id=1, source_target_pairs={{0,1},{2,3},{4,5},{6,7},{8,9},{10,11},{12,13},{14,15},{16,17},{18,... | collective-permute-start | bytes 196616 | tf_op jit(solution)/shard_map/ppermute | solution.py:248
  3.9 1.3 %collective-permute-start.1 = (bf16[1,4,8,1024]{3,2,1,0:T(8,128)(2,1)S(1)}, bf16[1,4,8,1024]{3,2,1,0:T(8,128)(2,1)S(1)}, u32[]{:S(2)}, u32[]{:S(2)}) collective-permute-start(bf16[1,4,8,1024]{3,2,1,0:T(8,128)(2,1)S(1)} %get-tuple-element.3), channel_id=1, source_target_pairs={{1,0},{3,2},{5,4},{7,6},{9,8},{11,10},{13,12},{15,14},{17,16},{19,... | collective-permute-start | bytes 196616 | tf_op jit(solution)/shard_map/ppermute | solution.py:249
  5.2 0.0 collective-permute-done.low_ref
  5.2 0.0 copy-start.2
  5.2 1.8 %collective-permute-done.1.high_ref = bf16[1,4,8,1024]{3,2,1,0:T(8,128)(2,1)S(1)} collective-permute-done((bf16[1,4,8,1024]{3,2,1,0:T(8,128)(2,1)S(1)}, bf16[1,4,8,1024]{3,2,1,0:T(8,128)(2,1)S(1)}, u32[]{:S(2)}, u32[]{:S(2)}) %collective-permute-start.1) | collective-permute-done | bytes 65568 | tf_op jit(solution)/shard_map/ppermute | solution.py:249
  7.0 0.0 copy-start.3
  7.0 0.0 copy-done.2
  7.0 0.6 copy-done.3
  7.7 14.7 %shard_map.94 = bf16[8,1,4,336,128]{4,3,2,1,0:T(8,128)(2,1)} custom-call(f32[2,4,7]{2,1,0:T(4,128)} %taps_ref.1, s32[1]{0:T(128)} %bitcast.where_ref, bf16[1,4,8,1024]{3,2,1,0:T(8,128)(2,1)} %copy-done.2, bf16[1,4,256,1024]{3,2,1,0:T(8,128)(2,1)} %x_ref.1, bf16[1,4,8,1024]{3,2,1,0:T(8,128)(2,1)} %copy-done.3), custom_call_target="tpu_custom_call" | custom-call | tf_op jit(solution)/shard_map/pallas_call | solution.py:131
  22.4 0.0 copy-start.1
  22.4 0.0 copy-start.7
  22.4 0.0 copy-start.4
  22.4 0.0 copy-start.5
  22.4 0.0 copy-start.6
  22.4 6.8 %all-to-all-start = ((bf16[8,1,4,336,128]{4,3,2,1,0:T(8,128)(2,1)}), bf16[8,1,4,336,128]{4,3,2,1,0:T(8,128)(2,1)S(1)}, u32[]{:S(2)}, u32[]{:S(2)}) async-start(bf16[8,1,4,336,128]{4,3,2,1,0:T(8,128)(2,1)} %shard_map.94), calls=%async_computation | async-start | bytes 5505024 | tf_op jit(solution)/shard_map/all_to_all | solution.py:252
  29.2 0.0 copy-done.1
  29.2 0.0 copy-done.7
  29.3 0.2 fusion.10
  29.5 0.0 copy-done.4
  29.5 0.0 copy-done.5
  29.5 0.0 copy-done.6
  29.6 0.4 fusion
  30.0 0.1 copy.16
  30.0 0.3 broadcast_in_dim.4
  30.3 1.0 pad.12.c0_ref
  31.4 0.2 broadcast_in_dim.10
  31.6 0.8 pad.13.c1_ref
  32.4 0.7 pad.14.c2_ref
  33.1 58.7 %all-to-all-done = bf16[8,1,4,336,128]{4,3,2,1,0:T(8,128)(2,1)S(1)} async-done(((bf16[8,1,4,336,128]{4,3,2,1,0:T(8,128)(2,1)}), bf16[8,1,4,336,128]{4,3,2,1,0:T(8,128)(2,1)S(1)}, u32[]{:S(2)}, u32[]{:S(2)}) %all-to-all-start) | async-done | bytes 2752544 | tf_op jit(solution)/shard_map/all_to_all | solution.py:252
  91.8 1.5 %copy-done = bf16[8,1,4,336,128]{4,3,2,1,0:T(8,128)(2,1)} copy-done((bf16[8,1,4,336,128]{4,3,2,1,0:T(8,128)(2,1)}, bf16[8,1,4,336,128]{4,3,2,1,0:T(8,128)(2,1)S(1)}, u32[]{:S(2)}) %copy-start) | copy-done | bytes 2752536
  93.4 14.6 %shard_map.95 = (bf16[8,4,32,1024]{3,2,1,0:T(8,128)(2,1)}, bf16[8,4,16,512]{3,2,1,0:T(8,128)(2,1)}, bf16[8,4,8,256]{3,2,1,0:T(8,128)(2,1)}) custom-call(bf16[8,4,336,128]{3,2,1,0:T(8,128)(2,1)} %bitcast.11, f32[2048,128]{1,0:T(8,128)} %pad.12.c0_ref, f32[1024,128]{1,0:T(8,128)} %pad.13.c1_ref, f32[512,128]{1,0:T(8,128)} %pad.14.c2_ref), custom_call_target="tpu_custom_call" | custom-call | tf_op jit(solution)/shard_map/pallas_call | solution.py:227
  (5 shorter events, 0.0 us)
Async XLA Ops:
  1.5 3.7 %collective-permute-start = (bf16[1,4,8,1024]{3,2,1,0:T(8,128)(2,1)S(1)}, bf16[1,4,8,1024]{3,2,1,0:T(8,128)(2,1)S(1)}, u32[]{:S(2)}, u32[]{:S(2)}) collective-permute-start(bf16[1,4,8,1024]{3,2,1,0:T(8,128)(2,1)S(1)} %get-tuple-element.4), channel_id=1, source_target_pairs={{0,1},{2,3},{4,5},{6,7},{8,9},{10,11},{12,13},{14,15},{16,17},{18,... | collective-permute-start | bytes 196616 | tf_op jit(solution)/shard_map/ppermute | solution.py:248
  3.9 3.1 %collective-permute-start.1 = (bf16[1,4,8,1024]{3,2,1,0:T(8,128)(2,1)S(1)}, bf16[1,4,8,1024]{3,2,1,0:T(8,128)(2,1)S(1)}, u32[]{:S(2)}, u32[]{:S(2)}) collective-permute-start(bf16[1,4,8,1024]{3,2,1,0:T(8,128)(2,1)S(1)} %get-tuple-element.3), channel_id=1, source_target_pairs={{1,0},{3,2},{5,4},{7,6},{9,8},{11,10},{13,12},{15,14},{17,16},{19,... | collective-permute-start | bytes 196616 | tf_op jit(solution)/shard_map/ppermute | solution.py:249
  5.2 1.8 %copy-start.2 = (bf16[1,4,8,1024]{3,2,1,0:T(8,128)(2,1)}, bf16[1,4,8,1024]{3,2,1,0:T(8,128)(2,1)S(1)}, u32[]{:S(2)}) copy-start(bf16[1,4,8,1024]{3,2,1,0:T(8,128)(2,1)S(1)} %collective-permute-done.low_ref) | copy-start | bytes 196612
  7.0 0.6 copy-start.3
  22.4 6.8 %copy-start.1 = (s32[8,8,8]{2,1,0:T(8,128)S(1)}, s32[8,8,8]{2,1,0:T(8,128)}, u32[]{:S(2)}) copy-start(s32[8,8,8]{2,1,0:T(8,128)} %param.9) | copy-start | bytes 6148
  22.4 6.9 %copy-start.7 = (f32[8,8,1]{0,1,2:T(8,128)S(1)}, f32[8,8,1]{0,1,2:T(8,128)}, u32[]{:S(2)}) copy-start(f32[8,8,1]{0,1,2:T(8,128)} %constant.36) | copy-start | bytes 772
  22.4 7.2 %copy-start.4 = (f32[8,8,1,1]{1,0,3,2:T(8,128)S(1)}, f32[8,8,1,1]{1,0,3,2:T(8,128)}, u32[]{:S(2)}) copy-start(f32[8,8,1,1]{1,0,3,2:T(8,128)} %constant.35) | copy-start | bytes 772
  22.4 7.2 %copy-start.5 = (f32[8,8]{0,1:T(8,128)S(1)}, f32[8,8]{0,1:T(8,128)}, u32[]{:S(2)}) copy-start(f32[8,8]{0,1:T(8,128)} %constant.34) | copy-start | bytes 772
  22.4 7.2 %copy-start.6 = (f32[8,8]{0,1:T(8,128)S(1)}, f32[8,8]{0,1:T(8,128)}, u32[]{:S(2)}) copy-start(f32[8,8]{0,1:T(8,128)} %constant.21.clone) | copy-start | bytes 772
  22.4 69.4 %all-to-all-start = ((bf16[8,1,4,336,128]{4,3,2,1,0:T(8,128)(2,1)}), bf16[8,1,4,336,128]{4,3,2,1,0:T(8,128)(2,1)S(1)}, u32[]{:S(2)}, u32[]{:S(2)}) async-start(bf16[8,1,4,336,128]{4,3,2,1,0:T(8,128)(2,1)} %shard_map.94), calls=%async_computation | async-start | bytes 5505024 | tf_op jit(solution)/shard_map/all_to_all | solution.py:252
  91.8 1.5 %copy-start = (bf16[8,1,4,336,128]{4,3,2,1,0:T(8,128)(2,1)}, bf16[8,1,4,336,128]{4,3,2,1,0:T(8,128)(2,1)S(1)}, u32[]{:S(2)}) copy-start(bf16[8,1,4,336,128]{4,3,2,1,0:T(8,128)(2,1)S(1)} %all-to-all-done) | copy-start | bytes 8257540

commit v15 on v14

--- a/solution.py
+++ b/solution.py
@@ -69,10 +69,7 @@
     column = [taps_ref[0, b, k] for k in range(7)]
     row = [taps_ref[1, b, k] for k in range(7)]
     table = band_table(3 * 128, 128, 125, (1, column))
-    t_high = table.astype(jnp.bfloat16)
-    rest = table - t_high.astype(jnp.float32)
-    t_mid = rest.astype(jnp.bfloat16)
-    t_low = (rest - t_mid.astype(jnp.float32)).astype(jnp.bfloat16)
+    t_high, t_low = split_two(table)
     sources = ((low_ref, 0), (x_ref, edge), (high_ref, edge + rows))
     for source_ref, at in sources:
         x = source_ref[0, 0]
@@ -83,7 +80,7 @@
             first = lo - (j - 1) * 128
             last = first + (hi_col - lo)
             window = x[:, lo:hi_col]
-            acc = mm(window, t_high[first:last]) + mm(window, t_mid[first:last]) + mm(window, t_low[first:last])
+            acc = mm(window, t_high[first:last]) + mm(window, t_low[first:last])
             across_ref[at : at + count, j * 128 : (j + 1) * 128] = acc
     used = 2 * edge + rows
     depth = across_ref.shape[0]

time: 108 us -> 107 us (level)
  Pallas kernels: 29.3 us -> 27.9 us
    pallas_call x1, Pallas kernels: 14.7 us -> 13.4 us  [pyramid(): pl.pallas_call(functools.partial(pyramid_kernel, ndate, total_rows), grid...]
where the time goes in v15:
time: 107 us
  waiting for transfers between devices  60.5 us (57%)
  Pallas kernels  27.9 us (26%)
  starting transfers between devices  10.5 us (10%)
  local copies, waits for them, and re-layouts  6.22 us (6%)
    all_to_all x1, waiting for transfers between devices, local(): lax.all_to_all(packed, 'date', split_axis=0, concat_axis=0, tiled=True)  58.7 us
    pallas_call x1, Pallas kernels, smooth_all(): pl.pallas_call(functools.partial(smooth_kernel, mask_cols, pieces), in_sp...  14.6 us
    pallas_call x1, Pallas kernels, pyramid(): pl.pallas_call(functools.partial(pyramid_kernel, ndate, total_rows), grid...  13.4 us
    all_to_all x1, starting transfers between devices, local(): lax.all_to_all(packed, 'date', split_axis=0, concat_axis=0, tiled=True)  6.81 us
    pad x3, local copies, waits for them, and re-layouts, smooth_all(): flat.append(jnp.pad(grown, ((0, 0), (0, 128 - mask_cols))))  2.62 us
    ppermute x1, starting transfers between devices, local(): low = lax.ppermute(scenes[:, :, rows - 8:], 'row', forward)  2.36 us
    unnamed x16, local copies, waits for them, and re-layouts  2.19 us
  transfers between devices with their start and end apart: 3, of which 2 were waited for; matrix products, arithmetic and copies ran while one was open for 4% of the time, Pallas kernels for 0%

profile of v15, /device:TPU:0, one launch (start us, length us, event | category | flops | bytes accessed | tf_op | source)
XLA Modules:
  0.0 106.6 jit_solution(13836852714020839878)
XLA Ops:
  0.6 0.9 fusion.12
  1.5 2.4 %collective-permute-start = (bf16[1,4,8,1024]{3,2,1,0:T(8,128)(2,1)S(1)}, bf16[1,4,8,1024]{3,2,1,0:T(8,128)(2,1)S(1)}, u32[]{:S(2)}, u32[]{:S(2)}) collective-permute-start(bf16[1,4,8,1024]{3,2,1,0:T(8,128)(2,1)S(1)} %get-tuple-element.4), channel_id=1, source_target_pairs={{0,1},{2,3},{4,5},{6,7},{8,9},{10,11},{12,13},{14,15},{16,17},{18,... | collective-permute-start | bytes 196616 | tf_op jit(solution)/shard_map/ppermute | solution.py:245
  3.9 1.3 %collective-permute-start.1 = (bf16[1,4,8,1024]{3,2,1,0:T(8,128)(2,1)S(1)}, bf16[1,4,8,1024]{3,2,1,0:T(8,128)(2,1)S(1)}, u32[]{:S(2)}, u32[]{:S(2)}) collective-permute-start(bf16[1,4,8,1024]{3,2,1,0:T(8,128)(2,1)S(1)} %get-tuple-element.3), channel_id=1, source_target_pairs={{1,0},{3,2},{5,4},{7,6},{9,8},{11,10},{13,12},{15,14},{17,16},{19,... | collective-permute-start | bytes 196616 | tf_op jit(solution)/shard_map/ppermute | solution.py:246
  5.2 0.0 collective-permute-done.low_ref
  5.2 0.0 copy-start.2
  5.2 1.8 %collective-permute-done.1.high_ref = bf16[1,4,8,1024]{3,2,1,0:T(8,128)(2,1)S(1)} collective-permute-done((bf16[1,4,8,1024]{3,2,1,0:T(8,128)(2,1)S(1)}, bf16[1,4,8,1024]{3,2,1,0:T(8,128)(2,1)S(1)}, u32[]{:S(2)}, u32[]{:S(2)}) %collective-permute-start.1) | collective-permute-done | bytes 65568 | tf_op jit(solution)/shard_map/ppermute | solution.py:246
  7.0 0.0 copy-start.3
  7.0 0.0 copy-done.2
  7.0 0.6 copy-done.3
  7.7 13.4 %shard_map.94 = bf16[8,1,4,336,128]{4,3,2,1,0:T(8,128)(2,1)} custom-call(f32[2,4,7]{2,1,0:T(4,128)} %taps_ref.1, s32[1]{0:T(128)} %bitcast.where_ref, bf16[1,4,8,1024]{3,2,1,0:T(8,128)(2,1)} %copy-done.2, bf16[1,4,256,1024]{3,2,1,0:T(8,128)(2,1)} %x_ref.1, bf16[1,4,8,1024]{3,2,1,0:T(8,128)(2,1)} %copy-done.3), custom_call_target="tpu_custom_call" | custom-call | tf_op jit(solution)/shard_map/pallas_call | solution.py:128
  21.0 0.0 copy-start.1
  21.0 0.0 copy-start.7
  21.0 0.0 copy-start.4
  21.0 0.0 copy-start.5
  21.0 0.0 copy-start.6
  21.1 6.8 %all-to-all-start = ((bf16[8,1,4,336,128]{4,3,2,1,0:T(8,128)(2,1)}), bf16[8,1,4,336,128]{4,3,2,1,0:T(8,128)(2,1)S(1)}, u32[]{:S(2)}, u32[]{:S(2)}) async-start(bf16[8,1,4,336,128]{4,3,2,1,0:T(8,128)(2,1)} %shard_map.94), calls=%async_computation | async-start | bytes 5505024 | tf_op jit(solution)/shard_map/all_to_all | solution.py:249
  27.9 0.0 copy-done.1
  27.9 0.0 copy-done.7
  27.9 0.2 fusion.10
  28.2 0.0 copy-done.4
  28.2 0.0 copy-done.5
  28.2 0.0 copy-done.6
  28.2 0.4 fusion
  28.6 0.1 copy.16
  28.7 0.3 broadcast_in_dim.4
  29.0 1.0 pad.12.c0_ref
  30.0 0.2 broadcast_in_dim.10
  30.2 0.8 pad.13.c1_ref
  31.0 0.7 pad.14.c2_ref
  31.8 58.7 %all-to-all-done = bf16[8,1,4,336,128]{4,3,2,1,0:T(8,128)(2,1)S(1)} async-done(((bf16[8,1,4,336,128]{4,3,2,1,0:T(8,128)(2,1)}), bf16[8,1,4,336,128]{4,3,2,1,0:T(8,128)(2,1)S(1)}, u32[]{:S(2)}, u32[]{:S(2)}) %all-to-all-start) | async-done | bytes 2752544 | tf_op jit(solution)/shard_map/all_to_all | solution.py:249
  90.5 1.5 %copy-done = bf16[8,1,4,336,128]{4,3,2,1,0:T(8,128)(2,1)} copy-done((bf16[8,1,4,336,128]{4,3,2,1,0:T(8,128)(2,1)}, bf16[8,1,4,336,128]{4,3,2,1,0:T(8,128)(2,1)S(1)}, u32[]{:S(2)}) %copy-start) | copy-done | bytes 2752536
  92.0 14.6 %shard_map.95 = (bf16[8,4,32,1024]{3,2,1,0:T(8,128)(2,1)}, bf16[8,4,16,512]{3,2,1,0:T(8,128)(2,1)}, bf16[8,4,8,256]{3,2,1,0:T(8,128)(2,1)}) custom-call(bf16[8,4,336,128]{3,2,1,0:T(8,128)(2,1)} %bitcast.11, f32[2048,128]{1,0:T(8,128)} %pad.12.c0_ref, f32[1024,128]{1,0:T(8,128)} %pad.13.c1_ref, f32[512,128]{1,0:T(8,128)} %pad.14.c2_ref), custom_call_target="tpu_custom_call" | custom-call | tf_op jit(solution)/shard_map/pallas_call | solution.py:224
  (5 shorter events, 0.0 us)
Async XLA Ops:
  1.5 3.7 %collective-permute-start = (bf16[1,4,8,1024]{3,2,1,0:T(8,128)(2,1)S(1)}, bf16[1,4,8,1024]{3,2,1,0:T(8,128)(2,1)S(1)}, u32[]{:S(2)}, u32[]{:S(2)}) collective-permute-start(bf16[1,4,8,1024]{3,2,1,0:T(8,128)(2,1)S(1)} %get-tuple-element.4), channel_id=1, source_target_pairs={{0,1},{2,3},{4,5},{6,7},{8,9},{10,11},{12,13},{14,15},{16,17},{18,... | collective-permute-start | bytes 196616 | tf_op jit(solution)/shard_map/ppermute | solution.py:245
  3.9 3.1 %collective-permute-start.1 = (bf16[1,4,8,1024]{3,2,1,0:T(8,128)(2,1)S(1)}, bf16[1,4,8,1024]{3,2,1,0:T(8,128)(2,1)S(1)}, u32[]{:S(2)}, u32[]{:S(2)}) collective-permute-start(bf16[1,4,8,1024]{3,2,1,0:T(8,128)(2,1)S(1)} %get-tuple-element.3), channel_id=1, source_target_pairs={{1,0},{3,2},{5,4},{7,6},{9,8},{11,10},{13,12},{15,14},{17,16},{19,... | collective-permute-start | bytes 196616 | tf_op jit(solution)/shard_map/ppermute | solution.py:246
  5.2 1.8 %copy-start.2 = (bf16[1,4,8,1024]{3,2,1,0:T(8,128)(2,1)}, bf16[1,4,8,1024]{3,2,1,0:T(8,128)(2,1)S(1)}, u32[]{:S(2)}) copy-start(bf16[1,4,8,1024]{3,2,1,0:T(8,128)(2,1)S(1)} %collective-permute-done.low_ref) | copy-start | bytes 196612
  7.0 0.6 copy-start.3
  21.0 6.8 %copy-start.1 = (s32[8,8,8]{2,1,0:T(8,128)S(1)}, s32[8,8,8]{2,1,0:T(8,128)}, u32[]{:S(2)}) copy-start(s32[8,8,8]{2,1,0:T(8,128)} %param.9) | copy-start | bytes 6148
  21.0 6.9 %copy-start.7 = (f32[8,8,1]{0,1,2:T(8,128)S(1)}, f32[8,8,1]{0,1,2:T(8,128)}, u32[]{:S(2)}) copy-start(f32[8,8,1]{0,1,2:T(8,128)} %constant.36) | copy-start | bytes 772
  21.0 7.2 %copy-start.4 = (f32[8,8,1,1]{1,0,3,2:T(8,128)S(1)}, f32[8,8,1,1]{1,0,3,2:T(8,128)}, u32[]{:S(2)}) copy-start(f32[8,8,1,1]{1,0,3,2:T(8,128)} %constant.35) | copy-start | bytes 772
  21.0 7.2 %copy-start.5 = (f32[8,8]{0,1:T(8,128)S(1)}, f32[8,8]{0,1:T(8,128)}, u32[]{:S(2)}) copy-start(f32[8,8]{0,1:T(8,128)} %constant.34) | copy-start | bytes 772
  21.0 7.2 %copy-start.6 = (f32[8,8]{0,1:T(8,128)S(1)}, f32[8,8]{0,1:T(8,128)}, u32[]{:S(2)}) copy-start(f32[8,8]{0,1:T(8,128)} %constant.21.clone) | copy-start | bytes 772
  21.1 69.4 %all-to-all-start = ((bf16[8,1,4,336,128]{4,3,2,1,0:T(8,128)(2,1)}), bf16[8,1,4,336,128]{4,3,2,1,0:T(8,128)(2,1)S(1)}, u32[]{:S(2)}, u32[]{:S(2)}) async-start(bf16[8,1,4,336,128]{4,3,2,1,0:T(8,128)(2,1)} %shard_map.94), calls=%async_computation | async-start | bytes 5505024 | tf_op jit(solution)/shard_map/all_to_all | solution.py:249
  90.5 1.5 %copy-start = (bf16[8,1,4,336,128]{4,3,2,1,0:T(8,128)(2,1)}, bf16[8,1,4,336,128]{4,3,2,1,0:T(8,128)(2,1)S(1)}, u32[]{:S(2)}) copy-start(bf16[8,1,4,336,128]{4,3,2,1,0:T(8,128)(2,1)S(1)} %all-to-all-done) | copy-start | bytes 8257540

commit v16 on v15

--- a/solution.py
+++ b/solution.py
@@ -173,7 +173,6 @@
     dates, bands, rows, width = out_ref.shape
     tiles = width // 128
     span = width // mask_cols
-    section_ref[...] = got_ref[:, :, start : start + tiles * piece, :].astype(jnp.float32)
     parts = split_two(coeff_ref[...])
     m_at = lax.broadcasted_iota(jnp.int32, (128, 128), 0)
     lane = lax.broadcasted_iota(jnp.int32, (128, 128), 1)
@@ -187,7 +186,7 @@
         def one_block(r, carry):
             r0 = pl.multiple_of(r * step, step)
             values = [
-                [section_ref[u, band, pl.ds(j * piece + r0, step), :] for band in range(bands)]
+                [got_ref[u, band, pl.ds(start + j * piece + r0, step), :].astype(jnp.float32) for band in range(bands)]
                 for u in range(dates)
             ]
             for t in range(dates):

time: 107 us -> 106 us (level)
  no operation moved by 1% of the time
where the time goes in v16:
time: 106 us
  waiting for transfers between devices  60.5 us (57%)
  Pallas kernels  27.2 us (26%)
  starting transfers between devices  10.5 us (10%)
  local copies, waits for them, and re-layouts  6.22 us (6%)
    all_to_all x1, waiting for transfers between devices, local(): lax.all_to_all(packed, 'date', split_axis=0, concat_axis=0, tiled=True)  58.7 us
    pallas_call x1, Pallas kernels, smooth_all(): pl.pallas_call(functools.partial(smooth_kernel, mask_cols, pieces), in_sp...  13.8 us
    pallas_call x1, Pallas kernels, pyramid(): pl.pallas_call(functools.partial(pyramid_kernel, ndate, total_rows), grid...  13.4 us
    all_to_all x1, starting transfers between devices, local(): lax.all_to_all(packed, 'date', split_axis=0, concat_axis=0, tiled=True)  6.81 us
    pad x3, local copies, waits for them, and re-layouts, smooth_all(): flat.append(jnp.pad(grown, ((0, 0), (0, 128 - mask_cols))))  2.62 us
    ppermute x1, starting transfers between devices, local(): low = lax.ppermute(scenes[:, :, rows - 8:], 'row', forward)  2.36 us
    unnamed x16, local copies, waits for them, and re-layouts  2.19 us
  transfers between devices with their start and end apart: 3, of which 2 were waited for; matrix products, arithmetic and copies ran while one was open for 4% of the time, Pallas kernels for 0%

profile of v16, /device:TPU:0, one launch (start us, length us, event | category | flops | bytes accessed | tf_op | source)
XLA Modules:
  0.0 105.8 jit_solution(4247890904984370419)
XLA Ops:
  0.6 0.9 fusion.12
  1.5 2.4 %collective-permute-start = (bf16[1,4,8,1024]{3,2,1,0:T(8,128)(2,1)S(1)}, bf16[1,4,8,1024]{3,2,1,0:T(8,128)(2,1)S(1)}, u32[]{:S(2)}, u32[]{:S(2)}) collective-permute-start(bf16[1,4,8,1024]{3,2,1,0:T(8,128)(2,1)S(1)} %get-tuple-element.4), channel_id=1, source_target_pairs={{0,1},{2,3},{4,5},{6,7},{8,9},{10,11},{12,13},{14,15},{16,17},{18,... | collective-permute-start | bytes 196616 | tf_op jit(solution)/shard_map/ppermute | solution.py:244
  3.9 1.3 %collective-permute-start.1 = (bf16[1,4,8,1024]{3,2,1,0:T(8,128)(2,1)S(1)}, bf16[1,4,8,1024]{3,2,1,0:T(8,128)(2,1)S(1)}, u32[]{:S(2)}, u32[]{:S(2)}) collective-permute-start(bf16[1,4,8,1024]{3,2,1,0:T(8,128)(2,1)S(1)} %get-tuple-element.3), channel_id=1, source_target_pairs={{1,0},{3,2},{5,4},{7,6},{9,8},{11,10},{13,12},{15,14},{17,16},{19,... | collective-permute-start | bytes 196616 | tf_op jit(solution)/shard_map/ppermute | solution.py:245
  5.2 0.0 collective-permute-done.low_ref
  5.2 0.0 copy-start.2
  5.2 1.8 %collective-permute-done.1.high_ref = bf16[1,4,8,1024]{3,2,1,0:T(8,128)(2,1)S(1)} collective-permute-done((bf16[1,4,8,1024]{3,2,1,0:T(8,128)(2,1)S(1)}, bf16[1,4,8,1024]{3,2,1,0:T(8,128)(2,1)S(1)}, u32[]{:S(2)}, u32[]{:S(2)}) %collective-permute-start.1) | collective-permute-done | bytes 65568 | tf_op jit(solution)/shard_map/ppermute | solution.py:245
  7.0 0.0 copy-start.3
  7.0 0.0 copy-done.2
  7.0 0.6 copy-done.3
  7.7 13.4 %shard_map.94 = bf16[8,1,4,336,128]{4,3,2,1,0:T(8,128)(2,1)} custom-call(f32[2,4,7]{2,1,0:T(4,128)} %taps_ref.1, s32[1]{0:T(128)} %bitcast.where_ref, bf16[1,4,8,1024]{3,2,1,0:T(8,128)(2,1)} %copy-done.2, bf16[1,4,256,1024]{3,2,1,0:T(8,128)(2,1)} %x_ref.1, bf16[1,4,8,1024]{3,2,1,0:T(8,128)(2,1)} %copy-done.3), custom_call_target="tpu_custom_call" | custom-call | tf_op jit(solution)/shard_map/pallas_call | solution.py:128
  21.0 0.0 copy-start.1
  21.0 0.0 copy-start.7
  21.0 0.0 copy-start.4
  21.0 0.0 copy-start.5
  21.0 0.0 copy-start.6
  21.1 6.8 %all-to-all-start = ((bf16[8,1,4,336,128]{4,3,2,1,0:T(8,128)(2,1)}), bf16[8,1,4,336,128]{4,3,2,1,0:T(8,128)(2,1)S(1)}, u32[]{:S(2)}, u32[]{:S(2)}) async-start(bf16[8,1,4,336,128]{4,3,2,1,0:T(8,128)(2,1)} %shard_map.94), calls=%async_computation | async-start | bytes 5505024 | tf_op jit(solution)/shard_map/all_to_all | solution.py:248
  27.9 0.0 copy-done.1
  27.9 0.0 copy-done.7
  27.9 0.2 fusion.10
  28.2 0.0 copy-done.4
  28.2 0.0 copy-done.5
  28.2 0.0 copy-done.6
  28.2 0.4 fusion
  28.6 0.1 copy.16
  28.7 0.3 broadcast_in_dim.4
  29.0 1.0 pad.12.c0_ref
  30.0 0.2 broadcast_in_dim.10
  30.2 0.8 pad.13.c1_ref
  31.0 0.7 pad.14.c2_ref
  31.8 58.7 %all-to-all-done = bf16[8,1,4,336,128]{4,3,2,1,0:T(8,128)(2,1)S(1)} async-done(((bf16[8,1,4,336,128]{4,3,2,1,0:T(8,128)(2,1)}), bf16[8,1,4,336,128]{4,3,2,1,0:T(8,128)(2,1)S(1)}, u32[]{:S(2)}, u32[]{:S(2)}) %all-to-all-start) | async-done | bytes 2752544 | tf_op jit(solution)/shard_map/all_to_all | solution.py:248
  90.5 1.5 %copy-done = bf16[8,1,4,336,128]{4,3,2,1,0:T(8,128)(2,1)} copy-done((bf16[8,1,4,336,128]{4,3,2,1,0:T(8,128)(2,1)}, bf16[8,1,4,336,128]{4,3,2,1,0:T(8,128)(2,1)S(1)}, u32[]{:S(2)}) %copy-start) | copy-done | bytes 2752536
  92.0 13.8 %shard_map.95 = (bf16[8,4,32,1024]{3,2,1,0:T(8,128)(2,1)}, bf16[8,4,16,512]{3,2,1,0:T(8,128)(2,1)}, bf16[8,4,8,256]{3,2,1,0:T(8,128)(2,1)}) custom-call(bf16[8,4,336,128]{3,2,1,0:T(8,128)(2,1)} %bitcast.11, f32[2048,128]{1,0:T(8,128)} %pad.12.c0_ref, f32[1024,128]{1,0:T(8,128)} %pad.13.c1_ref, f32[512,128]{1,0:T(8,128)} %pad.14.c2_ref), custom_call_target="tpu_custom_call" | custom-call | tf_op jit(solution)/shard_map/pallas_call | solution.py:223
  (5 shorter events, 0.0 us)
Async XLA Ops:
  1.5 3.7 %collective-permute-start = (bf16[1,4,8,1024]{3,2,1,0:T(8,128)(2,1)S(1)}, bf16[1,4,8,1024]{3,2,1,0:T(8,128)(2,1)S(1)}, u32[]{:S(2)}, u32[]{:S(2)}) collective-permute-start(bf16[1,4,8,1024]{3,2,1,0:T(8,128)(2,1)S(1)} %get-tuple-element.4), channel_id=1, source_target_pairs={{0,1},{2,3},{4,5},{6,7},{8,9},{10,11},{12,13},{14,15},{16,17},{18,... | collective-permute-start | bytes 196616 | tf_op jit(solution)/shard_map/ppermute | solution.py:244
  3.9 3.1 %collective-permute-start.1 = (bf16[1,4,8,1024]{3,2,1,0:T(8,128)(2,1)S(1)}, bf16[1,4,8,1024]{3,2,1,0:T(8,128)(2,1)S(1)}, u32[]{:S(2)}, u32[]{:S(2)}) collective-permute-start(bf16[1,4,8,1024]{3,2,1,0:T(8,128)(2,1)S(1)} %get-tuple-element.3), channel_id=1, source_target_pairs={{1,0},{3,2},{5,4},{7,6},{9,8},{11,10},{13,12},{15,14},{17,16},{19,... | collective-permute-start | bytes 196616 | tf_op jit(solution)/shard_map/ppermute | solution.py:245
  5.2 1.8 %copy-start.2 = (bf16[1,4,8,1024]{3,2,1,0:T(8,128)(2,1)}, bf16[1,4,8,1024]{3,2,1,0:T(8,128)(2,1)S(1)}, u32[]{:S(2)}) copy-start(bf16[1,4,8,1024]{3,2,1,0:T(8,128)(2,1)S(1)} %collective-permute-done.low_ref) | copy-start | bytes 196612
  7.0 0.6 copy-start.3
  21.0 6.8 %copy-start.1 = (s32[8,8,8]{2,1,0:T(8,128)S(1)}, s32[8,8,8]{2,1,0:T(8,128)}, u32[]{:S(2)}) copy-start(s32[8,8,8]{2,1,0:T(8,128)} %param.9) | copy-start | bytes 6148
  21.0 6.9 %copy-start.7 = (f32[8,8,1]{0,1,2:T(8,128)S(1)}, f32[8,8,1]{0,1,2:T(8,128)}, u32[]{:S(2)}) copy-start(f32[8,8,1]{0,1,2:T(8,128)} %constant.36) | copy-start | bytes 772
  21.0 7.2 %copy-start.4 = (f32[8,8,1,1]{1,0,3,2:T(8,128)S(1)}, f32[8,8,1,1]{1,0,3,2:T(8,128)}, u32[]{:S(2)}) copy-start(f32[8,8,1,1]{1,0,3,2:T(8,128)} %constant.35) | copy-start | bytes 772
  21.0 7.2 %copy-start.5 = (f32[8,8]{0,1:T(8,128)S(1)}, f32[8,8]{0,1:T(8,128)}, u32[]{:S(2)}) copy-start(f32[8,8]{0,1:T(8,128)} %constant.34) | copy-start | bytes 772
  21.0 7.2 %copy-start.6 = (f32[8,8]{0,1:T(8,128)S(1)}, f32[8,8]{0,1:T(8,128)}, u32[]{:S(2)}) copy-start(f32[8,8]{0,1:T(8,128)} %constant.21.clone) | copy-start | bytes 772
  21.1 69.4 %all-to-all-start = ((bf16[8,1,4,336,128]{4,3,2,1,0:T(8,128)(2,1)}), bf16[8,1,4,336,128]{4,3,2,1,0:T(8,128)(2,1)S(1)}, u32[]{:S(2)}, u32[]{:S(2)}) async-start(bf16[8,1,4,336,128]{4,3,2,1,0:T(8,128)(2,1)} %shard_map.94), calls=%async_computation | async-start | bytes 5505024 | tf_op jit(solution)/shard_map/all_to_all | solution.py:248
  90.5 1.5 %copy-start = (bf16[8,1,4,336,128]{4,3,2,1,0:T(8,128)(2,1)}, bf16[8,1,4,336,128]{4,3,2,1,0:T(8,128)(2,1)S(1)}, u32[]{:S(2)}) copy-start(bf16[8,1,4,336,128]{4,3,2,1,0:T(8,128)(2,1)S(1)} %all-to-all-done) | copy-start | bytes 8257540

commit v17 on v16

--- a/solution.py
+++ b/solution.py
@@ -198,7 +198,7 @@
                     out_ref[t, band, pl.ds(r0, step), 128 * j : 128 * (j + 1)] = acc.astype(out_ref.dtype)
             return carry
 
-        lax.fori_loop(0, rows // step, one_block, 0)
+        lax.fori_loop(0, rows // step, one_block, 0, unroll=True)
 
 
 def smooth_kernel(mask_cols, pieces, got_ref, c0_ref, c1_ref, c2_ref, o0_ref, o1_ref, o2_ref,

time: 106 us -> 100 us (0.943)
  Pallas kernels: 27.2 us -> 21.2 us
    pallas_call x1, Pallas kernels: 13.8 us -> 7.87 us  [smooth_all(): pl.pallas_call(functools.partial(smooth_kernel, mask_cols, pieces), in_sp...]
where the time goes in v17:
time: 100 us; the launch traced here: 99.9 us
  waiting for transfers between devices  60.5 us (60%)
  Pallas kernels  21.2 us (21%)
  starting transfers between devices  10.5 us (10%)
  local copies, waits for them, and re-layouts  6.22 us (6%)
    all_to_all x1, waiting for transfers between devices, local(): lax.all_to_all(packed, 'date', split_axis=0, concat_axis=0, tiled=True)  58.7 us
    pallas_call x1, Pallas kernels, pyramid(): pl.pallas_call(functools.partial(pyramid_kernel, ndate, total_rows), grid...  13.4 us
    pallas_call x1, Pallas kernels, smooth_all(): pl.pallas_call(functools.partial(smooth_kernel, mask_cols, pieces), in_sp...  7.87 us
    all_to_all x1, starting transfers between devices, local(): lax.all_to_all(packed, 'date', split_axis=0, concat_axis=0, tiled=True)  6.81 us
    pad x3, local copies, waits for them, and re-layouts, smooth_all(): flat.append(jnp.pad(grown, ((0, 0), (0, 128 - mask_cols))))  2.62 us
    ppermute x1, starting transfers between devices, local(): low = lax.ppermute(scenes[:, :, rows - 8:], 'row', forward)  2.36 us
    unnamed x16, local copies, waits for them, and re-layouts  2.19 us
  transfers between devices with their start and end apart: 3, of which 2 were waited for; matrix products, arithmetic and copies ran while one was open for 4% of the time, Pallas kernels for 0%

profile of v17, /device:TPU:0, one launch (start us, length us, event | category | flops | bytes accessed | tf_op | source)
XLA Modules:
  0.0 99.9 jit_solution(5094003526719209538)
XLA Ops:
  0.6 0.9 fusion.12
  1.5 2.4 %collective-permute-start = (bf16[1,4,8,1024]{3,2,1,0:T(8,128)(2,1)S(1)}, bf16[1,4,8,1024]{3,2,1,0:T(8,128)(2,1)S(1)}, u32[]{:S(2)}, u32[]{:S(2)}) collective-permute-start(bf16[1,4,8,1024]{3,2,1,0:T(8,128)(2,1)S(1)} %get-tuple-element.4), channel_id=1, source_target_pairs={{0,1},{2,3},{4,5},{6,7},{8,9},{10,11},{12,13},{14,15},{16,17},{18,... | collective-permute-start | bytes 196616 | tf_op jit(solution)/shard_map/ppermute | solution.py:244
  3.9 1.3 %collective-permute-start.1 = (bf16[1,4,8,1024]{3,2,1,0:T(8,128)(2,1)S(1)}, bf16[1,4,8,1024]{3,2,1,0:T(8,128)(2,1)S(1)}, u32[]{:S(2)}, u32[]{:S(2)}) collective-permute-start(bf16[1,4,8,1024]{3,2,1,0:T(8,128)(2,1)S(1)} %get-tuple-element.3), channel_id=1, source_target_pairs={{1,0},{3,2},{5,4},{7,6},{9,8},{11,10},{13,12},{15,14},{17,16},{19,... | collective-permute-start | bytes 196616 | tf_op jit(solution)/shard_map/ppermute | solution.py:245
  5.2 0.0 collective-permute-done.low_ref
  5.2 0.0 copy-start.2
  5.2 1.8 %collective-permute-done.1.high_ref = bf16[1,4,8,1024]{3,2,1,0:T(8,128)(2,1)S(1)} collective-permute-done((bf16[1,4,8,1024]{3,2,1,0:T(8,128)(2,1)S(1)}, bf16[1,4,8,1024]{3,2,1,0:T(8,128)(2,1)S(1)}, u32[]{:S(2)}, u32[]{:S(2)}) %collective-permute-start.1) | collective-permute-done | bytes 65568 | tf_op jit(solution)/shard_map/ppermute | solution.py:245
  7.0 0.0 copy-start.3
  7.0 0.0 copy-done.2
  7.0 0.6 copy-done.3
  7.7 13.4 %shard_map.94 = bf16[8,1,4,336,128]{4,3,2,1,0:T(8,128)(2,1)} custom-call(f32[2,4,7]{2,1,0:T(4,128)} %taps_ref.1, s32[1]{0:T(128)} %bitcast.where_ref, bf16[1,4,8,1024]{3,2,1,0:T(8,128)(2,1)} %copy-done.2, bf16[1,4,256,1024]{3,2,1,0:T(8,128)(2,1)} %x_ref.1, bf16[1,4,8,1024]{3,2,1,0:T(8,128)(2,1)} %copy-done.3), custom_call_target="tpu_custom_call" | custom-call | tf_op jit(solution)/shard_map/pallas_call | solution.py:128
  21.0 0.0 copy-start.7
  21.0 0.0 copy-start.4
  21.0 0.0 copy-start.5
  21.0 0.0 copy-start.6
  21.1 6.8 %all-to-all-start = ((bf16[8,1,4,336,128]{4,3,2,1,0:T(8,128)(2,1)}), bf16[8,1,4,336,128]{4,3,2,1,0:T(8,128)(2,1)S(1)}, u32[]{:S(2)}, u32[]{:S(2)}) async-start(bf16[8,1,4,336,128]{4,3,2,1,0:T(8,128)(2,1)} %shard_map.94), calls=%async_computation | async-start | bytes 5505024 | tf_op jit(solution)/shard_map/all_to_all | solution.py:248
  27.9 0.0 copy-done.1
  27.9 0.0 copy-done.7
  27.9 0.2 fusion.10
  28.2 0.0 copy-done.4
  28.2 0.0 copy-done.5
  28.2 0.0 copy-done.6
  28.2 0.4 fusion
  28.6 0.1 copy.16
  28.7 0.3 broadcast_in_dim.4
  29.0 1.0 %pad.12.c0_ref = f32[2048,128]{1,0:T(8,128)} pad(f32[2048,8]{1,0:T(8,128)S(1)} %bitcast.12, f32[]{:T(128)} %constant.20.clone.1), padding=0_0x0_120 | pad | bytes 1114116 | tf_op jit(solution)/shard_map/jit(_pad)/pad | solution.py:220
  30.0 0.2 broadcast_in_dim.10
  30.2 0.8 pad.13.c1_ref
  31.0 0.7 pad.14.c2_ref
  31.8 58.7 %all-to-all-done = bf16[8,1,4,336,128]{4,3,2,1,0:T(8,128)(2,1)S(1)} async-done(((bf16[8,1,4,336,128]{4,3,2,1,0:T(8,128)(2,1)}), bf16[8,1,4,336,128]{4,3,2,1,0:T(8,128)(2,1)S(1)}, u32[]{:S(2)}, u32[]{:S(2)}) %all-to-all-start) | async-done | bytes 2752544 | tf_op jit(solution)/shard_map/all_to_all | solution.py:248
  90.5 0.0 copy-start
  90.5 1.5 %copy-done = bf16[8,1,4,336,128]{4,3,2,1,0:T(8,128)(2,1)} copy-done((bf16[8,1,4,336,128]{4,3,2,1,0:T(8,128)(2,1)}, bf16[8,1,4,336,128]{4,3,2,1,0:T(8,128)(2,1)S(1)}, u32[]{:S(2)}) %copy-start) | copy-done | bytes 2752536
  92.0 7.9 %shard_map.95 = (bf16[8,4,32,1024]{3,2,1,0:T(8,128)(2,1)}, bf16[8,4,16,512]{3,2,1,0:T(8,128)(2,1)}, bf16[8,4,8,256]{3,2,1,0:T(8,128)(2,1)}) custom-call(bf16[8,4,336,128]{3,2,1,0:T(8,128)(2,1)} %bitcast.11, f32[2048,128]{1,0:T(8,128)} %pad.12.c0_ref, f32[1024,128]{1,0:T(8,128)} %pad.13.c1_ref, f32[512,128]{1,0:T(8,128)} %pad.14.c2_ref), custom_call_target="tpu_custom_call" | custom-call | tf_op jit(solution)/shard_map/pallas_call | solution.py:223
  (5 shorter events, 0.0 us)
Async XLA Ops:
  1.5 3.7 %collective-permute-start = (bf16[1,4,8,1024]{3,2,1,0:T(8,128)(2,1)S(1)}, bf16[1,4,8,1024]{3,2,1,0:T(8,128)(2,1)S(1)}, u32[]{:S(2)}, u32[]{:S(2)}) collective-permute-start(bf16[1,4,8,1024]{3,2,1,0:T(8,128)(2,1)S(1)} %get-tuple-element.4), channel_id=1, source_target_pairs={{0,1},{2,3},{4,5},{6,7},{8,9},{10,11},{12,13},{14,15},{16,17},{18,... | collective-permute-start | bytes 196616 | tf_op jit(solution)/shard_map/ppermute | solution.py:244
  3.9 3.1 %collective-permute-start.1 = (bf16[1,4,8,1024]{3,2,1,0:T(8,128)(2,1)S(1)}, bf16[1,4,8,1024]{3,2,1,0:T(8,128)(2,1)S(1)}, u32[]{:S(2)}, u32[]{:S(2)}) collective-permute-start(bf16[1,4,8,1024]{3,2,1,0:T(8,128)(2,1)S(1)} %get-tuple-element.3), channel_id=1, source_target_pairs={{1,0},{3,2},{5,4},{7,6},{9,8},{11,10},{13,12},{15,14},{17,16},{19,... | collective-permute-start | bytes 196616 | tf_op jit(solution)/shard_map/ppermute | solution.py:245
  5.2 1.8 %copy-start.2 = (bf16[1,4,8,1024]{3,2,1,0:T(8,128)(2,1)}, bf16[1,4,8,1024]{3,2,1,0:T(8,128)(2,1)S(1)}, u32[]{:S(2)}) copy-start(bf16[1,4,8,1024]{3,2,1,0:T(8,128)(2,1)S(1)} %collective-permute-done.low_ref) | copy-start | bytes 196612
  7.0 0.6 copy-start.3
  21.0 6.8 %copy-start.1 = (s32[8,8,8]{2,1,0:T(8,128)S(1)}, s32[8,8,8]{2,1,0:T(8,128)}, u32[]{:S(2)}) copy-start(s32[8,8,8]{2,1,0:T(8,128)} %param.9) | copy-start | bytes 6148
  21.0 6.9 %copy-start.7 = (f32[8,8,1]{0,1,2:T(8,128)S(1)}, f32[8,8,1]{0,1,2:T(8,128)}, u32[]{:S(2)}) copy-start(f32[8,8,1]{0,1,2:T(8,128)} %constant.36) | copy-start | bytes 772
  21.0 7.2 %copy-start.4 = (f32[8,8,1,1]{1,0,3,2:T(8,128)S(1)}, f32[8,8,1,1]{1,0,3,2:T(8,128)}, u32[]{:S(2)}) copy-start(f32[8,8,1,1]{1,0,3,2:T(8,128)} %constant.35) | copy-start | bytes 772
  21.0 7.2 %copy-start.5 = (f32[8,8]{0,1:T(8,128)S(1)}, f32[8,8]{0,1:T(8,128)}, u32[]{:S(2)}) copy-start(f32[8,8]{0,1:T(8,128)} %constant.34) | copy-start | bytes 772
  21.0 7.2 %copy-start.6 = (f32[8,8]{0,1:T(8,128)S(1)}, f32[8,8]{0,1:T(8,128)}, u32[]{:S(2)}) copy-start(f32[8,8]{0,1:T(8,128)} %constant.21.clone) | copy-start | bytes 772
  21.1 69.4 %all-to-all-start = ((bf16[8,1,4,336,128]{4,3,2,1,0:T(8,128)(2,1)}), bf16[8,1,4,336,128]{4,3,2,1,0:T(8,128)(2,1)S(1)}, u32[]{:S(2)}, u32[]{:S(2)}) async-start(bf16[8,1,4,336,128]{4,3,2,1,0:T(8,128)(2,1)} %shard_map.94), calls=%async_computation | async-start | bytes 5505024 | tf_op jit(solution)/shard_map/all_to_all | solution.py:248
  90.5 1.5 %copy-start = (bf16[8,1,4,336,128]{4,3,2,1,0:T(8,128)(2,1)}, bf16[8,1,4,336,128]{4,3,2,1,0:T(8,128)(2,1)S(1)}, u32[]{:S(2)}) copy-start(bf16[8,1,4,336,128]{4,3,2,1,0:T(8,128)(2,1)S(1)} %all-to-all-done) | copy-start | bytes 8257540

commit v18 on v17

--- a/solution.py
+++ b/solution.py
@@ -179,7 +179,7 @@
     for j in range(tiles):
         pick = (m_at == (128 * j + lane) // span).astype(jnp.bfloat16)
         grown = mm(parts[0], pick) + mm(parts[1], pick)
-        tiles_ref[...] = grown.reshape(tiles_ref.shape)
+        tiles_ref[j % 2] = grown.reshape(tiles_ref.shape[1:])
 
         step = min(rows, 8)
 
@@ -190,7 +190,7 @@
                 for u in range(dates)
             ]
             for t in range(dates):
-                weights = [tiles_ref[t, u, pl.ds(r0, step), :] for u in range(dates)]
+                weights = [tiles_ref[j % 2, t, u, pl.ds(r0, step), :] for u in range(dates)]
                 for band in range(bands):
                     acc = weights[0] * values[0][band]
                     for u in range(1, dates):
@@ -229,7 +229,7 @@
             pltpu.VMEM((dates, bands, (shape[3] // 128) * piece, 128), jnp.float32)
             for shape, piece in zip(shapes, pieces)
         ]
-        + [pltpu.VMEM((dates, dates, shape[2], 128), jnp.float32) for shape in shapes],
+        + [pltpu.VMEM((2, dates, dates, shape[2], 128), jnp.float32) for shape in shapes],
     )(got, *flat)
 
 

time: 100 us -> 100 us (level)
  no operation moved by 1% of the time
where the time goes in v18:
time: 100 us; the launch traced here: 99.9 us
  waiting for transfers between devices  60.5 us (60%)
  Pallas kernels  21.2 us (21%)
  starting transfers between devices  10.5 us (10%)
  local copies, waits for them, and re-layouts  6.22 us (6%)
    all_to_all x1, waiting for transfers between devices, local(): lax.all_to_all(packed, 'date', split_axis=0, concat_axis=0, tiled=True)  58.7 us
    pallas_call x1, Pallas kernels, pyramid(): pl.pallas_call(functools.partial(pyramid_kernel, ndate, total_rows), grid...  13.4 us
    pallas_call x1, Pallas kernels, smooth_all(): pl.pallas_call(functools.partial(smooth_kernel, mask_cols, pieces), in_sp...  7.87 us
    all_to_all x1, starting transfers between devices, local(): lax.all_to_all(packed, 'date', split_axis=0, concat_axis=0, tiled=True)  6.81 us
    pad x3, local copies, waits for them, and re-layouts, smooth_all(): flat.append(jnp.pad(grown, ((0, 0), (0, 128 - mask_cols))))  2.62 us
    ppermute x1, starting transfers between devices, local(): low = lax.ppermute(scenes[:, :, rows - 8:], 'row', forward)  2.36 us
    unnamed x16, local copies, waits for them, and re-layouts  2.19 us
  transfers between devices with their start and end apart: 3, of which 2 were waited for; matrix products, arithmetic and copies ran while one was open for 4% of the time, Pallas kernels for 0%

profile of v18, /device:TPU:0, one launch (start us, length us, event | category | flops | bytes accessed | tf_op | source)
XLA Modules:
  0.0 99.9 jit_solution(5094003526719209538)
XLA Ops:
  0.6 0.9 fusion.12
  1.5 2.4 %collective-permute-start = (bf16[1,4,8,1024]{3,2,1,0:T(8,128)(2,1)S(1)}, bf16[1,4,8,1024]{3,2,1,0:T(8,128)(2,1)S(1)}, u32[]{:S(2)}, u32[]{:S(2)}) collective-permute-start(bf16[1,4,8,1024]{3,2,1,0:T(8,128)(2,1)S(1)} %get-tuple-element.4), channel_id=1, source_target_pairs={{0,1},{2,3},{4,5},{6,7},{8,9},{10,11},{12,13},{14,15},{16,17},{18,... | collective-permute-start | bytes 196616 | tf_op jit(solution)/shard_map/ppermute | solution.py:244
  3.9 1.3 %collective-permute-start.1 = (bf16[1,4,8,1024]{3,2,1,0:T(8,128)(2,1)S(1)}, bf16[1,4,8,1024]{3,2,1,0:T(8,128)(2,1)S(1)}, u32[]{:S(2)}, u32[]{:S(2)}) collective-permute-start(bf16[1,4,8,1024]{3,2,1,0:T(8,128)(2,1)S(1)} %get-tuple-element.3), channel_id=1, source_target_pairs={{1,0},{3,2},{5,4},{7,6},{9,8},{11,10},{13,12},{15,14},{17,16},{19,... | collective-permute-start | bytes 196616 | tf_op jit(solution)/shard_map/ppermute | solution.py:245
  5.2 0.0 collective-permute-done.low_ref
  5.2 0.0 copy-start.2
  5.2 1.8 %collective-permute-done.1.high_ref = bf16[1,4,8,1024]{3,2,1,0:T(8,128)(2,1)S(1)} collective-permute-done((bf16[1,4,8,1024]{3,2,1,0:T(8,128)(2,1)S(1)}, bf16[1,4,8,1024]{3,2,1,0:T(8,128)(2,1)S(1)}, u32[]{:S(2)}, u32[]{:S(2)}) %collective-permute-start.1) | collective-permute-done | bytes 65568 | tf_op jit(solution)/shard_map/ppermute | solution.py:245
  7.0 0.0 copy-start.3
  7.0 0.0 copy-done.2
  7.0 0.6 copy-done.3
  7.7 13.4 %shard_map.94 = bf16[8,1,4,336,128]{4,3,2,1,0:T(8,128)(2,1)} custom-call(f32[2,4,7]{2,1,0:T(4,128)} %taps_ref.1, s32[1]{0:T(128)} %bitcast.where_ref, bf16[1,4,8,1024]{3,2,1,0:T(8,128)(2,1)} %copy-done.2, bf16[1,4,256,1024]{3,2,1,0:T(8,128)(2,1)} %x_ref.1, bf16[1,4,8,1024]{3,2,1,0:T(8,128)(2,1)} %copy-done.3), custom_call_target="tpu_custom_call" | custom-call | tf_op jit(solution)/shard_map/pallas_call | solution.py:128
  21.0 0.0 copy-start.7
  21.0 0.0 copy-start.4
  21.0 0.0 copy-start.5
  21.0 0.0 copy-start.6
  21.1 6.8 %all-to-all-start = ((bf16[8,1,4,336,128]{4,3,2,1,0:T(8,128)(2,1)}), bf16[8,1,4,336,128]{4,3,2,1,0:T(8,128)(2,1)S(1)}, u32[]{:S(2)}, u32[]{:S(2)}) async-start(bf16[8,1,4,336,128]{4,3,2,1,0:T(8,128)(2,1)} %shard_map.94), calls=%async_computation | async-start | bytes 5505024 | tf_op jit(solution)/shard_map/all_to_all | solution.py:248
  27.9 0.0 copy-done.1
  27.9 0.0 copy-done.7
  27.9 0.2 fusion.10
  28.2 0.0 copy-done.4
  28.2 0.0 copy-done.5
  28.2 0.0 copy-done.6
  28.2 0.4 fusion
  28.6 0.1 copy.16
  28.7 0.3 broadcast_in_dim.4
  29.0 1.0 %pad.12.c0_ref = f32[2048,128]{1,0:T(8,128)} pad(f32[2048,8]{1,0:T(8,128)S(1)} %bitcast.12, f32[]{:T(128)} %constant.20.clone.1), padding=0_0x0_120 | pad | bytes 1114116 | tf_op jit(solution)/shard_map/jit(_pad)/pad | solution.py:220
  30.0 0.2 broadcast_in_dim.10
  30.2 0.8 pad.13.c1_ref
  31.0 0.7 pad.14.c2_ref
  31.8 58.7 %all-to-all-done = bf16[8,1,4,336,128]{4,3,2,1,0:T(8,128)(2,1)S(1)} async-done(((bf16[8,1,4,336,128]{4,3,2,1,0:T(8,128)(2,1)}), bf16[8,1,4,336,128]{4,3,2,1,0:T(8,128)(2,1)S(1)}, u32[]{:S(2)}, u32[]{:S(2)}) %all-to-all-start) | async-done | bytes 2752544 | tf_op jit(solution)/shard_map/all_to_all | solution.py:248
  90.5 0.0 copy-start
  90.5 1.5 %copy-done = bf16[8,1,4,336,128]{4,3,2,1,0:T(8,128)(2,1)} copy-done((bf16[8,1,4,336,128]{4,3,2,1,0:T(8,128)(2,1)}, bf16[8,1,4,336,128]{4,3,2,1,0:T(8,128)(2,1)S(1)}, u32[]{:S(2)}) %copy-start) | copy-done | bytes 2752536
  92.0 7.9 %shard_map.95 = (bf16[8,4,32,1024]{3,2,1,0:T(8,128)(2,1)}, bf16[8,4,16,512]{3,2,1,0:T(8,128)(2,1)}, bf16[8,4,8,256]{3,2,1,0:T(8,128)(2,1)}) custom-call(bf16[8,4,336,128]{3,2,1,0:T(8,128)(2,1)} %bitcast.11, f32[2048,128]{1,0:T(8,128)} %pad.12.c0_ref, f32[1024,128]{1,0:T(8,128)} %pad.13.c1_ref, f32[512,128]{1,0:T(8,128)} %pad.14.c2_ref), custom_call_target="tpu_custom_call" | custom-call | tf_op jit(solution)/shard_map/pallas_call | solution.py:223
  (5 shorter events, 0.0 us)
Async XLA Ops:
  1.5 3.7 %collective-permute-start = (bf16[1,4,8,1024]{3,2,1,0:T(8,128)(2,1)S(1)}, bf16[1,4,8,1024]{3,2,1,0:T(8,128)(2,1)S(1)}, u32[]{:S(2)}, u32[]{:S(2)}) collective-permute-start(bf16[1,4,8,1024]{3,2,1,0:T(8,128)(2,1)S(1)} %get-tuple-element.4), channel_id=1, source_target_pairs={{0,1},{2,3},{4,5},{6,7},{8,9},{10,11},{12,13},{14,15},{16,17},{18,... | collective-permute-start | bytes 196616 | tf_op jit(solution)/shard_map/ppermute | solution.py:244
  3.9 3.1 %collective-permute-start.1 = (bf16[1,4,8,1024]{3,2,1,0:T(8,128)(2,1)S(1)}, bf16[1,4,8,1024]{3,2,1,0:T(8,128)(2,1)S(1)}, u32[]{:S(2)}, u32[]{:S(2)}) collective-permute-start(bf16[1,4,8,1024]{3,2,1,0:T(8,128)(2,1)S(1)} %get-tuple-element.3), channel_id=1, source_target_pairs={{1,0},{3,2},{5,4},{7,6},{9,8},{11,10},{13,12},{15,14},{17,16},{19,... | collective-permute-start | bytes 196616 | tf_op jit(solution)/shard_map/ppermute | solution.py:245
  5.2 1.8 %copy-start.2 = (bf16[1,4,8,1024]{3,2,1,0:T(8,128)(2,1)}, bf16[1,4,8,1024]{3,2,1,0:T(8,128)(2,1)S(1)}, u32[]{:S(2)}) copy-start(bf16[1,4,8,1024]{3,2,1,0:T(8,128)(2,1)S(1)} %collective-permute-done.low_ref) | copy-start | bytes 196612
  7.0 0.6 copy-start.3
  21.0 6.8 %copy-start.1 = (s32[8,8,8]{2,1,0:T(8,128)S(1)}, s32[8,8,8]{2,1,0:T(8,128)}, u32[]{:S(2)}) copy-start(s32[8,8,8]{2,1,0:T(8,128)} %param.9) | copy-start | bytes 6148
  21.0 6.9 %copy-start.7 = (f32[8,8,1]{0,1,2:T(8,128)S(1)}, f32[8,8,1]{0,1,2:T(8,128)}, u32[]{:S(2)}) copy-start(f32[8,8,1]{0,1,2:T(8,128)} %constant.36) | copy-start | bytes 772
  21.0 7.2 %copy-start.4 = (f32[8,8,1,1]{1,0,3,2:T(8,128)S(1)}, f32[8,8,1,1]{1,0,3,2:T(8,128)}, u32[]{:S(2)}) copy-start(f32[8,8,1,1]{1,0,3,2:T(8,128)} %constant.35) | copy-start | bytes 772
  21.0 7.2 %copy-start.5 = (f32[8,8]{0,1:T(8,128)S(1)}, f32[8,8]{0,1:T(8,128)}, u32[]{:S(2)}) copy-start(f32[8,8]{0,1:T(8,128)} %constant.34) | copy-start | bytes 772
  21.0 7.2 %copy-start.6 = (f32[8,8]{0,1:T(8,128)S(1)}, f32[8,8]{0,1:T(8,128)}, u32[]{:S(2)}) copy-start(f32[8,8]{0,1:T(8,128)} %constant.21.clone) | copy-start | bytes 772
  21.1 69.4 %all-to-all-start = ((bf16[8,1,4,336,128]{4,3,2,1,0:T(8,128)(2,1)}), bf16[8,1,4,336,128]{4,3,2,1,0:T(8,128)(2,1)S(1)}, u32[]{:S(2)}, u32[]{:S(2)}) async-start(bf16[8,1,4,336,128]{4,3,2,1,0:T(8,128)(2,1)} %shard_map.94), calls=%async_computation | async-start | bytes 5505024 | tf_op jit(solution)/shard_map/all_to_all | solution.py:248
  90.5 1.5 %copy-start = (bf16[8,1,4,336,128]{4,3,2,1,0:T(8,128)(2,1)}, bf16[8,1,4,336,128]{4,3,2,1,0:T(8,128)(2,1)S(1)}, u32[]{:S(2)}) copy-start(bf16[8,1,4,336,128]{4,3,2,1,0:T(8,128)(2,1)S(1)} %all-to-all-done) | copy-start | bytes 8257540
